TPU v7x, 512 devices: a whole 4x8x8 slice. The times are simulated.
512 devices in a mesh: chain: 64 (over y, z), cross: 8 (over x, core).
Axes of the slice: x: 4, y: 8, z: 8, core: 2. Of those that a mesh axis runs over, the one named last changes fastest.
Arguments:
- right_side: bfloat16 [64, 1024, 512], P('chain', 'cross'), may hold values from -6 to 6
- self_factor: bfloat16 [6, 64, 1024, 1024], P(None, 'chain', 'cross')
- lower_factor: bfloat16 [6, 64, 1024, 1024], P(None, 'chain', 'cross'), may hold values from -0.078125 to 0.078125
- upper_factor: bfloat16 [6, 64, 1024, 1024], P(None, 'chain', 'cross'), may hold values from -0.078125 to 0.078125
Outputs:
- solution: bfloat16 [64, 1024, 512], P('chain', 'cross')
All inputs are finite; a program needn't handle non-finite values.
Results may differ from a plain program's by a relative error of at most 0.014.
Values may be sent and summed in bfloat16 or wider, within the bound.
No kernel may reach another device: no remote copies, remote signals or barrier semaphores. Data moves between devices by JAX's collectives and lax.ppermute only.
A program may use at most 64 MiB of HBM per device.

v0:
```python
import jax
import jax.numpy as jnp
from jax import lax
from jax.sharding import PartitionSpec as P


def shifted(value, axis, steps):
    count = lax.axis_size(axis)
    initial, last = (max(0, -steps), min(count, count - steps))
    return lax.ppermute(value, axis, [(source, source + steps) for source in range(initial, last)])


def reach_full(piece, dist):
    lower = shifted(piece, "chain", dist)
    upper = shifted(piece, "chain", -dist)
    return (lower, upper)


def body(right_side, self_factor, lower_factor, upper_factor):
    levels = lax.axis_size("chain").bit_length() - 1
    current = right_side[0]
    for level in range(levels):
        dist = 2**level
        own_mat = self_factor[level, 0]
        low_mat = lower_factor[level, 0]
        up_mat = upper_factor[level, 0]
        whole = lax.all_gather(current, "cross", axis=0, tiled=True)
        lower, upper = reach_full(whole, dist)
        total = jnp.dot(own_mat, whole, preferred_element_type=jnp.float32)
        total = total - jnp.dot(low_mat, lower, preferred_element_type=jnp.float32)
        total = total - jnp.dot(up_mat, upper, preferred_element_type=jnp.float32)
        current = total.astype(jnp.bfloat16)
    return current[None]


def solution(mesh):
    return jax.shard_map(
        body,
        mesh=mesh,
        in_specs=(
            P("chain", "cross", None),
            P(None, "chain", "cross", None),
            P(None, "chain", "cross", None),
            P(None, "chain", "cross", None),
        ),
        out_specs=P("chain", "cross", None),
        check_vma=False,
    )
```

profile of v0, /device:TPU:1, one launch (start us, length us, event | category | flops | bytes accessed | tf_op | source)
XLA Modules:
  0.0 539.7 jit_solution(4165311589859038631)
XLA Ops:
  7.3 37.0 %all-gather.18.cloned.1.call-done = bf16[1,1024,512]{2,1,0:T(8,128)(2,1)} async-done(((bf16[1,128,512]{2,1,0:T(8,128)(2,1)}), bf16[1,1024,512]{2,1,0:T(8,128)(2,1)}) %all-gather.18.cloned.1.call-update) | async-done | bytes 1048592 | tf_op jit(solution)/shard_map/all_gather | solution.py:27
  44.3 3.2 collective-permute-start
  50.4 19.6 %collective-permute-done = bf16[1024,512]{1,0:T(8,128)(2,1)S(1)} collective-permute-done((bf16[1024,512]{1,0:T(8,128)(2,1)}, bf16[1024,512]{1,0:T(8,128)(2,1)S(1)}, u32[]{:S(2)}, u32[]{:S(2)}) %collective-permute-start) | collective-permute-done | bytes 1048608 | tf_op jit(solution)/shard_map/ppermute | solution.py:10
  70.3 3.4 collective-permute-done.1
  73.8 1.9 fusion
  75.8 30.0 %all-gather.8.cloned.1.call-done = bf16[1024,512]{1,0:T(8,128)(2,1)} async-done(((bf16[128,512]{1,0:T(8,128)(2,1)}), bf16[1024,512]{1,0:T(8,128)(2,1)}) %all-gather.8.cloned.1.call-update) | async-done | bytes 1048592 | tf_op jit(solution)/shard_map/all_gather | solution.py:27
  105.8 4.2 collective-permute-start.2
  111.4 1.7 fusion.29
  113.1 19.6 %collective-permute-done.2 = bf16[1024,512]{1,0:T(8,128)(2,1)S(1)} collective-permute-done((bf16[1024,512]{1,0:T(8,128)(2,1)}, bf16[1024,512]{1,0:T(8,128)(2,1)S(1)}, u32[]{:S(2)}, u32[]{:S(2)}) %collective-permute-start.2) | collective-permute-done | bytes 1048608 | tf_op jit(solution)/shard_map/ppermute | solution.py:10
  133.1 30.1 %collective-permute-done.3 = bf16[1024,512]{1,0:T(8,128)(2,1)S(1)} collective-permute-done((bf16[1024,512]{1,0:T(8,128)(2,1)}, bf16[1024,512]{1,0:T(8,128)(2,1)S(1)}, u32[]{:S(2)}, u32[]{:S(2)}) %collective-permute-start.3) | collective-permute-done | bytes 1048608 | tf_op jit(solution)/shard_map/ppermute | solution.py:10
  163.2 2.1 fusion.10
  165.4 25.3 %all-gather.10.cloned.1.call-done = bf16[1024,512]{0,1:T(8,128)(2,1)} async-done(((bf16[128,512]{0,1:T(8,128)(2,1)}), bf16[1024,512]{0,1:T(8,128)(2,1)}) %all-gather.10.cloned.1.call-update) | async-done | bytes 1048592 | tf_op jit(solution)/shard_map/all_gather | solution.py:27
  190.7 7.8 %collective-permute-start.4 = (bf16[1024,512]{0,1:T(8,128)(2,1)}, bf16[1024,512]{0,1:T(8,128)(2,1)S(1)}, u32[]{:S(2)}, u32[]{:S(2)}) collective-permute-start(bf16[1024,512]{0,1:T(8,128)(2,1)} %all-gather.10.cloned.1.call-done), channel_id=1, source_target_pairs={{0,32},{8,40},{16,48},{24,56},{32,64},{40,72},{48,80},{56,88},{64,... | collective-permute-start | bytes 3145736 | tf_op jit(solution)/shard_map/ppermute | solution.py:10
  199.8 1.7 fusion.25
  201.4 65.5 %collective-permute-done.4 = bf16[1024,512]{0,1:T(8,128)(2,1)S(1)} collective-permute-done((bf16[1024,512]{0,1:T(8,128)(2,1)}, bf16[1024,512]{0,1:T(8,128)(2,1)S(1)}, u32[]{:S(2)}, u32[]{:S(2)}) %collective-permute-start.4) | collective-permute-done | bytes 1048608 | tf_op jit(solution)/shard_map/ppermute | solution.py:10
  267.4 2.0 fusion.9
  269.5 54.1 %all-gather.12.cloned.1.call-done = bf16[1024,512]{0,1:T(8,128)(2,1)} async-done(((bf16[128,512]{0,1:T(8,128)(2,1)}), bf16[1024,512]{0,1:T(8,128)(2,1)}) %all-gather.12.cloned.1.call-update) | async-done | bytes 1048592 | tf_op jit(solution)/shard_map/all_gather | solution.py:27
  323.7 3.2 collective-permute-start.6
  329.8 19.5 %collective-permute-done.6 = bf16[1024,512]{0,1:T(8,128)(2,1)S(1)} collective-permute-done((bf16[1024,512]{0,1:T(8,128)(2,1)}, bf16[1024,512]{0,1:T(8,128)(2,1)S(1)}, u32[]{:S(2)}, u32[]{:S(2)}) %collective-permute-start.6) | collective-permute-done | bytes 1048608 | tf_op jit(solution)/shard_map/ppermute | solution.py:10
  349.8 3.3 collective-permute-done.7
  353.1 2.0 fusion.8
  355.2 31.2 %all-gather.14.cloned.1.call-done = bf16[1024,512]{0,1:T(8,128)(2,1)} async-done(((bf16[128,512]{0,1:T(8,128)(2,1)}), bf16[1024,512]{0,1:T(8,128)(2,1)}) %all-gather.14.cloned.1.call-update) | async-done | bytes 1048592 | tf_op jit(solution)/shard_map/all_gather | solution.py:27
  386.4 4.1 collective-permute-start.8
  391.8 1.7 fusion.17
  393.5 19.6 %collective-permute-done.8 = bf16[1024,512]{0,1:T(8,128)(2,1)S(1)} collective-permute-done((bf16[1024,512]{0,1:T(8,128)(2,1)}, bf16[1024,512]{0,1:T(8,128)(2,1)S(1)}, u32[]{:S(2)}, u32[]{:S(2)}) %collective-permute-start.8) | collective-permute-done | bytes 1048608 | tf_op jit(solution)/shard_map/ppermute | solution.py:10
  413.5 28.4 %collective-permute-done.9 = bf16[1024,512]{0,1:T(8,128)(2,1)S(1)} collective-permute-done((bf16[1024,512]{0,1:T(8,128)(2,1)}, bf16[1024,512]{0,1:T(8,128)(2,1)S(1)}, u32[]{:S(2)}, u32[]{:S(2)}) %collective-permute-start.9) | collective-permute-done | bytes 1048608 | tf_op jit(solution)/shard_map/ppermute | solution.py:10
  441.9 2.0 fusion.7
  444.0 28.5 %all-gather.16.cloned.1.call-done = bf16[1024,512]{0,1:T(8,128)(2,1)} async-done(((bf16[128,512]{0,1:T(8,128)(2,1)}), bf16[1024,512]{0,1:T(8,128)(2,1)}) %all-gather.16.cloned.1.call-update) | async-done | bytes 1048592 | tf_op jit(solution)/shard_map/all_gather | solution.py:27
  472.5 7.1 %collective-permute-start.10 = (bf16[1024,512]{0,1:T(8,128)(2,1)}, bf16[1024,512]{0,1:T(8,128)(2,1)S(1)}, u32[]{:S(2)}, u32[]{:S(2)}) collective-permute-start(bf16[1024,512]{0,1:T(8,128)(2,1)} %all-gather.16.cloned.1.call-done), channel_id=1, source_target_pairs={{0,256},{8,264},{16,272},{24,280},{32,288},{40,296},{48,304},{56,3... | collective-permute-start | bytes 3145736 | tf_op jit(solution)/shard_map/ppermute | solution.py:10
  481.0 1.7 fusion.13
  482.6 32.1 %collective-permute-done.10 = bf16[1024,512]{0,1:T(8,128)(2,1)S(1)} collective-permute-done((bf16[1024,512]{0,1:T(8,128)(2,1)}, bf16[1024,512]{0,1:T(8,128)(2,1)S(1)}, u32[]{:S(2)}, u32[]{:S(2)}) %collective-permute-start.10) | collective-permute-done | bytes 1048608 | tf_op jit(solution)/shard_map/ppermute | solution.py:10
  515.1 15.6 %collective-permute-done.11 = bf16[1024,512]{0,1:T(8,128)(2,1)S(1)} collective-permute-done((bf16[1024,512]{0,1:T(8,128)(2,1)}, bf16[1024,512]{0,1:T(8,128)(2,1)S(1)}, u32[]{:S(2)}, u32[]{:S(2)}) %collective-permute-start.11) | collective-permute-done | bytes 1048608 | tf_op jit(solution)/shard_map/ppermute | solution.py:10
  (33 shorter events, 16.8 us)
Async XLA Ops:
  6.5 63.5 %copy-start = (bf16[6,1,128,1024]{3,2,1,0:T(8,128)(2,1)S(1)}, bf16[6,1,128,1024]{3,2,1,0:T(8,128)(2,1)}, u32[]{:S(2)}) copy-start(bf16[6,1,128,1024]{3,2,1,0:T(8,128)(2,1)} %param.6) | copy-start | bytes 4718596
  6.5 37.8 %all-gather.18.cloned.1.call-start = ((), (), s32[]{:S(2)}) async-start(), calls=%async_computation.5 | async-start | bytes 1179648 | tf_op jit(solution)/shard_map/all_gather | solution.py:27
  7.3 98.6 %all-gather.8.cloned.1.call-start = ((), (), s32[]{:S(2)}) async-start(), calls=%async_computation | async-start | bytes 1179648 | tf_op jit(solution)/shard_map/all_gather | solution.py:27
  44.3 25.7 %collective-permute-start = (bf16[1024,512]{1,0:T(8,128)(2,1)}, bf16[1024,512]{1,0:T(8,128)(2,1)S(1)}, u32[]{:S(2)}, u32[]{:S(2)}) collective-permute-start(bf16[1024,512]{1,0:T(8,128)(2,1)} %bitcast.86), channel_id=1, source_target_pairs={{0,8},{8,16},{16,24},{24,32},{32,40},{40,48},{48,56},{56,64},{64,7... | collective-permute-start | bytes 3145736 | tf_op jit(solution)/shard_map/ppermute | solution.py:10
  47.5 26.3 %collective-permute-start.1 = (bf16[1024,512]{1,0:T(8,128)(2,1)}, bf16[1024,512]{1,0:T(8,128)(2,1)S(1)}, u32[]{:S(2)}, u32[]{:S(2)}) collective-permute-start(bf16[1024,512]{1,0:T(8,128)(2,1)} %bitcast.87), channel_id=1, source_target_pairs={{8,0},{16,8},{24,16},{32,24},{40,32},{48,40},{56,48},{64,56},{72,6... | collective-permute-start | bytes 3145736 | tf_op jit(solution)/shard_map/ppermute | solution.py:10
  50.4 61.0 %copy-start.1 = (bf16[6,1,128,1024]{3,2,1,0:T(8,128)(2,1)S(1)}, bf16[6,1,128,1024]{3,2,1,0:T(8,128)(2,1)}, u32[]{:S(2)}) copy-start(bf16[6,1,128,1024]{3,2,1,0:T(8,128)(2,1)} %param.5) | copy-start | bytes 4718596
  75.7 115.0 %all-gather.10.cloned.1.call-start = ((), (), s32[]{:S(2)}) async-start(), calls=%async_computation.1 | async-start | bytes 1179648 | tf_op jit(solution)/shard_map/all_gather | solution.py:27
  105.8 26.8 %collective-permute-start.2 = (bf16[1024,512]{1,0:T(8,128)(2,1)}, bf16[1024,512]{1,0:T(8,128)(2,1)S(1)}, u32[]{:S(2)}, u32[]{:S(2)}) collective-permute-start(bf16[1024,512]{1,0:T(8,128)(2,1)} %all-gather.8.cloned.1.call-done), channel_id=1, source_target_pairs={{0,16},{8,24},{16,32},{24,40},{32,48},{40,56},{48,64},{56,72},{64,... | collective-permute-start | bytes 3145736 | tf_op jit(solution)/shard_map/ppermute | solution.py:10
  110.1 53.2 %collective-permute-start.3 = (bf16[1024,512]{1,0:T(8,128)(2,1)}, bf16[1024,512]{1,0:T(8,128)(2,1)S(1)}, u32[]{:S(2)}, u32[]{:S(2)}) collective-permute-start(bf16[1024,512]{1,0:T(8,128)(2,1)} %all-gather.8.cloned.1.call-done), channel_id=1, source_target_pairs={{16,0},{24,8},{32,16},{40,24},{48,32},{56,40},{64,48},{72,56},{80,... | collective-permute-start | bytes 3145736 | tf_op jit(solution)/shard_map/ppermute | solution.py:10
  165.3 158.3 %all-gather.12.cloned.1.call-start = ((), (), s32[]{:S(2)}) async-start(), calls=%async_computation.2 | async-start | bytes 1179648 | tf_op jit(solution)/shard_map/all_gather | solution.py:27
  190.7 76.3 %collective-permute-start.4 = (bf16[1024,512]{0,1:T(8,128)(2,1)}, bf16[1024,512]{0,1:T(8,128)(2,1)S(1)}, u32[]{:S(2)}, u32[]{:S(2)}) collective-permute-start(bf16[1024,512]{0,1:T(8,128)(2,1)} %all-gather.10.cloned.1.call-done), channel_id=1, source_target_pairs={{0,32},{8,40},{16,48},{24,56},{32,64},{40,72},{48,80},{56,88},{64,... | collective-permute-start | bytes 3145736 | tf_op jit(solution)/shard_map/ppermute | solution.py:10
  198.5 69.0 %collective-permute-start.5 = (bf16[1024,512]{0,1:T(8,128)(2,1)}, bf16[1024,512]{0,1:T(8,128)(2,1)S(1)}, u32[]{:S(2)}, u32[]{:S(2)}) collective-permute-start(bf16[1024,512]{0,1:T(8,128)(2,1)} %all-gather.10.cloned.1.call-done), channel_id=1, source_target_pairs={{32,0},{40,8},{48,16},{56,24},{64,32},{72,40},{80,48},{88,56},{96,... | collective-permute-start | bytes 3145736 | tf_op jit(solution)/shard_map/ppermute | solution.py:10
  269.5 116.9 %all-gather.14.cloned.1.call-start = ((), (), s32[]{:S(2)}) async-start(), calls=%async_computation.3 | async-start | bytes 1179648 | tf_op jit(solution)/shard_map/all_gather | solution.py:27
  323.7 25.7 %collective-permute-start.6 = (bf16[1024,512]{0,1:T(8,128)(2,1)}, bf16[1024,512]{0,1:T(8,128)(2,1)S(1)}, u32[]{:S(2)}, u32[]{:S(2)}) collective-permute-start(bf16[1024,512]{0,1:T(8,128)(2,1)} %all-gather.12.cloned.1.call-done), channel_id=1, source_target_pairs={{0,64},{8,72},{16,80},{24,88},{32,96},{40,104},{48,112},{56,120},{... | collective-permute-start | bytes 3145736 | tf_op jit(solution)/shard_map/ppermute | solution.py:10
  326.8 26.3 %collective-permute-start.7 = (bf16[1024,512]{0,1:T(8,128)(2,1)}, bf16[1024,512]{0,1:T(8,128)(2,1)S(1)}, u32[]{:S(2)}, u32[]{:S(2)}) collective-permute-start(bf16[1024,512]{0,1:T(8,128)(2,1)} %all-gather.12.cloned.1.call-done), channel_id=1, source_target_pairs={{64,0},{72,8},{80,16},{88,24},{96,32},{104,40},{112,48},{120,56},{... | collective-permute-start | bytes 3145736 | tf_op jit(solution)/shard_map/ppermute | solution.py:10
  355.2 117.4 %all-gather.16.cloned.1.call-start = ((), (), s32[]{:S(2)}) async-start(), calls=%async_computation.4 | async-start | bytes 1179648 | tf_op jit(solution)/shard_map/all_gather | solution.py:27
  386.4 26.6 %collective-permute-start.8 = (bf16[1024,512]{0,1:T(8,128)(2,1)}, bf16[1024,512]{0,1:T(8,128)(2,1)S(1)}, u32[]{:S(2)}, u32[]{:S(2)}) collective-permute-start(bf16[1024,512]{0,1:T(8,128)(2,1)} %all-gather.14.cloned.1.call-done), channel_id=1, source_target_pairs={{0,128},{8,136},{16,144},{24,152},{32,160},{40,168},{48,176},{56,1... | collective-permute-start | bytes 3145736 | tf_op jit(solution)/shard_map/ppermute | solution.py:10
  390.5 51.5 %collective-permute-start.9 = (bf16[1024,512]{0,1:T(8,128)(2,1)}, bf16[1024,512]{0,1:T(8,128)(2,1)S(1)}, u32[]{:S(2)}, u32[]{:S(2)}) collective-permute-start(bf16[1024,512]{0,1:T(8,128)(2,1)} %all-gather.14.cloned.1.call-done), channel_id=1, source_target_pairs={{128,0},{136,8},{144,16},{152,24},{160,32},{168,40},{176,48},{184,... | collective-permute-start | bytes 3145736 | tf_op jit(solution)/shard_map/ppermute | solution.py:10
  472.5 42.2 %collective-permute-start.10 = (bf16[1024,512]{0,1:T(8,128)(2,1)}, bf16[1024,512]{0,1:T(8,128)(2,1)S(1)}, u32[]{:S(2)}, u32[]{:S(2)}) collective-permute-start(bf16[1024,512]{0,1:T(8,128)(2,1)} %all-gather.16.cloned.1.call-done), channel_id=1, source_target_pairs={{0,256},{8,264},{16,272},{24,280},{32,288},{40,296},{48,304},{56,3... | collective-permute-start | bytes 3145736 | tf_op jit(solution)/shard_map/ppermute | solution.py:10
  479.7 51.0 %collective-permute-start.11 = (bf16[1024,512]{0,1:T(8,128)(2,1)}, bf16[1024,512]{0,1:T(8,128)(2,1)S(1)}, u32[]{:S(2)}, u32[]{:S(2)}) collective-permute-start(bf16[1024,512]{0,1:T(8,128)(2,1)} %all-gather.16.cloned.1.call-done), channel_id=1, source_target_pairs={{256,0},{264,8},{272,16},{280,24},{288,32},{296,40},{304,48},{312,... | collective-permute-start | bytes 3145736 | tf_op jit(solution)/shard_map/ppermute | solution.py:10
Sparse Core Ops, SparseCore 0:
  9.5 34.7 all-gather.17
  75.8 29.9 all-gather.7
  165.5 25.1 all-gather.9
  269.6 53.9 all-gather.11
  355.3 31.0 all-gather.13
  444.1 28.3 all-gather.15
where the time goes:
time: 540 us
  waiting for transfers between devices  464 us (86%)
  starting transfers between devices  37.5 us (7%)
  matrix products  24.1 us (4%)
  between operations  13.7 us (3%)
    ppermute x12, waiting for transfers between devices, shifted(): lax.ppermute(value, axis, [(source, source + steps) for source in range(i...  257 us
    all_gather x6, waiting for transfers between devices, body(): whole = lax.all_gather(current, 'cross', axis=0, tiled=True)  206 us
    ppermute x12, starting transfers between devices, shifted(): lax.ppermute(value, axis, [(source, source + steps) for source in range(i...  37.3 us
    dot_general x6, matrix products, body(): total = total - jnp.dot(up_mat, upper, preferred_element_type=jnp.float32)  11.5 us
  transfers between devices with their start and end apart: 18, of which 17 were waited for; matrix products, arithmetic and copies ran while one was open for 2% of the time, Pallas kernels for 0%

commit v1 on v0

v1 whole, which is shorter than its diff:
```python
import jax
import jax.numpy as jnp
from jax import lax
from jax.sharding import PartitionSpec as P


def shifted(value, axis, steps):
    count = lax.axis_size(axis)
    initial, last = (max(0, -steps), min(count, count - steps))
    return lax.ppermute(value, axis, [(source, source + steps) for source in range(initial, last)])


def slot_sources(chips):
    del chips
    return [(0, 0), (0, 1), (-1, 0), (-1, 1), (-2, 0), (1, 1), (1, 0), (2, 1)]


def body(right_side, self_factor, lower_factor, upper_factor):
    levels = lax.axis_size("chain").bit_length() - 1
    ncross = lax.axis_size("cross")
    chips = ncross // 2
    rows = right_side.shape[1]
    cross = lax.axis_index("cross")
    chip = cross // 2
    core = cross % 2
    sign = 1 - 2 * core

    slots = slot_sources(chips)
    source = jnp.stack(
        [2 * ((chip + off * sign) % chips) + jnp.where(other == 1, 1 - core, core) for off, other in slots]
    )

    signed = jnp.stack([self_factor[:, 0], -lower_factor[:, 0], -upper_factor[:, 0]], axis=2)
    signed = signed.reshape(levels, rows, 3, ncross, rows)
    signed = jnp.take(signed, source, axis=3)
    signed = signed.transpose(0, 1, 3, 2, 4)

    swap = [(2 * c + b, 2 * c + 1 - b) for c in range(chips) for b in range(2)]
    ring = [(2 * c, 2 * ((c + 1) % chips)) for c in range(chips)] + [
        (2 * c + 1, 2 * ((c - 1) % chips) + 1) for c in range(chips)
    ]

    def part(mat, pieces):
        n = pieces.shape[0]
        return jnp.einsum(
            "ijbk,jbkr->ir",
            mat.reshape(rows, n, 3, rows),
            pieces,
            preferred_element_type=jnp.float32,
        )

    current = right_side[0]
    for level in range(levels):
        dist = 2**level
        lower = shifted(current, "chain", dist)
        upper = shifted(current, "chain", -dist)
        own = jnp.stack([current, lower, upper])
        other = lax.ppermute(own, "cross", swap)
        first = lax.ppermute(own, "cross", ring)
        second = lax.ppermute(jnp.stack([other, first]), "cross", ring)
        third = lax.ppermute(jnp.stack([first, second[0], second[1]]), "cross", swap)
        mat = signed[level].reshape(rows, ncross * 3 * rows)
        w = 3 * rows
        total = part(mat[:, : 3 * w], jnp.stack([own, other, first]))
        total = total + part(mat[:, 3 * w : 5 * w], second)
        total = total + part(mat[:, 5 * w :], third)
        current = total.astype(jnp.bfloat16)
    return current[None]


def solution(mesh):
    return jax.shard_map(
        body,
        mesh=mesh,
        in_specs=(
            P("chain", "cross", None),
            P(None, "chain", "cross", None),
            P(None, "chain", "cross", None),
            P(None, "chain", "cross", None),
        ),
        out_specs=P("chain", "cross", None),
        check_vma=False,
    )
```

time: 540 us -> 342 us (0.63)
  waiting for transfers between devices: 464 us -> 135 us
  starting transfers between devices: 37.5 us -> 130 us
  local copies, waits for them, and re-layouts: 0.78 us -> 37.1 us
  other arithmetic: 0 us -> 20.6 us
  between operations: 13.7 us -> 0.88 us
  matrix products: 24.1 us -> 16.6 us
    ppermute x12, waiting for transfers between devices: 257 us -> 46.7 us  [shifted(): lax.ppermute(value, axis, [(source, source + steps) for source in range(i...]
    all_gather x6 -> x0, waiting for transfers between devices: 206 us -> none  [body(): whole = lax.all_gather(current, 'cross', axis=0, tiled=True)]
    ppermute x0 -> x24, waiting for transfers between devices: none -> 88.7 us  [the longest x6 51.6 us: body(): second = lax.ppermute(jnp.stack([other, first]), 'cross', ring)]
    ppermute x0 -> x24, starting transfers between devices: none -> 88.1 us  [the longest x6 33.6 us: body(): lax.ppermute(jnp.stack([first, second[0], second[1]]), 'cross', swap)]
    slice x0 -> x19, local copies, waits for them, and re-layouts: none -> 18.3 us  [the longest x7 9.86 us: body(): mat = signed[level].reshape(rows, ncross * 3 * rows)]
    another operation x0 -> x19, other arithmetic: none -> 15.9 us  [the longest x11 8.67 us: body(): total = part(mat[:, :3 * w], jnp.stack([own, other, first]))]
    unnamed x4 -> x27, local copies, waits for them, and re-layouts: 0.01 us -> 7.52 us
    dot_general x18, matrix products: 24.1 us -> 16.6 us  [part(): jnp.einsum('ijbk,jbkr->ir', mat.reshape(rows, n, 3, rows), pieces, prefer...]
  transfers between devices with their start and end apart: 18 -> 36, of which waited for: 17 -> 25; matrix products, arithmetic and copies ran while one was open for 2% -> 14% of each run, Pallas kernels for 0% -> 0%
where the time goes in v1:
time: 342 us; the launch traced here: 341 us
  waiting for transfers between devices  135 us (39%)
  starting transfers between devices  130 us (38%)
  local copies, waits for them, and re-layouts  37.1 us (11%)
  other arithmetic  20.6 us (6%)
  matrix products  16.6 us (5%)
    ppermute x6, waiting for transfers between devices, body(): second = lax.ppermute(jnp.stack([other, first]), 'cross', ring)  51.6 us
    ppermute x12, waiting for transfers between devices, shifted(): lax.ppermute(value, axis, [(source, source + steps) for source in range(i...  46.7 us
    ppermute x12, starting transfers between devices, shifted(): lax.ppermute(value, axis, [(source, source + steps) for source in range(i...  41.8 us
    ppermute x6, waiting for transfers between devices, body(): first = lax.ppermute(own, 'cross', ring)  34.1 us
    ppermute x6, starting transfers between devices, body(): lax.ppermute(jnp.stack([first, second[0], second[1]]), 'cross', swap)  33.6 us
    ppermute x6, starting transfers between devices, body(): other = lax.ppermute(own, 'cross', swap)  20.3 us
    ppermute x6, starting transfers between devices, body(): second = lax.ppermute(jnp.stack([other, first]), 'cross', ring)  19.3 us
    dot_general x18, matrix products, part(): jnp.einsum('ijbk,jbkr->ir', mat.reshape(rows, n, 3, rows), pieces, prefer...  16.6 us
  transfers between devices with their start and end apart: 36, of which 25 were waited for; matrix products, arithmetic and copies ran while one was open for 14% of the time, Pallas kernels for 0%

profile of v1, /device:TPU:1, one launch (start us, length us, event | category | flops | bytes accessed | tf_op | source)
XLA Modules:
  0.0 340.5 jit_solution(13308170445339107465)
XLA Ops:
  0.0 4.8 %collective-permute-start = (bf16[128,512]{1,0:T(8,128)(2,1)}, bf16[128,512]{1,0:T(8,128)(2,1)S(1)}, u32[]{:S(2)}, u32[]{:S(2)}) collective-permute-start(bf16[128,512]{1,0:T(8,128)(2,1)} %bitcast.265), channel_id=1, source_target_pairs={{0,8},{8,16},{16,24},{24,32},{32,40},{40,48},{48,56},{56,64},{64,7... | collective-permute-start | bytes 393224 | tf_op jit(solution)/shard_map/ppermute | solution.py:10
  7.1 4.3 %collective-permute-done.1 = bf16[128,512]{1,0:T(8,128)(2,1)S(1)} collective-permute-done((bf16[128,512]{1,0:T(8,128)(2,1)}, bf16[128,512]{1,0:T(8,128)(2,1)S(1)}, u32[]{:S(2)}, u32[]{:S(2)}) %collective-permute-start.1) | collective-permute-done | bytes 131104 | tf_op jit(solution)/shard_map/ppermute | solution.py:10
  13.2 4.9 %collective-permute-start.3 = (bf16[3,128,512]{2,1,0:T(8,128)(2,1)}, bf16[3,128,512]{2,1,0:T(8,128)(2,1)S(1)}, u32[]{:S(2)}, u32[]{:S(2)}) collective-permute-start(bf16[3,128,512]{2,1,0:T(8,128)(2,1)} %get-tuple-element.44), channel_id=1, source_target_pairs={{0,2},{2,4},{4,6},{6,0},{1,7},{3,1},{5,3},{7,5},{8,10},{10,12},{12... | collective-permute-start | bytes 1179656 | tf_op jit(solution)/shard_map/ppermute | solution.py:59
  36.9 4.8 %collective-permute-start.4 = (bf16[2,3,128,512]{3,2,0,1:T(8,128)(2,1)}, bf16[2,3,128,512]{3,2,0,1:T(8,128)(2,1)}, u32[]{:S(2)}, u32[]{:S(2)}) collective-permute-start(bf16[2,3,128,512]{3,2,0,1:T(8,128)(2,1)} %pad_maximum_fusion.12), channel_id=1, source_target_pairs={{0,2},{2,4},{4,6},{6,0},{1,7},{3,1},{5,3},{7,5},{8,10},{10,12},{12... | collective-permute-start | bytes 2359304 | tf_op jit(solution)/shard_map/ppermute | solution.py:60
  44.3 5.7 %gather_fusion = bf16[8,6,128,3,128]{4,2,3,1,0:T(8,128)(2,1)} fusion(bf16[6,128,3,8,128]{4,1,3,2,0:T(8,128)(2,1)} %pad_maximum_fusion, s32[1024]{0:T(1024)S(1)} %pad_clamp_fusion), kind=kCustom, calls=%fused_computation | custom fusion | bytes 9437216 | tf_op jit(solution)/shard_map/jit(_take)/gather | solution.py:35
  69.3 6.7 %collective-permute-start.6 = (bf16[128,512]{1,0:T(8,128)(2,1)S(1)}, bf16[128,512]{1,0:T(8,128)(2,1)S(1)}, u32[]{:S(2)}, u32[]{:S(2)}) collective-permute-start(bf16[128,512]{1,0:T(8,128)(2,1)S(1)} %fusion.95), channel_id=1, source_target_pairs={{0,16},{8,24},{16,32},{24,40},{32,48},{40,56},{48,64},{56,72},{64,... | collective-permute-start | bytes 393224 | tf_op jit(solution)/shard_map/ppermute | solution.py:10
  79.0 4.7 %collective-permute-done.7 = bf16[128,512]{1,0:T(8,128)(2,1)S(1)} collective-permute-done((bf16[128,512]{1,0:T(8,128)(2,1)S(1)}, bf16[128,512]{1,0:T(8,128)(2,1)S(1)}, u32[]{:S(2)}, u32[]{:S(2)}) %collective-permute-start.7) | collective-permute-done | bytes 131104 | tf_op jit(solution)/shard_map/ppermute | solution.py:10
  83.8 4.3 %collective-permute-start.8 = (bf16[3,128,512]{2,1,0:T(8,128)(2,1)S(1)}, bf16[3,128,512]{2,1,0:T(8,128)(2,1)S(1)}, u32[]{:S(2)}, u32[]{:S(2)}) collective-permute-start(bf16[3,128,512]{2,1,0:T(8,128)(2,1)S(1)} %get-tuple-element.42), channel_id=1, source_target_pairs={{0,1},{1,0},{2,3},{3,2},{4,5},{5,4},{6,7},{7,6},{8,9},{9,8},{10,11... | collective-permute-start | bytes 1179656 | tf_op jit(solution)/shard_map/ppermute | solution.py:58
  90.4 6.6 %collective-permute-done.9 = bf16[3,128,512]{2,1,0:T(8,128)(2,1)S(1)} collective-permute-done((bf16[3,128,512]{2,1,0:T(8,128)(2,1)S(1)}, bf16[3,128,512]{2,1,0:T(8,128)(2,1)S(1)}, u32[]{:S(2)}, u32[]{:S(2)}) %collective-permute-start.9) | collective-permute-done | bytes 393248 | tf_op jit(solution)/shard_map/ppermute | solution.py:59
  100.2 9.9 %collective-permute-done.10 = bf16[2,3,128,512]{3,2,1,0:T(8,128)(2,1)S(1)} collective-permute-done((bf16[2,3,128,512]{3,2,1,0:T(8,128)(2,1)S(1)}, bf16[2,3,128,512]{3,2,1,0:T(8,128)(2,1)S(1)}, u32[]{:S(2)}, u32[]{:S(2)}) %collective-permute-start.10) | collective-permute-done | bytes 786464 | tf_op jit(solution)/shard_map/ppermute | solution.py:60
  111.3 6.0 %collective-permute-start.11 = (bf16[3,3,128,512]{3,2,1,0:T(8,128)(2,1)}, bf16[3,3,128,512]{3,2,1,0:T(8,128)(2,1)}, u32[]{:S(2)}, u32[]{:S(2)}) collective-permute-start(bf16[3,3,128,512]{3,2,1,0:T(8,128)(2,1)} %get-tuple-element.40), channel_id=1, source_target_pairs={{0,1},{1,0},{2,3},{3,2},{4,5},{5,4},{6,7},{7,6},{8,9},{9,8},{10,11... | collective-permute-start | bytes 3538952 | tf_op jit(solution)/shard_map/ppermute | solution.py:61
  124.1 6.2 %collective-permute-start.12 = (bf16[128,512]{1,0:T(8,128)(2,1)S(1)}, bf16[128,512]{1,0:T(8,128)(2,1)S(1)}, u32[]{:S(2)}, u32[]{:S(2)}) collective-permute-start(bf16[128,512]{1,0:T(8,128)(2,1)S(1)} %fusion.98), channel_id=1, source_target_pairs={{0,32},{8,40},{16,48},{24,56},{32,64},{40,72},{48,80},{56,88},{64,... | collective-permute-start | bytes 393224 | tf_op jit(solution)/shard_map/ppermute | solution.py:10
  133.2 10.0 %collective-permute-done.13 = bf16[128,512]{1,0:T(8,128)(2,1)S(1)} collective-permute-done((bf16[128,512]{1,0:T(8,128)(2,1)S(1)}, bf16[128,512]{1,0:T(8,128)(2,1)S(1)}, u32[]{:S(2)}, u32[]{:S(2)}) %collective-permute-start.13) | collective-permute-done | bytes 131104 | tf_op jit(solution)/shard_map/ppermute | solution.py:10
  143.3 3.7 %collective-permute-start.14 = (bf16[3,128,512]{2,1,0:T(8,128)(2,1)S(1)}, bf16[3,128,512]{2,1,0:T(8,128)(2,1)S(1)}, u32[]{:S(2)}, u32[]{:S(2)}) collective-permute-start(bf16[3,128,512]{2,1,0:T(8,128)(2,1)S(1)} %get-tuple-element.38), channel_id=1, source_target_pairs={{0,1},{1,0},{2,3},{3,2},{4,5},{5,4},{6,7},{7,6},{8,9},{9,8},{10,11... | collective-permute-start | bytes 1179656 | tf_op jit(solution)/shard_map/ppermute | solution.py:58
  148.9 6.9 %collective-permute-done.15 = bf16[3,128,512]{2,1,0:T(8,128)(2,1)S(1)} collective-permute-done((bf16[3,128,512]{2,1,0:T(8,128)(2,1)S(1)}, bf16[3,128,512]{2,1,0:T(8,128)(2,1)S(1)}, u32[]{:S(2)}, u32[]{:S(2)}) %collective-permute-start.15) | collective-permute-done | bytes 393248 | tf_op jit(solution)/shard_map/ppermute | solution.py:59
  158.7 10.2 %collective-permute-done.16 = bf16[2,3,128,512]{3,2,1,0:T(8,128)(2,1)S(1)} collective-permute-done((bf16[2,3,128,512]{3,2,1,0:T(8,128)(2,1)S(1)}, bf16[2,3,128,512]{3,2,1,0:T(8,128)(2,1)S(1)}, u32[]{:S(2)}, u32[]{:S(2)}) %collective-permute-start.16) | collective-permute-done | bytes 786464 | tf_op jit(solution)/shard_map/ppermute | solution.py:60
  170.3 6.0 %collective-permute-start.17 = (bf16[3,3,128,512]{3,2,1,0:T(8,128)(2,1)}, bf16[3,3,128,512]{3,2,1,0:T(8,128)(2,1)}, u32[]{:S(2)}, u32[]{:S(2)}) collective-permute-start(bf16[3,3,128,512]{3,2,1,0:T(8,128)(2,1)} %get-tuple-element.36), channel_id=1, source_target_pairs={{0,1},{1,0},{2,3},{3,2},{4,5},{5,4},{6,7},{7,6},{8,9},{9,8},{10,11... | collective-permute-start | bytes 3538952 | tf_op jit(solution)/shard_map/ppermute | solution.py:61
  183.1 4.7 %collective-permute-start.18 = (bf16[128,512]{1,0:T(8,128)(2,1)S(1)}, bf16[128,512]{1,0:T(8,128)(2,1)S(1)}, u32[]{:S(2)}, u32[]{:S(2)}) collective-permute-start(bf16[128,512]{1,0:T(8,128)(2,1)S(1)} %fusion.101), channel_id=1, source_target_pairs={{0,64},{8,72},{16,80},{24,88},{32,96},{40,104},{48,112},{56,120},{... | collective-permute-start | bytes 393224 | tf_op jit(solution)/shard_map/ppermute | solution.py:10
  190.6 3.8 %collective-permute-done.19 = bf16[128,512]{1,0:T(8,128)(2,1)S(1)} collective-permute-done((bf16[128,512]{1,0:T(8,128)(2,1)S(1)}, bf16[128,512]{1,0:T(8,128)(2,1)S(1)}, u32[]{:S(2)}, u32[]{:S(2)}) %collective-permute-start.19) | collective-permute-done | bytes 131104 | tf_op jit(solution)/shard_map/ppermute | solution.py:10
  199.5 6.9 %collective-permute-done.21 = bf16[3,128,512]{2,1,0:T(8,128)(2,1)S(1)} collective-permute-done((bf16[3,128,512]{2,1,0:T(8,128)(2,1)S(1)}, bf16[3,128,512]{2,1,0:T(8,128)(2,1)S(1)}, u32[]{:S(2)}, u32[]{:S(2)}) %collective-permute-start.21) | collective-permute-done | bytes 393248 | tf_op jit(solution)/shard_map/ppermute | solution.py:59
  209.3 10.2 %collective-permute-done.22 = bf16[2,3,128,512]{3,2,1,0:T(8,128)(2,1)S(1)} collective-permute-done((bf16[2,3,128,512]{3,2,1,0:T(8,128)(2,1)S(1)}, bf16[2,3,128,512]{3,2,1,0:T(8,128)(2,1)S(1)}, u32[]{:S(2)}, u32[]{:S(2)}) %collective-permute-start.22) | collective-permute-done | bytes 786464 | tf_op jit(solution)/shard_map/ppermute | solution.py:60
  220.7 6.2 %collective-permute-start.23 = (bf16[3,3,128,512]{3,2,1,0:T(8,128)(2,1)}, bf16[3,3,128,512]{3,2,1,0:T(8,128)(2,1)}, u32[]{:S(2)}, u32[]{:S(2)}) collective-permute-start(bf16[3,3,128,512]{3,2,1,0:T(8,128)(2,1)} %get-tuple-element.32), channel_id=1, source_target_pairs={{0,1},{1,0},{2,3},{3,2},{4,5},{5,4},{6,7},{7,6},{8,9},{9,8},{10,11... | collective-permute-start | bytes 3538952 | tf_op jit(solution)/shard_map/ppermute | solution.py:61
  232.6 7.2 %collective-permute-start.24 = (bf16[128,512]{1,0:T(8,128)(2,1)S(1)}, bf16[128,512]{1,0:T(8,128)(2,1)S(1)}, u32[]{:S(2)}, u32[]{:S(2)}) collective-permute-start(bf16[128,512]{1,0:T(8,128)(2,1)S(1)} %fusion.104), channel_id=1, source_target_pairs={{0,128},{8,136},{16,144},{24,152},{32,160},{40,168},{48,176},{56,1... | collective-permute-start | bytes 393224 | tf_op jit(solution)/shard_map/ppermute | solution.py:10
  242.7 4.7 %collective-permute-done.25 = bf16[128,512]{1,0:T(8,128)(2,1)S(1)} collective-permute-done((bf16[128,512]{1,0:T(8,128)(2,1)S(1)}, bf16[128,512]{1,0:T(8,128)(2,1)S(1)}, u32[]{:S(2)}, u32[]{:S(2)}) %collective-permute-start.25) | collective-permute-done | bytes 131104 | tf_op jit(solution)/shard_map/ppermute | solution.py:10
  252.7 6.9 %collective-permute-done.27 = bf16[3,128,512]{2,1,0:T(8,128)(2,1)S(1)} collective-permute-done((bf16[3,128,512]{2,1,0:T(8,128)(2,1)S(1)}, bf16[3,128,512]{2,1,0:T(8,128)(2,1)S(1)}, u32[]{:S(2)}, u32[]{:S(2)}) %collective-permute-start.27) | collective-permute-done | bytes 393248 | tf_op jit(solution)/shard_map/ppermute | solution.py:59
  262.5 10.2 %collective-permute-done.28 = bf16[2,3,128,512]{3,2,1,0:T(8,128)(2,1)S(1)} collective-permute-done((bf16[2,3,128,512]{3,2,1,0:T(8,128)(2,1)S(1)}, bf16[2,3,128,512]{3,2,1,0:T(8,128)(2,1)S(1)}, u32[]{:S(2)}, u32[]{:S(2)}) %collective-permute-start.28) | collective-permute-done | bytes 786464 | tf_op jit(solution)/shard_map/ppermute | solution.py:60
  274.0 6.0 %collective-permute-start.29 = (bf16[3,3,128,512]{3,2,1,0:T(8,128)(2,1)}, bf16[3,3,128,512]{3,2,1,0:T(8,128)(2,1)}, u32[]{:S(2)}, u32[]{:S(2)}) collective-permute-start(bf16[3,3,128,512]{3,2,1,0:T(8,128)(2,1)} %get-tuple-element.28), channel_id=1, source_target_pairs={{0,1},{1,0},{2,3},{3,2},{4,5},{5,4},{6,7},{7,6},{8,9},{9,8},{10,11... | collective-permute-start | bytes 3538952 | tf_op jit(solution)/shard_map/ppermute | solution.py:61
  284.8 4.4 %collective-permute-start.30 = (bf16[128,512]{1,0:T(8,128)(2,1)S(1)}, bf16[128,512]{1,0:T(8,128)(2,1)S(1)}, u32[]{:S(2)}, u32[]{:S(2)}) collective-permute-start(bf16[128,512]{1,0:T(8,128)(2,1)S(1)} %fusion.107), channel_id=1, source_target_pairs={{0,256},{8,264},{16,272},{24,280},{32,288},{40,296},{48,304},{56,3... | collective-permute-start | bytes 393224 | tf_op jit(solution)/shard_map/ppermute | solution.py:10
  291.8 10.7 %collective-permute-done.31 = bf16[128,512]{1,0:T(8,128)(2,1)S(1)} collective-permute-done((bf16[128,512]{1,0:T(8,128)(2,1)S(1)}, bf16[128,512]{1,0:T(8,128)(2,1)S(1)}, u32[]{:S(2)}, u32[]{:S(2)}) %collective-permute-start.31) | collective-permute-done | bytes 131104 | tf_op jit(solution)/shard_map/ppermute | solution.py:10
  307.7 6.9 %collective-permute-done.33 = bf16[3,128,512]{2,1,0:T(8,128)(2,1)S(1)} collective-permute-done((bf16[3,128,512]{2,1,0:T(8,128)(2,1)S(1)}, bf16[3,128,512]{2,1,0:T(8,128)(2,1)S(1)}, u32[]{:S(2)}, u32[]{:S(2)}) %collective-permute-start.33) | collective-permute-done | bytes 393248 | tf_op jit(solution)/shard_map/ppermute | solution.py:59
  317.5 10.2 %collective-permute-done.34 = bf16[2,3,128,512]{3,2,1,0:T(8,128)(2,1)S(1)} collective-permute-done((bf16[2,3,128,512]{3,2,1,0:T(8,128)(2,1)S(1)}, bf16[2,3,128,512]{3,2,1,0:T(8,128)(2,1)S(1)}, u32[]{:S(2)}, u32[]{:S(2)}) %collective-permute-start.34) | collective-permute-done | bytes 786464 | tf_op jit(solution)/shard_map/ppermute | solution.py:60
  329.0 6.0 %collective-permute-start.35 = (bf16[3,3,128,512]{3,2,1,0:T(8,128)(2,1)}, bf16[3,3,128,512]{3,2,1,0:T(8,128)(2,1)}, u32[]{:S(2)}, u32[]{:S(2)}) collective-permute-start(bf16[3,3,128,512]{3,2,1,0:T(8,128)(2,1)} %get-tuple-element.24), channel_id=1, source_target_pairs={{0,1},{1,0},{2,3},{3,2},{4,5},{5,4},{6,7},{7,6},{8,9},{9,8},{10,11... | collective-permute-start | bytes 3538952 | tf_op jit(solution)/shard_map/ppermute | solution.py:61
  (135 shorter events, 128.8 us)
Async XLA Ops:
  0.0 7.1 %collective-permute-start = (bf16[128,512]{1,0:T(8,128)(2,1)}, bf16[128,512]{1,0:T(8,128)(2,1)S(1)}, u32[]{:S(2)}, u32[]{:S(2)}) collective-permute-start(bf16[128,512]{1,0:T(8,128)(2,1)} %bitcast.265), channel_id=1, source_target_pairs={{0,8},{8,16},{16,24},{24,32},{32,40},{40,48},{48,56},{56,64},{64,7... | collective-permute-start | bytes 393224 | tf_op jit(solution)/shard_map/ppermute | solution.py:10
  4.8 6.6 %collective-permute-start.1 = (bf16[128,512]{1,0:T(8,128)(2,1)}, bf16[128,512]{1,0:T(8,128)(2,1)S(1)}, u32[]{:S(2)}, u32[]{:S(2)}) collective-permute-start(bf16[128,512]{1,0:T(8,128)(2,1)} %bitcast.266), channel_id=1, source_target_pairs={{8,0},{16,8},{24,16},{32,24},{40,32},{48,40},{56,48},{64,56},{72,6... | collective-permute-start | bytes 393224 | tf_op jit(solution)/shard_map/ppermute | solution.py:10
  13.2 21.6 %collective-permute-start.3 = (bf16[3,128,512]{2,1,0:T(8,128)(2,1)}, bf16[3,128,512]{2,1,0:T(8,128)(2,1)S(1)}, u32[]{:S(2)}, u32[]{:S(2)}) collective-permute-start(bf16[3,128,512]{2,1,0:T(8,128)(2,1)} %get-tuple-element.44), channel_id=1, source_target_pairs={{0,2},{2,4},{4,6},{6,0},{1,7},{3,1},{5,3},{7,5},{8,10},{10,12},{12... | collective-permute-start | bytes 1179656 | tf_op jit(solution)/shard_map/ppermute | solution.py:59
  18.2 16.7 %collective-permute-start.2 = (bf16[3,128,512]{2,1,0:T(8,128)(2,1)}, bf16[3,128,512]{2,1,0:T(8,128)(2,1)}, u32[]{:S(2)}, u32[]{:S(2)}) collective-permute-start(bf16[3,128,512]{2,1,0:T(8,128)(2,1)} %get-tuple-element.44), channel_id=1, source_target_pairs={{0,1},{1,0},{2,3},{3,2},{4,5},{5,4},{6,7},{7,6},{8,9},{9,8},{10,11... | collective-permute-start | bytes 1179656 | tf_op jit(solution)/shard_map/ppermute | solution.py:58
  36.9 14.1 %collective-permute-start.4 = (bf16[2,3,128,512]{3,2,0,1:T(8,128)(2,1)}, bf16[2,3,128,512]{3,2,0,1:T(8,128)(2,1)}, u32[]{:S(2)}, u32[]{:S(2)}) collective-permute-start(bf16[2,3,128,512]{3,2,0,1:T(8,128)(2,1)} %pad_maximum_fusion.12), channel_id=1, source_target_pairs={{0,2},{2,4},{4,6},{6,0},{1,7},{3,1},{5,3},{7,5},{8,10},{10,12},{12... | collective-permute-start | bytes 2359304 | tf_op jit(solution)/shard_map/ppermute | solution.py:60
  53.3 12.9 %collective-permute-start.5 = (bf16[3,3,128,512]{3,2,0,1:T(8,128)(2,1)}, bf16[3,3,128,512]{3,2,0,1:T(8,128)(2,1)}, u32[]{:S(2)}, u32[]{:S(2)}) collective-permute-start(bf16[3,3,128,512]{3,2,0,1:T(8,128)(2,1)} %pad_maximum_fusion.1), channel_id=1, source_target_pairs={{0,1},{1,0},{2,3},{3,2},{4,5},{5,4},{6,7},{7,6},{8,9},{9,8},{10,11... | collective-permute-start | bytes 3538952 | tf_op jit(solution)/shard_map/ppermute | solution.py:61
  69.3 9.6 %collective-permute-start.6 = (bf16[128,512]{1,0:T(8,128)(2,1)S(1)}, bf16[128,512]{1,0:T(8,128)(2,1)S(1)}, u32[]{:S(2)}, u32[]{:S(2)}) collective-permute-start(bf16[128,512]{1,0:T(8,128)(2,1)S(1)} %fusion.95), channel_id=1, source_target_pairs={{0,16},{8,24},{16,32},{24,40},{32,48},{40,56},{48,64},{56,72},{64,... | collective-permute-start | bytes 393224 | tf_op jit(solution)/shard_map/ppermute | solution.py:10
  76.1 7.6 %collective-permute-start.7 = (bf16[128,512]{1,0:T(8,128)(2,1)S(1)}, bf16[128,512]{1,0:T(8,128)(2,1)S(1)}, u32[]{:S(2)}, u32[]{:S(2)}) collective-permute-start(bf16[128,512]{1,0:T(8,128)(2,1)S(1)} %fusion.95), channel_id=1, source_target_pairs={{16,0},{24,8},{32,16},{40,24},{48,32},{56,40},{64,48},{72,56},{80,... | collective-permute-start | bytes 393224 | tf_op jit(solution)/shard_map/ppermute | solution.py:10
  83.8 6.6 %collective-permute-start.8 = (bf16[3,128,512]{2,1,0:T(8,128)(2,1)S(1)}, bf16[3,128,512]{2,1,0:T(8,128)(2,1)S(1)}, u32[]{:S(2)}, u32[]{:S(2)}) collective-permute-start(bf16[3,128,512]{2,1,0:T(8,128)(2,1)S(1)} %get-tuple-element.42), channel_id=1, source_target_pairs={{0,1},{1,0},{2,3},{3,2},{4,5},{5,4},{6,7},{7,6},{8,9},{9,8},{10,11... | collective-permute-start | bytes 1179656 | tf_op jit(solution)/shard_map/ppermute | solution.py:58
  88.1 8.8 %collective-permute-start.9 = (bf16[3,128,512]{2,1,0:T(8,128)(2,1)S(1)}, bf16[3,128,512]{2,1,0:T(8,128)(2,1)S(1)}, u32[]{:S(2)}, u32[]{:S(2)}) collective-permute-start(bf16[3,128,512]{2,1,0:T(8,128)(2,1)S(1)} %get-tuple-element.42), channel_id=1, source_target_pairs={{0,2},{2,4},{4,6},{6,0},{1,7},{3,1},{5,3},{7,5},{8,10},{10,12},{12... | collective-permute-start | bytes 1179656 | tf_op jit(solution)/shard_map/ppermute | solution.py:59
  97.0 13.0 %collective-permute-start.10 = (bf16[2,3,128,512]{3,2,1,0:T(8,128)(2,1)S(1)}, bf16[2,3,128,512]{3,2,1,0:T(8,128)(2,1)S(1)}, u32[]{:S(2)}, u32[]{:S(2)}) collective-permute-start(bf16[2,3,128,512]{3,2,1,0:T(8,128)(2,1)S(1)} %pad_maximum_fusion.13), channel_id=1, source_target_pairs={{0,2},{2,4},{4,6},{6,0},{1,7},{3,1},{5,3},{7,5},{8,10},{10,12},{12... | collective-permute-start | bytes 2359304 | tf_op jit(solution)/shard_map/ppermute | solution.py:60
  111.3 10.8 %collective-permute-start.11 = (bf16[3,3,128,512]{3,2,1,0:T(8,128)(2,1)}, bf16[3,3,128,512]{3,2,1,0:T(8,128)(2,1)}, u32[]{:S(2)}, u32[]{:S(2)}) collective-permute-start(bf16[3,3,128,512]{3,2,1,0:T(8,128)(2,1)} %get-tuple-element.40), channel_id=1, source_target_pairs={{0,1},{1,0},{2,3},{3,2},{4,5},{5,4},{6,7},{7,6},{8,9},{9,8},{10,11... | collective-permute-start | bytes 3538952 | tf_op jit(solution)/shard_map/ppermute | solution.py:61
  124.1 9.1 %collective-permute-start.12 = (bf16[128,512]{1,0:T(8,128)(2,1)S(1)}, bf16[128,512]{1,0:T(8,128)(2,1)S(1)}, u32[]{:S(2)}, u32[]{:S(2)}) collective-permute-start(bf16[128,512]{1,0:T(8,128)(2,1)S(1)} %fusion.98), channel_id=1, source_target_pairs={{0,32},{8,40},{16,48},{24,56},{32,64},{40,72},{48,80},{56,88},{64,... | collective-permute-start | bytes 393224 | tf_op jit(solution)/shard_map/ppermute | solution.py:10
  130.4 12.9 %collective-permute-start.13 = (bf16[128,512]{1,0:T(8,128)(2,1)S(1)}, bf16[128,512]{1,0:T(8,128)(2,1)S(1)}, u32[]{:S(2)}, u32[]{:S(2)}) collective-permute-start(bf16[128,512]{1,0:T(8,128)(2,1)S(1)} %fusion.98), channel_id=1, source_target_pairs={{32,0},{40,8},{48,16},{56,24},{64,32},{72,40},{80,48},{88,56},{96,... | collective-permute-start | bytes 393224 | tf_op jit(solution)/shard_map/ppermute | solution.py:10
  147.0 8.8 %collective-permute-start.15 = (bf16[3,128,512]{2,1,0:T(8,128)(2,1)S(1)}, bf16[3,128,512]{2,1,0:T(8,128)(2,1)S(1)}, u32[]{:S(2)}, u32[]{:S(2)}) collective-permute-start(bf16[3,128,512]{2,1,0:T(8,128)(2,1)S(1)} %get-tuple-element.38), channel_id=1, source_target_pairs={{0,2},{2,4},{4,6},{6,0},{1,7},{3,1},{5,3},{7,5},{8,10},{10,12},{12... | collective-permute-start | bytes 1179656 | tf_op jit(solution)/shard_map/ppermute | solution.py:59
  155.9 13.0 %collective-permute-start.16 = (bf16[2,3,128,512]{3,2,1,0:T(8,128)(2,1)S(1)}, bf16[2,3,128,512]{3,2,1,0:T(8,128)(2,1)S(1)}, u32[]{:S(2)}, u32[]{:S(2)}) collective-permute-start(bf16[2,3,128,512]{3,2,1,0:T(8,128)(2,1)S(1)} %pad_maximum_fusion.14), channel_id=1, source_target_pairs={{0,2},{2,4},{4,6},{6,0},{1,7},{3,1},{5,3},{7,5},{8,10},{10,12},{12... | collective-permute-start | bytes 2359304 | tf_op jit(solution)/shard_map/ppermute | solution.py:60
  170.3 10.8 %collective-permute-start.17 = (bf16[3,3,128,512]{3,2,1,0:T(8,128)(2,1)}, bf16[3,3,128,512]{3,2,1,0:T(8,128)(2,1)}, u32[]{:S(2)}, u32[]{:S(2)}) collective-permute-start(bf16[3,3,128,512]{3,2,1,0:T(8,128)(2,1)} %get-tuple-element.36), channel_id=1, source_target_pairs={{0,1},{1,0},{2,3},{3,2},{4,5},{5,4},{6,7},{7,6},{8,9},{9,8},{10,11... | collective-permute-start | bytes 3538952 | tf_op jit(solution)/shard_map/ppermute | solution.py:61
  183.1 7.6 %collective-permute-start.18 = (bf16[128,512]{1,0:T(8,128)(2,1)S(1)}, bf16[128,512]{1,0:T(8,128)(2,1)S(1)}, u32[]{:S(2)}, u32[]{:S(2)}) collective-permute-start(bf16[128,512]{1,0:T(8,128)(2,1)S(1)} %fusion.101), channel_id=1, source_target_pairs={{0,64},{8,72},{16,80},{24,88},{32,96},{40,104},{48,112},{56,120},{... | collective-permute-start | bytes 393224 | tf_op jit(solution)/shard_map/ppermute | solution.py:10
  187.7 6.7 %collective-permute-start.19 = (bf16[128,512]{1,0:T(8,128)(2,1)S(1)}, bf16[128,512]{1,0:T(8,128)(2,1)S(1)}, u32[]{:S(2)}, u32[]{:S(2)}) collective-permute-start(bf16[128,512]{1,0:T(8,128)(2,1)S(1)} %fusion.101), channel_id=1, source_target_pairs={{64,0},{72,8},{80,16},{88,24},{96,32},{104,40},{112,48},{120,56},{... | collective-permute-start | bytes 393224 | tf_op jit(solution)/shard_map/ppermute | solution.py:10
  197.5 8.8 %collective-permute-start.21 = (bf16[3,128,512]{2,1,0:T(8,128)(2,1)S(1)}, bf16[3,128,512]{2,1,0:T(8,128)(2,1)S(1)}, u32[]{:S(2)}, u32[]{:S(2)}) collective-permute-start(bf16[3,128,512]{2,1,0:T(8,128)(2,1)S(1)} %get-tuple-element.34), channel_id=1, source_target_pairs={{0,2},{2,4},{4,6},{6,0},{1,7},{3,1},{5,3},{7,5},{8,10},{10,12},{12... | collective-permute-start | bytes 1179656 | tf_op jit(solution)/shard_map/ppermute | solution.py:59
  206.4 13.0 %collective-permute-start.22 = (bf16[2,3,128,512]{3,2,1,0:T(8,128)(2,1)S(1)}, bf16[2,3,128,512]{3,2,1,0:T(8,128)(2,1)S(1)}, u32[]{:S(2)}, u32[]{:S(2)}) collective-permute-start(bf16[2,3,128,512]{3,2,1,0:T(8,128)(2,1)S(1)} %pad_maximum_fusion.15), channel_id=1, source_target_pairs={{0,2},{2,4},{4,6},{6,0},{1,7},{3,1},{5,3},{7,5},{8,10},{10,12},{12... | collective-permute-start | bytes 2359304 | tf_op jit(solution)/shard_map/ppermute | solution.py:60
  220.7 9.8 %collective-permute-start.23 = (bf16[3,3,128,512]{3,2,1,0:T(8,128)(2,1)}, bf16[3,3,128,512]{3,2,1,0:T(8,128)(2,1)}, u32[]{:S(2)}, u32[]{:S(2)}) collective-permute-start(bf16[3,3,128,512]{3,2,1,0:T(8,128)(2,1)} %get-tuple-element.32), channel_id=1, source_target_pairs={{0,1},{1,0},{2,3},{3,2},{4,5},{5,4},{6,7},{7,6},{8,9},{9,8},{10,11... | collective-permute-start | bytes 3538952 | tf_op jit(solution)/shard_map/ppermute | solution.py:61
  232.6 10.1 %collective-permute-start.24 = (bf16[128,512]{1,0:T(8,128)(2,1)S(1)}, bf16[128,512]{1,0:T(8,128)(2,1)S(1)}, u32[]{:S(2)}, u32[]{:S(2)}) collective-permute-start(bf16[128,512]{1,0:T(8,128)(2,1)S(1)} %fusion.104), channel_id=1, source_target_pairs={{0,128},{8,136},{16,144},{24,152},{32,160},{40,168},{48,176},{56,1... | collective-permute-start | bytes 393224 | tf_op jit(solution)/shard_map/ppermute | solution.py:10
  239.8 7.6 %collective-permute-start.25 = (bf16[128,512]{1,0:T(8,128)(2,1)S(1)}, bf16[128,512]{1,0:T(8,128)(2,1)S(1)}, u32[]{:S(2)}, u32[]{:S(2)}) collective-permute-start(bf16[128,512]{1,0:T(8,128)(2,1)S(1)} %fusion.104), channel_id=1, source_target_pairs={{128,0},{136,8},{144,16},{152,24},{160,32},{168,40},{176,48},{184,... | collective-permute-start | bytes 393224 | tf_op jit(solution)/shard_map/ppermute | solution.py:10
  250.8 8.8 %collective-permute-start.27 = (bf16[3,128,512]{2,1,0:T(8,128)(2,1)S(1)}, bf16[3,128,512]{2,1,0:T(8,128)(2,1)S(1)}, u32[]{:S(2)}, u32[]{:S(2)}) collective-permute-start(bf16[3,128,512]{2,1,0:T(8,128)(2,1)S(1)} %get-tuple-element.30), channel_id=1, source_target_pairs={{0,2},{2,4},{4,6},{6,0},{1,7},{3,1},{5,3},{7,5},{8,10},{10,12},{12... | collective-permute-start | bytes 1179656 | tf_op jit(solution)/shard_map/ppermute | solution.py:59
  259.7 13.0 %collective-permute-start.28 = (bf16[2,3,128,512]{3,2,1,0:T(8,128)(2,1)S(1)}, bf16[2,3,128,512]{3,2,1,0:T(8,128)(2,1)S(1)}, u32[]{:S(2)}, u32[]{:S(2)}) collective-permute-start(bf16[2,3,128,512]{3,2,1,0:T(8,128)(2,1)S(1)} %pad_maximum_fusion.16), channel_id=1, source_target_pairs={{0,2},{2,4},{4,6},{6,0},{1,7},{3,1},{5,3},{7,5},{8,10},{10,12},{12... | collective-permute-start | bytes 2359304 | tf_op jit(solution)/shard_map/ppermute | solution.py:60
  274.0 8.8 %collective-permute-start.29 = (bf16[3,3,128,512]{3,2,1,0:T(8,128)(2,1)}, bf16[3,3,128,512]{3,2,1,0:T(8,128)(2,1)}, u32[]{:S(2)}, u32[]{:S(2)}) collective-permute-start(bf16[3,3,128,512]{3,2,1,0:T(8,128)(2,1)} %get-tuple-element.28), channel_id=1, source_target_pairs={{0,1},{1,0},{2,3},{3,2},{4,5},{5,4},{6,7},{7,6},{8,9},{9,8},{10,11... | collective-permute-start | bytes 3538952 | tf_op jit(solution)/shard_map/ppermute | solution.py:61
  284.8 6.9 %collective-permute-start.30 = (bf16[128,512]{1,0:T(8,128)(2,1)S(1)}, bf16[128,512]{1,0:T(8,128)(2,1)S(1)}, u32[]{:S(2)}, u32[]{:S(2)}) collective-permute-start(bf16[128,512]{1,0:T(8,128)(2,1)S(1)} %fusion.107), channel_id=1, source_target_pairs={{0,256},{8,264},{16,272},{24,280},{32,288},{40,296},{48,304},{56,3... | collective-permute-start | bytes 393224 | tf_op jit(solution)/shard_map/ppermute | solution.py:10
  289.3 13.2 %collective-permute-start.31 = (bf16[128,512]{1,0:T(8,128)(2,1)S(1)}, bf16[128,512]{1,0:T(8,128)(2,1)S(1)}, u32[]{:S(2)}, u32[]{:S(2)}) collective-permute-start(bf16[128,512]{1,0:T(8,128)(2,1)S(1)} %fusion.107), channel_id=1, source_target_pairs={{256,0},{264,8},{272,16},{280,24},{288,32},{296,40},{304,48},{312,... | collective-permute-start | bytes 393224 | tf_op jit(solution)/shard_map/ppermute | solution.py:10
  305.8 8.8 %collective-permute-start.33 = (bf16[3,128,512]{2,1,0:T(8,128)(2,1)S(1)}, bf16[3,128,512]{2,1,0:T(8,128)(2,1)S(1)}, u32[]{:S(2)}, u32[]{:S(2)}) collective-permute-start(bf16[3,128,512]{2,1,0:T(8,128)(2,1)S(1)} %get-tuple-element.26), channel_id=1, source_target_pairs={{0,2},{2,4},{4,6},{6,0},{1,7},{3,1},{5,3},{7,5},{8,10},{10,12},{12... | collective-permute-start | bytes 1179656 | tf_op jit(solution)/shard_map/ppermute | solution.py:59
  314.7 13.0 %collective-permute-start.34 = (bf16[2,3,128,512]{3,2,1,0:T(8,128)(2,1)S(1)}, bf16[2,3,128,512]{3,2,1,0:T(8,128)(2,1)S(1)}, u32[]{:S(2)}, u32[]{:S(2)}) collective-permute-start(bf16[2,3,128,512]{3,2,1,0:T(8,128)(2,1)S(1)} %pad_maximum_fusion.17), channel_id=1, source_target_pairs={{0,2},{2,4},{4,6},{6,0},{1,7},{3,1},{5,3},{7,5},{8,10},{10,12},{12... | collective-permute-start | bytes 2359304 | tf_op jit(solution)/shard_map/ppermute | solution.py:60
  329.0 8.8 %collective-permute-start.35 = (bf16[3,3,128,512]{3,2,1,0:T(8,128)(2,1)}, bf16[3,3,128,512]{3,2,1,0:T(8,128)(2,1)}, u32[]{:S(2)}, u32[]{:S(2)}) collective-permute-start(bf16[3,3,128,512]{3,2,1,0:T(8,128)(2,1)} %get-tuple-element.24), channel_id=1, source_target_pairs={{0,1},{1,0},{2,3},{3,2},{4,5},{5,4},{6,7},{7,6},{8,9},{9,8},{10,11... | collective-permute-start | bytes 3538952 | tf_op jit(solution)/shard_map/ppermute | solution.py:61
  (16 other events, 60.5 us)

commit v2 on v0

v2 whole, which is shorter than its diff:
```python
import jax
import jax.numpy as jnp
from jax import lax
from jax.sharding import PartitionSpec as P


def shifted(value, axis, steps):
    count = lax.axis_size(axis)
    initial, last = (max(0, -steps), min(count, count - steps))
    return lax.ppermute(value, axis, [(source, source + steps) for source in range(initial, last)])


OFFSETS = (0, -1, 1, 2)


def body(right_side, self_factor, lower_factor, upper_factor):
    levels = lax.axis_size("chain").bit_length() - 1
    ncross = lax.axis_size("cross")
    chips = ncross // 2
    rows = right_side.shape[1]
    cross = lax.axis_index("cross")
    chip = cross // 2
    core = cross % 2

    def columns_for(which_core):
        return jnp.stack([2 * ((chip + off) % chips) + which_core for off in OFFSETS])

    signed = jnp.stack([self_factor[:, 0], -lower_factor[:, 0], -upper_factor[:, 0]], axis=2)
    signed = signed.reshape(levels, rows, 3, ncross, rows)

    def pick(which_core):
        part = jnp.take(signed, columns_for(which_core), axis=3)
        return part.transpose(0, 1, 3, 2, 4)

    mine = pick(core)
    swap = [(2 * c + b, 2 * c + 1 - b) for c in range(chips) for b in range(2)]
    theirs = lax.ppermute(pick(1 - core), "cross", swap)

    def same_core(offset):
        return [(2 * c + b, 2 * ((c + offset) % chips) + b) for c in range(chips) for b in range(2)]

    def partial(mat, pieces):
        total = None
        for j, piece in enumerate(pieces):
            term = jnp.einsum("ibk,bkr->ir", mat[:, j], piece, preferred_element_type=jnp.float32)
            total = term if total is None else total + term
        return total

    current = right_side[0]
    for level in range(levels):
        dist = 2**level
        lower = shifted(current, "chain", dist)
        upper = shifted(current, "chain", -dist)
        own = jnp.stack([current, lower, upper])
        pieces = [own] + [lax.ppermute(own, "cross", same_core(-off)) for off in OFFSETS[1:]]
        given = lax.ppermute(partial(theirs[level], pieces), "cross", swap)
        total = partial(mine[level], pieces) + given
        current = total.astype(jnp.bfloat16)
    return current[None]


def solution(mesh):
    return jax.shard_map(
        body,
        mesh=mesh,
        in_specs=(
            P("chain", "cross", None),
            P(None, "chain", "cross", None),
            P(None, "chain", "cross", None),
            P(None, "chain", "cross", None),
        ),
        out_specs=P("chain", "cross", None),
        check_vma=False,
    )
```

time: 540 us -> 280 us (0.52)
  waiting for transfers between devices: 464 us -> 104 us
  starting transfers between devices: 37.5 us -> 135 us
  local copies, waits for them, and re-layouts: 0.78 us -> 20.5 us
  between operations: 13.7 us -> 0.82 us
  matrix products: 24.1 us -> 11.7 us
  other arithmetic: 0 us -> 7.78 us
    ppermute x12, waiting for transfers between devices: 257 us -> 22.9 us  [shifted(): lax.ppermute(value, axis, [(source, source + steps) for source in range(i...]
    all_gather x6 -> x0, waiting for transfers between devices: 206 us -> none  [body(): whole = lax.all_gather(current, 'cross', axis=0, tiled=True)]
    ppermute x0 -> x25, waiting for transfers between devices: none -> 80.8 us  [the longest x18 77.9 us: body(): lax.ppermute(own, 'cross', same_core(-off))]
    ppermute x0 -> x25, starting transfers between devices: none -> 77.6 us  [the longest x18 50.3 us: body(): lax.ppermute(own, 'cross', same_core(-off))]
    ppermute x12, starting transfers between devices: 37.3 us -> 56.9 us  [shifted(): lax.ppermute(value, axis, [(source, source + steps) for source in range(i...]
    dot_general x18 -> x48, matrix products: 24.1 us -> 11.7 us  [partial(): jnp.einsum('ibk,bkr->ir', mat[:, j], piece, preferred_element_type=jnp.fl...]
    gather x0 -> x2, local copies, waits for them, and re-layouts: none -> 6.67 us  [pick(): part = jnp.take(signed, columns_for(which_core), axis=3)]
    unnamed x4 -> x5, local copies, waits for them, and re-layouts: 0.01 us -> 6.42 us
  transfers between devices with their start and end apart: 18 -> 37, of which waited for: 17 -> 30; matrix products, arithmetic and copies ran while one was open for 2% -> 4% of each run, Pallas kernels for 0% -> 0%
where the time goes in v2:
time: 280 us; the launch traced here: 279 us
  starting transfers between devices  135 us (48%)
  waiting for transfers between devices  104 us (37%)
  local copies, waits for them, and re-layouts  20.5 us (7%)
  matrix products  11.7 us (4%)
  other arithmetic  7.78 us (3%)
    ppermute x18, waiting for transfers between devices, body(): lax.ppermute(own, 'cross', same_core(-off))  77.9 us
    ppermute x12, starting transfers between devices, shifted(): lax.ppermute(value, axis, [(source, source + steps) for source in range(i...  56.9 us
    ppermute x18, starting transfers between devices, body(): lax.ppermute(own, 'cross', same_core(-off))  50.3 us
    ppermute x12, waiting for transfers between devices, shifted(): lax.ppermute(value, axis, [(source, source + steps) for source in range(i...  22.9 us
    ppermute x6, starting transfers between devices, body(): given = lax.ppermute(partial(theirs[level], pieces), 'cross', swap)  18.5 us
    dot_general x48, matrix products, partial(): jnp.einsum('ibk,bkr->ir', mat[:, j], piece, preferred_element_type=jnp.fl...  11.7 us
    ppermute x1, starting transfers between devices, body(): theirs = lax.ppermute(pick(1 - core), 'cross', swap)  8.78 us
    gather x2, local copies, waits for them, and re-layouts, pick(): part = jnp.take(signed, columns_for(which_core), axis=3)  6.67 us
  transfers between devices with their start and end apart: 37, of which 30 were waited for; matrix products, arithmetic and copies ran while one was open for 4% of the time, Pallas kernels for 0%

profile of v2, /device:TPU:1, one launch (start us, length us, event | category | flops | bytes accessed | tf_op | source)
XLA Modules:
  0.0 279.2 jit_solution(18333980911287312295)
XLA Ops:
  13.8 3.5 %pad_maximum_fusion = bf16[6,128,3,8,128]{4,1,3,2,0:T(8,128)(2,1)} fusion(bf16[6,128,1,8,128]{4,1,3,2,0:T(8,128)(2,1)S(1)} %copy.12, bf16[6,128,1,8,128]{4,1,3,2,0:T(8,128)(2,1)S(1)} %copy.11, bf16[6,128,1,8,128]{4,1,3,2,0:T(8,128)(2,1)} %copy.10), kind=kLoop, calls=%fused_computation.2 | loop fusion | flops 4718592 | bytes 9437184 | tf_op jit(solution)/shard_map/stack | solution.py:28
  22.4 8.8 %collective-permute-start.5 = (bf16[6,128,4,3,128]{4,1,3,2,0:T(8,128)(2,1)}, bf16[6,128,4,3,128]{4,1,3,2,0:T(8,128)(2,1)}, u32[]{:S(2)}, u32[]{:S(2)}) collective-permute-start(bf16[6,128,4,3,128]{4,1,3,2,0:T(8,128)(2,1)} %fusion), channel_id=1, source_target_pairs={{0,1},{1,0},{2,3},{3,2},{4,5},{5,4},{6,7},{7,6},{8,9},{9,8},{10,11... | collective-permute-start | bytes 7077896 | tf_op jit(solution)/shard_map/ppermute | solution.py:37
  32.5 4.0 %collective-permute-start = (bf16[128,512]{1,0:T(8,128)(2,1)S(1)}, bf16[128,512]{1,0:T(8,128)(2,1)S(1)}, u32[]{:S(2)}, u32[]{:S(2)}) collective-permute-start(bf16[128,512]{1,0:T(8,128)(2,1)S(1)} %bitcast.456), channel_id=1, source_target_pairs={{0,8},{8,16},{16,24},{24,32},{32,40},{40,48},{48,56},{56,64},{64,7... | collective-permute-start | bytes 393224 | tf_op jit(solution)/shard_map/ppermute | solution.py:10
  47.8 5.7 %collective-permute-done.4 = bf16[3,128,512]{2,1,0:T(8,128)(2,1)S(1)} collective-permute-done((bf16[3,128,512]{2,1,0:T(8,128)(2,1)S(1)}, bf16[3,128,512]{2,1,0:T(8,128)(2,1)S(1)}, u32[]{:S(2)}, u32[]{:S(2)}) %collective-permute-start.4) | collective-permute-done | bytes 393248 | tf_op jit(solution)/shard_map/ppermute | solution.py:55
  57.9 5.0 %collective-permute-done.2 = bf16[3,128,512]{2,1,0:T(8,128)(2,1)S(1)} collective-permute-done((bf16[3,128,512]{2,1,0:T(8,128)(2,1)S(1)}, bf16[3,128,512]{2,1,0:T(8,128)(2,1)S(1)}, u32[]{:S(2)}, u32[]{:S(2)}) %collective-permute-start.2) | collective-permute-done | bytes 393248 | tf_op jit(solution)/shard_map/ppermute | solution.py:55
  68.4 4.9 %collective-permute-start.7 = (bf16[128,512]{1,0:T(8,128)(2,1)S(1)}, bf16[128,512]{1,0:T(8,128)(2,1)S(1)}, u32[]{:S(2)}, u32[]{:S(2)}) collective-permute-start(bf16[128,512]{1,0:T(8,128)(2,1)S(1)} %fusion.49), channel_id=1, source_target_pairs={{0,16},{8,24},{16,32},{24,40},{32,48},{40,56},{48,64},{56,72},{64,... | collective-permute-start | bytes 393224 | tf_op jit(solution)/shard_map/ppermute | solution.py:10
  80.3 3.4 %collective-permute-start.9 = (bf16[3,128,512]{2,1,0:T(8,128)(2,1)S(1)}, bf16[3,128,512]{2,1,0:T(8,128)(2,1)S(1)}, u32[]{:S(2)}, u32[]{:S(2)}) collective-permute-start(bf16[3,128,512]{2,1,0:T(8,128)(2,1)S(1)} %pad_maximum_fusion.2), channel_id=1, source_target_pairs={{0,2},{1,3},{2,4},{3,5},{4,6},{5,7},{6,0},{7,1},{8,10},{9,11},{10,... | collective-permute-start | bytes 1179656 | tf_op jit(solution)/shard_map/ppermute | solution.py:55
  83.7 4.5 %collective-permute-done.11 = bf16[3,128,512]{2,1,0:T(8,128)(2,1)S(1)} collective-permute-done((bf16[3,128,512]{2,1,0:T(8,128)(2,1)S(1)}, bf16[3,128,512]{2,1,0:T(8,128)(2,1)S(1)}, u32[]{:S(2)}, u32[]{:S(2)}) %collective-permute-start.11) | collective-permute-done | bytes 393248 | tf_op jit(solution)/shard_map/ppermute | solution.py:55
  88.5 6.9 %collective-permute-done.10 = bf16[3,128,512]{2,1,0:T(8,128)(2,1)S(1)} collective-permute-done((bf16[3,128,512]{2,1,0:T(8,128)(2,1)S(1)}, bf16[3,128,512]{2,1,0:T(8,128)(2,1)S(1)}, u32[]{:S(2)}, u32[]{:S(2)}) %collective-permute-start.10) | collective-permute-done | bytes 393248 | tf_op jit(solution)/shard_map/ppermute | solution.py:55
  104.9 12.6 %collective-permute-start.13 = (bf16[128,512]{1,0:T(8,128)(2,1)S(1)}, bf16[128,512]{1,0:T(8,128)(2,1)S(1)}, u32[]{:S(2)}, u32[]{:S(2)}) collective-permute-start(bf16[128,512]{1,0:T(8,128)(2,1)S(1)} %fusion.48), channel_id=1, source_target_pairs={{0,32},{8,40},{16,48},{24,56},{32,64},{40,72},{48,80},{56,88},{64,... | collective-permute-start | bytes 393224 | tf_op jit(solution)/shard_map/ppermute | solution.py:10
  119.2 6.2 %collective-permute-done.13 = bf16[128,512]{1,0:T(8,128)(2,1)S(1)} collective-permute-done((bf16[128,512]{1,0:T(8,128)(2,1)S(1)}, bf16[128,512]{1,0:T(8,128)(2,1)S(1)}, u32[]{:S(2)}, u32[]{:S(2)}) %collective-permute-start.13) | collective-permute-done | bytes 131104 | tf_op jit(solution)/shard_map/ppermute | solution.py:10
  125.4 3.7 %collective-permute-start.17 = (bf16[3,128,512]{2,1,0:T(8,128)(2,1)S(1)}, bf16[3,128,512]{2,1,0:T(8,128)(2,1)S(1)}, u32[]{:S(2)}, u32[]{:S(2)}) collective-permute-start(bf16[3,128,512]{2,1,0:T(8,128)(2,1)S(1)} %pad_maximum_fusion.3), channel_id=1, source_target_pairs={{0,4},{1,5},{2,6},{3,7},{4,0},{5,1},{6,2},{7,3},{8,12},{9,13},{10,... | collective-permute-start | bytes 1179656 | tf_op jit(solution)/shard_map/ppermute | solution.py:55
  134.5 4.6 %collective-permute-done.17 = bf16[3,128,512]{2,1,0:T(8,128)(2,1)S(1)} collective-permute-done((bf16[3,128,512]{2,1,0:T(8,128)(2,1)S(1)}, bf16[3,128,512]{2,1,0:T(8,128)(2,1)S(1)}, u32[]{:S(2)}, u32[]{:S(2)}) %collective-permute-start.17) | collective-permute-done | bytes 393248 | tf_op jit(solution)/shard_map/ppermute | solution.py:55
  139.3 8.2 %collective-permute-done.16 = bf16[3,128,512]{2,1,0:T(8,128)(2,1)S(1)} collective-permute-done((bf16[3,128,512]{2,1,0:T(8,128)(2,1)S(1)}, bf16[3,128,512]{2,1,0:T(8,128)(2,1)S(1)}, u32[]{:S(2)}, u32[]{:S(2)}) %collective-permute-start.16) | collective-permute-done | bytes 393248 | tf_op jit(solution)/shard_map/ppermute | solution.py:55
  154.2 11.5 %collective-permute-start.19 = (bf16[128,512]{1,0:T(8,128)(2,1)S(1)}, bf16[128,512]{1,0:T(8,128)(2,1)S(1)}, u32[]{:S(2)}, u32[]{:S(2)}) collective-permute-start(bf16[128,512]{1,0:T(8,128)(2,1)S(1)} %fusion.47), channel_id=1, source_target_pairs={{0,64},{8,72},{16,80},{24,88},{32,96},{40,104},{48,112},{56,120},{... | collective-permute-start | bytes 393224 | tf_op jit(solution)/shard_map/ppermute | solution.py:10
  168.2 3.8 %collective-permute-start.23 = (bf16[3,128,512]{2,1,0:T(8,128)(2,1)S(1)}, bf16[3,128,512]{2,1,0:T(8,128)(2,1)S(1)}, u32[]{:S(2)}, u32[]{:S(2)}) collective-permute-start(bf16[3,128,512]{2,1,0:T(8,128)(2,1)S(1)} %pad_maximum_fusion.4), channel_id=1, source_target_pairs={{0,4},{1,5},{2,6},{3,7},{4,0},{5,1},{6,2},{7,3},{8,12},{9,13},{10,... | collective-permute-start | bytes 1179656 | tf_op jit(solution)/shard_map/ppermute | solution.py:55
  172.0 3.5 %collective-permute-start.22 = (bf16[3,128,512]{2,1,0:T(8,128)(2,1)S(1)}, bf16[3,128,512]{2,1,0:T(8,128)(2,1)S(1)}, u32[]{:S(2)}, u32[]{:S(2)}) collective-permute-start(bf16[3,128,512]{2,1,0:T(8,128)(2,1)S(1)} %pad_maximum_fusion.4), channel_id=1, source_target_pairs={{0,6},{1,7},{2,0},{3,1},{4,2},{5,3},{6,4},{7,5},{8,14},{9,15},{10,... | collective-permute-start | bytes 1179656 | tf_op jit(solution)/shard_map/ppermute | solution.py:55
  177.5 3.6 %collective-permute-done.23 = bf16[3,128,512]{2,1,0:T(8,128)(2,1)S(1)} collective-permute-done((bf16[3,128,512]{2,1,0:T(8,128)(2,1)S(1)}, bf16[3,128,512]{2,1,0:T(8,128)(2,1)S(1)}, u32[]{:S(2)}, u32[]{:S(2)}) %collective-permute-start.23) | collective-permute-done | bytes 393248 | tf_op jit(solution)/shard_map/ppermute | solution.py:55
  181.3 8.8 %collective-permute-done.22 = bf16[3,128,512]{2,1,0:T(8,128)(2,1)S(1)} collective-permute-done((bf16[3,128,512]{2,1,0:T(8,128)(2,1)S(1)}, bf16[3,128,512]{2,1,0:T(8,128)(2,1)S(1)}, u32[]{:S(2)}, u32[]{:S(2)}) %collective-permute-start.22) | collective-permute-done | bytes 393248 | tf_op jit(solution)/shard_map/ppermute | solution.py:55
  190.8 3.5 %collective-permute-start.24 = (f32[128,512]{1,0:T(8,128)S(1)}, f32[128,512]{1,0:T(8,128)S(1)}, u32[]{:S(2)}, u32[]{:S(2)}) collective-permute-start(f32[128,512]{1,0:T(8,128)S(1)} %fusion.29), channel_id=1, source_target_pairs={{0,1},{1,0},{2,3},{3,2},{4,5},{5,4},{6,7},{7,6},{8,9},{9,8},{10,11... | collective-permute-start | bytes 786440 | tf_op jit(solution)/shard_map/ppermute | solution.py:56
  196.9 5.7 %collective-permute-start.25 = (bf16[128,512]{1,0:T(8,128)(2,1)S(1)}, bf16[128,512]{1,0:T(8,128)(2,1)S(1)}, u32[]{:S(2)}, u32[]{:S(2)}) collective-permute-start(bf16[128,512]{1,0:T(8,128)(2,1)S(1)} %fusion.46), channel_id=1, source_target_pairs={{0,128},{8,136},{16,144},{24,152},{32,160},{40,168},{48,176},{56,1... | collective-permute-start | bytes 393224 | tf_op jit(solution)/shard_map/ppermute | solution.py:10
  202.6 4.4 %collective-permute-done.26 = bf16[128,512]{1,0:T(8,128)(2,1)S(1)} collective-permute-done((bf16[128,512]{1,0:T(8,128)(2,1)S(1)}, bf16[128,512]{1,0:T(8,128)(2,1)S(1)}, u32[]{:S(2)}, u32[]{:S(2)}) %collective-permute-start.26) | collective-permute-done | bytes 131104 | tf_op jit(solution)/shard_map/ppermute | solution.py:10
  207.1 3.6 %collective-permute-start.29 = (bf16[3,128,512]{2,1,0:T(8,128)(2,1)S(1)}, bf16[3,128,512]{2,1,0:T(8,128)(2,1)S(1)}, u32[]{:S(2)}, u32[]{:S(2)}) collective-permute-start(bf16[3,128,512]{2,1,0:T(8,128)(2,1)S(1)} %pad_maximum_fusion.5), channel_id=1, source_target_pairs={{0,4},{1,5},{2,6},{3,7},{4,0},{5,1},{6,2},{7,3},{8,12},{9,13},{10,... | collective-permute-start | bytes 1179656 | tf_op jit(solution)/shard_map/ppermute | solution.py:55
  210.6 3.7 %collective-permute-start.28 = (bf16[3,128,512]{2,1,0:T(8,128)(2,1)S(1)}, bf16[3,128,512]{2,1,0:T(8,128)(2,1)S(1)}, u32[]{:S(2)}, u32[]{:S(2)}) collective-permute-start(bf16[3,128,512]{2,1,0:T(8,128)(2,1)S(1)} %pad_maximum_fusion.5), channel_id=1, source_target_pairs={{0,6},{1,7},{2,0},{3,1},{4,2},{5,3},{6,4},{7,5},{8,14},{9,15},{10,... | collective-permute-start | bytes 1179656 | tf_op jit(solution)/shard_map/ppermute | solution.py:55
  216.2 4.0 %collective-permute-done.29 = bf16[3,128,512]{2,1,0:T(8,128)(2,1)S(1)} collective-permute-done((bf16[3,128,512]{2,1,0:T(8,128)(2,1)S(1)}, bf16[3,128,512]{2,1,0:T(8,128)(2,1)S(1)}, u32[]{:S(2)}, u32[]{:S(2)}) %collective-permute-start.29) | collective-permute-done | bytes 393248 | tf_op jit(solution)/shard_map/ppermute | solution.py:55
  220.5 8.4 %collective-permute-done.28 = bf16[3,128,512]{2,1,0:T(8,128)(2,1)S(1)} collective-permute-done((bf16[3,128,512]{2,1,0:T(8,128)(2,1)S(1)}, bf16[3,128,512]{2,1,0:T(8,128)(2,1)S(1)}, u32[]{:S(2)}, u32[]{:S(2)}) %collective-permute-start.28) | collective-permute-done | bytes 393248 | tf_op jit(solution)/shard_map/ppermute | solution.py:55
  229.6 3.4 %collective-permute-start.30 = (f32[128,512]{1,0:T(8,128)S(1)}, f32[128,512]{1,0:T(8,128)S(1)}, u32[]{:S(2)}, u32[]{:S(2)}) collective-permute-start(f32[128,512]{1,0:T(8,128)S(1)} %fusion.36), channel_id=1, source_target_pairs={{0,1},{1,0},{2,3},{3,2},{4,5},{5,4},{6,7},{7,6},{8,9},{9,8},{10,11... | collective-permute-start | bytes 786440 | tf_op jit(solution)/shard_map/ppermute | solution.py:56
  235.7 10.5 %collective-permute-start.31 = (bf16[128,512]{1,0:T(8,128)(2,1)S(1)}, bf16[128,512]{1,0:T(8,128)(2,1)S(1)}, u32[]{:S(2)}, u32[]{:S(2)}) collective-permute-start(bf16[128,512]{1,0:T(8,128)(2,1)S(1)} %fusion.45), channel_id=1, source_target_pairs={{0,256},{8,264},{16,272},{24,280},{32,288},{40,296},{48,304},{56,3... | collective-permute-start | bytes 393224 | tf_op jit(solution)/shard_map/ppermute | solution.py:10
  247.8 3.5 %collective-permute-done.31 = bf16[128,512]{1,0:T(8,128)(2,1)S(1)} collective-permute-done((bf16[128,512]{1,0:T(8,128)(2,1)S(1)}, bf16[128,512]{1,0:T(8,128)(2,1)S(1)}, u32[]{:S(2)}, u32[]{:S(2)}) %collective-permute-start.31) | collective-permute-done | bytes 131104 | tf_op jit(solution)/shard_map/ppermute | solution.py:10
  254.3 3.7 %collective-permute-start.34 = (bf16[3,128,512]{2,1,0:T(8,128)(2,1)S(1)}, bf16[3,128,512]{2,1,0:T(8,128)(2,1)S(1)}, u32[]{:S(2)}, u32[]{:S(2)}) collective-permute-start(bf16[3,128,512]{2,1,0:T(8,128)(2,1)S(1)} %pad_maximum_fusion.6), channel_id=1, source_target_pairs={{0,6},{1,7},{2,0},{3,1},{4,2},{5,3},{6,4},{7,5},{8,14},{9,15},{10,... | collective-permute-start | bytes 1179656 | tf_op jit(solution)/shard_map/ppermute | solution.py:55
  259.9 4.3 %collective-permute-done.35 = bf16[3,128,512]{2,1,0:T(8,128)(2,1)S(1)} collective-permute-done((bf16[3,128,512]{2,1,0:T(8,128)(2,1)S(1)}, bf16[3,128,512]{2,1,0:T(8,128)(2,1)S(1)}, u32[]{:S(2)}, u32[]{:S(2)}) %collective-permute-start.35) | collective-permute-done | bytes 393248 | tf_op jit(solution)/shard_map/ppermute | solution.py:55
  264.4 8.1 %collective-permute-done.34 = bf16[3,128,512]{2,1,0:T(8,128)(2,1)S(1)} collective-permute-done((bf16[3,128,512]{2,1,0:T(8,128)(2,1)S(1)}, bf16[3,128,512]{2,1,0:T(8,128)(2,1)S(1)}, u32[]{:S(2)}, u32[]{:S(2)}) %collective-permute-start.34) | collective-permute-done | bytes 393248 | tf_op jit(solution)/shard_map/ppermute | solution.py:55
  (117 shorter events, 98.6 us)
Async XLA Ops:
  22.4 31.4 %collective-permute-start.5 = (bf16[6,128,4,3,128]{4,1,3,2,0:T(8,128)(2,1)}, bf16[6,128,4,3,128]{4,1,3,2,0:T(8,128)(2,1)}, u32[]{:S(2)}, u32[]{:S(2)}) collective-permute-start(bf16[6,128,4,3,128]{4,1,3,2,0:T(8,128)(2,1)} %fusion), channel_id=1, source_target_pairs={{0,1},{1,0},{2,3},{3,2},{4,5},{5,4},{6,7},{7,6},{8,9},{9,8},{10,11... | collective-permute-start | bytes 7077896 | tf_op jit(solution)/shard_map/ppermute | solution.py:37
  31.2 8.8 %collective-permute-start.1 = (bf16[128,512]{1,0:T(8,128)(2,1)S(1)}, bf16[128,512]{1,0:T(8,128)(2,1)S(1)}, u32[]{:S(2)}, u32[]{:S(2)}) collective-permute-start(bf16[128,512]{1,0:T(8,128)(2,1)S(1)} %bitcast.455), channel_id=1, source_target_pairs={{8,0},{16,8},{24,16},{32,24},{40,32},{48,40},{56,48},{64,56},{72,6... | collective-permute-start | bytes 393224 | tf_op jit(solution)/shard_map/ppermute | solution.py:10
  32.5 7.5 %collective-permute-start = (bf16[128,512]{1,0:T(8,128)(2,1)S(1)}, bf16[128,512]{1,0:T(8,128)(2,1)S(1)}, u32[]{:S(2)}, u32[]{:S(2)}) collective-permute-start(bf16[128,512]{1,0:T(8,128)(2,1)S(1)} %bitcast.456), channel_id=1, source_target_pairs={{0,8},{8,16},{16,24},{24,32},{32,40},{40,48},{48,56},{56,64},{64,7... | collective-permute-start | bytes 393224 | tf_op jit(solution)/shard_map/ppermute | solution.py:10
  40.0 13.5 %collective-permute-start.4 = (bf16[3,128,512]{2,1,0:T(8,128)(2,1)S(1)}, bf16[3,128,512]{2,1,0:T(8,128)(2,1)S(1)}, u32[]{:S(2)}, u32[]{:S(2)}) collective-permute-start(bf16[3,128,512]{2,1,0:T(8,128)(2,1)S(1)} %pad_maximum_fusion.1), channel_id=1, source_target_pairs={{0,4},{1,5},{2,6},{3,7},{4,0},{5,1},{6,2},{7,3},{8,12},{9,13},{10,... | collective-permute-start | bytes 1179656 | tf_op jit(solution)/shard_map/ppermute | solution.py:55
  42.5 15.1 %collective-permute-start.3 = (bf16[3,128,512]{2,1,0:T(8,128)(2,1)S(1)}, bf16[3,128,512]{2,1,0:T(8,128)(2,1)S(1)}, u32[]{:S(2)}, u32[]{:S(2)}) collective-permute-start(bf16[3,128,512]{2,1,0:T(8,128)(2,1)S(1)} %pad_maximum_fusion.1), channel_id=1, source_target_pairs={{0,6},{1,7},{2,0},{3,1},{4,2},{5,3},{6,4},{7,5},{8,14},{9,15},{10,... | collective-permute-start | bytes 1179656 | tf_op jit(solution)/shard_map/ppermute | solution.py:55
  44.4 18.4 %collective-permute-start.2 = (bf16[3,128,512]{2,1,0:T(8,128)(2,1)S(1)}, bf16[3,128,512]{2,1,0:T(8,128)(2,1)S(1)}, u32[]{:S(2)}, u32[]{:S(2)}) collective-permute-start(bf16[3,128,512]{2,1,0:T(8,128)(2,1)S(1)} %pad_maximum_fusion.1), channel_id=1, source_target_pairs={{0,2},{1,3},{2,4},{3,5},{4,6},{5,7},{6,0},{7,1},{8,10},{9,11},{10,... | collective-permute-start | bytes 1179656 | tf_op jit(solution)/shard_map/ppermute | solution.py:55
  67.1 9.3 %collective-permute-start.8 = (bf16[128,512]{1,0:T(8,128)(2,1)S(1)}, bf16[128,512]{1,0:T(8,128)(2,1)S(1)}, u32[]{:S(2)}, u32[]{:S(2)}) collective-permute-start(bf16[128,512]{1,0:T(8,128)(2,1)S(1)} %fusion.49), channel_id=1, source_target_pairs={{16,0},{24,8},{32,16},{40,24},{48,32},{56,40},{64,48},{72,56},{80,... | collective-permute-start | bytes 393224 | tf_op jit(solution)/shard_map/ppermute | solution.py:10
  68.4 8.0 %collective-permute-start.7 = (bf16[128,512]{1,0:T(8,128)(2,1)S(1)}, bf16[128,512]{1,0:T(8,128)(2,1)S(1)}, u32[]{:S(2)}, u32[]{:S(2)}) collective-permute-start(bf16[128,512]{1,0:T(8,128)(2,1)S(1)} %fusion.49), channel_id=1, source_target_pairs={{0,16},{8,24},{16,32},{24,40},{32,48},{40,56},{48,64},{56,72},{64,... | collective-permute-start | bytes 393224 | tf_op jit(solution)/shard_map/ppermute | solution.py:10
  76.5 11.8 %collective-permute-start.11 = (bf16[3,128,512]{2,1,0:T(8,128)(2,1)S(1)}, bf16[3,128,512]{2,1,0:T(8,128)(2,1)S(1)}, u32[]{:S(2)}, u32[]{:S(2)}) collective-permute-start(bf16[3,128,512]{2,1,0:T(8,128)(2,1)S(1)} %pad_maximum_fusion.2), channel_id=1, source_target_pairs={{0,4},{1,5},{2,6},{3,7},{4,0},{5,1},{6,2},{7,3},{8,12},{9,13},{10,... | collective-permute-start | bytes 1179656 | tf_op jit(solution)/shard_map/ppermute | solution.py:55
  78.4 16.9 %collective-permute-start.10 = (bf16[3,128,512]{2,1,0:T(8,128)(2,1)S(1)}, bf16[3,128,512]{2,1,0:T(8,128)(2,1)S(1)}, u32[]{:S(2)}, u32[]{:S(2)}) collective-permute-start(bf16[3,128,512]{2,1,0:T(8,128)(2,1)S(1)} %pad_maximum_fusion.2), channel_id=1, source_target_pairs={{0,6},{1,7},{2,0},{3,1},{4,2},{5,3},{6,4},{7,5},{8,14},{9,15},{10,... | collective-permute-start | bytes 1179656 | tf_op jit(solution)/shard_map/ppermute | solution.py:55
  80.3 18.3 %collective-permute-start.9 = (bf16[3,128,512]{2,1,0:T(8,128)(2,1)S(1)}, bf16[3,128,512]{2,1,0:T(8,128)(2,1)S(1)}, u32[]{:S(2)}, u32[]{:S(2)}) collective-permute-start(bf16[3,128,512]{2,1,0:T(8,128)(2,1)S(1)} %pad_maximum_fusion.2), channel_id=1, source_target_pairs={{0,2},{1,3},{2,4},{3,5},{4,6},{5,7},{6,0},{7,1},{8,10},{9,11},{10,... | collective-permute-start | bytes 1179656 | tf_op jit(solution)/shard_map/ppermute | solution.py:55
  103.6 15.5 %collective-permute-start.14 = (bf16[128,512]{1,0:T(8,128)(2,1)S(1)}, bf16[128,512]{1,0:T(8,128)(2,1)S(1)}, u32[]{:S(2)}, u32[]{:S(2)}) collective-permute-start(bf16[128,512]{1,0:T(8,128)(2,1)S(1)} %fusion.48), channel_id=1, source_target_pairs={{32,0},{40,8},{48,16},{56,24},{64,32},{72,40},{80,48},{88,56},{96,... | collective-permute-start | bytes 393224 | tf_op jit(solution)/shard_map/ppermute | solution.py:10
  104.9 20.4 %collective-permute-start.13 = (bf16[128,512]{1,0:T(8,128)(2,1)S(1)}, bf16[128,512]{1,0:T(8,128)(2,1)S(1)}, u32[]{:S(2)}, u32[]{:S(2)}) collective-permute-start(bf16[128,512]{1,0:T(8,128)(2,1)S(1)} %fusion.48), channel_id=1, source_target_pairs={{0,32},{8,40},{16,48},{24,56},{32,64},{40,72},{48,80},{56,88},{64,... | collective-permute-start | bytes 393224 | tf_op jit(solution)/shard_map/ppermute | solution.py:10
  125.4 13.6 %collective-permute-start.17 = (bf16[3,128,512]{2,1,0:T(8,128)(2,1)S(1)}, bf16[3,128,512]{2,1,0:T(8,128)(2,1)S(1)}, u32[]{:S(2)}, u32[]{:S(2)}) collective-permute-start(bf16[3,128,512]{2,1,0:T(8,128)(2,1)S(1)} %pad_maximum_fusion.3), channel_id=1, source_target_pairs={{0,4},{1,5},{2,6},{3,7},{4,0},{5,1},{6,2},{7,3},{8,12},{9,13},{10,... | collective-permute-start | bytes 1179656 | tf_op jit(solution)/shard_map/ppermute | solution.py:55
  129.2 18.3 %collective-permute-start.16 = (bf16[3,128,512]{2,1,0:T(8,128)(2,1)S(1)}, bf16[3,128,512]{2,1,0:T(8,128)(2,1)S(1)}, u32[]{:S(2)}, u32[]{:S(2)}) collective-permute-start(bf16[3,128,512]{2,1,0:T(8,128)(2,1)S(1)} %pad_maximum_fusion.3), channel_id=1, source_target_pairs={{0,6},{1,7},{2,0},{3,1},{4,2},{5,3},{6,4},{7,5},{8,14},{9,15},{10,... | collective-permute-start | bytes 1179656 | tf_op jit(solution)/shard_map/ppermute | solution.py:55
  132.3 15.9 %collective-permute-start.15 = (bf16[3,128,512]{2,1,0:T(8,128)(2,1)S(1)}, bf16[3,128,512]{2,1,0:T(8,128)(2,1)S(1)}, u32[]{:S(2)}, u32[]{:S(2)}) collective-permute-start(bf16[3,128,512]{2,1,0:T(8,128)(2,1)S(1)} %pad_maximum_fusion.3), channel_id=1, source_target_pairs={{0,2},{1,3},{2,4},{3,5},{4,6},{5,7},{6,0},{7,1},{8,10},{9,11},{10,... | collective-permute-start | bytes 1179656 | tf_op jit(solution)/shard_map/ppermute | solution.py:55
  152.9 14.4 %collective-permute-start.20 = (bf16[128,512]{1,0:T(8,128)(2,1)S(1)}, bf16[128,512]{1,0:T(8,128)(2,1)S(1)}, u32[]{:S(2)}, u32[]{:S(2)}) collective-permute-start(bf16[128,512]{1,0:T(8,128)(2,1)S(1)} %fusion.47), channel_id=1, source_target_pairs={{64,0},{72,8},{80,16},{88,24},{96,32},{104,40},{112,48},{120,56},{... | collective-permute-start | bytes 393224 | tf_op jit(solution)/shard_map/ppermute | solution.py:10
  154.2 14.0 %collective-permute-start.19 = (bf16[128,512]{1,0:T(8,128)(2,1)S(1)}, bf16[128,512]{1,0:T(8,128)(2,1)S(1)}, u32[]{:S(2)}, u32[]{:S(2)}) collective-permute-start(bf16[128,512]{1,0:T(8,128)(2,1)S(1)} %fusion.47), channel_id=1, source_target_pairs={{0,64},{8,72},{16,80},{24,88},{32,96},{40,104},{48,112},{56,120},{... | collective-permute-start | bytes 393224 | tf_op jit(solution)/shard_map/ppermute | solution.py:10
  168.2 12.8 %collective-permute-start.23 = (bf16[3,128,512]{2,1,0:T(8,128)(2,1)S(1)}, bf16[3,128,512]{2,1,0:T(8,128)(2,1)S(1)}, u32[]{:S(2)}, u32[]{:S(2)}) collective-permute-start(bf16[3,128,512]{2,1,0:T(8,128)(2,1)S(1)} %pad_maximum_fusion.4), channel_id=1, source_target_pairs={{0,4},{1,5},{2,6},{3,7},{4,0},{5,1},{6,2},{7,3},{8,12},{9,13},{10,... | collective-permute-start | bytes 1179656 | tf_op jit(solution)/shard_map/ppermute | solution.py:55
  172.0 18.0 %collective-permute-start.22 = (bf16[3,128,512]{2,1,0:T(8,128)(2,1)S(1)}, bf16[3,128,512]{2,1,0:T(8,128)(2,1)S(1)}, u32[]{:S(2)}, u32[]{:S(2)}) collective-permute-start(bf16[3,128,512]{2,1,0:T(8,128)(2,1)S(1)} %pad_maximum_fusion.4), channel_id=1, source_target_pairs={{0,6},{1,7},{2,0},{3,1},{4,2},{5,3},{6,4},{7,5},{8,14},{9,15},{10,... | collective-permute-start | bytes 1179656 | tf_op jit(solution)/shard_map/ppermute | solution.py:55
  175.5 14.7 %collective-permute-start.21 = (bf16[3,128,512]{2,1,0:T(8,128)(2,1)S(1)}, bf16[3,128,512]{2,1,0:T(8,128)(2,1)S(1)}, u32[]{:S(2)}, u32[]{:S(2)}) collective-permute-start(bf16[3,128,512]{2,1,0:T(8,128)(2,1)S(1)} %pad_maximum_fusion.4), channel_id=1, source_target_pairs={{0,2},{1,3},{2,4},{3,5},{4,6},{5,7},{6,0},{7,1},{8,10},{9,11},{10,... | collective-permute-start | bytes 1179656 | tf_op jit(solution)/shard_map/ppermute | solution.py:55
  190.8 4.6 %collective-permute-start.24 = (f32[128,512]{1,0:T(8,128)S(1)}, f32[128,512]{1,0:T(8,128)S(1)}, u32[]{:S(2)}, u32[]{:S(2)}) collective-permute-start(f32[128,512]{1,0:T(8,128)S(1)} %fusion.29), channel_id=1, source_target_pairs={{0,1},{1,0},{2,3},{3,2},{4,5},{5,4},{6,7},{7,6},{8,9},{9,8},{10,11... | collective-permute-start | bytes 786440 | tf_op jit(solution)/shard_map/ppermute | solution.py:56
  195.6 11.4 %collective-permute-start.26 = (bf16[128,512]{1,0:T(8,128)(2,1)S(1)}, bf16[128,512]{1,0:T(8,128)(2,1)S(1)}, u32[]{:S(2)}, u32[]{:S(2)}) collective-permute-start(bf16[128,512]{1,0:T(8,128)(2,1)S(1)} %fusion.46), channel_id=1, source_target_pairs={{128,0},{136,8},{144,16},{152,24},{160,32},{168,40},{176,48},{184,... | collective-permute-start | bytes 393224 | tf_op jit(solution)/shard_map/ppermute | solution.py:10
  196.9 10.1 %collective-permute-start.25 = (bf16[128,512]{1,0:T(8,128)(2,1)S(1)}, bf16[128,512]{1,0:T(8,128)(2,1)S(1)}, u32[]{:S(2)}, u32[]{:S(2)}) collective-permute-start(bf16[128,512]{1,0:T(8,128)(2,1)S(1)} %fusion.46), channel_id=1, source_target_pairs={{0,128},{8,136},{16,144},{24,152},{32,160},{40,168},{48,176},{56,1... | collective-permute-start | bytes 393224 | tf_op jit(solution)/shard_map/ppermute | solution.py:10
  207.1 13.1 %collective-permute-start.29 = (bf16[3,128,512]{2,1,0:T(8,128)(2,1)S(1)}, bf16[3,128,512]{2,1,0:T(8,128)(2,1)S(1)}, u32[]{:S(2)}, u32[]{:S(2)}) collective-permute-start(bf16[3,128,512]{2,1,0:T(8,128)(2,1)S(1)} %pad_maximum_fusion.5), channel_id=1, source_target_pairs={{0,4},{1,5},{2,6},{3,7},{4,0},{5,1},{6,2},{7,3},{8,12},{9,13},{10,... | collective-permute-start | bytes 1179656 | tf_op jit(solution)/shard_map/ppermute | solution.py:55
  210.6 18.2 %collective-permute-start.28 = (bf16[3,128,512]{2,1,0:T(8,128)(2,1)S(1)}, bf16[3,128,512]{2,1,0:T(8,128)(2,1)S(1)}, u32[]{:S(2)}, u32[]{:S(2)}) collective-permute-start(bf16[3,128,512]{2,1,0:T(8,128)(2,1)S(1)} %pad_maximum_fusion.5), channel_id=1, source_target_pairs={{0,6},{1,7},{2,0},{3,1},{4,2},{5,3},{6,4},{7,5},{8,14},{9,15},{10,... | collective-permute-start | bytes 1179656 | tf_op jit(solution)/shard_map/ppermute | solution.py:55
  214.3 14.8 %collective-permute-start.27 = (bf16[3,128,512]{2,1,0:T(8,128)(2,1)S(1)}, bf16[3,128,512]{2,1,0:T(8,128)(2,1)S(1)}, u32[]{:S(2)}, u32[]{:S(2)}) collective-permute-start(bf16[3,128,512]{2,1,0:T(8,128)(2,1)S(1)} %pad_maximum_fusion.5), channel_id=1, source_target_pairs={{0,2},{1,3},{2,4},{3,5},{4,6},{5,7},{6,0},{7,1},{8,10},{9,11},{10,... | collective-permute-start | bytes 1179656 | tf_op jit(solution)/shard_map/ppermute | solution.py:55
  234.4 13.4 %collective-permute-start.32 = (bf16[128,512]{1,0:T(8,128)(2,1)S(1)}, bf16[128,512]{1,0:T(8,128)(2,1)S(1)}, u32[]{:S(2)}, u32[]{:S(2)}) collective-permute-start(bf16[128,512]{1,0:T(8,128)(2,1)S(1)} %fusion.45), channel_id=1, source_target_pairs={{256,0},{264,8},{272,16},{280,24},{288,32},{296,40},{304,48},{312,... | collective-permute-start | bytes 393224 | tf_op jit(solution)/shard_map/ppermute | solution.py:10
  235.7 15.6 %collective-permute-start.31 = (bf16[128,512]{1,0:T(8,128)(2,1)S(1)}, bf16[128,512]{1,0:T(8,128)(2,1)S(1)}, u32[]{:S(2)}, u32[]{:S(2)}) collective-permute-start(bf16[128,512]{1,0:T(8,128)(2,1)S(1)} %fusion.45), channel_id=1, source_target_pairs={{0,256},{8,264},{16,272},{24,280},{32,288},{40,296},{48,304},{56,3... | collective-permute-start | bytes 393224 | tf_op jit(solution)/shard_map/ppermute | solution.py:10
  251.4 12.8 %collective-permute-start.35 = (bf16[3,128,512]{2,1,0:T(8,128)(2,1)S(1)}, bf16[3,128,512]{2,1,0:T(8,128)(2,1)S(1)}, u32[]{:S(2)}, u32[]{:S(2)}) collective-permute-start(bf16[3,128,512]{2,1,0:T(8,128)(2,1)S(1)} %pad_maximum_fusion.6), channel_id=1, source_target_pairs={{0,4},{1,5},{2,6},{3,7},{4,0},{5,1},{6,2},{7,3},{8,12},{9,13},{10,... | collective-permute-start | bytes 1179656 | tf_op jit(solution)/shard_map/ppermute | solution.py:55
  254.3 18.2 %collective-permute-start.34 = (bf16[3,128,512]{2,1,0:T(8,128)(2,1)S(1)}, bf16[3,128,512]{2,1,0:T(8,128)(2,1)S(1)}, u32[]{:S(2)}, u32[]{:S(2)}) collective-permute-start(bf16[3,128,512]{2,1,0:T(8,128)(2,1)S(1)} %pad_maximum_fusion.6), channel_id=1, source_target_pairs={{0,6},{1,7},{2,0},{3,1},{4,2},{5,3},{6,4},{7,5},{8,14},{9,15},{10,... | collective-permute-start | bytes 1179656 | tf_op jit(solution)/shard_map/ppermute | solution.py:55
  258.0 15.4 %collective-permute-start.33 = (bf16[3,128,512]{2,1,0:T(8,128)(2,1)S(1)}, bf16[3,128,512]{2,1,0:T(8,128)(2,1)S(1)}, u32[]{:S(2)}, u32[]{:S(2)}) collective-permute-start(bf16[3,128,512]{2,1,0:T(8,128)(2,1)S(1)} %pad_maximum_fusion.6), channel_id=1, source_target_pairs={{0,2},{1,3},{2,4},{3,5},{4,6},{5,7},{6,0},{7,1},{8,10},{9,11},{10,... | collective-permute-start | bytes 1179656 | tf_op jit(solution)/shard_map/ppermute | solution.py:55
  (6 other events, 31.3 us)

commit v3 on v2

v3 whole, which is shorter than its diff:
```python
import jax
import jax.numpy as jnp
from jax import lax
from jax.sharding import PartitionSpec as P


OFFSETS = (0, -1, 1, 2)


def body(right_side, self_factor, lower_factor, upper_factor):
    nchain = lax.axis_size("chain")
    levels = nchain.bit_length() - 1
    ncross = lax.axis_size("cross")
    chips = ncross // 2
    rows = right_side.shape[1]
    cross = lax.axis_index("cross")
    chip = cross // 2
    core = cross % 2

    swap = [(2 * c + b, 2 * c + 1 - b) for c in range(chips) for b in range(2)]

    def same_core(offset):
        return [(2 * c + b, 2 * ((c + offset) % chips) + b) for c in range(chips) for b in range(2)]

    def neighbour_pairs(dist):
        pairs = []
        for p in range(nchain):
            for c in range(ncross):
                q = p + dist if c % 2 == 0 else p - dist
                if 0 <= q < nchain:
                    pairs.append((p * ncross + c, q * ncross + c))
        return pairs

    own = right_side[0]
    pair = jnp.concatenate([own, lax.ppermute(own, "cross", swap)])
    first = lax.ppermute(pair, ("chain", "cross"), neighbour_pairs(1))

    first, self_factor, lower_factor, upper_factor = lax.optimization_barrier(
        (first, self_factor, lower_factor, upper_factor)
    )
    s_blocks = self_factor[:, 0].reshape(levels, rows, ncross, rows)
    neighbour = jnp.where(core == 0, lower_factor[:, 0], upper_factor[:, 0]).reshape(levels, rows, ncross, rows)
    given = jnp.where(core == 0, upper_factor[:, 0], lower_factor[:, 0]).reshape(levels, rows, ncross, rows)

    def arrange(s_part, n_part, which_core):
        slot_chips = [(chip + off) % chips for off in OFFSETS]
        s_idx = jnp.stack([2 * c + which_core for c in slot_chips])
        n_idx = jnp.stack([2 * c + t for c in slot_chips for t in (which_core, 1 - which_core)])
        s_sel = jnp.take(s_part, s_idx, axis=2)[:, :, :, None]
        n_sel = jnp.take(n_part, n_idx, axis=2).reshape(levels, rows, len(OFFSETS), 2, rows)
        return jnp.concatenate([s_sel, -n_sel], axis=3)

    mine = arrange(s_blocks, neighbour, core)
    theirs = lax.ppermute(arrange(s_blocks, given, 1 - core), "cross", swap)

    def partial(mat, pieces):
        total = None
        for j, piece in enumerate(pieces):
            term = jnp.einsum(
                "ibk,bkr->ir", mat[:, j], piece.reshape(3, rows, -1), preferred_element_type=jnp.float32
            )
            total = term if total is None else total + term
        return total

    for level in range(levels):
        near = first if level == 0 else lax.ppermute(pair, ("chain", "cross"), neighbour_pairs(2**level))
        piece = jnp.concatenate([pair[:rows], near])
        pieces = [piece] + [lax.ppermute(piece, "cross", same_core(-off)) for off in OFFSETS[1:]]
        mine_part = partial(mine[level], pieces)
        their_part = partial(theirs[level], pieces)
        back = lax.ppermute(jnp.stack([mine_part, their_part]), "cross", swap)
        pair = jnp.concatenate([mine_part + back[1], their_part + back[0]]).astype(jnp.bfloat16)
    return pair[None, :rows]


def solution(mesh):
    return jax.shard_map(
        body,
        mesh=mesh,
        in_specs=(
            P("chain", "cross", None),
            P(None, "chain", "cross", None),
            P(None, "chain", "cross", None),
            P(None, "chain", "cross", None),
        ),
        out_specs=P("chain", "cross", None),
        check_vma=False,
    )
```

time: 280 us -> 288 us (1.029)
  waiting for transfers between devices: 104 us -> 133 us
  starting transfers between devices: 135 us -> 108 us
  matrix products: 11.7 us -> 16.9 us
  local copies, waits for them, and re-layouts: 20.5 us -> 16.7 us
    ppermute x37 -> x32, waiting for transfers between devices: 104 us -> 133 us  [the longest x5 58.2 us: body(): lax.ppermute(pair, ('chain', 'cross'), neighbour_pairs(2 ** level))]
    ppermute x37 -> x32, starting transfers between devices: 135 us -> 108 us  [the longest x18 61.4 us: body(): lax.ppermute(piece, 'cross', same_core(-off))]
    dot_general x48, matrix products: 11.7 us -> 16.9 us  [partial(): jnp.einsum('ibk,bkr->ir', mat[:, j], piece.reshape(3, rows, -1), preferre...]
    unnamed x5 -> x10, local copies, waits for them, and re-layouts: 6.42 us -> 1.48 us
    optimization_barrier x0 -> x3, local copies, waits for them, and re-layouts: none -> 4.4 us  [body(): lax.optimization_barrier((first, self_factor, lower_factor, upper_factor))]
    concatenate x0 -> x13, other arithmetic: none -> 3.82 us  [the longest x1 1.65 us: arrange(): return jnp.concatenate([s_sel, -n_sel], axis=3)]
    another operation x7 -> x6, other arithmetic: 3.81 us -> 0.22 us  [body(): back = lax.ppermute(jnp.stack([mine_part, their_part]), 'cross', swap)]
    gather x2 -> x4, local copies, waits for them, and re-layouts: 6.67 us -> 4.77 us  [the longest x2 3.07 us: arrange(): s_sel = jnp.take(s_part, s_idx, axis=2)[:, :, :, None]]
  transfers between devices with their start and end apart: 37 -> 32, of which waited for: 30 -> 30; matrix products, arithmetic and copies ran while one was open for 4% -> 5% of each run, Pallas kernels for 0% -> 0%
where the time goes in v3:
time: 288 us; the launch traced here: 286 us
  waiting for transfers between devices  133 us (46%)
  starting transfers between devices  108 us (38%)
  matrix products  16.9 us (6%)
  local copies, waits for them, and re-layouts  16.7 us (6%)
  other arithmetic  10.5 us (4%)
    ppermute x18, starting transfers between devices, body(): lax.ppermute(piece, 'cross', same_core(-off))  61.4 us
    ppermute x5, waiting for transfers between devices, body(): lax.ppermute(pair, ('chain', 'cross'), neighbour_pairs(2 ** level))  58.2 us
    ppermute x18, waiting for transfers between devices, body(): lax.ppermute(piece, 'cross', same_core(-off))  57.9 us
    ppermute x6, starting transfers between devices, body(): back = lax.ppermute(jnp.stack([mine_part, their_part]), 'cross', swap)  28 us
    dot_general x48, matrix products, partial(): jnp.einsum('ibk,bkr->ir', mat[:, j], piece.reshape(3, rows, -1), preferre...  16.9 us
    ppermute x6, waiting for transfers between devices, body(): back = lax.ppermute(jnp.stack([mine_part, their_part]), 'cross', swap)  9.81 us
    ppermute x1, starting transfers between devices, body(): pair = jnp.concatenate([own, lax.ppermute(own, 'cross', swap)])  8.78 us
    ppermute x5, starting transfers between devices, body(): lax.ppermute(pair, ('chain', 'cross'), neighbour_pairs(2 ** level))  6.46 us
  transfers between devices with their start and end apart: 32, of which 30 were waited for; matrix products, arithmetic and copies ran while one was open for 5% of the time, Pallas kernels for 0%

profile of v3, /device:TPU:1, one launch (start us, length us, event | category | flops | bytes accessed | tf_op | source)
XLA Modules:
  0.0 285.8 jit_solution(2189116064899951290)
XLA Ops:
  0.0 8.8 %collective-permute-start = (bf16[128,512]{1,0:T(8,128)(2,1)}, bf16[128,512]{1,0:T(8,128)(2,1)S(1)}, u32[]{:S(2)}, u32[]{:S(2)}) collective-permute-start(bf16[128,512]{1,0:T(8,128)(2,1)} %bitcast.577), channel_id=1, source_target_pairs={{0,1},{1,0},{2,3},{3,2},{4,5},{5,4},{6,7},{7,6},{8,9},{9,8},{10,11... | collective-permute-start | bytes 393224 | tf_op jit(solution)/shard_map/ppermute | solution.py:35
  12.2 5.9 %collective-permute-done.1 = bf16[256,512]{1,0:T(8,128)(2,1)} collective-permute-done((bf16[256,512]{1,0:T(8,128)(2,1)S(1)}, bf16[256,512]{1,0:T(8,128)(2,1)}, u32[]{:S(2)}, u32[]{:S(2)}) %collective-permute-start.1) | collective-permute-done | bytes 262176 | tf_op jit(solution)/shard_map/ppermute | solution.py:36
  40.1 4.6 %collective-permute-start.3 = (bf16[384,512]{1,0:T(8,128)(2,1)S(1)}, bf16[384,512]{1,0:T(8,128)(2,1)}, u32[]{:S(2)}, u32[]{:S(2)}) collective-permute-start(bf16[384,512]{1,0:T(8,128)(2,1)S(1)} %pad_maximum_fusion.8), channel_id=1, source_target_pairs={{0,6},{1,7},{2,0},{3,1},{4,2},{5,3},{6,4},{7,5},{8,14},{9,15},{10,... | collective-permute-start | bytes 1179656 | tf_op jit(solution)/shard_map/ppermute | solution.py:68
  54.2 3.6 %collective-permute-done.4 = bf16[384,512]{1,0:T(8,128)(2,1)} collective-permute-done((bf16[384,512]{1,0:T(8,128)(2,1)S(1)}, bf16[384,512]{1,0:T(8,128)(2,1)}, u32[]{:S(2)}, u32[]{:S(2)}) %collective-permute-start.4) | collective-permute-done | bytes 393248 | tf_op jit(solution)/shard_map/ppermute | solution.py:68
  66.9 6.8 %collective-permute-start.6 = (f32[2,128,512]{2,1,0:T(8,128)S(1)}, f32[2,128,512]{2,1,0:T(8,128)S(1)}, u32[]{:S(2)}, u32[]{:S(2)}) collective-permute-start(f32[2,128,512]{2,1,0:T(8,128)S(1)} %pad_maximum_fusion.1), channel_id=1, source_target_pairs={{0,1},{1,0},{2,3},{3,2},{4,5},{5,4},{6,7},{7,6},{8,9},{9,8},{10,11... | collective-permute-start | bytes 1572872 | tf_op jit(solution)/shard_map/ppermute | solution.py:71
  76.7 9.9 %collective-permute-done.7 = bf16[256,512]{1,0:T(8,128)(2,1)S(1)} collective-permute-done((bf16[256,512]{1,0:T(8,128)(2,1)S(1)}, bf16[256,512]{1,0:T(8,128)(2,1)S(1)}, u32[]{:S(2)}, u32[]{:S(2)}) %collective-permute-start.7) | collective-permute-done | bytes 262176 | tf_op jit(solution)/shard_map/ppermute | solution.py:66
  88.5 5.5 %collective-permute-start.9 = (bf16[384,512]{1,0:T(8,128)(2,1)S(1)}, bf16[384,512]{1,0:T(8,128)(2,1)S(1)}, u32[]{:S(2)}, u32[]{:S(2)}) collective-permute-start(bf16[384,512]{1,0:T(8,128)(2,1)S(1)} %pad_maximum_fusion.9), channel_id=1, source_target_pairs={{0,6},{1,7},{2,0},{3,1},{4,2},{5,3},{6,4},{7,5},{8,14},{9,15},{10,... | collective-permute-start | bytes 1179656 | tf_op jit(solution)/shard_map/ppermute | solution.py:68
  94.0 3.1 %collective-permute-start.10 = (bf16[384,512]{1,0:T(8,128)(2,1)S(1)}, bf16[384,512]{1,0:T(8,128)(2,1)S(1)}, u32[]{:S(2)}, u32[]{:S(2)}) collective-permute-start(bf16[384,512]{1,0:T(8,128)(2,1)S(1)} %pad_maximum_fusion.9), channel_id=1, source_target_pairs={{0,4},{1,5},{2,6},{3,7},{4,0},{5,1},{6,2},{7,3},{8,12},{9,13},{10,... | collective-permute-start | bytes 1179656 | tf_op jit(solution)/shard_map/ppermute | solution.py:68
  99.1 8.0 %collective-permute-done.9 = bf16[384,512]{1,0:T(8,128)(2,1)S(1)} collective-permute-done((bf16[384,512]{1,0:T(8,128)(2,1)S(1)}, bf16[384,512]{1,0:T(8,128)(2,1)S(1)}, u32[]{:S(2)}, u32[]{:S(2)}) %collective-permute-start.9) | collective-permute-done | bytes 393248 | tf_op jit(solution)/shard_map/ppermute | solution.py:68
  114.0 14.7 %collective-permute-done.12 = bf16[256,512]{1,0:T(8,128)(2,1)S(1)} collective-permute-done((bf16[256,512]{1,0:T(8,128)(2,1)S(1)}, bf16[256,512]{1,0:T(8,128)(2,1)S(1)}, u32[]{:S(2)}, u32[]{:S(2)}) %collective-permute-start.12) | collective-permute-done | bytes 262176 | tf_op jit(solution)/shard_map/ppermute | solution.py:66
  128.8 3.9 %collective-permute-start.13 = (bf16[384,512]{1,0:T(8,128)(2,1)S(1)}, bf16[384,512]{1,0:T(8,128)(2,1)S(1)}, u32[]{:S(2)}, u32[]{:S(2)}) collective-permute-start(bf16[384,512]{1,0:T(8,128)(2,1)S(1)} %pad_maximum_fusion.10), channel_id=1, source_target_pairs={{0,2},{1,3},{2,4},{3,5},{4,6},{5,7},{6,0},{7,1},{8,10},{9,11},{10,... | collective-permute-start | bytes 1179656 | tf_op jit(solution)/shard_map/ppermute | solution.py:68
  132.7 3.3 %collective-permute-start.14 = (bf16[384,512]{1,0:T(8,128)(2,1)S(1)}, bf16[384,512]{1,0:T(8,128)(2,1)S(1)}, u32[]{:S(2)}, u32[]{:S(2)}) collective-permute-start(bf16[384,512]{1,0:T(8,128)(2,1)S(1)} %pad_maximum_fusion.10), channel_id=1, source_target_pairs={{0,6},{1,7},{2,0},{3,1},{4,2},{5,3},{6,4},{7,5},{8,14},{9,15},{10,... | collective-permute-start | bytes 1179656 | tf_op jit(solution)/shard_map/ppermute | solution.py:68
  136.0 3.1 %collective-permute-start.15 = (bf16[384,512]{1,0:T(8,128)(2,1)S(1)}, bf16[384,512]{1,0:T(8,128)(2,1)S(1)}, u32[]{:S(2)}, u32[]{:S(2)}) collective-permute-start(bf16[384,512]{1,0:T(8,128)(2,1)S(1)} %pad_maximum_fusion.10), channel_id=1, source_target_pairs={{0,4},{1,5},{2,6},{3,7},{4,0},{5,1},{6,2},{7,3},{8,12},{9,13},{10,... | collective-permute-start | bytes 1179656 | tf_op jit(solution)/shard_map/ppermute | solution.py:68
  141.9 6.4 %collective-permute-done.15 = bf16[384,512]{1,0:T(8,128)(2,1)S(1)} collective-permute-done((bf16[384,512]{1,0:T(8,128)(2,1)S(1)}, bf16[384,512]{1,0:T(8,128)(2,1)S(1)}, u32[]{:S(2)}, u32[]{:S(2)}) %collective-permute-start.15) | collective-permute-done | bytes 393248 | tf_op jit(solution)/shard_map/ppermute | solution.py:68
  149.3 8.7 %collective-permute-start.16 = (f32[2,128,512]{2,1,0:T(8,128)S(1)}, f32[2,128,512]{2,1,0:T(8,128)S(1)}, u32[]{:S(2)}, u32[]{:S(2)}) collective-permute-start(f32[2,128,512]{2,1,0:T(8,128)S(1)} %pad_maximum_fusion.3), channel_id=1, source_target_pairs={{0,1},{1,0},{2,3},{3,2},{4,5},{5,4},{6,7},{7,6},{8,9},{9,8},{10,11... | collective-permute-start | bytes 1572872 | tf_op jit(solution)/shard_map/ppermute | solution.py:71
  161.0 10.6 %collective-permute-done.17 = bf16[256,512]{1,0:T(8,128)(2,1)S(1)} collective-permute-done((bf16[256,512]{1,0:T(8,128)(2,1)S(1)}, bf16[256,512]{1,0:T(8,128)(2,1)S(1)}, u32[]{:S(2)}, u32[]{:S(2)}) %collective-permute-start.17) | collective-permute-done | bytes 262176 | tf_op jit(solution)/shard_map/ppermute | solution.py:66
  171.6 4.7 %collective-permute-start.18 = (bf16[384,512]{1,0:T(8,128)(2,1)S(1)}, bf16[384,512]{1,0:T(8,128)(2,1)S(1)}, u32[]{:S(2)}, u32[]{:S(2)}) collective-permute-start(bf16[384,512]{1,0:T(8,128)(2,1)S(1)} %pad_maximum_fusion.11), channel_id=1, source_target_pairs={{0,2},{1,3},{2,4},{3,5},{4,6},{5,7},{6,0},{7,1},{8,10},{9,11},{10,... | collective-permute-start | bytes 1179656 | tf_op jit(solution)/shard_map/ppermute | solution.py:68
  178.9 3.1 %collective-permute-start.20 = (bf16[384,512]{1,0:T(8,128)(2,1)S(1)}, bf16[384,512]{1,0:T(8,128)(2,1)S(1)}, u32[]{:S(2)}, u32[]{:S(2)}) collective-permute-start(bf16[384,512]{1,0:T(8,128)(2,1)S(1)} %pad_maximum_fusion.11), channel_id=1, source_target_pairs={{0,4},{1,5},{2,6},{3,7},{4,0},{5,1},{6,2},{7,3},{8,12},{9,13},{10,... | collective-permute-start | bytes 1179656 | tf_op jit(solution)/shard_map/ppermute | solution.py:68
  182.0 3.7 %collective-permute-done.18 = bf16[384,512]{1,0:T(8,128)(2,1)S(1)} collective-permute-done((bf16[384,512]{1,0:T(8,128)(2,1)S(1)}, bf16[384,512]{1,0:T(8,128)(2,1)S(1)}, u32[]{:S(2)}, u32[]{:S(2)}) %collective-permute-start.18) | collective-permute-done | bytes 393248 | tf_op jit(solution)/shard_map/ppermute | solution.py:68
  188.5 6.5 %collective-permute-done.20 = bf16[384,512]{1,0:T(8,128)(2,1)S(1)} collective-permute-done((bf16[384,512]{1,0:T(8,128)(2,1)S(1)}, bf16[384,512]{1,0:T(8,128)(2,1)S(1)}, u32[]{:S(2)}, u32[]{:S(2)}) %collective-permute-start.20) | collective-permute-done | bytes 393248 | tf_op jit(solution)/shard_map/ppermute | solution.py:68
  195.9 3.6 %collective-permute-start.21 = (f32[2,128,512]{2,1,0:T(8,128)S(1)}, f32[2,128,512]{2,1,0:T(8,128)S(1)}, u32[]{:S(2)}, u32[]{:S(2)}) collective-permute-start(f32[2,128,512]{2,1,0:T(8,128)S(1)} %pad_maximum_fusion.4), channel_id=1, source_target_pairs={{0,1},{1,0},{2,3},{3,2},{4,5},{5,4},{6,7},{7,6},{8,9},{9,8},{10,11... | collective-permute-start | bytes 1572872 | tf_op jit(solution)/shard_map/ppermute | solution.py:71
  202.4 9.9 %collective-permute-done.22 = bf16[256,512]{1,0:T(8,128)(2,1)S(1)} collective-permute-done((bf16[256,512]{1,0:T(8,128)(2,1)S(1)}, bf16[256,512]{1,0:T(8,128)(2,1)S(1)}, u32[]{:S(2)}, u32[]{:S(2)}) %collective-permute-start.22) | collective-permute-done | bytes 262176 | tf_op jit(solution)/shard_map/ppermute | solution.py:66
  212.3 4.7 %collective-permute-start.23 = (bf16[384,512]{1,0:T(8,128)(2,1)S(1)}, bf16[384,512]{1,0:T(8,128)(2,1)S(1)}, u32[]{:S(2)}, u32[]{:S(2)}) collective-permute-start(bf16[384,512]{1,0:T(8,128)(2,1)S(1)} %pad_maximum_fusion.12), channel_id=1, source_target_pairs={{0,2},{1,3},{2,4},{3,5},{4,6},{5,7},{6,0},{7,1},{8,10},{9,11},{10,... | collective-permute-start | bytes 1179656 | tf_op jit(solution)/shard_map/ppermute | solution.py:68
  220.1 3.1 %collective-permute-start.25 = (bf16[384,512]{1,0:T(8,128)(2,1)S(1)}, bf16[384,512]{1,0:T(8,128)(2,1)S(1)}, u32[]{:S(2)}, u32[]{:S(2)}) collective-permute-start(bf16[384,512]{1,0:T(8,128)(2,1)S(1)} %pad_maximum_fusion.12), channel_id=1, source_target_pairs={{0,4},{1,5},{2,6},{3,7},{4,0},{5,1},{6,2},{7,3},{8,12},{9,13},{10,... | collective-permute-start | bytes 1179656 | tf_op jit(solution)/shard_map/ppermute | solution.py:68
  226.4 3.7 %collective-permute-done.24 = bf16[384,512]{1,0:T(8,128)(2,1)S(1)} collective-permute-done((bf16[384,512]{1,0:T(8,128)(2,1)S(1)}, bf16[384,512]{1,0:T(8,128)(2,1)S(1)}, u32[]{:S(2)}, u32[]{:S(2)}) %collective-permute-start.24) | collective-permute-done | bytes 393248 | tf_op jit(solution)/shard_map/ppermute | solution.py:68
  230.8 4.8 %collective-permute-done.25 = bf16[384,512]{1,0:T(8,128)(2,1)S(1)} collective-permute-done((bf16[384,512]{1,0:T(8,128)(2,1)S(1)}, bf16[384,512]{1,0:T(8,128)(2,1)S(1)}, u32[]{:S(2)}, u32[]{:S(2)}) %collective-permute-start.25) | collective-permute-done | bytes 393248 | tf_op jit(solution)/shard_map/ppermute | solution.py:68
  241.8 13.2 %collective-permute-done.27 = bf16[256,512]{1,0:T(8,128)(2,1)S(1)} collective-permute-done((bf16[256,512]{1,0:T(8,128)(2,1)S(1)}, bf16[256,512]{1,0:T(8,128)(2,1)S(1)}, u32[]{:S(2)}, u32[]{:S(2)}) %collective-permute-start.27) | collective-permute-done | bytes 262176 | tf_op jit(solution)/shard_map/ppermute | solution.py:66
  255.0 4.7 %collective-permute-start.28 = (bf16[384,512]{1,0:T(8,128)(2,1)S(1)}, bf16[384,512]{1,0:T(8,128)(2,1)S(1)}, u32[]{:S(2)}, u32[]{:S(2)}) collective-permute-start(bf16[384,512]{1,0:T(8,128)(2,1)S(1)} %pad_maximum_fusion.13), channel_id=1, source_target_pairs={{0,2},{1,3},{2,4},{3,5},{4,6},{5,7},{6,0},{7,1},{8,10},{9,11},{10,... | collective-permute-start | bytes 1179656 | tf_op jit(solution)/shard_map/ppermute | solution.py:68
  259.7 3.3 %collective-permute-start.29 = (bf16[384,512]{1,0:T(8,128)(2,1)S(1)}, bf16[384,512]{1,0:T(8,128)(2,1)S(1)}, u32[]{:S(2)}, u32[]{:S(2)}) collective-permute-start(bf16[384,512]{1,0:T(8,128)(2,1)S(1)} %pad_maximum_fusion.13), channel_id=1, source_target_pairs={{0,6},{1,7},{2,0},{3,1},{4,2},{5,3},{6,4},{7,5},{8,14},{9,15},{10,... | collective-permute-start | bytes 1179656 | tf_op jit(solution)/shard_map/ppermute | solution.py:68
  263.0 3.1 %collective-permute-start.30 = (bf16[384,512]{1,0:T(8,128)(2,1)S(1)}, bf16[384,512]{1,0:T(8,128)(2,1)S(1)}, u32[]{:S(2)}, u32[]{:S(2)}) collective-permute-start(bf16[384,512]{1,0:T(8,128)(2,1)S(1)} %pad_maximum_fusion.13), channel_id=1, source_target_pairs={{0,4},{1,5},{2,6},{3,7},{4,0},{5,1},{6,2},{7,3},{8,12},{9,13},{10,... | collective-permute-start | bytes 1179656 | tf_op jit(solution)/shard_map/ppermute | solution.py:68
  269.3 8.3 %collective-permute-done.30 = bf16[384,512]{1,0:T(8,128)(2,1)S(1)} collective-permute-done((bf16[384,512]{1,0:T(8,128)(2,1)S(1)}, bf16[384,512]{1,0:T(8,128)(2,1)S(1)}, u32[]{:S(2)}, u32[]{:S(2)}) %collective-permute-start.30) | collective-permute-done | bytes 393248 | tf_op jit(solution)/shard_map/ppermute | solution.py:68
  278.6 5.0 %collective-permute-start.31 = (f32[2,128,512]{2,1,0:T(8,128)S(1)}, f32[2,128,512]{2,1,0:T(8,128)S(1)}, u32[]{:S(2)}, u32[]{:S(2)}) collective-permute-start(f32[2,128,512]{2,1,0:T(8,128)S(1)} %pad_maximum_fusion.6), channel_id=1, source_target_pairs={{0,1},{1,0},{2,3},{3,2},{4,5},{5,4},{6,7},{7,6},{8,9},{9,8},{10,11... | collective-permute-start | bytes 1572872 | tf_op jit(solution)/shard_map/ppermute | solution.py:71
  (146 shorter events, 92.7 us)
Async XLA Ops:
  0.0 10.0 %collective-permute-start = (bf16[128,512]{1,0:T(8,128)(2,1)}, bf16[128,512]{1,0:T(8,128)(2,1)S(1)}, u32[]{:S(2)}, u32[]{:S(2)}) collective-permute-start(bf16[128,512]{1,0:T(8,128)(2,1)} %bitcast.577), channel_id=1, source_target_pairs={{0,1},{1,0},{2,3},{3,2},{4,5},{5,4},{6,7},{7,6},{8,9},{9,8},{10,11... | collective-permute-start | bytes 393224 | tf_op jit(solution)/shard_map/ppermute | solution.py:35
  10.9 7.2 %collective-permute-start.1 = (bf16[256,512]{1,0:T(8,128)(2,1)S(1)}, bf16[256,512]{1,0:T(8,128)(2,1)}, u32[]{:S(2)}, u32[]{:S(2)}) collective-permute-start(bf16[256,512]{1,0:T(8,128)(2,1)S(1)} %pad_maximum_fusion.14), channel_id=1, source_target_pairs={{0,8},{2,10},{4,12},{6,14},{8,16},{9,1},{10,18},{11,3},{12,20},{13... | collective-permute-start | bytes 786440 | tf_op jit(solution)/shard_map/ppermute | solution.py:36
  34.8 26.3 %collective-permute-start.5 = (bf16[6,128,4,3,128]{4,1,3,2,0:T(8,128)(2,1)}, bf16[6,128,4,3,128]{4,1,3,2,0:T(8,128)(2,1)}, u32[]{:S(2)}, u32[]{:S(2)}) collective-permute-start(bf16[6,128,4,3,128]{4,1,3,2,0:T(8,128)(2,1)} %pad_maximum_fusion), channel_id=1, source_target_pairs={{0,1},{1,0},{2,3},{3,2},{4,5},{5,4},{6,7},{7,6},{8,9},{9,8},{10,11... | collective-permute-start | bytes 7077896 | tf_op jit(solution)/shard_map/ppermute | solution.py:54
  38.1 21.8 %collective-permute-start.2 = (bf16[384,512]{1,0:T(8,128)(2,1)S(1)}, bf16[384,512]{1,0:T(8,128)(2,1)}, u32[]{:S(2)}, u32[]{:S(2)}) collective-permute-start(bf16[384,512]{1,0:T(8,128)(2,1)S(1)} %pad_maximum_fusion.8), channel_id=1, source_target_pairs={{0,2},{1,3},{2,4},{3,5},{4,6},{5,7},{6,0},{7,1},{8,10},{9,11},{10,... | collective-permute-start | bytes 1179656 | tf_op jit(solution)/shard_map/ppermute | solution.py:68
  40.1 12.9 %collective-permute-start.3 = (bf16[384,512]{1,0:T(8,128)(2,1)S(1)}, bf16[384,512]{1,0:T(8,128)(2,1)}, u32[]{:S(2)}, u32[]{:S(2)}) collective-permute-start(bf16[384,512]{1,0:T(8,128)(2,1)S(1)} %pad_maximum_fusion.8), channel_id=1, source_target_pairs={{0,6},{1,7},{2,0},{3,1},{4,2},{5,3},{6,4},{7,5},{8,14},{9,15},{10,... | collective-permute-start | bytes 1179656 | tf_op jit(solution)/shard_map/ppermute | solution.py:68
  44.6 13.1 %collective-permute-start.4 = (bf16[384,512]{1,0:T(8,128)(2,1)S(1)}, bf16[384,512]{1,0:T(8,128)(2,1)}, u32[]{:S(2)}, u32[]{:S(2)}) collective-permute-start(bf16[384,512]{1,0:T(8,128)(2,1)S(1)} %pad_maximum_fusion.8), channel_id=1, source_target_pairs={{0,4},{1,5},{2,6},{3,7},{4,0},{5,1},{6,2},{7,3},{8,12},{9,13},{10,... | collective-permute-start | bytes 1179656 | tf_op jit(solution)/shard_map/ppermute | solution.py:68
  66.9 8.3 %collective-permute-start.6 = (f32[2,128,512]{2,1,0:T(8,128)S(1)}, f32[2,128,512]{2,1,0:T(8,128)S(1)}, u32[]{:S(2)}, u32[]{:S(2)}) collective-permute-start(f32[2,128,512]{2,1,0:T(8,128)S(1)} %pad_maximum_fusion.1), channel_id=1, source_target_pairs={{0,1},{1,0},{2,3},{3,2},{4,5},{5,4},{6,7},{7,6},{8,9},{9,8},{10,11... | collective-permute-start | bytes 1572872 | tf_op jit(solution)/shard_map/ppermute | solution.py:71
  75.4 11.2 %collective-permute-start.7 = (bf16[256,512]{1,0:T(8,128)(2,1)S(1)}, bf16[256,512]{1,0:T(8,128)(2,1)S(1)}, u32[]{:S(2)}, u32[]{:S(2)}) collective-permute-start(bf16[256,512]{1,0:T(8,128)(2,1)S(1)} %pad_maximum_fusion.15), channel_id=1, source_target_pairs={{0,16},{2,18},{4,20},{6,22},{8,24},{10,26},{12,28},{14,30},{16,32}... | collective-permute-start | bytes 786440 | tf_op jit(solution)/shard_map/ppermute | solution.py:66
  86.6 12.3 %collective-permute-start.8 = (bf16[384,512]{1,0:T(8,128)(2,1)S(1)}, bf16[384,512]{1,0:T(8,128)(2,1)S(1)}, u32[]{:S(2)}, u32[]{:S(2)}) collective-permute-start(bf16[384,512]{1,0:T(8,128)(2,1)S(1)} %pad_maximum_fusion.9), channel_id=1, source_target_pairs={{0,2},{1,3},{2,4},{3,5},{4,6},{5,7},{6,0},{7,1},{8,10},{9,11},{10,... | collective-permute-start | bytes 1179656 | tf_op jit(solution)/shard_map/ppermute | solution.py:68
  88.5 18.6 %collective-permute-start.9 = (bf16[384,512]{1,0:T(8,128)(2,1)S(1)}, bf16[384,512]{1,0:T(8,128)(2,1)S(1)}, u32[]{:S(2)}, u32[]{:S(2)}) collective-permute-start(bf16[384,512]{1,0:T(8,128)(2,1)S(1)} %pad_maximum_fusion.9), channel_id=1, source_target_pairs={{0,6},{1,7},{2,0},{3,1},{4,2},{5,3},{6,4},{7,5},{8,14},{9,15},{10,... | collective-permute-start | bytes 1179656 | tf_op jit(solution)/shard_map/ppermute | solution.py:68
  94.0 13.8 %collective-permute-start.10 = (bf16[384,512]{1,0:T(8,128)(2,1)S(1)}, bf16[384,512]{1,0:T(8,128)(2,1)S(1)}, u32[]{:S(2)}, u32[]{:S(2)}) collective-permute-start(bf16[384,512]{1,0:T(8,128)(2,1)S(1)} %pad_maximum_fusion.9), channel_id=1, source_target_pairs={{0,4},{1,5},{2,6},{3,7},{4,0},{5,1},{6,2},{7,3},{8,12},{9,13},{10,... | collective-permute-start | bytes 1179656 | tf_op jit(solution)/shard_map/ppermute | solution.py:68
  108.8 3.8 %collective-permute-start.11 = (f32[2,128,512]{2,1,0:T(8,128)S(1)}, f32[2,128,512]{2,1,0:T(8,128)S(1)}, u32[]{:S(2)}, u32[]{:S(2)}) collective-permute-start(f32[2,128,512]{2,1,0:T(8,128)S(1)} %pad_maximum_fusion.2), channel_id=1, source_target_pairs={{0,1},{1,0},{2,3},{3,2},{4,5},{5,4},{6,7},{7,6},{8,9},{9,8},{10,11... | collective-permute-start | bytes 1572872 | tf_op jit(solution)/shard_map/ppermute | solution.py:71
  112.7 16.0 %collective-permute-start.12 = (bf16[256,512]{1,0:T(8,128)(2,1)S(1)}, bf16[256,512]{1,0:T(8,128)(2,1)S(1)}, u32[]{:S(2)}, u32[]{:S(2)}) collective-permute-start(bf16[256,512]{1,0:T(8,128)(2,1)S(1)} %pad_maximum_fusion.16), channel_id=1, source_target_pairs={{0,32},{2,34},{4,36},{6,38},{8,40},{10,42},{12,44},{14,46},{16,48}... | collective-permute-start | bytes 786440 | tf_op jit(solution)/shard_map/ppermute | solution.py:66
  128.8 10.4 %collective-permute-start.13 = (bf16[384,512]{1,0:T(8,128)(2,1)S(1)}, bf16[384,512]{1,0:T(8,128)(2,1)S(1)}, u32[]{:S(2)}, u32[]{:S(2)}) collective-permute-start(bf16[384,512]{1,0:T(8,128)(2,1)S(1)} %pad_maximum_fusion.10), channel_id=1, source_target_pairs={{0,2},{1,3},{2,4},{3,5},{4,6},{5,7},{6,0},{7,1},{8,10},{9,11},{10,... | collective-permute-start | bytes 1179656 | tf_op jit(solution)/shard_map/ppermute | solution.py:68
  132.7 8.5 %collective-permute-start.14 = (bf16[384,512]{1,0:T(8,128)(2,1)S(1)}, bf16[384,512]{1,0:T(8,128)(2,1)S(1)}, u32[]{:S(2)}, u32[]{:S(2)}) collective-permute-start(bf16[384,512]{1,0:T(8,128)(2,1)S(1)} %pad_maximum_fusion.10), channel_id=1, source_target_pairs={{0,6},{1,7},{2,0},{3,1},{4,2},{5,3},{6,4},{7,5},{8,14},{9,15},{10,... | collective-permute-start | bytes 1179656 | tf_op jit(solution)/shard_map/ppermute | solution.py:68
  136.0 12.3 %collective-permute-start.15 = (bf16[384,512]{1,0:T(8,128)(2,1)S(1)}, bf16[384,512]{1,0:T(8,128)(2,1)S(1)}, u32[]{:S(2)}, u32[]{:S(2)}) collective-permute-start(bf16[384,512]{1,0:T(8,128)(2,1)S(1)} %pad_maximum_fusion.10), channel_id=1, source_target_pairs={{0,4},{1,5},{2,6},{3,7},{4,0},{5,1},{6,2},{7,3},{8,12},{9,13},{10,... | collective-permute-start | bytes 1179656 | tf_op jit(solution)/shard_map/ppermute | solution.py:68
  149.3 10.2 %collective-permute-start.16 = (f32[2,128,512]{2,1,0:T(8,128)S(1)}, f32[2,128,512]{2,1,0:T(8,128)S(1)}, u32[]{:S(2)}, u32[]{:S(2)}) collective-permute-start(f32[2,128,512]{2,1,0:T(8,128)S(1)} %pad_maximum_fusion.3), channel_id=1, source_target_pairs={{0,1},{1,0},{2,3},{3,2},{4,5},{5,4},{6,7},{7,6},{8,9},{9,8},{10,11... | collective-permute-start | bytes 1572872 | tf_op jit(solution)/shard_map/ppermute | solution.py:71
  159.7 11.9 %collective-permute-start.17 = (bf16[256,512]{1,0:T(8,128)(2,1)S(1)}, bf16[256,512]{1,0:T(8,128)(2,1)S(1)}, u32[]{:S(2)}, u32[]{:S(2)}) collective-permute-start(bf16[256,512]{1,0:T(8,128)(2,1)S(1)} %pad_maximum_fusion.17), channel_id=1, source_target_pairs={{0,64},{2,66},{4,68},{6,70},{8,72},{10,74},{12,76},{14,78},{16,80}... | collective-permute-start | bytes 786440 | tf_op jit(solution)/shard_map/ppermute | solution.py:66
  171.6 14.0 %collective-permute-start.18 = (bf16[384,512]{1,0:T(8,128)(2,1)S(1)}, bf16[384,512]{1,0:T(8,128)(2,1)S(1)}, u32[]{:S(2)}, u32[]{:S(2)}) collective-permute-start(bf16[384,512]{1,0:T(8,128)(2,1)S(1)} %pad_maximum_fusion.11), channel_id=1, source_target_pairs={{0,2},{1,3},{2,4},{3,5},{4,6},{5,7},{6,0},{7,1},{8,10},{9,11},{10,... | collective-permute-start | bytes 1179656 | tf_op jit(solution)/shard_map/ppermute | solution.py:68
  176.3 11.4 %collective-permute-start.19 = (bf16[384,512]{1,0:T(8,128)(2,1)S(1)}, bf16[384,512]{1,0:T(8,128)(2,1)S(1)}, u32[]{:S(2)}, u32[]{:S(2)}) collective-permute-start(bf16[384,512]{1,0:T(8,128)(2,1)S(1)} %pad_maximum_fusion.11), channel_id=1, source_target_pairs={{0,6},{1,7},{2,0},{3,1},{4,2},{5,3},{6,4},{7,5},{8,14},{9,15},{10,... | collective-permute-start | bytes 1179656 | tf_op jit(solution)/shard_map/ppermute | solution.py:68
  178.9 16.1 %collective-permute-start.20 = (bf16[384,512]{1,0:T(8,128)(2,1)S(1)}, bf16[384,512]{1,0:T(8,128)(2,1)S(1)}, u32[]{:S(2)}, u32[]{:S(2)}) collective-permute-start(bf16[384,512]{1,0:T(8,128)(2,1)S(1)} %pad_maximum_fusion.11), channel_id=1, source_target_pairs={{0,4},{1,5},{2,6},{3,7},{4,0},{5,1},{6,2},{7,3},{8,12},{9,13},{10,... | collective-permute-start | bytes 1179656 | tf_op jit(solution)/shard_map/ppermute | solution.py:68
  195.9 5.1 %collective-permute-start.21 = (f32[2,128,512]{2,1,0:T(8,128)S(1)}, f32[2,128,512]{2,1,0:T(8,128)S(1)}, u32[]{:S(2)}, u32[]{:S(2)}) collective-permute-start(f32[2,128,512]{2,1,0:T(8,128)S(1)} %pad_maximum_fusion.4), channel_id=1, source_target_pairs={{0,1},{1,0},{2,3},{3,2},{4,5},{5,4},{6,7},{7,6},{8,9},{9,8},{10,11... | collective-permute-start | bytes 1572872 | tf_op jit(solution)/shard_map/ppermute | solution.py:71
  201.1 11.2 %collective-permute-start.22 = (bf16[256,512]{1,0:T(8,128)(2,1)S(1)}, bf16[256,512]{1,0:T(8,128)(2,1)S(1)}, u32[]{:S(2)}, u32[]{:S(2)}) collective-permute-start(bf16[256,512]{1,0:T(8,128)(2,1)S(1)} %pad_maximum_fusion.18), channel_id=1, source_target_pairs={{0,128},{2,130},{4,132},{6,134},{8,136},{10,138},{12,140},{14,142}... | collective-permute-start | bytes 786440 | tf_op jit(solution)/shard_map/ppermute | solution.py:66
  212.3 13.8 %collective-permute-start.23 = (bf16[384,512]{1,0:T(8,128)(2,1)S(1)}, bf16[384,512]{1,0:T(8,128)(2,1)S(1)}, u32[]{:S(2)}, u32[]{:S(2)}) collective-permute-start(bf16[384,512]{1,0:T(8,128)(2,1)S(1)} %pad_maximum_fusion.12), channel_id=1, source_target_pairs={{0,2},{1,3},{2,4},{3,5},{4,6},{5,7},{6,0},{7,1},{8,10},{9,11},{10,... | collective-permute-start | bytes 1179656 | tf_op jit(solution)/shard_map/ppermute | solution.py:68
  217.0 13.1 %collective-permute-start.24 = (bf16[384,512]{1,0:T(8,128)(2,1)S(1)}, bf16[384,512]{1,0:T(8,128)(2,1)S(1)}, u32[]{:S(2)}, u32[]{:S(2)}) collective-permute-start(bf16[384,512]{1,0:T(8,128)(2,1)S(1)} %pad_maximum_fusion.12), channel_id=1, source_target_pairs={{0,6},{1,7},{2,0},{3,1},{4,2},{5,3},{6,4},{7,5},{8,14},{9,15},{10,... | collective-permute-start | bytes 1179656 | tf_op jit(solution)/shard_map/ppermute | solution.py:68
  220.1 15.5 %collective-permute-start.25 = (bf16[384,512]{1,0:T(8,128)(2,1)S(1)}, bf16[384,512]{1,0:T(8,128)(2,1)S(1)}, u32[]{:S(2)}, u32[]{:S(2)}) collective-permute-start(bf16[384,512]{1,0:T(8,128)(2,1)S(1)} %pad_maximum_fusion.12), channel_id=1, source_target_pairs={{0,4},{1,5},{2,6},{3,7},{4,0},{5,1},{6,2},{7,3},{8,12},{9,13},{10,... | collective-permute-start | bytes 1179656 | tf_op jit(solution)/shard_map/ppermute | solution.py:68
  236.6 3.8 %collective-permute-start.26 = (f32[2,128,512]{2,1,0:T(8,128)S(1)}, f32[2,128,512]{2,1,0:T(8,128)S(1)}, u32[]{:S(2)}, u32[]{:S(2)}) collective-permute-start(f32[2,128,512]{2,1,0:T(8,128)S(1)} %pad_maximum_fusion.5), channel_id=1, source_target_pairs={{0,1},{1,0},{2,3},{3,2},{4,5},{5,4},{6,7},{7,6},{8,9},{9,8},{10,11... | collective-permute-start | bytes 1572872 | tf_op jit(solution)/shard_map/ppermute | solution.py:71
  240.5 14.5 %collective-permute-start.27 = (bf16[256,512]{1,0:T(8,128)(2,1)S(1)}, bf16[256,512]{1,0:T(8,128)(2,1)S(1)}, u32[]{:S(2)}, u32[]{:S(2)}) collective-permute-start(bf16[256,512]{1,0:T(8,128)(2,1)S(1)} %pad_maximum_fusion.19), channel_id=1, source_target_pairs={{0,256},{2,258},{4,260},{6,262},{8,264},{10,266},{12,268},{14,270}... | collective-permute-start | bytes 786440 | tf_op jit(solution)/shard_map/ppermute | solution.py:66
  255.0 12.1 %collective-permute-start.28 = (bf16[384,512]{1,0:T(8,128)(2,1)S(1)}, bf16[384,512]{1,0:T(8,128)(2,1)S(1)}, u32[]{:S(2)}, u32[]{:S(2)}) collective-permute-start(bf16[384,512]{1,0:T(8,128)(2,1)S(1)} %pad_maximum_fusion.13), channel_id=1, source_target_pairs={{0,2},{1,3},{2,4},{3,5},{4,6},{5,7},{6,0},{7,1},{8,10},{9,11},{10,... | collective-permute-start | bytes 1179656 | tf_op jit(solution)/shard_map/ppermute | solution.py:68
  259.7 8.8 %collective-permute-start.29 = (bf16[384,512]{1,0:T(8,128)(2,1)S(1)}, bf16[384,512]{1,0:T(8,128)(2,1)S(1)}, u32[]{:S(2)}, u32[]{:S(2)}) collective-permute-start(bf16[384,512]{1,0:T(8,128)(2,1)S(1)} %pad_maximum_fusion.13), channel_id=1, source_target_pairs={{0,6},{1,7},{2,0},{3,1},{4,2},{5,3},{6,4},{7,5},{8,14},{9,15},{10,... | collective-permute-start | bytes 1179656 | tf_op jit(solution)/shard_map/ppermute | solution.py:68
  263.0 14.6 %collective-permute-start.30 = (bf16[384,512]{1,0:T(8,128)(2,1)S(1)}, bf16[384,512]{1,0:T(8,128)(2,1)S(1)}, u32[]{:S(2)}, u32[]{:S(2)}) collective-permute-start(bf16[384,512]{1,0:T(8,128)(2,1)S(1)} %pad_maximum_fusion.13), channel_id=1, source_target_pairs={{0,4},{1,5},{2,6},{3,7},{4,0},{5,1},{6,2},{7,3},{8,12},{9,13},{10,... | collective-permute-start | bytes 1179656 | tf_op jit(solution)/shard_map/ppermute | solution.py:68
  278.6 6.6 %collective-permute-start.31 = (f32[2,128,512]{2,1,0:T(8,128)S(1)}, f32[2,128,512]{2,1,0:T(8,128)S(1)}, u32[]{:S(2)}, u32[]{:S(2)}) collective-permute-start(f32[2,128,512]{2,1,0:T(8,128)S(1)} %pad_maximum_fusion.6), channel_id=1, source_target_pairs={{0,1},{1,0},{2,3},{3,2},{4,5},{5,4},{6,7},{7,6},{8,9},{9,8},{10,11... | collective-permute-start | bytes 1572872 | tf_op jit(solution)/shard_map/ppermute | solution.py:71
  (5 other events, 27.0 us)

commit v4 on v2

--- a/solution.py
+++ b/solution.py
@@ -25,16 +25,14 @@
     def columns_for(which_core):
         return jnp.stack([2 * ((chip + off) % chips) + which_core for off in OFFSETS])
 
-    signed = jnp.stack([self_factor[:, 0], -lower_factor[:, 0], -upper_factor[:, 0]], axis=2)
-    signed = signed.reshape(levels, rows, 3, ncross, rows)
+    def arrange(level, which_core):
+        signed = jnp.stack([self_factor[level, 0], -lower_factor[level, 0], -upper_factor[level, 0]], axis=1)
+        signed = signed.reshape(rows, 3, ncross, rows)
+        part = jnp.take(signed, columns_for(which_core), axis=2)
+        return part.transpose(0, 2, 1, 3)
 
-    def pick(which_core):
-        part = jnp.take(signed, columns_for(which_core), axis=3)
-        return part.transpose(0, 1, 3, 2, 4)
-
-    mine = pick(core)
     swap = [(2 * c + b, 2 * c + 1 - b) for c in range(chips) for b in range(2)]
-    theirs = lax.ppermute(pick(1 - core), "cross", swap)
+    theirs = lax.ppermute(arrange(0, 1 - core), "cross", swap)
 
     def same_core(offset):
         return [(2 * c + b, 2 * ((c + offset) % chips) + b) for c in range(chips) for b in range(2)]
@@ -53,8 +51,12 @@
         upper = shifted(current, "chain", -dist)
         own = jnp.stack([current, lower, upper])
         pieces = [own] + [lax.ppermute(own, "cross", same_core(-off)) for off in OFFSETS[1:]]
-        given = lax.ppermute(partial(theirs[level], pieces), "cross", swap)
-        total = partial(mine[level], pieces) + given
+        their_part = partial(theirs, pieces)
+        if level + 1 < levels:
+            given, theirs = lax.ppermute((their_part, arrange(level + 1, 1 - core)), "cross", swap)
+        else:
+            given = lax.ppermute(their_part, "cross", swap)
+        total = partial(arrange(level, core), pieces) + given
         current = total.astype(jnp.bfloat16)
     return current[None]
 

time: 280 us -> 313 us (1.12)
  starting transfers between devices: 135 us -> 152 us
  local copies, waits for them, and re-layouts: 20.5 us -> 35.5 us
  waiting for transfers between devices: 104 us -> 91 us
  other arithmetic: 7.78 us -> 13.7 us
  matrix products: 11.7 us -> 16.3 us
    ppermute x7 -> x12, starting transfers between devices: 27.3 us -> 43.7 us  [the longest x10 31.6 us: body(): lax.ppermute((their_part, arrange(level + 1, 1 - core)), 'cross', swap)]
    ppermute x12, waiting for transfers between devices: 22.9 us -> 9.21 us  [shifted(): lax.ppermute(value, axis, [(source, source + steps) for source in range(i...]
    gather x2 -> x12, local copies, waits for them, and re-layouts: 6.67 us -> 17 us  [arrange(): part = jnp.take(signed, columns_for(which_core), axis=2)]
    neg x2 -> x12, local copies, waits for them, and re-layouts: 2.81 us -> 8.9 us  [the longest x6 5.14 us: arrange(): -lower_factor[level, 0]]
    dot_general x48, matrix products: 11.7 us -> 16.3 us  [partial(): jnp.einsum('ibk,bkr->ir', mat[:, j], piece, preferred_element_type=jnp.fl...]
    unnamed x5 -> x56, local copies, waits for them, and re-layouts: 6.42 us -> 3.19 us
    another operation x1 -> x6, other arithmetic: 3.54 us -> 6.58 us  [arrange(): jnp.stack([self_factor[level, 0], -lower_factor[level, 0], -upper_factor[...]
  transfers between devices with their start and end apart: 37 -> 42, of which waited for: 30 -> 25; matrix products, arithmetic and copies ran while one was open for 4% -> 19% of each run, Pallas kernels for 0% -> 0%
where the time goes in v4:
time: 313 us; the launch traced here: 310 us
  starting transfers between devices  152 us (49%)
  waiting for transfers between devices  91 us (29%)
  local copies, waits for them, and re-layouts  35.5 us (11%)
  matrix products  16.3 us (5%)
  other arithmetic  13.7 us (4%)
    ppermute x18, waiting for transfers between devices, body(): lax.ppermute(own, 'cross', same_core(-off))  79.4 us
    ppermute x12, starting transfers between devices, shifted(): lax.ppermute(value, axis, [(source, source + steps) for source in range(i...  57.4 us
    ppermute x18, starting transfers between devices, body(): lax.ppermute(own, 'cross', same_core(-off))  51.1 us
    ppermute x10, starting transfers between devices, body(): lax.ppermute((their_part, arrange(level + 1, 1 - core)), 'cross', swap)  31.6 us
    gather x12, local copies, waits for them, and re-layouts, arrange(): part = jnp.take(signed, columns_for(which_core), axis=2)  17 us
    dot_general x48, matrix products, partial(): jnp.einsum('ibk,bkr->ir', mat[:, j], piece, preferred_element_type=jnp.fl...  16.3 us
    ppermute x12, waiting for transfers between devices, shifted(): lax.ppermute(value, axis, [(source, source + steps) for source in range(i...  9.21 us
    ppermute x1, starting transfers between devices, body(): theirs = lax.ppermute(arrange(0, 1 - core), 'cross', swap)  7.87 us
  transfers between devices with their start and end apart: 42, of which 25 were waited for; matrix products, arithmetic and copies ran while one was open for 19% of the time, Pallas kernels for 0%

profile of v4, /device:TPU:1, one launch (start us, length us, event | category | flops | bytes accessed | tf_op | source)
XLA Modules:
  0.0 310.2 jit_solution(14624257072746874211)
XLA Ops:
  1.3 6.1 %collective-permute-start = (bf16[128,512]{1,0:T(8,128)(2,1)}, bf16[128,512]{1,0:T(8,128)(2,1)}, u32[]{:S(2)}, u32[]{:S(2)}) collective-permute-start(bf16[128,512]{1,0:T(8,128)(2,1)} %bitcast.484), channel_id=1, source_target_pairs={{0,8},{8,16},{16,24},{24,32},{32,40},{40,48},{48,56},{56,64},{64,7... | collective-permute-start | bytes 393224 | tf_op jit(solution)/shard_map/ppermute | solution.py:10
  46.0 7.9 %collective-permute-start.5 = (bf16[128,4,3,128]{3,0,2,1:T(8,128)(2,1)}, bf16[128,4,3,128]{3,0,2,1:T(8,128)(2,1)}, u32[]{:S(2)}, u32[]{:S(2)}) collective-permute-start(bf16[128,4,3,128]{3,0,2,1:T(8,128)(2,1)} %get-tuple-element.39), channel_id=1, source_target_pairs={{0,1},{1,0},{2,3},{3,2},{4,5},{5,4},{6,7},{7,6},{8,9},{9,8},{10,11... | collective-permute-start | bytes 1179656 | tf_op jit(solution)/shard_map/ppermute | solution.py:35
  67.1 3.4 %collective-permute-start.2 = (bf16[3,128,512]{2,1,0:T(8,128)(2,1)}, bf16[3,128,512]{2,1,0:T(8,128)(2,1)S(1)}, u32[]{:S(2)}, u32[]{:S(2)}) collective-permute-start(bf16[3,128,512]{2,1,0:T(8,128)(2,1)} %pad_maximum_fusion.6), channel_id=1, source_target_pairs={{0,2},{1,3},{2,4},{3,5},{4,6},{5,7},{6,0},{7,1},{8,10},{9,11},{10,... | collective-permute-start | bytes 1179656 | tf_op jit(solution)/shard_map/ppermute | solution.py:53
  73.0 5.0 %collective-permute-done.3 = bf16[3,128,512]{2,1,0:T(8,128)(2,1)S(1)} collective-permute-done((bf16[3,128,512]{2,1,0:T(8,128)(2,1)}, bf16[3,128,512]{2,1,0:T(8,128)(2,1)S(1)}, u32[]{:S(2)}, u32[]{:S(2)}) %collective-permute-start.3) | collective-permute-done | bytes 393248 | tf_op jit(solution)/shard_map/ppermute | solution.py:53
  90.5 4.9 %collective-permute-start.7 = (bf16[128,512]{1,0:T(8,128)(2,1)S(1)}, bf16[128,512]{1,0:T(8,128)(2,1)S(1)}, u32[]{:S(2)}, u32[]{:S(2)}) collective-permute-start(bf16[128,512]{1,0:T(8,128)(2,1)S(1)} %fusion.47), channel_id=1, source_target_pairs={{0,16},{8,24},{16,32},{24,40},{32,48},{40,56},{48,64},{56,72},{64,... | collective-permute-start | bytes 393224 | tf_op jit(solution)/shard_map/ppermute | solution.py:10
  98.4 4.2 %collective-permute-start.10 = (bf16[3,128,512]{2,1,0:T(8,128)(2,1)S(1)}, bf16[3,128,512]{2,1,0:T(8,128)(2,1)S(1)}, u32[]{:S(2)}, u32[]{:S(2)}) collective-permute-start(bf16[3,128,512]{2,1,0:T(8,128)(2,1)S(1)} %pad_maximum_fusion.7), channel_id=1, source_target_pairs={{0,6},{1,7},{2,0},{3,1},{4,2},{5,3},{6,4},{7,5},{8,14},{9,15},{10,... | collective-permute-start | bytes 1179656 | tf_op jit(solution)/shard_map/ppermute | solution.py:53
  104.5 3.1 collective-permute-start.11
  107.7 3.1 collective-permute-done.10
  111.0 13.1 %collective-permute-done.9 = bf16[3,128,512]{2,1,0:T(8,128)(2,1)S(1)} collective-permute-done((bf16[3,128,512]{2,1,0:T(8,128)(2,1)S(1)}, bf16[3,128,512]{2,1,0:T(8,128)(2,1)S(1)}, u32[]{:S(2)}, u32[]{:S(2)}) %collective-permute-start.9) | collective-permute-done | bytes 393248 | tf_op jit(solution)/shard_map/ppermute | solution.py:53
  124.8 3.5 %collective-permute-start.13 = (f32[128,512]{1,0:T(8,128)S(1)}, f32[128,512]{1,0:T(8,128)S(1)}, u32[]{:S(2)}, u32[]{:S(2)}) collective-permute-start(f32[128,512]{1,0:T(8,128)S(1)} %fusion.13), channel_id=1, source_target_pairs={{0,1},{1,0},{2,3},{3,2},{4,5},{5,4},{6,7},{7,6},{8,9},{9,8},{10,11... | collective-permute-start | bytes 786440 | tf_op jit(solution)/shard_map/ppermute | solution.py:56
  131.0 10.4 %collective-permute-start.14 = (bf16[128,512]{1,0:T(8,128)(2,1)S(1)}, bf16[128,512]{1,0:T(8,128)(2,1)S(1)}, u32[]{:S(2)}, u32[]{:S(2)}) collective-permute-start(bf16[128,512]{1,0:T(8,128)(2,1)S(1)} %fusion.46), channel_id=1, source_target_pairs={{0,32},{8,40},{16,48},{24,56},{32,64},{40,72},{48,80},{56,88},{64,... | collective-permute-start | bytes 393224 | tf_op jit(solution)/shard_map/ppermute | solution.py:10
  144.0 4.8 %collective-permute-done.14 = bf16[128,512]{1,0:T(8,128)(2,1)S(1)} collective-permute-done((bf16[128,512]{1,0:T(8,128)(2,1)S(1)}, bf16[128,512]{1,0:T(8,128)(2,1)S(1)}, u32[]{:S(2)}, u32[]{:S(2)}) %collective-permute-start.14) | collective-permute-done | bytes 131104 | tf_op jit(solution)/shard_map/ppermute | solution.py:10
  150.8 3.4 %collective-permute-start.16 = (bf16[3,128,512]{2,1,0:T(8,128)(2,1)S(1)}, bf16[3,128,512]{2,1,0:T(8,128)(2,1)S(1)}, u32[]{:S(2)}, u32[]{:S(2)}) collective-permute-start(bf16[3,128,512]{2,1,0:T(8,128)(2,1)S(1)} %pad_maximum_fusion.8), channel_id=1, source_target_pairs={{0,2},{1,3},{2,4},{3,5},{4,6},{5,7},{6,0},{7,1},{8,10},{9,11},{10,... | collective-permute-start | bytes 1179656 | tf_op jit(solution)/shard_map/ppermute | solution.py:53
  154.2 3.4 %collective-permute-start.18 = (bf16[3,128,512]{2,1,0:T(8,128)(2,1)S(1)}, bf16[3,128,512]{2,1,0:T(8,128)(2,1)S(1)}, u32[]{:S(2)}, u32[]{:S(2)}) collective-permute-start(bf16[3,128,512]{2,1,0:T(8,128)(2,1)S(1)} %pad_maximum_fusion.8), channel_id=1, source_target_pairs={{0,4},{1,5},{2,6},{3,7},{4,0},{5,1},{6,2},{7,3},{8,12},{9,13},{10,... | collective-permute-start | bytes 1179656 | tf_op jit(solution)/shard_map/ppermute | solution.py:53
  157.6 3.4 %collective-permute-done.17 = bf16[3,128,512]{2,1,0:T(8,128)(2,1)S(1)} collective-permute-done((bf16[3,128,512]{2,1,0:T(8,128)(2,1)S(1)}, bf16[3,128,512]{2,1,0:T(8,128)(2,1)S(1)}, u32[]{:S(2)}, u32[]{:S(2)}) %collective-permute-start.17) | collective-permute-done | bytes 393248 | tf_op jit(solution)/shard_map/ppermute | solution.py:53
  164.4 8.1 %collective-permute-done.18 = bf16[3,128,512]{2,1,0:T(8,128)(2,1)S(1)} collective-permute-done((bf16[3,128,512]{2,1,0:T(8,128)(2,1)S(1)}, bf16[3,128,512]{2,1,0:T(8,128)(2,1)S(1)}, u32[]{:S(2)}, u32[]{:S(2)}) %collective-permute-start.18) | collective-permute-done | bytes 393248 | tf_op jit(solution)/shard_map/ppermute | solution.py:53
  173.0 3.7 %collective-permute-start.20 = (f32[128,512]{1,0:T(8,128)S(1)}, f32[128,512]{1,0:T(8,128)S(1)}, u32[]{:S(2)}, u32[]{:S(2)}) collective-permute-start(f32[128,512]{1,0:T(8,128)S(1)} %fusion.20), channel_id=1, source_target_pairs={{0,1},{1,0},{2,3},{3,2},{4,5},{5,4},{6,7},{7,6},{8,9},{9,8},{10,11... | collective-permute-start | bytes 786440 | tf_op jit(solution)/shard_map/ppermute | solution.py:56
  179.2 10.6 %collective-permute-start.21 = (bf16[128,512]{1,0:T(8,128)(2,1)S(1)}, bf16[128,512]{1,0:T(8,128)(2,1)S(1)}, u32[]{:S(2)}, u32[]{:S(2)}) collective-permute-start(bf16[128,512]{1,0:T(8,128)(2,1)S(1)} %fusion.45), channel_id=1, source_target_pairs={{0,64},{8,72},{16,80},{24,88},{32,96},{40,104},{48,112},{56,120},{... | collective-permute-start | bytes 393224 | tf_op jit(solution)/shard_map/ppermute | solution.py:10
  194.4 3.4 %collective-permute-start.23 = (bf16[3,128,512]{2,1,0:T(8,128)(2,1)S(1)}, bf16[3,128,512]{2,1,0:T(8,128)(2,1)S(1)}, u32[]{:S(2)}, u32[]{:S(2)}) collective-permute-start(bf16[3,128,512]{2,1,0:T(8,128)(2,1)S(1)} %pad_maximum_fusion.9), channel_id=1, source_target_pairs={{0,2},{1,3},{2,4},{3,5},{4,6},{5,7},{6,0},{7,1},{8,10},{9,11},{10,... | collective-permute-start | bytes 1179656 | tf_op jit(solution)/shard_map/ppermute | solution.py:53
  197.8 3.4 %collective-permute-start.25 = (bf16[3,128,512]{2,1,0:T(8,128)(2,1)S(1)}, bf16[3,128,512]{2,1,0:T(8,128)(2,1)S(1)}, u32[]{:S(2)}, u32[]{:S(2)}) collective-permute-start(bf16[3,128,512]{2,1,0:T(8,128)(2,1)S(1)} %pad_maximum_fusion.9), channel_id=1, source_target_pairs={{0,4},{1,5},{2,6},{3,7},{4,0},{5,1},{6,2},{7,3},{8,12},{9,13},{10,... | collective-permute-start | bytes 1179656 | tf_op jit(solution)/shard_map/ppermute | solution.py:53
  207.3 8.1 %collective-permute-done.25 = bf16[3,128,512]{2,1,0:T(8,128)(2,1)S(1)} collective-permute-done((bf16[3,128,512]{2,1,0:T(8,128)(2,1)S(1)}, bf16[3,128,512]{2,1,0:T(8,128)(2,1)S(1)}, u32[]{:S(2)}, u32[]{:S(2)}) %collective-permute-start.25) | collective-permute-done | bytes 393248 | tf_op jit(solution)/shard_map/ppermute | solution.py:53
  215.9 4.2 %collective-permute-start.27 = (f32[128,512]{1,0:T(8,128)S(1)}, f32[128,512]{1,0:T(8,128)S(1)}, u32[]{:S(2)}, u32[]{:S(2)}) collective-permute-start(f32[128,512]{1,0:T(8,128)S(1)} %fusion.27), channel_id=1, source_target_pairs={{0,1},{1,0},{2,3},{3,2},{4,5},{5,4},{6,7},{7,6},{8,9},{9,8},{10,11... | collective-permute-start | bytes 786440 | tf_op jit(solution)/shard_map/ppermute | solution.py:56
  222.8 5.5 %collective-permute-start.28 = (bf16[128,512]{1,0:T(8,128)(2,1)S(1)}, bf16[128,512]{1,0:T(8,128)(2,1)S(1)}, u32[]{:S(2)}, u32[]{:S(2)}) collective-permute-start(bf16[128,512]{1,0:T(8,128)(2,1)S(1)} %fusion.44), channel_id=1, source_target_pairs={{0,128},{8,136},{16,144},{24,152},{32,160},{40,168},{48,176},{56,1... | collective-permute-start | bytes 393224 | tf_op jit(solution)/shard_map/ppermute | solution.py:10
  234.7 3.4 %collective-permute-start.30 = (bf16[3,128,512]{2,1,0:T(8,128)(2,1)S(1)}, bf16[3,128,512]{2,1,0:T(8,128)(2,1)S(1)}, u32[]{:S(2)}, u32[]{:S(2)}) collective-permute-start(bf16[3,128,512]{2,1,0:T(8,128)(2,1)S(1)} %pad_maximum_fusion.10), channel_id=1, source_target_pairs={{0,2},{1,3},{2,4},{3,5},{4,6},{5,7},{6,0},{7,1},{8,10},{9,11},{10,... | collective-permute-start | bytes 1179656 | tf_op jit(solution)/shard_map/ppermute | solution.py:53
  238.1 3.4 %collective-permute-start.32 = (bf16[3,128,512]{2,1,0:T(8,128)(2,1)S(1)}, bf16[3,128,512]{2,1,0:T(8,128)(2,1)S(1)}, u32[]{:S(2)}, u32[]{:S(2)}) collective-permute-start(bf16[3,128,512]{2,1,0:T(8,128)(2,1)S(1)} %pad_maximum_fusion.10), channel_id=1, source_target_pairs={{0,4},{1,5},{2,6},{3,7},{4,0},{5,1},{6,2},{7,3},{8,12},{9,13},{10,... | collective-permute-start | bytes 1179656 | tf_op jit(solution)/shard_map/ppermute | solution.py:53
  247.8 8.2 %collective-permute-done.32 = bf16[3,128,512]{2,1,0:T(8,128)(2,1)S(1)} collective-permute-done((bf16[3,128,512]{2,1,0:T(8,128)(2,1)S(1)}, bf16[3,128,512]{2,1,0:T(8,128)(2,1)S(1)}, u32[]{:S(2)}, u32[]{:S(2)}) %collective-permute-start.32) | collective-permute-done | bytes 393248 | tf_op jit(solution)/shard_map/ppermute | solution.py:53
  256.4 4.0 %collective-permute-start.34 = (f32[128,512]{1,0:T(8,128)S(1)}, f32[128,512]{1,0:T(8,128)S(1)}, u32[]{:S(2)}, u32[]{:S(2)}) collective-permute-start(f32[128,512]{1,0:T(8,128)S(1)} %fusion.34), channel_id=1, source_target_pairs={{0,1},{1,0},{2,3},{3,2},{4,5},{5,4},{6,7},{7,6},{8,9},{9,8},{10,11... | collective-permute-start | bytes 786440 | tf_op jit(solution)/shard_map/ppermute | solution.py:56
  263.1 12.2 %collective-permute-start.35 = (bf16[128,512]{1,0:T(8,128)(2,1)S(1)}, bf16[128,512]{1,0:T(8,128)(2,1)S(1)}, u32[]{:S(2)}, u32[]{:S(2)}) collective-permute-start(bf16[128,512]{1,0:T(8,128)(2,1)S(1)} %fusion.43), channel_id=1, source_target_pairs={{0,256},{8,264},{16,272},{24,280},{32,288},{40,296},{48,304},{56,3... | collective-permute-start | bytes 393224 | tf_op jit(solution)/shard_map/ppermute | solution.py:10
  282.4 3.4 %collective-permute-start.37 = (bf16[3,128,512]{2,1,0:T(8,128)(2,1)S(1)}, bf16[3,128,512]{2,1,0:T(8,128)(2,1)S(1)}, u32[]{:S(2)}, u32[]{:S(2)}) collective-permute-start(bf16[3,128,512]{2,1,0:T(8,128)(2,1)S(1)} %pad_maximum_fusion.11), channel_id=1, source_target_pairs={{0,2},{1,3},{2,4},{3,5},{4,6},{5,7},{6,0},{7,1},{8,10},{9,11},{10,... | collective-permute-start | bytes 1179656 | tf_op jit(solution)/shard_map/ppermute | solution.py:53
  285.8 3.4 %collective-permute-start.39 = (bf16[3,128,512]{2,1,0:T(8,128)(2,1)S(1)}, bf16[3,128,512]{2,1,0:T(8,128)(2,1)S(1)}, u32[]{:S(2)}, u32[]{:S(2)}) collective-permute-start(bf16[3,128,512]{2,1,0:T(8,128)(2,1)S(1)} %pad_maximum_fusion.11), channel_id=1, source_target_pairs={{0,4},{1,5},{2,6},{3,7},{4,0},{5,1},{6,2},{7,3},{8,12},{9,13},{10,... | collective-permute-start | bytes 1179656 | tf_op jit(solution)/shard_map/ppermute | solution.py:53
  295.2 8.1 %collective-permute-done.39 = bf16[3,128,512]{2,1,0:T(8,128)(2,1)S(1)} collective-permute-done((bf16[3,128,512]{2,1,0:T(8,128)(2,1)S(1)}, bf16[3,128,512]{2,1,0:T(8,128)(2,1)S(1)}, u32[]{:S(2)}, u32[]{:S(2)}) %collective-permute-start.39) | collective-permute-done | bytes 393248 | tf_op jit(solution)/shard_map/ppermute | solution.py:53
  303.8 4.3 %collective-permute-start.41 = (f32[128,512]{1,0:T(8,128)S(1)}, f32[128,512]{1,0:T(8,128)S(1)}, u32[]{:S(2)}, u32[]{:S(2)}) collective-permute-start(f32[128,512]{1,0:T(8,128)S(1)} %fusion.41), channel_id=1, source_target_pairs={{0,1},{1,0},{2,3},{3,2},{4,5},{5,4},{6,7},{7,6},{8,9},{9,8},{10,11... | collective-permute-start | bytes 786440 | tf_op jit(solution)/shard_map/ppermute | solution.py:58
  (219 shorter events, 131.9 us)
Async XLA Ops:
  0.0 54.0 %collective-permute-start.1 = (bf16[128,512]{1,0:T(8,128)(2,1)}, bf16[128,512]{1,0:T(8,128)(2,1)}, u32[]{:S(2)}, u32[]{:S(2)}) collective-permute-start(bf16[128,512]{1,0:T(8,128)(2,1)} %bitcast.483), channel_id=1, source_target_pairs={{8,0},{16,8},{24,16},{32,24},{40,32},{48,40},{56,48},{64,56},{72,6... | collective-permute-start | bytes 393224 | tf_op jit(solution)/shard_map/ppermute | solution.py:10
  1.3 52.7 %collective-permute-start = (bf16[128,512]{1,0:T(8,128)(2,1)}, bf16[128,512]{1,0:T(8,128)(2,1)}, u32[]{:S(2)}, u32[]{:S(2)}) collective-permute-start(bf16[128,512]{1,0:T(8,128)(2,1)} %bitcast.484), channel_id=1, source_target_pairs={{0,8},{8,16},{16,24},{24,32},{32,40},{40,48},{48,56},{56,64},{64,7... | collective-permute-start | bytes 393224 | tf_op jit(solution)/shard_map/ppermute | solution.py:10
  46.0 25.8 %collective-permute-start.5 = (bf16[128,4,3,128]{3,0,2,1:T(8,128)(2,1)}, bf16[128,4,3,128]{3,0,2,1:T(8,128)(2,1)}, u32[]{:S(2)}, u32[]{:S(2)}) collective-permute-start(bf16[128,4,3,128]{3,0,2,1:T(8,128)(2,1)} %get-tuple-element.39), channel_id=1, source_target_pairs={{0,1},{1,0},{2,3},{3,2},{4,5},{5,4},{6,7},{7,6},{8,9},{9,8},{10,11... | collective-permute-start | bytes 1179656 | tf_op jit(solution)/shard_map/ppermute | solution.py:35
  55.9 16.0 %collective-permute-start.4 = (bf16[3,128,512]{2,1,0:T(8,128)(2,1)}, bf16[3,128,512]{2,1,0:T(8,128)(2,1)S(1)}, u32[]{:S(2)}, u32[]{:S(2)}) collective-permute-start(bf16[3,128,512]{2,1,0:T(8,128)(2,1)} %pad_maximum_fusion.6), channel_id=1, source_target_pairs={{0,4},{1,5},{2,6},{3,7},{4,0},{5,1},{6,2},{7,3},{8,12},{9,13},{10,... | collective-permute-start | bytes 1179656 | tf_op jit(solution)/shard_map/ppermute | solution.py:53
  65.2 12.8 %collective-permute-start.3 = (bf16[3,128,512]{2,1,0:T(8,128)(2,1)}, bf16[3,128,512]{2,1,0:T(8,128)(2,1)S(1)}, u32[]{:S(2)}, u32[]{:S(2)}) collective-permute-start(bf16[3,128,512]{2,1,0:T(8,128)(2,1)} %pad_maximum_fusion.6), channel_id=1, source_target_pairs={{0,6},{1,7},{2,0},{3,1},{4,2},{5,3},{6,4},{7,5},{8,14},{9,15},{10,... | collective-permute-start | bytes 1179656 | tf_op jit(solution)/shard_map/ppermute | solution.py:53
  67.1 14.3 %collective-permute-start.2 = (bf16[3,128,512]{2,1,0:T(8,128)(2,1)}, bf16[3,128,512]{2,1,0:T(8,128)(2,1)S(1)}, u32[]{:S(2)}, u32[]{:S(2)}) collective-permute-start(bf16[3,128,512]{2,1,0:T(8,128)(2,1)} %pad_maximum_fusion.6), channel_id=1, source_target_pairs={{0,2},{1,3},{2,4},{3,5},{4,6},{5,7},{6,0},{7,1},{8,10},{9,11},{10,... | collective-permute-start | bytes 1179656 | tf_op jit(solution)/shard_map/ppermute | solution.py:53
  95.5 12.2 %collective-permute-start.12 = (bf16[128,4,3,128]{3,0,2,1:T(8,128)(2,1)S(1)}, bf16[128,4,3,128]{3,0,2,1:T(8,128)(2,1)S(1)}, u32[]{:S(2)}, u32[]{:S(2)}) collective-permute-start(bf16[128,4,3,128]{3,0,2,1:T(8,128)(2,1)S(1)} %copy-done.18), channel_id=1, source_target_pairs={{0,1},{1,0},{2,3},{3,2},{4,5},{5,4},{6,7},{7,6},{8,9},{9,8},{10,11... | collective-permute-start | bytes 1179656 | tf_op jit(solution)/shard_map/ppermute | solution.py:56
  98.4 12.4 %collective-permute-start.10 = (bf16[3,128,512]{2,1,0:T(8,128)(2,1)S(1)}, bf16[3,128,512]{2,1,0:T(8,128)(2,1)S(1)}, u32[]{:S(2)}, u32[]{:S(2)}) collective-permute-start(bf16[3,128,512]{2,1,0:T(8,128)(2,1)S(1)} %pad_maximum_fusion.7), channel_id=1, source_target_pairs={{0,6},{1,7},{2,0},{3,1},{4,2},{5,3},{6,4},{7,5},{8,14},{9,15},{10,... | collective-permute-start | bytes 1179656 | tf_op jit(solution)/shard_map/ppermute | solution.py:53
  102.6 21.4 %collective-permute-start.9 = (bf16[3,128,512]{2,1,0:T(8,128)(2,1)S(1)}, bf16[3,128,512]{2,1,0:T(8,128)(2,1)S(1)}, u32[]{:S(2)}, u32[]{:S(2)}) collective-permute-start(bf16[3,128,512]{2,1,0:T(8,128)(2,1)S(1)} %pad_maximum_fusion.7), channel_id=1, source_target_pairs={{0,2},{1,3},{2,4},{3,5},{4,6},{5,7},{6,0},{7,1},{8,10},{9,11},{10,... | collective-permute-start | bytes 1179656 | tf_op jit(solution)/shard_map/ppermute | solution.py:53
  104.5 19.7 %collective-permute-start.11 = (bf16[3,128,512]{2,1,0:T(8,128)(2,1)S(1)}, bf16[3,128,512]{2,1,0:T(8,128)(2,1)S(1)}, u32[]{:S(2)}, u32[]{:S(2)}) collective-permute-start(bf16[3,128,512]{2,1,0:T(8,128)(2,1)S(1)} %pad_maximum_fusion.7), channel_id=1, source_target_pairs={{0,4},{1,5},{2,6},{3,7},{4,0},{5,1},{6,2},{7,3},{8,12},{9,13},{10,... | collective-permute-start | bytes 1179656 | tf_op jit(solution)/shard_map/ppermute | solution.py:53
  129.7 14.3 %collective-permute-start.15 = (bf16[128,512]{1,0:T(8,128)(2,1)S(1)}, bf16[128,512]{1,0:T(8,128)(2,1)S(1)}, u32[]{:S(2)}, u32[]{:S(2)}) collective-permute-start(bf16[128,512]{1,0:T(8,128)(2,1)S(1)} %fusion.46), channel_id=1, source_target_pairs={{32,0},{40,8},{48,16},{56,24},{64,32},{72,40},{80,48},{88,56},{96,... | collective-permute-start | bytes 393224 | tf_op jit(solution)/shard_map/ppermute | solution.py:10
  131.0 17.8 %collective-permute-start.14 = (bf16[128,512]{1,0:T(8,128)(2,1)S(1)}, bf16[128,512]{1,0:T(8,128)(2,1)S(1)}, u32[]{:S(2)}, u32[]{:S(2)}) collective-permute-start(bf16[128,512]{1,0:T(8,128)(2,1)S(1)} %fusion.46), channel_id=1, source_target_pairs={{0,32},{8,40},{16,48},{24,56},{32,64},{40,72},{48,80},{56,88},{64,... | collective-permute-start | bytes 393224 | tf_op jit(solution)/shard_map/ppermute | solution.py:10
  141.4 16.2 %collective-permute-start.19 = (bf16[128,4,3,128]{3,0,2,1:T(8,128)(2,1)S(1)}, bf16[128,4,3,128]{3,0,2,1:T(8,128)(2,1)S(1)}, u32[]{:S(2)}, u32[]{:S(2)}) collective-permute-start(bf16[128,4,3,128]{3,0,2,1:T(8,128)(2,1)S(1)} %copy-done.17), channel_id=1, source_target_pairs={{0,1},{1,0},{2,3},{3,2},{4,5},{5,4},{6,7},{7,6},{8,9},{9,8},{10,11... | collective-permute-start | bytes 1179656 | tf_op jit(solution)/shard_map/ppermute | solution.py:56
  148.9 12.1 %collective-permute-start.17 = (bf16[3,128,512]{2,1,0:T(8,128)(2,1)S(1)}, bf16[3,128,512]{2,1,0:T(8,128)(2,1)S(1)}, u32[]{:S(2)}, u32[]{:S(2)}) collective-permute-start(bf16[3,128,512]{2,1,0:T(8,128)(2,1)S(1)} %pad_maximum_fusion.8), channel_id=1, source_target_pairs={{0,6},{1,7},{2,0},{3,1},{4,2},{5,3},{6,4},{7,5},{8,14},{9,15},{10,... | collective-permute-start | bytes 1179656 | tf_op jit(solution)/shard_map/ppermute | solution.py:53
  150.8 13.3 %collective-permute-start.16 = (bf16[3,128,512]{2,1,0:T(8,128)(2,1)S(1)}, bf16[3,128,512]{2,1,0:T(8,128)(2,1)S(1)}, u32[]{:S(2)}, u32[]{:S(2)}) collective-permute-start(bf16[3,128,512]{2,1,0:T(8,128)(2,1)S(1)} %pad_maximum_fusion.8), channel_id=1, source_target_pairs={{0,2},{1,3},{2,4},{3,5},{4,6},{5,7},{6,0},{7,1},{8,10},{9,11},{10,... | collective-permute-start | bytes 1179656 | tf_op jit(solution)/shard_map/ppermute | solution.py:53
  154.2 18.3 %collective-permute-start.18 = (bf16[3,128,512]{2,1,0:T(8,128)(2,1)S(1)}, bf16[3,128,512]{2,1,0:T(8,128)(2,1)S(1)}, u32[]{:S(2)}, u32[]{:S(2)}) collective-permute-start(bf16[3,128,512]{2,1,0:T(8,128)(2,1)S(1)} %pad_maximum_fusion.8), channel_id=1, source_target_pairs={{0,4},{1,5},{2,6},{3,7},{4,0},{5,1},{6,2},{7,3},{8,12},{9,13},{10,... | collective-permute-start | bytes 1179656 | tf_op jit(solution)/shard_map/ppermute | solution.py:53
  177.9 14.5 %collective-permute-start.22 = (bf16[128,512]{1,0:T(8,128)(2,1)S(1)}, bf16[128,512]{1,0:T(8,128)(2,1)S(1)}, u32[]{:S(2)}, u32[]{:S(2)}) collective-permute-start(bf16[128,512]{1,0:T(8,128)(2,1)S(1)} %fusion.45), channel_id=1, source_target_pairs={{64,0},{72,8},{80,16},{88,24},{96,32},{104,40},{112,48},{120,56},{... | collective-permute-start | bytes 393224 | tf_op jit(solution)/shard_map/ppermute | solution.py:10
  179.2 13.2 %collective-permute-start.21 = (bf16[128,512]{1,0:T(8,128)(2,1)S(1)}, bf16[128,512]{1,0:T(8,128)(2,1)S(1)}, u32[]{:S(2)}, u32[]{:S(2)}) collective-permute-start(bf16[128,512]{1,0:T(8,128)(2,1)S(1)} %fusion.45), channel_id=1, source_target_pairs={{0,64},{8,72},{16,80},{24,88},{32,96},{40,104},{48,112},{56,120},{... | collective-permute-start | bytes 393224 | tf_op jit(solution)/shard_map/ppermute | solution.py:10
  189.9 11.3 %collective-permute-start.26 = (bf16[128,4,3,128]{3,0,2,1:T(8,128)(2,1)S(1)}, bf16[128,4,3,128]{3,0,2,1:T(8,128)(2,1)S(1)}, u32[]{:S(2)}, u32[]{:S(2)}) collective-permute-start(bf16[128,4,3,128]{3,0,2,1:T(8,128)(2,1)S(1)} %copy-done.16), channel_id=1, source_target_pairs={{0,1},{1,0},{2,3},{3,2},{4,5},{5,4},{6,7},{7,6},{8,9},{9,8},{10,11... | collective-permute-start | bytes 1179656 | tf_op jit(solution)/shard_map/ppermute | solution.py:56
  192.5 11.4 %collective-permute-start.24 = (bf16[3,128,512]{2,1,0:T(8,128)(2,1)S(1)}, bf16[3,128,512]{2,1,0:T(8,128)(2,1)S(1)}, u32[]{:S(2)}, u32[]{:S(2)}) collective-permute-start(bf16[3,128,512]{2,1,0:T(8,128)(2,1)S(1)} %pad_maximum_fusion.9), channel_id=1, source_target_pairs={{0,6},{1,7},{2,0},{3,1},{4,2},{5,3},{6,4},{7,5},{8,14},{9,15},{10,... | collective-permute-start | bytes 1179656 | tf_op jit(solution)/shard_map/ppermute | solution.py:53
  194.4 12.7 %collective-permute-start.23 = (bf16[3,128,512]{2,1,0:T(8,128)(2,1)S(1)}, bf16[3,128,512]{2,1,0:T(8,128)(2,1)S(1)}, u32[]{:S(2)}, u32[]{:S(2)}) collective-permute-start(bf16[3,128,512]{2,1,0:T(8,128)(2,1)S(1)} %pad_maximum_fusion.9), channel_id=1, source_target_pairs={{0,2},{1,3},{2,4},{3,5},{4,6},{5,7},{6,0},{7,1},{8,10},{9,11},{10,... | collective-permute-start | bytes 1179656 | tf_op jit(solution)/shard_map/ppermute | solution.py:53
  197.8 17.6 %collective-permute-start.25 = (bf16[3,128,512]{2,1,0:T(8,128)(2,1)S(1)}, bf16[3,128,512]{2,1,0:T(8,128)(2,1)S(1)}, u32[]{:S(2)}, u32[]{:S(2)}) collective-permute-start(bf16[3,128,512]{2,1,0:T(8,128)(2,1)S(1)} %pad_maximum_fusion.9), channel_id=1, source_target_pairs={{0,4},{1,5},{2,6},{3,7},{4,0},{5,1},{6,2},{7,3},{8,12},{9,13},{10,... | collective-permute-start | bytes 1179656 | tf_op jit(solution)/shard_map/ppermute | solution.py:53
  228.3 13.2 %collective-permute-start.33 = (bf16[128,4,3,128]{3,0,2,1:T(8,128)(2,1)S(1)}, bf16[128,4,3,128]{3,0,2,1:T(8,128)(2,1)S(1)}, u32[]{:S(2)}, u32[]{:S(2)}) collective-permute-start(bf16[128,4,3,128]{3,0,2,1:T(8,128)(2,1)S(1)} %copy-done.15), channel_id=1, source_target_pairs={{0,1},{1,0},{2,3},{3,2},{4,5},{5,4},{6,7},{7,6},{8,9},{9,8},{10,11... | collective-permute-start | bytes 1179656 | tf_op jit(solution)/shard_map/ppermute | solution.py:56
  232.8 11.6 %collective-permute-start.31 = (bf16[3,128,512]{2,1,0:T(8,128)(2,1)S(1)}, bf16[3,128,512]{2,1,0:T(8,128)(2,1)S(1)}, u32[]{:S(2)}, u32[]{:S(2)}) collective-permute-start(bf16[3,128,512]{2,1,0:T(8,128)(2,1)S(1)} %pad_maximum_fusion.10), channel_id=1, source_target_pairs={{0,6},{1,7},{2,0},{3,1},{4,2},{5,3},{6,4},{7,5},{8,14},{9,15},{10,... | collective-permute-start | bytes 1179656 | tf_op jit(solution)/shard_map/ppermute | solution.py:53
  234.7 12.9 %collective-permute-start.30 = (bf16[3,128,512]{2,1,0:T(8,128)(2,1)S(1)}, bf16[3,128,512]{2,1,0:T(8,128)(2,1)S(1)}, u32[]{:S(2)}, u32[]{:S(2)}) collective-permute-start(bf16[3,128,512]{2,1,0:T(8,128)(2,1)S(1)} %pad_maximum_fusion.10), channel_id=1, source_target_pairs={{0,2},{1,3},{2,4},{3,5},{4,6},{5,7},{6,0},{7,1},{8,10},{9,11},{10,... | collective-permute-start | bytes 1179656 | tf_op jit(solution)/shard_map/ppermute | solution.py:53
  238.1 17.9 %collective-permute-start.32 = (bf16[3,128,512]{2,1,0:T(8,128)(2,1)S(1)}, bf16[3,128,512]{2,1,0:T(8,128)(2,1)S(1)}, u32[]{:S(2)}, u32[]{:S(2)}) collective-permute-start(bf16[3,128,512]{2,1,0:T(8,128)(2,1)S(1)} %pad_maximum_fusion.10), channel_id=1, source_target_pairs={{0,4},{1,5},{2,6},{3,7},{4,0},{5,1},{6,2},{7,3},{8,12},{9,13},{10,... | collective-permute-start | bytes 1179656 | tf_op jit(solution)/shard_map/ppermute | solution.py:53
  261.8 16.1 %collective-permute-start.36 = (bf16[128,512]{1,0:T(8,128)(2,1)S(1)}, bf16[128,512]{1,0:T(8,128)(2,1)S(1)}, u32[]{:S(2)}, u32[]{:S(2)}) collective-permute-start(bf16[128,512]{1,0:T(8,128)(2,1)S(1)} %fusion.43), channel_id=1, source_target_pairs={{256,0},{264,8},{272,16},{280,24},{288,32},{296,40},{304,48},{312,... | collective-permute-start | bytes 393224 | tf_op jit(solution)/shard_map/ppermute | solution.py:10
  263.1 17.3 %collective-permute-start.35 = (bf16[128,512]{1,0:T(8,128)(2,1)S(1)}, bf16[128,512]{1,0:T(8,128)(2,1)S(1)}, u32[]{:S(2)}, u32[]{:S(2)}) collective-permute-start(bf16[128,512]{1,0:T(8,128)(2,1)S(1)} %fusion.43), channel_id=1, source_target_pairs={{0,256},{8,264},{16,272},{24,280},{32,288},{40,296},{48,304},{56,3... | collective-permute-start | bytes 393224 | tf_op jit(solution)/shard_map/ppermute | solution.py:10
  275.4 13.8 %collective-permute-start.40 = (bf16[128,4,3,128]{3,0,2,1:T(8,128)(2,1)S(1)}, bf16[128,4,3,128]{3,0,2,1:T(8,128)(2,1)S(1)}, u32[]{:S(2)}, u32[]{:S(2)}) collective-permute-start(bf16[128,4,3,128]{3,0,2,1:T(8,128)(2,1)S(1)} %copy-done.14), channel_id=1, source_target_pairs={{0,1},{1,0},{2,3},{3,2},{4,5},{5,4},{6,7},{7,6},{8,9},{9,8},{10,11... | collective-permute-start | bytes 1179656 | tf_op jit(solution)/shard_map/ppermute | solution.py:56
  280.5 11.3 %collective-permute-start.38 = (bf16[3,128,512]{2,1,0:T(8,128)(2,1)S(1)}, bf16[3,128,512]{2,1,0:T(8,128)(2,1)S(1)}, u32[]{:S(2)}, u32[]{:S(2)}) collective-permute-start(bf16[3,128,512]{2,1,0:T(8,128)(2,1)S(1)} %pad_maximum_fusion.11), channel_id=1, source_target_pairs={{0,6},{1,7},{2,0},{3,1},{4,2},{5,3},{6,4},{7,5},{8,14},{9,15},{10,... | collective-permute-start | bytes 1179656 | tf_op jit(solution)/shard_map/ppermute | solution.py:53
  282.4 12.6 %collective-permute-start.37 = (bf16[3,128,512]{2,1,0:T(8,128)(2,1)S(1)}, bf16[3,128,512]{2,1,0:T(8,128)(2,1)S(1)}, u32[]{:S(2)}, u32[]{:S(2)}) collective-permute-start(bf16[3,128,512]{2,1,0:T(8,128)(2,1)S(1)} %pad_maximum_fusion.11), channel_id=1, source_target_pairs={{0,2},{1,3},{2,4},{3,5},{4,6},{5,7},{6,0},{7,1},{8,10},{9,11},{10,... | collective-permute-start | bytes 1179656 | tf_op jit(solution)/shard_map/ppermute | solution.py:53
  285.8 17.5 %collective-permute-start.39 = (bf16[3,128,512]{2,1,0:T(8,128)(2,1)S(1)}, bf16[3,128,512]{2,1,0:T(8,128)(2,1)S(1)}, u32[]{:S(2)}, u32[]{:S(2)}) collective-permute-start(bf16[3,128,512]{2,1,0:T(8,128)(2,1)S(1)} %pad_maximum_fusion.11), channel_id=1, source_target_pairs={{0,4},{1,5},{2,6},{3,7},{4,0},{5,1},{6,2},{7,3},{8,12},{9,13},{10,... | collective-permute-start | bytes 1179656 | tf_op jit(solution)/shard_map/ppermute | solution.py:53
  (29 other events, 186.9 us)

commit v5 on v2

--- a/solution.py
+++ b/solution.py
@@ -25,12 +25,12 @@
     def columns_for(which_core):
         return jnp.stack([2 * ((chip + off) % chips) + which_core for off in OFFSETS])
 
-    signed = jnp.stack([self_factor[:, 0], -lower_factor[:, 0], -upper_factor[:, 0]], axis=2)
-    signed = signed.reshape(levels, rows, 3, ncross, rows)
+    blocks = [f[:, 0].reshape(levels, rows, ncross, rows) for f in (self_factor, lower_factor, upper_factor)]
 
     def pick(which_core):
-        part = jnp.take(signed, columns_for(which_core), axis=3)
-        return part.transpose(0, 1, 3, 2, 4)
+        idx = columns_for(which_core)
+        parts = [jnp.take(blocks[0], idx, axis=2)] + [-jnp.take(f, idx, axis=2) for f in blocks[1:]]
+        return jnp.stack(parts, axis=3)
 
     mine = pick(core)
     swap = [(2 * c + b, 2 * c + 1 - b) for c in range(chips) for b in range(2)]

time: 280 us -> 293 us (1.046)
  waiting for transfers between devices: 104 us -> 111 us
  local copies, waits for them, and re-layouts: 20.5 us -> 25 us
  starting transfers between devices: 135 us -> 138 us
    ppermute x18, waiting for transfers between devices: 77.9 us -> 85.5 us  [body(): lax.ppermute(own, 'cross', same_core(-off))]
    ppermute x6, starting transfers between devices: 18.5 us -> 22.3 us  [body(): given = lax.ppermute(partial(theirs[level], pieces), 'cross', swap)]
    gather x2 -> x6, local copies, waits for them, and re-layouts: 6.67 us -> 10.4 us  [the longest x4 7.36 us: pick(): jnp.take(f, idx, axis=2)]
    unnamed x5 -> x7, local copies, waits for them, and re-layouts: 6.42 us -> 7.09 us
  transfers between devices with their start and end apart: 37 -> 37, of which waited for: 30 -> 30; matrix products, arithmetic and copies ran while one was open for 4% -> 5% of each run, Pallas kernels for 0% -> 0%
where the time goes in v5:
time: 293 us; the launch traced here: 292 us
  starting transfers between devices  138 us (47%)
  waiting for transfers between devices  111 us (38%)
  local copies, waits for them, and re-layouts  25 us (9%)
  matrix products  11.7 us (4%)
  other arithmetic  5.84 us (2%)
    ppermute x18, waiting for transfers between devices, body(): lax.ppermute(own, 'cross', same_core(-off))  85.5 us
    ppermute x12, starting transfers between devices, shifted(): lax.ppermute(value, axis, [(source, source + steps) for source in range(i...  58.8 us
    ppermute x18, starting transfers between devices, body(): lax.ppermute(own, 'cross', same_core(-off))  47.7 us
    ppermute x12, waiting for transfers between devices, shifted(): lax.ppermute(value, axis, [(source, source + steps) for source in range(i...  22.7 us
    ppermute x6, starting transfers between devices, body(): given = lax.ppermute(partial(theirs[level], pieces), 'cross', swap)  22.3 us
    dot_general x48, matrix products, partial(): jnp.einsum('ibk,bkr->ir', mat[:, j], piece, preferred_element_type=jnp.fl...  11.7 us
    ppermute x1, starting transfers between devices, body(): theirs = lax.ppermute(pick(1 - core), 'cross', swap)  8.78 us
    gather x4, local copies, waits for them, and re-layouts, pick(): jnp.take(f, idx, axis=2)  7.36 us
  transfers between devices with their start and end apart: 37, of which 30 were waited for; matrix products, arithmetic and copies ran while one was open for 5% of the time, Pallas kernels for 0%

profile of v5, /device:TPU:1, one launch (start us, length us, event | category | flops | bytes accessed | tf_op | source)
XLA Modules:
  0.0 292.2 jit_solution(5888418277975177709)
XLA Ops:
  23.3 8.8 %collective-permute-start.5 = (bf16[6,128,4,3,128]{4,1,3,2,0:T(8,128)(2,1)}, bf16[6,128,4,3,128]{4,1,3,2,0:T(8,128)(2,1)}, u32[]{:S(2)}, u32[]{:S(2)}) collective-permute-start(bf16[6,128,4,3,128]{4,1,3,2,0:T(8,128)(2,1)} %pad_maximum_fusion.1), channel_id=1, source_target_pairs={{0,1},{1,0},{2,3},{3,2},{4,5},{5,4},{6,7},{7,6},{8,9},{9,8},{10,11... | collective-permute-start | bytes 7077896 | tf_op jit(solution)/shard_map/ppermute | solution.py:37
  33.4 4.0 %collective-permute-start = (bf16[128,512]{1,0:T(8,128)(2,1)S(1)}, bf16[128,512]{1,0:T(8,128)(2,1)S(1)}, u32[]{:S(2)}, u32[]{:S(2)}) collective-permute-start(bf16[128,512]{1,0:T(8,128)(2,1)S(1)} %bitcast.480), channel_id=1, source_target_pairs={{0,8},{8,16},{16,24},{24,32},{32,40},{40,48},{48,56},{56,64},{64,7... | collective-permute-start | bytes 393224 | tf_op jit(solution)/shard_map/ppermute | solution.py:10
  46.9 3.4 %collective-permute-start.2 = (bf16[3,128,512]{2,1,0:T(8,128)(2,1)S(1)}, bf16[3,128,512]{2,1,0:T(8,128)(2,1)S(1)}, u32[]{:S(2)}, u32[]{:S(2)}) collective-permute-start(bf16[3,128,512]{2,1,0:T(8,128)(2,1)S(1)} %pad_maximum_fusion.2), channel_id=1, source_target_pairs={{0,2},{1,3},{2,4},{3,5},{4,6},{5,7},{6,0},{7,1},{8,10},{9,11},{10,... | collective-permute-start | bytes 1179656 | tf_op jit(solution)/shard_map/ppermute | solution.py:55
  50.3 5.8 %collective-permute-done.4 = bf16[3,128,512]{2,1,0:T(8,128)(2,1)S(1)} collective-permute-done((bf16[3,128,512]{2,1,0:T(8,128)(2,1)S(1)}, bf16[3,128,512]{2,1,0:T(8,128)(2,1)S(1)}, u32[]{:S(2)}, u32[]{:S(2)}) %collective-permute-start.4) | collective-permute-done | bytes 393248 | tf_op jit(solution)/shard_map/ppermute | solution.py:55
  60.4 5.0 %collective-permute-done.2 = bf16[3,128,512]{2,1,0:T(8,128)(2,1)S(1)} collective-permute-done((bf16[3,128,512]{2,1,0:T(8,128)(2,1)S(1)}, bf16[3,128,512]{2,1,0:T(8,128)(2,1)S(1)}, u32[]{:S(2)}, u32[]{:S(2)}) %collective-permute-start.2) | collective-permute-done | bytes 393248 | tf_op jit(solution)/shard_map/ppermute | solution.py:55
  71.0 4.9 %collective-permute-start.7 = (bf16[128,512]{1,0:T(8,128)(2,1)S(1)}, bf16[128,512]{1,0:T(8,128)(2,1)S(1)}, u32[]{:S(2)}, u32[]{:S(2)}) collective-permute-start(bf16[128,512]{1,0:T(8,128)(2,1)S(1)} %fusion.47), channel_id=1, source_target_pairs={{0,16},{8,24},{16,32},{24,40},{32,48},{40,56},{48,64},{56,72},{64,... | collective-permute-start | bytes 393224 | tf_op jit(solution)/shard_map/ppermute | solution.py:10
  80.9 3.4 %collective-permute-start.9 = (bf16[3,128,512]{2,1,0:T(8,128)(2,1)S(1)}, bf16[3,128,512]{2,1,0:T(8,128)(2,1)S(1)}, u32[]{:S(2)}, u32[]{:S(2)}) collective-permute-start(bf16[3,128,512]{2,1,0:T(8,128)(2,1)S(1)} %pad_maximum_fusion.3), channel_id=1, source_target_pairs={{0,2},{1,3},{2,4},{3,5},{4,6},{5,7},{6,0},{7,1},{8,10},{9,11},{10,... | collective-permute-start | bytes 1179656 | tf_op jit(solution)/shard_map/ppermute | solution.py:55
  86.2 4.6 %collective-permute-done.10 = bf16[3,128,512]{2,1,0:T(8,128)(2,1)S(1)} collective-permute-done((bf16[3,128,512]{2,1,0:T(8,128)(2,1)S(1)}, bf16[3,128,512]{2,1,0:T(8,128)(2,1)S(1)}, u32[]{:S(2)}, u32[]{:S(2)}) %collective-permute-start.10) | collective-permute-done | bytes 393248 | tf_op jit(solution)/shard_map/ppermute | solution.py:55
  91.1 10.7 %collective-permute-done.9 = bf16[3,128,512]{2,1,0:T(8,128)(2,1)S(1)} collective-permute-done((bf16[3,128,512]{2,1,0:T(8,128)(2,1)S(1)}, bf16[3,128,512]{2,1,0:T(8,128)(2,1)S(1)}, u32[]{:S(2)}, u32[]{:S(2)}) %collective-permute-start.9) | collective-permute-done | bytes 393248 | tf_op jit(solution)/shard_map/ppermute | solution.py:55
  102.5 4.1 %collective-permute-start.12 = (f32[128,512]{1,0:T(8,128)S(1)}, f32[128,512]{1,0:T(8,128)S(1)}, u32[]{:S(2)}, u32[]{:S(2)}) collective-permute-start(f32[128,512]{1,0:T(8,128)S(1)} %fusion.13), channel_id=1, source_target_pairs={{0,1},{1,0},{2,3},{3,2},{4,5},{5,4},{6,7},{7,6},{8,9},{9,8},{10,11... | collective-permute-start | bytes 786440 | tf_op jit(solution)/shard_map/ppermute | solution.py:56
  109.3 12.9 %collective-permute-start.13 = (bf16[128,512]{1,0:T(8,128)(2,1)S(1)}, bf16[128,512]{1,0:T(8,128)(2,1)S(1)}, u32[]{:S(2)}, u32[]{:S(2)}) collective-permute-start(bf16[128,512]{1,0:T(8,128)(2,1)S(1)} %fusion.46), channel_id=1, source_target_pairs={{0,32},{8,40},{16,48},{24,56},{32,64},{40,72},{48,80},{56,88},{64,... | collective-permute-start | bytes 393224 | tf_op jit(solution)/shard_map/ppermute | solution.py:10
  123.8 6.1 %collective-permute-done.13 = bf16[128,512]{1,0:T(8,128)(2,1)S(1)} collective-permute-done((bf16[128,512]{1,0:T(8,128)(2,1)S(1)}, bf16[128,512]{1,0:T(8,128)(2,1)S(1)}, u32[]{:S(2)}, u32[]{:S(2)}) %collective-permute-start.13) | collective-permute-done | bytes 131104 | tf_op jit(solution)/shard_map/ppermute | solution.py:10
  131.8 3.4 %collective-permute-start.15 = (bf16[3,128,512]{2,1,0:T(8,128)(2,1)S(1)}, bf16[3,128,512]{2,1,0:T(8,128)(2,1)S(1)}, u32[]{:S(2)}, u32[]{:S(2)}) collective-permute-start(bf16[3,128,512]{2,1,0:T(8,128)(2,1)S(1)} %pad_maximum_fusion.4), channel_id=1, source_target_pairs={{0,2},{1,3},{2,4},{3,5},{4,6},{5,7},{6,0},{7,1},{8,10},{9,11},{10,... | collective-permute-start | bytes 1179656 | tf_op jit(solution)/shard_map/ppermute | solution.py:55
  137.2 4.8 %collective-permute-done.16 = bf16[3,128,512]{2,1,0:T(8,128)(2,1)S(1)} collective-permute-done((bf16[3,128,512]{2,1,0:T(8,128)(2,1)S(1)}, bf16[3,128,512]{2,1,0:T(8,128)(2,1)S(1)}, u32[]{:S(2)}, u32[]{:S(2)}) %collective-permute-start.16) | collective-permute-done | bytes 393248 | tf_op jit(solution)/shard_map/ppermute | solution.py:55
  142.3 11.3 %collective-permute-done.15 = bf16[3,128,512]{2,1,0:T(8,128)(2,1)S(1)} collective-permute-done((bf16[3,128,512]{2,1,0:T(8,128)(2,1)S(1)}, bf16[3,128,512]{2,1,0:T(8,128)(2,1)S(1)}, u32[]{:S(2)}, u32[]{:S(2)}) %collective-permute-start.15) | collective-permute-done | bytes 393248 | tf_op jit(solution)/shard_map/ppermute | solution.py:55
  160.3 11.3 %collective-permute-start.19 = (bf16[128,512]{1,0:T(8,128)(2,1)S(1)}, bf16[128,512]{1,0:T(8,128)(2,1)S(1)}, u32[]{:S(2)}, u32[]{:S(2)}) collective-permute-start(bf16[128,512]{1,0:T(8,128)(2,1)S(1)} %fusion.45), channel_id=1, source_target_pairs={{0,64},{8,72},{16,80},{24,88},{32,96},{40,104},{48,112},{56,120},{... | collective-permute-start | bytes 393224 | tf_op jit(solution)/shard_map/ppermute | solution.py:10
  176.0 3.4 %collective-permute-start.21 = (bf16[3,128,512]{2,1,0:T(8,128)(2,1)S(1)}, bf16[3,128,512]{2,1,0:T(8,128)(2,1)S(1)}, u32[]{:S(2)}, u32[]{:S(2)}) collective-permute-start(bf16[3,128,512]{2,1,0:T(8,128)(2,1)S(1)} %pad_maximum_fusion.5), channel_id=1, source_target_pairs={{0,2},{1,3},{2,4},{3,5},{4,6},{5,7},{6,0},{7,1},{8,10},{9,11},{10,... | collective-permute-start | bytes 1179656 | tf_op jit(solution)/shard_map/ppermute | solution.py:55
  179.4 3.4 %collective-permute-start.23 = (bf16[3,128,512]{2,1,0:T(8,128)(2,1)S(1)}, bf16[3,128,512]{2,1,0:T(8,128)(2,1)S(1)}, u32[]{:S(2)}, u32[]{:S(2)}) collective-permute-start(bf16[3,128,512]{2,1,0:T(8,128)(2,1)S(1)} %pad_maximum_fusion.5), channel_id=1, source_target_pairs={{0,4},{1,5},{2,6},{3,7},{4,0},{5,1},{6,2},{7,3},{8,12},{9,13},{10,... | collective-permute-start | bytes 1179656 | tf_op jit(solution)/shard_map/ppermute | solution.py:55
  188.8 8.2 %collective-permute-done.23 = bf16[3,128,512]{2,1,0:T(8,128)(2,1)S(1)} collective-permute-done((bf16[3,128,512]{2,1,0:T(8,128)(2,1)S(1)}, bf16[3,128,512]{2,1,0:T(8,128)(2,1)S(1)}, u32[]{:S(2)}, u32[]{:S(2)}) %collective-permute-start.23) | collective-permute-done | bytes 393248 | tf_op jit(solution)/shard_map/ppermute | solution.py:55
  197.4 4.3 %collective-permute-start.24 = (f32[128,512]{1,0:T(8,128)S(1)}, f32[128,512]{1,0:T(8,128)S(1)}, u32[]{:S(2)}, u32[]{:S(2)}) collective-permute-start(f32[128,512]{1,0:T(8,128)S(1)} %fusion.27), channel_id=1, source_target_pairs={{0,1},{1,0},{2,3},{3,2},{4,5},{5,4},{6,7},{7,6},{8,9},{9,8},{10,11... | collective-permute-start | bytes 786440 | tf_op jit(solution)/shard_map/ppermute | solution.py:56
  204.5 5.6 %collective-permute-start.25 = (bf16[128,512]{1,0:T(8,128)(2,1)S(1)}, bf16[128,512]{1,0:T(8,128)(2,1)S(1)}, u32[]{:S(2)}, u32[]{:S(2)}) collective-permute-start(bf16[128,512]{1,0:T(8,128)(2,1)S(1)} %fusion.44), channel_id=1, source_target_pairs={{0,128},{8,136},{16,144},{24,152},{32,160},{40,168},{48,176},{56,1... | collective-permute-start | bytes 393224 | tf_op jit(solution)/shard_map/ppermute | solution.py:10
  210.1 4.4 %collective-permute-done.26 = bf16[128,512]{1,0:T(8,128)(2,1)S(1)} collective-permute-done((bf16[128,512]{1,0:T(8,128)(2,1)S(1)}, bf16[128,512]{1,0:T(8,128)(2,1)S(1)}, u32[]{:S(2)}, u32[]{:S(2)}) %collective-permute-start.26) | collective-permute-done | bytes 131104 | tf_op jit(solution)/shard_map/ppermute | solution.py:10
  216.5 3.4 %collective-permute-start.27 = (bf16[3,128,512]{2,1,0:T(8,128)(2,1)S(1)}, bf16[3,128,512]{2,1,0:T(8,128)(2,1)S(1)}, u32[]{:S(2)}, u32[]{:S(2)}) collective-permute-start(bf16[3,128,512]{2,1,0:T(8,128)(2,1)S(1)} %pad_maximum_fusion.6), channel_id=1, source_target_pairs={{0,2},{1,3},{2,4},{3,5},{4,6},{5,7},{6,0},{7,1},{8,10},{9,11},{10,... | collective-permute-start | bytes 1179656 | tf_op jit(solution)/shard_map/ppermute | solution.py:55
  219.9 3.4 %collective-permute-start.29 = (bf16[3,128,512]{2,1,0:T(8,128)(2,1)S(1)}, bf16[3,128,512]{2,1,0:T(8,128)(2,1)S(1)}, u32[]{:S(2)}, u32[]{:S(2)}) collective-permute-start(bf16[3,128,512]{2,1,0:T(8,128)(2,1)S(1)} %pad_maximum_fusion.6), channel_id=1, source_target_pairs={{0,4},{1,5},{2,6},{3,7},{4,0},{5,1},{6,2},{7,3},{8,12},{9,13},{10,... | collective-permute-start | bytes 1179656 | tf_op jit(solution)/shard_map/ppermute | solution.py:55
  229.6 8.1 %collective-permute-done.29 = bf16[3,128,512]{2,1,0:T(8,128)(2,1)S(1)} collective-permute-done((bf16[3,128,512]{2,1,0:T(8,128)(2,1)S(1)}, bf16[3,128,512]{2,1,0:T(8,128)(2,1)S(1)}, u32[]{:S(2)}, u32[]{:S(2)}) %collective-permute-start.29) | collective-permute-done | bytes 393248 | tf_op jit(solution)/shard_map/ppermute | solution.py:55
  238.2 4.0 %collective-permute-start.30 = (f32[128,512]{1,0:T(8,128)S(1)}, f32[128,512]{1,0:T(8,128)S(1)}, u32[]{:S(2)}, u32[]{:S(2)}) collective-permute-start(f32[128,512]{1,0:T(8,128)S(1)} %fusion.34), channel_id=1, source_target_pairs={{0,1},{1,0},{2,3},{3,2},{4,5},{5,4},{6,7},{7,6},{8,9},{9,8},{10,11... | collective-permute-start | bytes 786440 | tf_op jit(solution)/shard_map/ppermute | solution.py:56
  244.9 12.4 %collective-permute-start.31 = (bf16[128,512]{1,0:T(8,128)(2,1)S(1)}, bf16[128,512]{1,0:T(8,128)(2,1)S(1)}, u32[]{:S(2)}, u32[]{:S(2)}) collective-permute-start(bf16[128,512]{1,0:T(8,128)(2,1)S(1)} %fusion.43), channel_id=1, source_target_pairs={{0,256},{8,264},{16,272},{24,280},{32,288},{40,296},{48,304},{56,3... | collective-permute-start | bytes 393224 | tf_op jit(solution)/shard_map/ppermute | solution.py:10
  258.9 3.5 %collective-permute-done.31 = bf16[128,512]{1,0:T(8,128)(2,1)S(1)} collective-permute-done((bf16[128,512]{1,0:T(8,128)(2,1)S(1)}, bf16[128,512]{1,0:T(8,128)(2,1)S(1)}, u32[]{:S(2)}, u32[]{:S(2)}) %collective-permute-start.31) | collective-permute-done | bytes 131104 | tf_op jit(solution)/shard_map/ppermute | solution.py:10
  264.4 3.4 %collective-permute-start.33 = (bf16[3,128,512]{2,1,0:T(8,128)(2,1)S(1)}, bf16[3,128,512]{2,1,0:T(8,128)(2,1)S(1)}, u32[]{:S(2)}, u32[]{:S(2)}) collective-permute-start(bf16[3,128,512]{2,1,0:T(8,128)(2,1)S(1)} %pad_maximum_fusion.7), channel_id=1, source_target_pairs={{0,2},{1,3},{2,4},{3,5},{4,6},{5,7},{6,0},{7,1},{8,10},{9,11},{10,... | collective-permute-start | bytes 1179656 | tf_op jit(solution)/shard_map/ppermute | solution.py:55
  267.8 3.4 %collective-permute-start.35 = (bf16[3,128,512]{2,1,0:T(8,128)(2,1)S(1)}, bf16[3,128,512]{2,1,0:T(8,128)(2,1)S(1)}, u32[]{:S(2)}, u32[]{:S(2)}) collective-permute-start(bf16[3,128,512]{2,1,0:T(8,128)(2,1)S(1)} %pad_maximum_fusion.7), channel_id=1, source_target_pairs={{0,4},{1,5},{2,6},{3,7},{4,0},{5,1},{6,2},{7,3},{8,12},{9,13},{10,... | collective-permute-start | bytes 1179656 | tf_op jit(solution)/shard_map/ppermute | solution.py:55
  277.1 8.2 %collective-permute-done.35 = bf16[3,128,512]{2,1,0:T(8,128)(2,1)S(1)} collective-permute-done((bf16[3,128,512]{2,1,0:T(8,128)(2,1)S(1)}, bf16[3,128,512]{2,1,0:T(8,128)(2,1)S(1)}, u32[]{:S(2)}, u32[]{:S(2)}) %collective-permute-start.35) | collective-permute-done | bytes 393248 | tf_op jit(solution)/shard_map/ppermute | solution.py:55
  285.8 4.3 %collective-permute-start.36 = (f32[128,512]{1,0:T(8,128)S(1)}, f32[128,512]{1,0:T(8,128)S(1)}, u32[]{:S(2)}, u32[]{:S(2)}) collective-permute-start(f32[128,512]{1,0:T(8,128)S(1)} %fusion.41), channel_id=1, source_target_pairs={{0,1},{1,0},{2,3},{3,2},{4,5},{5,4},{6,7},{7,6},{8,9},{9,8},{10,11... | collective-permute-start | bytes 786440 | tf_op jit(solution)/shard_map/ppermute | solution.py:56
  (124 shorter events, 103.7 us)
Async XLA Ops:
  23.3 33.0 %collective-permute-start.5 = (bf16[6,128,4,3,128]{4,1,3,2,0:T(8,128)(2,1)}, bf16[6,128,4,3,128]{4,1,3,2,0:T(8,128)(2,1)}, u32[]{:S(2)}, u32[]{:S(2)}) collective-permute-start(bf16[6,128,4,3,128]{4,1,3,2,0:T(8,128)(2,1)} %pad_maximum_fusion.1), channel_id=1, source_target_pairs={{0,1},{1,0},{2,3},{3,2},{4,5},{5,4},{6,7},{7,6},{8,9},{9,8},{10,11... | collective-permute-start | bytes 7077896 | tf_op jit(solution)/shard_map/ppermute | solution.py:37
  32.1 10.3 %collective-permute-start.1 = (bf16[128,512]{1,0:T(8,128)(2,1)S(1)}, bf16[128,512]{1,0:T(8,128)(2,1)S(1)}, u32[]{:S(2)}, u32[]{:S(2)}) collective-permute-start(bf16[128,512]{1,0:T(8,128)(2,1)S(1)} %bitcast.479), channel_id=1, source_target_pairs={{8,0},{16,8},{24,16},{32,24},{40,32},{48,40},{56,48},{64,56},{72,6... | collective-permute-start | bytes 393224 | tf_op jit(solution)/shard_map/ppermute | solution.py:10
  33.4 9.1 %collective-permute-start = (bf16[128,512]{1,0:T(8,128)(2,1)S(1)}, bf16[128,512]{1,0:T(8,128)(2,1)S(1)}, u32[]{:S(2)}, u32[]{:S(2)}) collective-permute-start(bf16[128,512]{1,0:T(8,128)(2,1)S(1)} %bitcast.480), channel_id=1, source_target_pairs={{0,8},{8,16},{16,24},{24,32},{32,40},{40,48},{48,56},{56,64},{64,7... | collective-permute-start | bytes 393224 | tf_op jit(solution)/shard_map/ppermute | solution.py:10
  42.5 13.5 %collective-permute-start.4 = (bf16[3,128,512]{2,1,0:T(8,128)(2,1)S(1)}, bf16[3,128,512]{2,1,0:T(8,128)(2,1)S(1)}, u32[]{:S(2)}, u32[]{:S(2)}) collective-permute-start(bf16[3,128,512]{2,1,0:T(8,128)(2,1)S(1)} %pad_maximum_fusion.2), channel_id=1, source_target_pairs={{0,4},{1,5},{2,6},{3,7},{4,0},{5,1},{6,2},{7,3},{8,12},{9,13},{10,... | collective-permute-start | bytes 1179656 | tf_op jit(solution)/shard_map/ppermute | solution.py:55
  45.0 15.2 %collective-permute-start.3 = (bf16[3,128,512]{2,1,0:T(8,128)(2,1)S(1)}, bf16[3,128,512]{2,1,0:T(8,128)(2,1)S(1)}, u32[]{:S(2)}, u32[]{:S(2)}) collective-permute-start(bf16[3,128,512]{2,1,0:T(8,128)(2,1)S(1)} %pad_maximum_fusion.2), channel_id=1, source_target_pairs={{0,6},{1,7},{2,0},{3,1},{4,2},{5,3},{6,4},{7,5},{8,14},{9,15},{10,... | collective-permute-start | bytes 1179656 | tf_op jit(solution)/shard_map/ppermute | solution.py:55
  46.9 18.5 %collective-permute-start.2 = (bf16[3,128,512]{2,1,0:T(8,128)(2,1)S(1)}, bf16[3,128,512]{2,1,0:T(8,128)(2,1)S(1)}, u32[]{:S(2)}, u32[]{:S(2)}) collective-permute-start(bf16[3,128,512]{2,1,0:T(8,128)(2,1)S(1)} %pad_maximum_fusion.2), channel_id=1, source_target_pairs={{0,2},{1,3},{2,4},{3,5},{4,6},{5,7},{6,0},{7,1},{8,10},{9,11},{10,... | collective-permute-start | bytes 1179656 | tf_op jit(solution)/shard_map/ppermute | solution.py:55
  69.7 9.2 %collective-permute-start.8 = (bf16[128,512]{1,0:T(8,128)(2,1)S(1)}, bf16[128,512]{1,0:T(8,128)(2,1)S(1)}, u32[]{:S(2)}, u32[]{:S(2)}) collective-permute-start(bf16[128,512]{1,0:T(8,128)(2,1)S(1)} %fusion.47), channel_id=1, source_target_pairs={{16,0},{24,8},{32,16},{40,24},{48,32},{56,40},{64,48},{72,56},{80,... | collective-permute-start | bytes 393224 | tf_op jit(solution)/shard_map/ppermute | solution.py:10
  71.0 7.9 %collective-permute-start.7 = (bf16[128,512]{1,0:T(8,128)(2,1)S(1)}, bf16[128,512]{1,0:T(8,128)(2,1)S(1)}, u32[]{:S(2)}, u32[]{:S(2)}) collective-permute-start(bf16[128,512]{1,0:T(8,128)(2,1)S(1)} %fusion.47), channel_id=1, source_target_pairs={{0,16},{8,24},{16,32},{24,40},{32,48},{40,56},{48,64},{56,72},{64,... | collective-permute-start | bytes 393224 | tf_op jit(solution)/shard_map/ppermute | solution.py:10
  79.0 11.9 %collective-permute-start.10 = (bf16[3,128,512]{2,1,0:T(8,128)(2,1)S(1)}, bf16[3,128,512]{2,1,0:T(8,128)(2,1)S(1)}, u32[]{:S(2)}, u32[]{:S(2)}) collective-permute-start(bf16[3,128,512]{2,1,0:T(8,128)(2,1)S(1)} %pad_maximum_fusion.3), channel_id=1, source_target_pairs={{0,6},{1,7},{2,0},{3,1},{4,2},{5,3},{6,4},{7,5},{8,14},{9,15},{10,... | collective-permute-start | bytes 1179656 | tf_op jit(solution)/shard_map/ppermute | solution.py:55
  80.9 20.8 %collective-permute-start.9 = (bf16[3,128,512]{2,1,0:T(8,128)(2,1)S(1)}, bf16[3,128,512]{2,1,0:T(8,128)(2,1)S(1)}, u32[]{:S(2)}, u32[]{:S(2)}) collective-permute-start(bf16[3,128,512]{2,1,0:T(8,128)(2,1)S(1)} %pad_maximum_fusion.3), channel_id=1, source_target_pairs={{0,2},{1,3},{2,4},{3,5},{4,6},{5,7},{6,0},{7,1},{8,10},{9,11},{10,... | collective-permute-start | bytes 1179656 | tf_op jit(solution)/shard_map/ppermute | solution.py:55
  84.3 17.7 %collective-permute-start.11 = (bf16[3,128,512]{2,1,0:T(8,128)(2,1)S(1)}, bf16[3,128,512]{2,1,0:T(8,128)(2,1)S(1)}, u32[]{:S(2)}, u32[]{:S(2)}) collective-permute-start(bf16[3,128,512]{2,1,0:T(8,128)(2,1)S(1)} %pad_maximum_fusion.3), channel_id=1, source_target_pairs={{0,4},{1,5},{2,6},{3,7},{4,0},{5,1},{6,2},{7,3},{8,12},{9,13},{10,... | collective-permute-start | bytes 1179656 | tf_op jit(solution)/shard_map/ppermute | solution.py:55
  108.0 15.8 %collective-permute-start.14 = (bf16[128,512]{1,0:T(8,128)(2,1)S(1)}, bf16[128,512]{1,0:T(8,128)(2,1)S(1)}, u32[]{:S(2)}, u32[]{:S(2)}) collective-permute-start(bf16[128,512]{1,0:T(8,128)(2,1)S(1)} %fusion.46), channel_id=1, source_target_pairs={{32,0},{40,8},{48,16},{56,24},{64,32},{72,40},{80,48},{88,56},{96,... | collective-permute-start | bytes 393224 | tf_op jit(solution)/shard_map/ppermute | solution.py:10
  109.3 20.5 %collective-permute-start.13 = (bf16[128,512]{1,0:T(8,128)(2,1)S(1)}, bf16[128,512]{1,0:T(8,128)(2,1)S(1)}, u32[]{:S(2)}, u32[]{:S(2)}) collective-permute-start(bf16[128,512]{1,0:T(8,128)(2,1)S(1)} %fusion.46), channel_id=1, source_target_pairs={{0,32},{8,40},{16,48},{24,56},{32,64},{40,72},{48,80},{56,88},{64,... | collective-permute-start | bytes 393224 | tf_op jit(solution)/shard_map/ppermute | solution.py:10
  129.9 12.1 %collective-permute-start.16 = (bf16[3,128,512]{2,1,0:T(8,128)(2,1)S(1)}, bf16[3,128,512]{2,1,0:T(8,128)(2,1)S(1)}, u32[]{:S(2)}, u32[]{:S(2)}) collective-permute-start(bf16[3,128,512]{2,1,0:T(8,128)(2,1)S(1)} %pad_maximum_fusion.4), channel_id=1, source_target_pairs={{0,6},{1,7},{2,0},{3,1},{4,2},{5,3},{6,4},{7,5},{8,14},{9,15},{10,... | collective-permute-start | bytes 1179656 | tf_op jit(solution)/shard_map/ppermute | solution.py:55
  131.8 21.7 %collective-permute-start.15 = (bf16[3,128,512]{2,1,0:T(8,128)(2,1)S(1)}, bf16[3,128,512]{2,1,0:T(8,128)(2,1)S(1)}, u32[]{:S(2)}, u32[]{:S(2)}) collective-permute-start(bf16[3,128,512]{2,1,0:T(8,128)(2,1)S(1)} %pad_maximum_fusion.4), channel_id=1, source_target_pairs={{0,2},{1,3},{2,4},{3,5},{4,6},{5,7},{6,0},{7,1},{8,10},{9,11},{10,... | collective-permute-start | bytes 1179656 | tf_op jit(solution)/shard_map/ppermute | solution.py:55
  135.2 18.6 %collective-permute-start.17 = (bf16[3,128,512]{2,1,0:T(8,128)(2,1)S(1)}, bf16[3,128,512]{2,1,0:T(8,128)(2,1)S(1)}, u32[]{:S(2)}, u32[]{:S(2)}) collective-permute-start(bf16[3,128,512]{2,1,0:T(8,128)(2,1)S(1)} %pad_maximum_fusion.4), channel_id=1, source_target_pairs={{0,4},{1,5},{2,6},{3,7},{4,0},{5,1},{6,2},{7,3},{8,12},{9,13},{10,... | collective-permute-start | bytes 1179656 | tf_op jit(solution)/shard_map/ppermute | solution.py:55
  159.0 14.2 %collective-permute-start.20 = (bf16[128,512]{1,0:T(8,128)(2,1)S(1)}, bf16[128,512]{1,0:T(8,128)(2,1)S(1)}, u32[]{:S(2)}, u32[]{:S(2)}) collective-permute-start(bf16[128,512]{1,0:T(8,128)(2,1)S(1)} %fusion.45), channel_id=1, source_target_pairs={{64,0},{72,8},{80,16},{88,24},{96,32},{104,40},{112,48},{120,56},{... | collective-permute-start | bytes 393224 | tf_op jit(solution)/shard_map/ppermute | solution.py:10
  160.3 13.8 %collective-permute-start.19 = (bf16[128,512]{1,0:T(8,128)(2,1)S(1)}, bf16[128,512]{1,0:T(8,128)(2,1)S(1)}, u32[]{:S(2)}, u32[]{:S(2)}) collective-permute-start(bf16[128,512]{1,0:T(8,128)(2,1)S(1)} %fusion.45), channel_id=1, source_target_pairs={{0,64},{8,72},{16,80},{24,88},{32,96},{40,104},{48,112},{56,120},{... | collective-permute-start | bytes 393224 | tf_op jit(solution)/shard_map/ppermute | solution.py:10
  174.1 11.3 %collective-permute-start.22 = (bf16[3,128,512]{2,1,0:T(8,128)(2,1)S(1)}, bf16[3,128,512]{2,1,0:T(8,128)(2,1)S(1)}, u32[]{:S(2)}, u32[]{:S(2)}) collective-permute-start(bf16[3,128,512]{2,1,0:T(8,128)(2,1)S(1)} %pad_maximum_fusion.5), channel_id=1, source_target_pairs={{0,6},{1,7},{2,0},{3,1},{4,2},{5,3},{6,4},{7,5},{8,14},{9,15},{10,... | collective-permute-start | bytes 1179656 | tf_op jit(solution)/shard_map/ppermute | solution.py:55
  176.0 12.5 %collective-permute-start.21 = (bf16[3,128,512]{2,1,0:T(8,128)(2,1)S(1)}, bf16[3,128,512]{2,1,0:T(8,128)(2,1)S(1)}, u32[]{:S(2)}, u32[]{:S(2)}) collective-permute-start(bf16[3,128,512]{2,1,0:T(8,128)(2,1)S(1)} %pad_maximum_fusion.5), channel_id=1, source_target_pairs={{0,2},{1,3},{2,4},{3,5},{4,6},{5,7},{6,0},{7,1},{8,10},{9,11},{10,... | collective-permute-start | bytes 1179656 | tf_op jit(solution)/shard_map/ppermute | solution.py:55
  179.4 17.6 %collective-permute-start.23 = (bf16[3,128,512]{2,1,0:T(8,128)(2,1)S(1)}, bf16[3,128,512]{2,1,0:T(8,128)(2,1)S(1)}, u32[]{:S(2)}, u32[]{:S(2)}) collective-permute-start(bf16[3,128,512]{2,1,0:T(8,128)(2,1)S(1)} %pad_maximum_fusion.5), channel_id=1, source_target_pairs={{0,4},{1,5},{2,6},{3,7},{4,0},{5,1},{6,2},{7,3},{8,12},{9,13},{10,... | collective-permute-start | bytes 1179656 | tf_op jit(solution)/shard_map/ppermute | solution.py:55
  197.4 5.5 %collective-permute-start.24 = (f32[128,512]{1,0:T(8,128)S(1)}, f32[128,512]{1,0:T(8,128)S(1)}, u32[]{:S(2)}, u32[]{:S(2)}) collective-permute-start(f32[128,512]{1,0:T(8,128)S(1)} %fusion.27), channel_id=1, source_target_pairs={{0,1},{1,0},{2,3},{3,2},{4,5},{5,4},{6,7},{7,6},{8,9},{9,8},{10,11... | collective-permute-start | bytes 786440 | tf_op jit(solution)/shard_map/ppermute | solution.py:56
  203.2 11.3 %collective-permute-start.26 = (bf16[128,512]{1,0:T(8,128)(2,1)S(1)}, bf16[128,512]{1,0:T(8,128)(2,1)S(1)}, u32[]{:S(2)}, u32[]{:S(2)}) collective-permute-start(bf16[128,512]{1,0:T(8,128)(2,1)S(1)} %fusion.44), channel_id=1, source_target_pairs={{128,0},{136,8},{144,16},{152,24},{160,32},{168,40},{176,48},{184,... | collective-permute-start | bytes 393224 | tf_op jit(solution)/shard_map/ppermute | solution.py:10
  204.5 10.0 %collective-permute-start.25 = (bf16[128,512]{1,0:T(8,128)(2,1)S(1)}, bf16[128,512]{1,0:T(8,128)(2,1)S(1)}, u32[]{:S(2)}, u32[]{:S(2)}) collective-permute-start(bf16[128,512]{1,0:T(8,128)(2,1)S(1)} %fusion.44), channel_id=1, source_target_pairs={{0,128},{8,136},{16,144},{24,152},{32,160},{40,168},{48,176},{56,1... | collective-permute-start | bytes 393224 | tf_op jit(solution)/shard_map/ppermute | solution.py:10
  214.6 11.6 %collective-permute-start.28 = (bf16[3,128,512]{2,1,0:T(8,128)(2,1)S(1)}, bf16[3,128,512]{2,1,0:T(8,128)(2,1)S(1)}, u32[]{:S(2)}, u32[]{:S(2)}) collective-permute-start(bf16[3,128,512]{2,1,0:T(8,128)(2,1)S(1)} %pad_maximum_fusion.6), channel_id=1, source_target_pairs={{0,6},{1,7},{2,0},{3,1},{4,2},{5,3},{6,4},{7,5},{8,14},{9,15},{10,... | collective-permute-start | bytes 1179656 | tf_op jit(solution)/shard_map/ppermute | solution.py:55
  216.5 12.9 %collective-permute-start.27 = (bf16[3,128,512]{2,1,0:T(8,128)(2,1)S(1)}, bf16[3,128,512]{2,1,0:T(8,128)(2,1)S(1)}, u32[]{:S(2)}, u32[]{:S(2)}) collective-permute-start(bf16[3,128,512]{2,1,0:T(8,128)(2,1)S(1)} %pad_maximum_fusion.6), channel_id=1, source_target_pairs={{0,2},{1,3},{2,4},{3,5},{4,6},{5,7},{6,0},{7,1},{8,10},{9,11},{10,... | collective-permute-start | bytes 1179656 | tf_op jit(solution)/shard_map/ppermute | solution.py:55
  219.9 17.9 %collective-permute-start.29 = (bf16[3,128,512]{2,1,0:T(8,128)(2,1)S(1)}, bf16[3,128,512]{2,1,0:T(8,128)(2,1)S(1)}, u32[]{:S(2)}, u32[]{:S(2)}) collective-permute-start(bf16[3,128,512]{2,1,0:T(8,128)(2,1)S(1)} %pad_maximum_fusion.6), channel_id=1, source_target_pairs={{0,4},{1,5},{2,6},{3,7},{4,0},{5,1},{6,2},{7,3},{8,12},{9,13},{10,... | collective-permute-start | bytes 1179656 | tf_op jit(solution)/shard_map/ppermute | solution.py:55
  243.6 15.3 %collective-permute-start.32 = (bf16[128,512]{1,0:T(8,128)(2,1)S(1)}, bf16[128,512]{1,0:T(8,128)(2,1)S(1)}, u32[]{:S(2)}, u32[]{:S(2)}) collective-permute-start(bf16[128,512]{1,0:T(8,128)(2,1)S(1)} %fusion.43), channel_id=1, source_target_pairs={{256,0},{264,8},{272,16},{280,24},{288,32},{296,40},{304,48},{312,... | collective-permute-start | bytes 393224 | tf_op jit(solution)/shard_map/ppermute | solution.py:10
  244.9 17.5 %collective-permute-start.31 = (bf16[128,512]{1,0:T(8,128)(2,1)S(1)}, bf16[128,512]{1,0:T(8,128)(2,1)S(1)}, u32[]{:S(2)}, u32[]{:S(2)}) collective-permute-start(bf16[128,512]{1,0:T(8,128)(2,1)S(1)} %fusion.43), channel_id=1, source_target_pairs={{0,256},{8,264},{16,272},{24,280},{32,288},{40,296},{48,304},{56,3... | collective-permute-start | bytes 393224 | tf_op jit(solution)/shard_map/ppermute | solution.py:10
  262.5 11.3 %collective-permute-start.34 = (bf16[3,128,512]{2,1,0:T(8,128)(2,1)S(1)}, bf16[3,128,512]{2,1,0:T(8,128)(2,1)S(1)}, u32[]{:S(2)}, u32[]{:S(2)}) collective-permute-start(bf16[3,128,512]{2,1,0:T(8,128)(2,1)S(1)} %pad_maximum_fusion.7), channel_id=1, source_target_pairs={{0,6},{1,7},{2,0},{3,1},{4,2},{5,3},{6,4},{7,5},{8,14},{9,15},{10,... | collective-permute-start | bytes 1179656 | tf_op jit(solution)/shard_map/ppermute | solution.py:55
  264.4 12.5 %collective-permute-start.33 = (bf16[3,128,512]{2,1,0:T(8,128)(2,1)S(1)}, bf16[3,128,512]{2,1,0:T(8,128)(2,1)S(1)}, u32[]{:S(2)}, u32[]{:S(2)}) collective-permute-start(bf16[3,128,512]{2,1,0:T(8,128)(2,1)S(1)} %pad_maximum_fusion.7), channel_id=1, source_target_pairs={{0,2},{1,3},{2,4},{3,5},{4,6},{5,7},{6,0},{7,1},{8,10},{9,11},{10,... | collective-permute-start | bytes 1179656 | tf_op jit(solution)/shard_map/ppermute | solution.py:55
  267.8 17.6 %collective-permute-start.35 = (bf16[3,128,512]{2,1,0:T(8,128)(2,1)S(1)}, bf16[3,128,512]{2,1,0:T(8,128)(2,1)S(1)}, u32[]{:S(2)}, u32[]{:S(2)}) collective-permute-start(bf16[3,128,512]{2,1,0:T(8,128)(2,1)S(1)} %pad_maximum_fusion.7), channel_id=1, source_target_pairs={{0,4},{1,5},{2,6},{3,7},{4,0},{5,1},{6,2},{7,3},{8,12},{9,13},{10,... | collective-permute-start | bytes 1179656 | tf_op jit(solution)/shard_map/ppermute | solution.py:55
  (7 other events, 36.8 us)

commit v6 on v2

--- a/solution.py
+++ b/solution.py
@@ -25,16 +25,20 @@
     def columns_for(which_core):
         return jnp.stack([2 * ((chip + off) % chips) + which_core for off in OFFSETS])
 
-    signed = jnp.stack([self_factor[:, 0], -lower_factor[:, 0], -upper_factor[:, 0]], axis=2)
-    signed = signed.reshape(levels, rows, 3, ncross, rows)
+    swap = [(2 * c + b, 2 * c + 1 - b) for c in range(chips) for b in range(2)]
 
-    def pick(which_core):
+    def arranged(factors, which_core):
+        count = factors[0].shape[0]
+        signed = jnp.stack([factors[0][:, 0], -factors[1][:, 0], -factors[2][:, 0]], axis=2)
+        signed = signed.reshape(count, rows, 3, ncross, rows)
         part = jnp.take(signed, columns_for(which_core), axis=3)
         return part.transpose(0, 1, 3, 2, 4)
 
-    mine = pick(core)
-    swap = [(2 * c + b, 2 * c + 1 - b) for c in range(chips) for b in range(2)]
-    theirs = lax.ppermute(pick(1 - core), "cross", swap)
+    def prepare(factors):
+        return arranged(factors, core), lax.ppermute(arranged(factors, 1 - core), "cross", swap)
+
+    factors = (self_factor, lower_factor, upper_factor)
+    mine, theirs = prepare(tuple(f[:1] for f in factors))
 
     def same_core(offset):
         return [(2 * c + b, 2 * ((c + offset) % chips) + b) for c in range(chips) for b in range(2)]
@@ -53,8 +57,13 @@
         upper = shifted(current, "chain", -dist)
         own = jnp.stack([current, lower, upper])
         pieces = [own] + [lax.ppermute(own, "cross", same_core(-off)) for off in OFFSETS[1:]]
-        given = lax.ppermute(partial(theirs[level], pieces), "cross", swap)
-        total = partial(mine[level], pieces) + given
+        if level == 0 and levels > 1:
+            pieces, rest = lax.optimization_barrier((pieces, tuple(f[1:] for f in factors)))
+            later_mine, later_theirs = prepare(rest)
+        at = 0 if level == 0 else level - 1
+        use_mine, use_theirs = (mine, theirs) if level == 0 else (later_mine, later_theirs)
+        given = lax.ppermute(partial(use_theirs[at], pieces), "cross", swap)
+        total = partial(use_mine[at], pieces) + given
         current = total.astype(jnp.bfloat16)
     return current[None]
 

time: 280 us -> 288 us (1.029); the launches traced: 279 us -> 284 us
  waiting for transfers between devices: 104 us -> 82.7 us
  local copies, waits for them, and re-layouts: 20.5 us -> 28.3 us
  matrix products: 11.7 us -> 18.9 us
  starting transfers between devices: 135 us -> 142 us
  other arithmetic: 7.78 us -> 11.3 us
    ppermute x18, waiting for transfers between devices: 77.9 us -> 61.8 us  [body(): lax.ppermute(own, 'cross', same_core(-off))]
    dot_general x48, matrix products: 11.7 us -> 18.9 us  [partial(): jnp.einsum('ibk,bkr->ir', mat[:, j], piece, preferred_element_type=jnp.fl...]
    unnamed x5 -> x21, local copies, waits for them, and re-layouts: 6.42 us -> 1.2 us
    optimization_barrier x0 -> x3, local copies, waits for them, and re-layouts: none -> 4.98 us  [body(): lax.optimization_barrier((pieces, tuple((f[1:] for f in factors))))]
    ppermute x18, starting transfers between devices: 50.3 us -> 55.1 us  [body(): lax.ppermute(own, 'cross', same_core(-off))]
    ppermute x12, waiting for transfers between devices: 22.9 us -> 18.4 us  [shifted(): lax.ppermute(value, axis, [(source, source + steps) for source in range(i...]
    slice x0 -> x9, local copies, waits for them, and re-layouts: none -> 4.24 us  [the longest x4 3 us: body(): f[1:]]
    gather x2 -> x4, local copies, waits for them, and re-layouts: 6.67 us -> 9.17 us  [arranged(): part = jnp.take(signed, columns_for(which_core), axis=3)]
  transfers between devices with their start and end apart: 37 -> 38, of which waited for: 30 -> 30; matrix products, arithmetic and copies ran while one was open for 4% -> 11% of each run, Pallas kernels for 0% -> 0%
where the time goes in v6:
time: 288 us; the launch traced here: 284 us
  starting transfers between devices  142 us (49%)
  waiting for transfers between devices  82.7 us (29%)
  local copies, waits for them, and re-layouts  28.3 us (10%)
  matrix products  18.9 us (7%)
  other arithmetic  11.3 us (4%)
    ppermute x18, waiting for transfers between devices, body(): lax.ppermute(own, 'cross', same_core(-off))  61.8 us
    ppermute x12, starting transfers between devices, shifted(): lax.ppermute(value, axis, [(source, source + steps) for source in range(i...  56.7 us
    ppermute x18, starting transfers between devices, body(): lax.ppermute(own, 'cross', same_core(-off))  55.1 us
    dot_general x48, matrix products, partial(): jnp.einsum('ibk,bkr->ir', mat[:, j], piece, preferred_element_type=jnp.fl...  18.9 us
    ppermute x6, starting transfers between devices, body(): given = lax.ppermute(partial(use_theirs[at], pieces), 'cross', swap)  18.7 us
    ppermute x12, waiting for transfers between devices, shifted(): lax.ppermute(value, axis, [(source, source + steps) for source in range(i...  18.4 us
    ppermute x2, starting transfers between devices, prepare(): lax.ppermute(arranged(factors, 1 - core), 'cross', swap)  11.2 us
    gather x4, local copies, waits for them, and re-layouts, arranged(): part = jnp.take(signed, columns_for(which_core), axis=3)  9.17 us
  transfers between devices with their start and end apart: 38, of which 30 were waited for; matrix products, arithmetic and copies ran while one was open for 11% of the time, Pallas kernels for 0%

profile of v6, /device:TPU:1, one launch (start us, length us, event | category | flops | bytes accessed | tf_op | source)
XLA Modules:
  0.0 283.9 jit_solution(131803096344293834)
XLA Ops:
  1.4 5.5 %collective-permute-start = (bf16[128,512]{1,0:T(8,128)(2,1)}, bf16[128,512]{1,0:T(8,128)(2,1)S(1)}, u32[]{:S(2)}, u32[]{:S(2)}) collective-permute-start(bf16[128,512]{1,0:T(8,128)(2,1)} %bitcast.512), channel_id=1, source_target_pairs={{0,8},{8,16},{16,24},{24,32},{32,40},{40,48},{48,56},{56,64},{64,7... | collective-permute-start | bytes 393224 | tf_op jit(solution)/shard_map/ppermute | solution.py:10
  11.2 7.9 %collective-permute-start.5 = (bf16[1,128,4,3,128]{4,1,3,2,0:T(8,128)(2,1)}, bf16[1,128,4,3,128]{4,1,3,2,0:T(8,128)(2,1)}, u32[]{:S(2)}, u32[]{:S(2)}) collective-permute-start(bf16[1,128,4,3,128]{4,1,3,2,0:T(8,128)(2,1)} %fusion.51), channel_id=1, source_target_pairs={{0,1},{1,0},{2,3},{3,2},{4,5},{5,4},{6,7},{7,6},{8,9},{9,8},{10,11... | collective-permute-start | bytes 1179656 | tf_op jit(solution)/shard_map/ppermute | solution.py:38
  21.1 4.6 %collective-permute-start.3 = (bf16[3,128,512]{2,1,0:T(8,128)(2,1)S(1)}, bf16[3,128,512]{2,1,0:T(8,128)(2,1)}, u32[]{:S(2)}, u32[]{:S(2)}) collective-permute-start(bf16[3,128,512]{2,1,0:T(8,128)(2,1)S(1)} %pad_maximum_fusion.1), channel_id=1, source_target_pairs={{0,6},{1,7},{2,0},{3,1},{4,2},{5,3},{6,4},{7,5},{8,14},{9,15},{10,... | collective-permute-start | bytes 1179656 | tf_op jit(solution)/shard_map/ppermute | solution.py:59
  55.2 3.4 %pad_maximum_fusion = bf16[5,128,3,8,128]{4,1,3,2,0:T(8,128)(2,1)} fusion(bf16[5,128,1,8,128]{4,1,3,2,0:T(8,128)(2,1)S(1)} %copy-done.1, bf16[5,128,1,8,128]{4,1,3,2,0:T(8,128)(2,1)} %copy.11, bf16[5,128,1,8,128]{4,1,3,2,0:T(8,128)(2,1)} %copy.10), kind=kLoop, calls=%fused_computation.4 | loop fusion | flops 3932160 | bytes 7864320 | tf_op jit(solution)/shard_map/stack | solution.py:32
  74.9 4.9 %collective-permute-start.7 = (bf16[128,512]{1,0:T(8,128)(2,1)S(1)}, bf16[128,512]{1,0:T(8,128)(2,1)S(1)}, u32[]{:S(2)}, u32[]{:S(2)}) collective-permute-start(bf16[128,512]{1,0:T(8,128)(2,1)S(1)} %fusion.49), channel_id=1, source_target_pairs={{0,16},{8,24},{16,32},{24,40},{32,48},{40,56},{48,64},{56,72},{64,... | collective-permute-start | bytes 393224 | tf_op jit(solution)/shard_map/ppermute | solution.py:10
  86.8 4.2 %collective-permute-start.10 = (bf16[3,128,512]{2,1,0:T(8,128)(2,1)S(1)}, bf16[3,128,512]{2,1,0:T(8,128)(2,1)S(1)}, u32[]{:S(2)}, u32[]{:S(2)}) collective-permute-start(bf16[3,128,512]{2,1,0:T(8,128)(2,1)S(1)} %pad_maximum_fusion.2), channel_id=1, source_target_pairs={{0,6},{1,7},{2,0},{3,1},{4,2},{5,3},{6,4},{7,5},{8,14},{9,15},{10,... | collective-permute-start | bytes 1179656 | tf_op jit(solution)/shard_map/ppermute | solution.py:59
  98.6 7.6 %collective-permute-done.10 = bf16[3,128,512]{2,1,0:T(8,128)(2,1)S(1)} collective-permute-done((bf16[3,128,512]{2,1,0:T(8,128)(2,1)S(1)}, bf16[3,128,512]{2,1,0:T(8,128)(2,1)S(1)}, u32[]{:S(2)}, u32[]{:S(2)}) %collective-permute-start.10) | collective-permute-done | bytes 393248 | tf_op jit(solution)/shard_map/ppermute | solution.py:59
  106.9 3.5 %collective-permute-start.13 = (f32[128,512]{1,0:T(8,128)S(1)}, f32[128,512]{1,0:T(8,128)S(1)}, u32[]{:S(2)}, u32[]{:S(2)}) collective-permute-start(f32[128,512]{1,0:T(8,128)S(1)} %fusion.15), channel_id=1, source_target_pairs={{0,1},{1,0},{2,3},{3,2},{4,5},{5,4},{6,7},{7,6},{8,9},{9,8},{10,11... | collective-permute-start | bytes 786440 | tf_op jit(solution)/shard_map/ppermute | solution.py:65
  113.1 8.6 %collective-permute-start.14 = (bf16[128,512]{1,0:T(8,128)(2,1)S(1)}, bf16[128,512]{1,0:T(8,128)(2,1)S(1)}, u32[]{:S(2)}, u32[]{:S(2)}) collective-permute-start(bf16[128,512]{1,0:T(8,128)(2,1)S(1)} %fusion.48), channel_id=1, source_target_pairs={{0,32},{8,40},{16,48},{24,56},{32,64},{40,72},{48,80},{56,88},{64,... | collective-permute-start | bytes 393224 | tf_op jit(solution)/shard_map/ppermute | solution.py:10
  123.4 6.2 %collective-permute-done.14 = bf16[128,512]{1,0:T(8,128)(2,1)S(1)} collective-permute-done((bf16[128,512]{1,0:T(8,128)(2,1)S(1)}, bf16[128,512]{1,0:T(8,128)(2,1)S(1)}, u32[]{:S(2)}, u32[]{:S(2)}) %collective-permute-start.14) | collective-permute-done | bytes 131104 | tf_op jit(solution)/shard_map/ppermute | solution.py:10
  132.8 3.7 %collective-permute-start.17 = (bf16[3,128,512]{2,1,0:T(8,128)(2,1)S(1)}, bf16[3,128,512]{2,1,0:T(8,128)(2,1)S(1)}, u32[]{:S(2)}, u32[]{:S(2)}) collective-permute-start(bf16[3,128,512]{2,1,0:T(8,128)(2,1)S(1)} %pad_maximum_fusion.3), channel_id=1, source_target_pairs={{0,6},{1,7},{2,0},{3,1},{4,2},{5,3},{6,4},{7,5},{8,14},{9,15},{10,... | collective-permute-start | bytes 1179656 | tf_op jit(solution)/shard_map/ppermute | solution.py:59
  138.5 4.8 %collective-permute-done.18 = bf16[3,128,512]{2,1,0:T(8,128)(2,1)S(1)} collective-permute-done((bf16[3,128,512]{2,1,0:T(8,128)(2,1)S(1)}, bf16[3,128,512]{2,1,0:T(8,128)(2,1)S(1)}, u32[]{:S(2)}, u32[]{:S(2)}) %collective-permute-start.18) | collective-permute-done | bytes 393248 | tf_op jit(solution)/shard_map/ppermute | solution.py:59
  143.5 8.2 %collective-permute-done.17 = bf16[3,128,512]{2,1,0:T(8,128)(2,1)S(1)} collective-permute-done((bf16[3,128,512]{2,1,0:T(8,128)(2,1)S(1)}, bf16[3,128,512]{2,1,0:T(8,128)(2,1)S(1)}, u32[]{:S(2)}, u32[]{:S(2)}) %collective-permute-start.17) | collective-permute-done | bytes 393248 | tf_op jit(solution)/shard_map/ppermute | solution.py:59
  158.3 9.8 %collective-permute-start.20 = (bf16[128,512]{1,0:T(8,128)(2,1)S(1)}, bf16[128,512]{1,0:T(8,128)(2,1)S(1)}, u32[]{:S(2)}, u32[]{:S(2)}) collective-permute-start(bf16[128,512]{1,0:T(8,128)(2,1)S(1)} %fusion.47), channel_id=1, source_target_pairs={{0,64},{8,72},{16,80},{24,88},{32,96},{40,104},{48,112},{56,120},{... | collective-permute-start | bytes 393224 | tf_op jit(solution)/shard_map/ppermute | solution.py:10
  170.7 3.8 %collective-permute-start.24 = (bf16[3,128,512]{2,1,0:T(8,128)(2,1)S(1)}, bf16[3,128,512]{2,1,0:T(8,128)(2,1)S(1)}, u32[]{:S(2)}, u32[]{:S(2)}) collective-permute-start(bf16[3,128,512]{2,1,0:T(8,128)(2,1)S(1)} %pad_maximum_fusion.4), channel_id=1, source_target_pairs={{0,4},{1,5},{2,6},{3,7},{4,0},{5,1},{6,2},{7,3},{8,12},{9,13},{10,... | collective-permute-start | bytes 1179656 | tf_op jit(solution)/shard_map/ppermute | solution.py:59
  174.6 3.7 %collective-permute-start.23 = (bf16[3,128,512]{2,1,0:T(8,128)(2,1)S(1)}, bf16[3,128,512]{2,1,0:T(8,128)(2,1)S(1)}, u32[]{:S(2)}, u32[]{:S(2)}) collective-permute-start(bf16[3,128,512]{2,1,0:T(8,128)(2,1)S(1)} %pad_maximum_fusion.4), channel_id=1, source_target_pairs={{0,6},{1,7},{2,0},{3,1},{4,2},{5,3},{6,4},{7,5},{8,14},{9,15},{10,... | collective-permute-start | bytes 1179656 | tf_op jit(solution)/shard_map/ppermute | solution.py:59
  180.2 3.4 %collective-permute-done.24 = bf16[3,128,512]{2,1,0:T(8,128)(2,1)S(1)} collective-permute-done((bf16[3,128,512]{2,1,0:T(8,128)(2,1)S(1)}, bf16[3,128,512]{2,1,0:T(8,128)(2,1)S(1)}, u32[]{:S(2)}, u32[]{:S(2)}) %collective-permute-start.24) | collective-permute-done | bytes 393248 | tf_op jit(solution)/shard_map/ppermute | solution.py:59
  183.8 8.7 %collective-permute-done.23 = bf16[3,128,512]{2,1,0:T(8,128)(2,1)S(1)} collective-permute-done((bf16[3,128,512]{2,1,0:T(8,128)(2,1)S(1)}, bf16[3,128,512]{2,1,0:T(8,128)(2,1)S(1)}, u32[]{:S(2)}, u32[]{:S(2)}) %collective-permute-start.23) | collective-permute-done | bytes 393248 | tf_op jit(solution)/shard_map/ppermute | solution.py:59
  193.2 3.5 %collective-permute-start.25 = (f32[128,512]{1,0:T(8,128)S(1)}, f32[128,512]{1,0:T(8,128)S(1)}, u32[]{:S(2)}, u32[]{:S(2)}) collective-permute-start(f32[128,512]{1,0:T(8,128)S(1)} %fusion.29), channel_id=1, source_target_pairs={{0,1},{1,0},{2,3},{3,2},{4,5},{5,4},{6,7},{7,6},{8,9},{9,8},{10,11... | collective-permute-start | bytes 786440 | tf_op jit(solution)/shard_map/ppermute | solution.py:65
  199.4 5.7 %collective-permute-start.26 = (bf16[128,512]{1,0:T(8,128)(2,1)S(1)}, bf16[128,512]{1,0:T(8,128)(2,1)S(1)}, u32[]{:S(2)}, u32[]{:S(2)}) collective-permute-start(bf16[128,512]{1,0:T(8,128)(2,1)S(1)} %fusion.46), channel_id=1, source_target_pairs={{0,128},{8,136},{16,144},{24,152},{32,160},{40,168},{48,176},{56,1... | collective-permute-start | bytes 393224 | tf_op jit(solution)/shard_map/ppermute | solution.py:10
  207.7 3.6 %collective-permute-start.30 = (bf16[3,128,512]{2,1,0:T(8,128)(2,1)S(1)}, bf16[3,128,512]{2,1,0:T(8,128)(2,1)S(1)}, u32[]{:S(2)}, u32[]{:S(2)}) collective-permute-start(bf16[3,128,512]{2,1,0:T(8,128)(2,1)S(1)} %pad_maximum_fusion.5), channel_id=1, source_target_pairs={{0,4},{1,5},{2,6},{3,7},{4,0},{5,1},{6,2},{7,3},{8,12},{9,13},{10,... | collective-permute-start | bytes 1179656 | tf_op jit(solution)/shard_map/ppermute | solution.py:59
  211.4 3.7 %collective-permute-start.29 = (bf16[3,128,512]{2,1,0:T(8,128)(2,1)S(1)}, bf16[3,128,512]{2,1,0:T(8,128)(2,1)S(1)}, u32[]{:S(2)}, u32[]{:S(2)}) collective-permute-start(bf16[3,128,512]{2,1,0:T(8,128)(2,1)S(1)} %pad_maximum_fusion.5), channel_id=1, source_target_pairs={{0,6},{1,7},{2,0},{3,1},{4,2},{5,3},{6,4},{7,5},{8,14},{9,15},{10,... | collective-permute-start | bytes 1179656 | tf_op jit(solution)/shard_map/ppermute | solution.py:59
  217.0 3.6 %collective-permute-done.30 = bf16[3,128,512]{2,1,0:T(8,128)(2,1)S(1)} collective-permute-done((bf16[3,128,512]{2,1,0:T(8,128)(2,1)S(1)}, bf16[3,128,512]{2,1,0:T(8,128)(2,1)S(1)}, u32[]{:S(2)}, u32[]{:S(2)}) %collective-permute-start.30) | collective-permute-done | bytes 393248 | tf_op jit(solution)/shard_map/ppermute | solution.py:59
  220.8 8.5 %collective-permute-done.29 = bf16[3,128,512]{2,1,0:T(8,128)(2,1)S(1)} collective-permute-done((bf16[3,128,512]{2,1,0:T(8,128)(2,1)S(1)}, bf16[3,128,512]{2,1,0:T(8,128)(2,1)S(1)}, u32[]{:S(2)}, u32[]{:S(2)}) %collective-permute-start.29) | collective-permute-done | bytes 393248 | tf_op jit(solution)/shard_map/ppermute | solution.py:59
  230.1 3.5 %collective-permute-start.31 = (f32[128,512]{1,0:T(8,128)S(1)}, f32[128,512]{1,0:T(8,128)S(1)}, u32[]{:S(2)}, u32[]{:S(2)}) collective-permute-start(f32[128,512]{1,0:T(8,128)S(1)} %fusion.36), channel_id=1, source_target_pairs={{0,1},{1,0},{2,3},{3,2},{4,5},{5,4},{6,7},{7,6},{8,9},{9,8},{10,11... | collective-permute-start | bytes 786440 | tf_op jit(solution)/shard_map/ppermute | solution.py:65
  236.3 14.3 %collective-permute-start.32 = (bf16[128,512]{1,0:T(8,128)(2,1)S(1)}, bf16[128,512]{1,0:T(8,128)(2,1)S(1)}, u32[]{:S(2)}, u32[]{:S(2)}) collective-permute-start(bf16[128,512]{1,0:T(8,128)(2,1)S(1)} %fusion.45), channel_id=1, source_target_pairs={{0,256},{8,264},{16,272},{24,280},{32,288},{40,296},{48,304},{56,3... | collective-permute-start | bytes 393224 | tf_op jit(solution)/shard_map/ppermute | solution.py:10
  252.2 3.6 %collective-permute-done.32 = bf16[128,512]{1,0:T(8,128)(2,1)S(1)} collective-permute-done((bf16[128,512]{1,0:T(8,128)(2,1)S(1)}, bf16[128,512]{1,0:T(8,128)(2,1)S(1)}, u32[]{:S(2)}, u32[]{:S(2)}) %collective-permute-start.32) | collective-permute-done | bytes 131104 | tf_op jit(solution)/shard_map/ppermute | solution.py:10
  255.9 3.9 %collective-permute-start.36 = (bf16[3,128,512]{2,1,0:T(8,128)(2,1)S(1)}, bf16[3,128,512]{2,1,0:T(8,128)(2,1)S(1)}, u32[]{:S(2)}, u32[]{:S(2)}) collective-permute-start(bf16[3,128,512]{2,1,0:T(8,128)(2,1)S(1)} %pad_maximum_fusion.6), channel_id=1, source_target_pairs={{0,4},{1,5},{2,6},{3,7},{4,0},{5,1},{6,2},{7,3},{8,12},{9,13},{10,... | collective-permute-start | bytes 1179656 | tf_op jit(solution)/shard_map/ppermute | solution.py:59
  259.8 3.6 %collective-permute-start.35 = (bf16[3,128,512]{2,1,0:T(8,128)(2,1)S(1)}, bf16[3,128,512]{2,1,0:T(8,128)(2,1)S(1)}, u32[]{:S(2)}, u32[]{:S(2)}) collective-permute-start(bf16[3,128,512]{2,1,0:T(8,128)(2,1)S(1)} %pad_maximum_fusion.6), channel_id=1, source_target_pairs={{0,6},{1,7},{2,0},{3,1},{4,2},{5,3},{6,4},{7,5},{8,14},{9,15},{10,... | collective-permute-start | bytes 1179656 | tf_op jit(solution)/shard_map/ppermute | solution.py:59
  265.3 3.4 %collective-permute-done.36 = bf16[3,128,512]{2,1,0:T(8,128)(2,1)S(1)} collective-permute-done((bf16[3,128,512]{2,1,0:T(8,128)(2,1)S(1)}, bf16[3,128,512]{2,1,0:T(8,128)(2,1)S(1)}, u32[]{:S(2)}, u32[]{:S(2)}) %collective-permute-start.36) | collective-permute-done | bytes 393248 | tf_op jit(solution)/shard_map/ppermute | solution.py:59
  268.9 8.7 %collective-permute-done.35 = bf16[3,128,512]{2,1,0:T(8,128)(2,1)S(1)} collective-permute-done((bf16[3,128,512]{2,1,0:T(8,128)(2,1)S(1)}, bf16[3,128,512]{2,1,0:T(8,128)(2,1)S(1)}, u32[]{:S(2)}, u32[]{:S(2)}) %collective-permute-start.35) | collective-permute-done | bytes 393248 | tf_op jit(solution)/shard_map/ppermute | solution.py:59
  278.4 3.5 %collective-permute-start.37 = (f32[128,512]{1,0:T(8,128)S(1)}, f32[128,512]{1,0:T(8,128)S(1)}, u32[]{:S(2)}, u32[]{:S(2)}) collective-permute-start(f32[128,512]{1,0:T(8,128)S(1)} %fusion.43), channel_id=1, source_target_pairs={{0,1},{1,0},{2,3},{3,2},{4,5},{5,4},{6,7},{7,6},{8,9},{9,8},{10,11... | collective-permute-start | bytes 786440 | tf_op jit(solution)/shard_map/ppermute | solution.py:65
  (157 shorter events, 107.5 us)
Async XLA Ops:
  0.0 19.1 %collective-permute-start.1 = (bf16[128,512]{1,0:T(8,128)(2,1)}, bf16[128,512]{1,0:T(8,128)(2,1)S(1)}, u32[]{:S(2)}, u32[]{:S(2)}) collective-permute-start(bf16[128,512]{1,0:T(8,128)(2,1)} %bitcast.511), channel_id=1, source_target_pairs={{8,0},{16,8},{24,16},{32,24},{40,32},{48,40},{56,48},{64,56},{72,6... | collective-permute-start | bytes 393224 | tf_op jit(solution)/shard_map/ppermute | solution.py:10
  1.4 17.7 %collective-permute-start = (bf16[128,512]{1,0:T(8,128)(2,1)}, bf16[128,512]{1,0:T(8,128)(2,1)S(1)}, u32[]{:S(2)}, u32[]{:S(2)}) collective-permute-start(bf16[128,512]{1,0:T(8,128)(2,1)} %bitcast.512), channel_id=1, source_target_pairs={{0,8},{8,16},{16,24},{24,32},{32,40},{40,48},{48,56},{56,64},{64,7... | collective-permute-start | bytes 393224 | tf_op jit(solution)/shard_map/ppermute | solution.py:10
  11.2 31.0 %collective-permute-start.5 = (bf16[1,128,4,3,128]{4,1,3,2,0:T(8,128)(2,1)}, bf16[1,128,4,3,128]{4,1,3,2,0:T(8,128)(2,1)}, u32[]{:S(2)}, u32[]{:S(2)}) collective-permute-start(bf16[1,128,4,3,128]{4,1,3,2,0:T(8,128)(2,1)} %fusion.51), channel_id=1, source_target_pairs={{0,1},{1,0},{2,3},{3,2},{4,5},{5,4},{6,7},{7,6},{8,9},{9,8},{10,11... | collective-permute-start | bytes 1179656 | tf_op jit(solution)/shard_map/ppermute | solution.py:38
  19.2 22.3 %collective-permute-start.2 = (bf16[3,128,512]{2,1,0:T(8,128)(2,1)S(1)}, bf16[3,128,512]{2,1,0:T(8,128)(2,1)S(1)}, u32[]{:S(2)}, u32[]{:S(2)}) collective-permute-start(bf16[3,128,512]{2,1,0:T(8,128)(2,1)S(1)} %pad_maximum_fusion.1), channel_id=1, source_target_pairs={{0,2},{1,3},{2,4},{3,5},{4,6},{5,7},{6,0},{7,1},{8,10},{9,11},{10,... | collective-permute-start | bytes 1179656 | tf_op jit(solution)/shard_map/ppermute | solution.py:59
  21.1 21.1 %collective-permute-start.3 = (bf16[3,128,512]{2,1,0:T(8,128)(2,1)S(1)}, bf16[3,128,512]{2,1,0:T(8,128)(2,1)}, u32[]{:S(2)}, u32[]{:S(2)}) collective-permute-start(bf16[3,128,512]{2,1,0:T(8,128)(2,1)S(1)} %pad_maximum_fusion.1), channel_id=1, source_target_pairs={{0,6},{1,7},{2,0},{3,1},{4,2},{5,3},{6,4},{7,5},{8,14},{9,15},{10,... | collective-permute-start | bytes 1179656 | tf_op jit(solution)/shard_map/ppermute | solution.py:59
  25.7 16.5 %collective-permute-start.4 = (bf16[3,128,512]{2,1,0:T(8,128)(2,1)S(1)}, bf16[3,128,512]{2,1,0:T(8,128)(2,1)}, u32[]{:S(2)}, u32[]{:S(2)}) collective-permute-start(bf16[3,128,512]{2,1,0:T(8,128)(2,1)S(1)} %pad_maximum_fusion.1), channel_id=1, source_target_pairs={{0,4},{1,5},{2,6},{3,7},{4,0},{5,1},{6,2},{7,3},{8,12},{9,13},{10,... | collective-permute-start | bytes 1179656 | tf_op jit(solution)/shard_map/ppermute | solution.py:59
  63.2 33.6 %collective-permute-start.12 = (bf16[5,128,4,3,128]{4,1,3,2,0:T(8,128)(2,1)}, bf16[5,128,4,3,128]{4,1,3,2,0:T(8,128)(2,1)}, u32[]{:S(2)}, u32[]{:S(2)}) collective-permute-start(bf16[5,128,4,3,128]{4,1,3,2,0:T(8,128)(2,1)} %fusion), channel_id=1, source_target_pairs={{0,1},{1,0},{2,3},{3,2},{4,5},{5,4},{6,7},{7,6},{8,9},{9,8},{10,11... | collective-permute-start | bytes 5898248 | tf_op jit(solution)/shard_map/ppermute | solution.py:38
  73.6 9.6 %collective-permute-start.8 = (bf16[128,512]{1,0:T(8,128)(2,1)S(1)}, bf16[128,512]{1,0:T(8,128)(2,1)S(1)}, u32[]{:S(2)}, u32[]{:S(2)}) collective-permute-start(bf16[128,512]{1,0:T(8,128)(2,1)S(1)} %fusion.49), channel_id=1, source_target_pairs={{16,0},{24,8},{32,16},{40,24},{48,32},{56,40},{64,48},{72,56},{80,... | collective-permute-start | bytes 393224 | tf_op jit(solution)/shard_map/ppermute | solution.py:10
  74.9 8.3 %collective-permute-start.7 = (bf16[128,512]{1,0:T(8,128)(2,1)S(1)}, bf16[128,512]{1,0:T(8,128)(2,1)S(1)}, u32[]{:S(2)}, u32[]{:S(2)}) collective-permute-start(bf16[128,512]{1,0:T(8,128)(2,1)S(1)} %fusion.49), channel_id=1, source_target_pairs={{0,16},{8,24},{16,32},{24,40},{32,48},{40,56},{48,64},{56,72},{64,... | collective-permute-start | bytes 393224 | tf_op jit(solution)/shard_map/ppermute | solution.py:10
  83.3 13.3 %collective-permute-start.11 = (bf16[3,128,512]{2,1,0:T(8,128)(2,1)S(1)}, bf16[3,128,512]{2,1,0:T(8,128)(2,1)S(1)}, u32[]{:S(2)}, u32[]{:S(2)}) collective-permute-start(bf16[3,128,512]{2,1,0:T(8,128)(2,1)S(1)} %pad_maximum_fusion.2), channel_id=1, source_target_pairs={{0,4},{1,5},{2,6},{3,7},{4,0},{5,1},{6,2},{7,3},{8,12},{9,13},{10,... | collective-permute-start | bytes 1179656 | tf_op jit(solution)/shard_map/ppermute | solution.py:59
  86.8 19.4 %collective-permute-start.10 = (bf16[3,128,512]{2,1,0:T(8,128)(2,1)S(1)}, bf16[3,128,512]{2,1,0:T(8,128)(2,1)S(1)}, u32[]{:S(2)}, u32[]{:S(2)}) collective-permute-start(bf16[3,128,512]{2,1,0:T(8,128)(2,1)S(1)} %pad_maximum_fusion.2), channel_id=1, source_target_pairs={{0,6},{1,7},{2,0},{3,1},{4,2},{5,3},{6,4},{7,5},{8,14},{9,15},{10,... | collective-permute-start | bytes 1179656 | tf_op jit(solution)/shard_map/ppermute | solution.py:59
  91.1 15.3 %collective-permute-start.9 = (bf16[3,128,512]{2,1,0:T(8,128)(2,1)S(1)}, bf16[3,128,512]{2,1,0:T(8,128)(2,1)S(1)}, u32[]{:S(2)}, u32[]{:S(2)}) collective-permute-start(bf16[3,128,512]{2,1,0:T(8,128)(2,1)S(1)} %pad_maximum_fusion.2), channel_id=1, source_target_pairs={{0,2},{1,3},{2,4},{3,5},{4,6},{5,7},{6,0},{7,1},{8,10},{9,11},{10,... | collective-permute-start | bytes 1179656 | tf_op jit(solution)/shard_map/ppermute | solution.py:59
  111.8 11.6 %collective-permute-start.15 = (bf16[128,512]{1,0:T(8,128)(2,1)S(1)}, bf16[128,512]{1,0:T(8,128)(2,1)S(1)}, u32[]{:S(2)}, u32[]{:S(2)}) collective-permute-start(bf16[128,512]{1,0:T(8,128)(2,1)S(1)} %fusion.48), channel_id=1, source_target_pairs={{32,0},{40,8},{48,16},{56,24},{64,32},{72,40},{80,48},{88,56},{96,... | collective-permute-start | bytes 393224 | tf_op jit(solution)/shard_map/ppermute | solution.py:10
  113.1 16.5 %collective-permute-start.14 = (bf16[128,512]{1,0:T(8,128)(2,1)S(1)}, bf16[128,512]{1,0:T(8,128)(2,1)S(1)}, u32[]{:S(2)}, u32[]{:S(2)}) collective-permute-start(bf16[128,512]{1,0:T(8,128)(2,1)S(1)} %fusion.48), channel_id=1, source_target_pairs={{0,32},{8,40},{16,48},{24,56},{32,64},{40,72},{48,80},{56,88},{64,... | collective-permute-start | bytes 393224 | tf_op jit(solution)/shard_map/ppermute | solution.py:10
  129.7 13.6 %collective-permute-start.18 = (bf16[3,128,512]{2,1,0:T(8,128)(2,1)S(1)}, bf16[3,128,512]{2,1,0:T(8,128)(2,1)S(1)}, u32[]{:S(2)}, u32[]{:S(2)}) collective-permute-start(bf16[3,128,512]{2,1,0:T(8,128)(2,1)S(1)} %pad_maximum_fusion.3), channel_id=1, source_target_pairs={{0,4},{1,5},{2,6},{3,7},{4,0},{5,1},{6,2},{7,3},{8,12},{9,13},{10,... | collective-permute-start | bytes 1179656 | tf_op jit(solution)/shard_map/ppermute | solution.py:59
  132.8 18.9 %collective-permute-start.17 = (bf16[3,128,512]{2,1,0:T(8,128)(2,1)S(1)}, bf16[3,128,512]{2,1,0:T(8,128)(2,1)S(1)}, u32[]{:S(2)}, u32[]{:S(2)}) collective-permute-start(bf16[3,128,512]{2,1,0:T(8,128)(2,1)S(1)} %pad_maximum_fusion.3), channel_id=1, source_target_pairs={{0,6},{1,7},{2,0},{3,1},{4,2},{5,3},{6,4},{7,5},{8,14},{9,15},{10,... | collective-permute-start | bytes 1179656 | tf_op jit(solution)/shard_map/ppermute | solution.py:59
  136.5 15.8 %collective-permute-start.16 = (bf16[3,128,512]{2,1,0:T(8,128)(2,1)S(1)}, bf16[3,128,512]{2,1,0:T(8,128)(2,1)S(1)}, u32[]{:S(2)}, u32[]{:S(2)}) collective-permute-start(bf16[3,128,512]{2,1,0:T(8,128)(2,1)S(1)} %pad_maximum_fusion.3), channel_id=1, source_target_pairs={{0,2},{1,3},{2,4},{3,5},{4,6},{5,7},{6,0},{7,1},{8,10},{9,11},{10,... | collective-permute-start | bytes 1179656 | tf_op jit(solution)/shard_map/ppermute | solution.py:59
  157.0 12.8 %collective-permute-start.21 = (bf16[128,512]{1,0:T(8,128)(2,1)S(1)}, bf16[128,512]{1,0:T(8,128)(2,1)S(1)}, u32[]{:S(2)}, u32[]{:S(2)}) collective-permute-start(bf16[128,512]{1,0:T(8,128)(2,1)S(1)} %fusion.47), channel_id=1, source_target_pairs={{64,0},{72,8},{80,16},{88,24},{96,32},{104,40},{112,48},{120,56},{... | collective-permute-start | bytes 393224 | tf_op jit(solution)/shard_map/ppermute | solution.py:10
  158.3 12.3 %collective-permute-start.20 = (bf16[128,512]{1,0:T(8,128)(2,1)S(1)}, bf16[128,512]{1,0:T(8,128)(2,1)S(1)}, u32[]{:S(2)}, u32[]{:S(2)}) collective-permute-start(bf16[128,512]{1,0:T(8,128)(2,1)S(1)} %fusion.47), channel_id=1, source_target_pairs={{0,64},{8,72},{16,80},{24,88},{32,96},{40,104},{48,112},{56,120},{... | collective-permute-start | bytes 393224 | tf_op jit(solution)/shard_map/ppermute | solution.py:10
  170.7 12.8 %collective-permute-start.24 = (bf16[3,128,512]{2,1,0:T(8,128)(2,1)S(1)}, bf16[3,128,512]{2,1,0:T(8,128)(2,1)S(1)}, u32[]{:S(2)}, u32[]{:S(2)}) collective-permute-start(bf16[3,128,512]{2,1,0:T(8,128)(2,1)S(1)} %pad_maximum_fusion.4), channel_id=1, source_target_pairs={{0,4},{1,5},{2,6},{3,7},{4,0},{5,1},{6,2},{7,3},{8,12},{9,13},{10,... | collective-permute-start | bytes 1179656 | tf_op jit(solution)/shard_map/ppermute | solution.py:59
  174.6 17.9 %collective-permute-start.23 = (bf16[3,128,512]{2,1,0:T(8,128)(2,1)S(1)}, bf16[3,128,512]{2,1,0:T(8,128)(2,1)S(1)}, u32[]{:S(2)}, u32[]{:S(2)}) collective-permute-start(bf16[3,128,512]{2,1,0:T(8,128)(2,1)S(1)} %pad_maximum_fusion.4), channel_id=1, source_target_pairs={{0,6},{1,7},{2,0},{3,1},{4,2},{5,3},{6,4},{7,5},{8,14},{9,15},{10,... | collective-permute-start | bytes 1179656 | tf_op jit(solution)/shard_map/ppermute | solution.py:59
  178.2 14.5 %collective-permute-start.22 = (bf16[3,128,512]{2,1,0:T(8,128)(2,1)S(1)}, bf16[3,128,512]{2,1,0:T(8,128)(2,1)S(1)}, u32[]{:S(2)}, u32[]{:S(2)}) collective-permute-start(bf16[3,128,512]{2,1,0:T(8,128)(2,1)S(1)} %pad_maximum_fusion.4), channel_id=1, source_target_pairs={{0,2},{1,3},{2,4},{3,5},{4,6},{5,7},{6,0},{7,1},{8,10},{9,11},{10,... | collective-permute-start | bytes 1179656 | tf_op jit(solution)/shard_map/ppermute | solution.py:59
  198.1 8.7 %collective-permute-start.27 = (bf16[128,512]{1,0:T(8,128)(2,1)S(1)}, bf16[128,512]{1,0:T(8,128)(2,1)S(1)}, u32[]{:S(2)}, u32[]{:S(2)}) collective-permute-start(bf16[128,512]{1,0:T(8,128)(2,1)S(1)} %fusion.46), channel_id=1, source_target_pairs={{128,0},{136,8},{144,16},{152,24},{160,32},{168,40},{176,48},{184,... | collective-permute-start | bytes 393224 | tf_op jit(solution)/shard_map/ppermute | solution.py:10
  199.4 8.2 %collective-permute-start.26 = (bf16[128,512]{1,0:T(8,128)(2,1)S(1)}, bf16[128,512]{1,0:T(8,128)(2,1)S(1)}, u32[]{:S(2)}, u32[]{:S(2)}) collective-permute-start(bf16[128,512]{1,0:T(8,128)(2,1)S(1)} %fusion.46), channel_id=1, source_target_pairs={{0,128},{8,136},{16,144},{24,152},{32,160},{40,168},{48,176},{56,1... | collective-permute-start | bytes 393224 | tf_op jit(solution)/shard_map/ppermute | solution.py:10
  207.7 12.8 %collective-permute-start.30 = (bf16[3,128,512]{2,1,0:T(8,128)(2,1)S(1)}, bf16[3,128,512]{2,1,0:T(8,128)(2,1)S(1)}, u32[]{:S(2)}, u32[]{:S(2)}) collective-permute-start(bf16[3,128,512]{2,1,0:T(8,128)(2,1)S(1)} %pad_maximum_fusion.5), channel_id=1, source_target_pairs={{0,4},{1,5},{2,6},{3,7},{4,0},{5,1},{6,2},{7,3},{8,12},{9,13},{10,... | collective-permute-start | bytes 1179656 | tf_op jit(solution)/shard_map/ppermute | solution.py:59
  211.4 17.9 %collective-permute-start.29 = (bf16[3,128,512]{2,1,0:T(8,128)(2,1)S(1)}, bf16[3,128,512]{2,1,0:T(8,128)(2,1)S(1)}, u32[]{:S(2)}, u32[]{:S(2)}) collective-permute-start(bf16[3,128,512]{2,1,0:T(8,128)(2,1)S(1)} %pad_maximum_fusion.5), channel_id=1, source_target_pairs={{0,6},{1,7},{2,0},{3,1},{4,2},{5,3},{6,4},{7,5},{8,14},{9,15},{10,... | collective-permute-start | bytes 1179656 | tf_op jit(solution)/shard_map/ppermute | solution.py:59
  215.0 14.6 %collective-permute-start.28 = (bf16[3,128,512]{2,1,0:T(8,128)(2,1)S(1)}, bf16[3,128,512]{2,1,0:T(8,128)(2,1)S(1)}, u32[]{:S(2)}, u32[]{:S(2)}) collective-permute-start(bf16[3,128,512]{2,1,0:T(8,128)(2,1)S(1)} %pad_maximum_fusion.5), channel_id=1, source_target_pairs={{0,2},{1,3},{2,4},{3,5},{4,6},{5,7},{6,0},{7,1},{8,10},{9,11},{10,... | collective-permute-start | bytes 1179656 | tf_op jit(solution)/shard_map/ppermute | solution.py:59
  235.0 17.2 %collective-permute-start.33 = (bf16[128,512]{1,0:T(8,128)(2,1)S(1)}, bf16[128,512]{1,0:T(8,128)(2,1)S(1)}, u32[]{:S(2)}, u32[]{:S(2)}) collective-permute-start(bf16[128,512]{1,0:T(8,128)(2,1)S(1)} %fusion.45), channel_id=1, source_target_pairs={{256,0},{264,8},{272,16},{280,24},{288,32},{296,40},{304,48},{312,... | collective-permute-start | bytes 393224 | tf_op jit(solution)/shard_map/ppermute | solution.py:10
  236.3 19.5 %collective-permute-start.32 = (bf16[128,512]{1,0:T(8,128)(2,1)S(1)}, bf16[128,512]{1,0:T(8,128)(2,1)S(1)}, u32[]{:S(2)}, u32[]{:S(2)}) collective-permute-start(bf16[128,512]{1,0:T(8,128)(2,1)S(1)} %fusion.45), channel_id=1, source_target_pairs={{0,256},{8,264},{16,272},{24,280},{32,288},{40,296},{48,304},{56,3... | collective-permute-start | bytes 393224 | tf_op jit(solution)/shard_map/ppermute | solution.py:10
  255.9 12.8 %collective-permute-start.36 = (bf16[3,128,512]{2,1,0:T(8,128)(2,1)S(1)}, bf16[3,128,512]{2,1,0:T(8,128)(2,1)S(1)}, u32[]{:S(2)}, u32[]{:S(2)}) collective-permute-start(bf16[3,128,512]{2,1,0:T(8,128)(2,1)S(1)} %pad_maximum_fusion.6), channel_id=1, source_target_pairs={{0,4},{1,5},{2,6},{3,7},{4,0},{5,1},{6,2},{7,3},{8,12},{9,13},{10,... | collective-permute-start | bytes 1179656 | tf_op jit(solution)/shard_map/ppermute | solution.py:59
  259.8 17.8 %collective-permute-start.35 = (bf16[3,128,512]{2,1,0:T(8,128)(2,1)S(1)}, bf16[3,128,512]{2,1,0:T(8,128)(2,1)S(1)}, u32[]{:S(2)}, u32[]{:S(2)}) collective-permute-start(bf16[3,128,512]{2,1,0:T(8,128)(2,1)S(1)} %pad_maximum_fusion.6), channel_id=1, source_target_pairs={{0,6},{1,7},{2,0},{3,1},{4,2},{5,3},{6,4},{7,5},{8,14},{9,15},{10,... | collective-permute-start | bytes 1179656 | tf_op jit(solution)/shard_map/ppermute | solution.py:59
  263.4 14.5 %collective-permute-start.34 = (bf16[3,128,512]{2,1,0:T(8,128)(2,1)S(1)}, bf16[3,128,512]{2,1,0:T(8,128)(2,1)S(1)}, u32[]{:S(2)}, u32[]{:S(2)}) collective-permute-start(bf16[3,128,512]{2,1,0:T(8,128)(2,1)S(1)} %pad_maximum_fusion.6), channel_id=1, source_target_pairs={{0,2},{1,3},{2,4},{3,5},{4,6},{5,7},{6,0},{7,1},{8,10},{9,11},{10,... | collective-permute-start | bytes 1179656 | tf_op jit(solution)/shard_map/ppermute | solution.py:59
  (18 other events, 113.6 us)

commit v7 on v2

--- a/solution.py
+++ b/solution.py
@@ -32,7 +32,10 @@
         part = jnp.take(signed, columns_for(which_core), axis=3)
         return part.transpose(0, 1, 3, 2, 4)
 
-    mine = pick(core)
+    def pick_level(level, which_core):
+        part = jnp.take(signed[level], columns_for(which_core), axis=2)
+        return part.transpose(0, 2, 1, 3)
+
     swap = [(2 * c + b, 2 * c + 1 - b) for c in range(chips) for b in range(2)]
     theirs = lax.ppermute(pick(1 - core), "cross", swap)
 
@@ -54,7 +57,7 @@
         own = jnp.stack([current, lower, upper])
         pieces = [own] + [lax.ppermute(own, "cross", same_core(-off)) for off in OFFSETS[1:]]
         given = lax.ppermute(partial(theirs[level], pieces), "cross", swap)
-        total = partial(mine[level], pieces) + given
+        total = partial(pick_level(level, core), pieces) + given
         current = total.astype(jnp.bfloat16)
     return current[None]
 

time: 280 us -> 321 us (1.15); the launches traced: 279 us -> 317 us
  local copies, waits for them, and re-layouts: 20.5 us -> 38.4 us
  other arithmetic: 7.78 us -> 16.1 us
  waiting for transfers between devices: 104 us -> 110 us
  starting transfers between devices: 135 us -> 140 us
    ppermute x12, waiting for transfers between devices: 22.9 us -> 41.6 us  [shifted(): lax.ppermute(value, axis, [(source, source + steps) for source in range(i...]
    ppermute x12, starting transfers between devices: 56.9 us -> 39.2 us  [shifted(): lax.ppermute(value, axis, [(source, source + steps) for source in range(i...]
    ppermute x18, waiting for transfers between devices: 77.9 us -> 65.5 us  [body(): lax.ppermute(own, 'cross', same_core(-off))]
    ppermute x6, starting transfers between devices: 18.5 us -> 30.4 us  [body(): given = lax.ppermute(partial(theirs[level], pieces), 'cross', swap)]
    ppermute x18, starting transfers between devices: 50.3 us -> 61.2 us  [body(): lax.ppermute(own, 'cross', same_core(-off))]
    gather x0 -> x6, local copies, waits for them, and re-layouts: none -> 10.8 us  [pick_level(): part = jnp.take(signed[level], columns_for(which_core), axis=2)]
    squeeze x1 -> x6, local copies, waits for them, and re-layouts: 0.28 us -> 6.9 us  [pick_level(): part = jnp.take(signed[level], columns_for(which_core), axis=2)]
    neg x1, other arithmetic: 0.31 us -> 4.47 us  [body(): -upper_factor[:, 0]]
  transfers between devices with their start and end apart: 37 -> 37, of which waited for: 30 -> 34; matrix products, arithmetic and copies ran while one was open for 4% -> 10% of each run, Pallas kernels for 0% -> 0%
where the time goes in v7:
time: 321 us; the launch traced here: 317 us
  starting transfers between devices  140 us (44%)
  waiting for transfers between devices  110 us (34%)
  local copies, waits for them, and re-layouts  38.4 us (12%)
  other arithmetic  16.1 us (5%)
  matrix products  11.7 us (4%)
    ppermute x18, waiting for transfers between devices, body(): lax.ppermute(own, 'cross', same_core(-off))  65.5 us
    ppermute x18, starting transfers between devices, body(): lax.ppermute(own, 'cross', same_core(-off))  61.2 us
    ppermute x12, waiting for transfers between devices, shifted(): lax.ppermute(value, axis, [(source, source + steps) for source in range(i...  41.6 us
    ppermute x12, starting transfers between devices, shifted(): lax.ppermute(value, axis, [(source, source + steps) for source in range(i...  39.2 us
    ppermute x6, starting transfers between devices, body(): given = lax.ppermute(partial(theirs[level], pieces), 'cross', swap)  30.4 us
    dot_general x48, matrix products, partial(): jnp.einsum('ibk,bkr->ir', mat[:, j], piece, preferred_element_type=jnp.fl...  11.7 us
    gather x6, local copies, waits for them, and re-layouts, pick_level(): part = jnp.take(signed[level], columns_for(which_core), axis=2)  10.8 us
    ppermute x1, starting transfers between devices, body(): theirs = lax.ppermute(pick(1 - core), 'cross', swap)  8.77 us
  transfers between devices with their start and end apart: 37, of which 34 were waited for; matrix products, arithmetic and copies ran while one was open for 10% of the time, Pallas kernels for 0%

profile of v7, /device:TPU:1, one launch (start us, length us, event | category | flops | bytes accessed | tf_op | source)
XLA Modules:
  0.0 316.6 jit_solution(13352217552027437569)
XLA Ops:
  5.3 4.5 %negate_bitcast_fusion = (bf16[6,128,1,1024]{1,3,2,0:T(8,128)(2,1)S(1)}, bf16[6,1,128,1024]{2,3,0,1:T(8,128)(2,1)}, bf16[6,1,128,1024]{2,3,0,1:T(8,128)(2,1)}, bf16[6,128,1,1024]{1,3,2,0:T(8,128)(2,1)}) fusion(bf16[6,1,128,1024]{2,3,0,1:T(8,128)(2,1)} %copy.10, bf16[6,1,128,1024]{2,3,0,1:T(8,128)(2,1)} %copy.9), kind=kLoop, calls=%fused_computation.182 | loop fusion | flops 1572864 | bytes 9437184 | tf_op jit(solution)/shard_map/neg | solution.py:28
  16.6 5.0 %pad_maximum_fusion.1 = bf16[6,128,3,8,128]{4,1,3,2,0:T(8,128)(2,1)} fusion(bf16[6,128,1,8,128]{4,1,3,2,0:T(8,128)(2,1)} %copy.20, bf16[6,128,1,8,128]{4,1,3,2,0:T(8,128)(2,1)} %copy.19, bf16[6,128,1,8,128]{4,1,3,2,0:T(8,128)(2,1)} %copy.18), kind=kLoop, calls=%fused_computation.8 | loop fusion | flops 4718592 | bytes 9437184 | tf_op jit(solution)/shard_map/stack | solution.py:28
  21.6 4.6 %gather_fusion = bf16[4,6,128,3,128]{4,2,3,1,0:T(8,128)(2,1)} fusion(bf16[6,128,3,8,128]{4,1,3,2,0:T(8,128)(2,1)} %pad_maximum_fusion.1, s32[1024]{0:T(1024)S(1)} %pad_clamp_fusion), kind=kCustom, calls=%fused_computation.6 | custom fusion | bytes 4718608 | tf_op jit(solution)/shard_map/jit(_take)/gather | solution.py:32
  29.8 8.8 %collective-permute-start.5 = (bf16[6,128,4,3,128]{4,1,3,2,0:T(8,128)(2,1)}, bf16[6,128,4,3,128]{4,1,3,2,0:T(8,128)(2,1)}, u32[]{:S(2)}, u32[]{:S(2)}) collective-permute-start(bf16[6,128,4,3,128]{4,1,3,2,0:T(8,128)(2,1)} %fusion), channel_id=1, source_target_pairs={{0,1},{1,0},{2,3},{3,2},{4,5},{5,4},{6,7},{7,6},{8,9},{9,8},{10,11... | collective-permute-start | bytes 7077896 | tf_op jit(solution)/shard_map/ppermute | solution.py:40
  69.4 4.6 %collective-permute-start.3 = (bf16[3,128,512]{2,1,0:T(8,128)(2,1)}, bf16[3,128,512]{2,1,0:T(8,128)(2,1)S(1)}, u32[]{:S(2)}, u32[]{:S(2)}) collective-permute-start(bf16[3,128,512]{2,1,0:T(8,128)(2,1)} %pad_maximum_fusion.2), channel_id=1, source_target_pairs={{0,6},{1,7},{2,0},{3,1},{4,2},{5,3},{6,4},{7,5},{8,14},{9,15},{10,... | collective-permute-start | bytes 1179656 | tf_op jit(solution)/shard_map/ppermute | solution.py:58
  78.2 4.0 %collective-permute-done.3 = bf16[3,128,512]{2,1,0:T(8,128)(2,1)S(1)} collective-permute-done((bf16[3,128,512]{2,1,0:T(8,128)(2,1)}, bf16[3,128,512]{2,1,0:T(8,128)(2,1)S(1)}, u32[]{:S(2)}, u32[]{:S(2)}) %collective-permute-start.3) | collective-permute-done | bytes 393248 | tf_op jit(solution)/shard_map/ppermute | solution.py:58
  82.5 4.3 %collective-permute-done.4 = bf16[3,128,512]{2,1,0:T(8,128)(2,1)S(1)} collective-permute-done((bf16[3,128,512]{2,1,0:T(8,128)(2,1)}, bf16[3,128,512]{2,1,0:T(8,128)(2,1)S(1)}, u32[]{:S(2)}, u32[]{:S(2)}) %collective-permute-start.4) | collective-permute-done | bytes 393248 | tf_op jit(solution)/shard_map/ppermute | solution.py:58
  87.3 7.3 %collective-permute-start.6 = (f32[128,512]{1,0:T(8,128)S(1)}, f32[128,512]{1,0:T(8,128)S(1)}, u32[]{:S(2)}, u32[]{:S(2)}) collective-permute-start(f32[128,512]{1,0:T(8,128)S(1)} %fusion.7), channel_id=1, source_target_pairs={{0,1},{1,0},{2,3},{3,2},{4,5},{5,4},{6,7},{7,6},{8,9},{9,8},{10,11... | collective-permute-start | bytes 786440 | tf_op jit(solution)/shard_map/ppermute | solution.py:59
  96.1 5.0 %collective-permute-start.7 = (bf16[128,512]{1,0:T(8,128)(2,1)S(1)}, bf16[128,512]{1,0:T(8,128)(2,1)S(1)}, u32[]{:S(2)}, u32[]{:S(2)}) collective-permute-start(bf16[128,512]{1,0:T(8,128)(2,1)S(1)} %fusion.48), channel_id=1, source_target_pairs={{0,16},{8,24},{16,32},{24,40},{32,48},{40,56},{48,64},{56,72},{64,... | collective-permute-start | bytes 393224 | tf_op jit(solution)/shard_map/ppermute | solution.py:10
  103.6 4.7 %collective-permute-done.8 = bf16[128,512]{1,0:T(8,128)(2,1)S(1)} collective-permute-done((bf16[128,512]{1,0:T(8,128)(2,1)S(1)}, bf16[128,512]{1,0:T(8,128)(2,1)S(1)}, u32[]{:S(2)}, u32[]{:S(2)}) %collective-permute-start.8) | collective-permute-done | bytes 131104 | tf_op jit(solution)/shard_map/ppermute | solution.py:10
  108.3 4.1 %collective-permute-start.9 = (bf16[3,128,512]{2,1,0:T(8,128)(2,1)S(1)}, bf16[3,128,512]{2,1,0:T(8,128)(2,1)S(1)}, u32[]{:S(2)}, u32[]{:S(2)}) collective-permute-start(bf16[3,128,512]{2,1,0:T(8,128)(2,1)S(1)} %pad_maximum_fusion.3), channel_id=1, source_target_pairs={{0,2},{1,3},{2,4},{3,5},{4,6},{5,7},{6,0},{7,1},{8,10},{9,11},{10,... | collective-permute-start | bytes 1179656 | tf_op jit(solution)/shard_map/ppermute | solution.py:58
  121.7 8.3 %collective-permute-done.11 = bf16[3,128,512]{2,1,0:T(8,128)(2,1)S(1)} collective-permute-done((bf16[3,128,512]{2,1,0:T(8,128)(2,1)S(1)}, bf16[3,128,512]{2,1,0:T(8,128)(2,1)S(1)}, u32[]{:S(2)}, u32[]{:S(2)}) %collective-permute-start.11) | collective-permute-done | bytes 393248 | tf_op jit(solution)/shard_map/ppermute | solution.py:58
  130.5 5.0 %collective-permute-start.12 = (f32[128,512]{1,0:T(8,128)S(1)}, f32[128,512]{1,0:T(8,128)S(1)}, u32[]{:S(2)}, u32[]{:S(2)}) collective-permute-start(f32[128,512]{1,0:T(8,128)S(1)} %fusion.14), channel_id=1, source_target_pairs={{0,1},{1,0},{2,3},{3,2},{4,5},{5,4},{6,7},{7,6},{8,9},{9,8},{10,11... | collective-permute-start | bytes 786440 | tf_op jit(solution)/shard_map/ppermute | solution.py:59
  137.0 5.8 %collective-permute-start.13 = (bf16[128,512]{1,0:T(8,128)(2,1)S(1)}, bf16[128,512]{1,0:T(8,128)(2,1)S(1)}, u32[]{:S(2)}, u32[]{:S(2)}) collective-permute-start(bf16[128,512]{1,0:T(8,128)(2,1)S(1)} %fusion.47), channel_id=1, source_target_pairs={{0,32},{8,40},{16,48},{24,56},{32,64},{40,72},{48,80},{56,88},{64,... | collective-permute-start | bytes 393224 | tf_op jit(solution)/shard_map/ppermute | solution.py:10
  145.2 11.3 %collective-permute-done.14 = bf16[128,512]{1,0:T(8,128)(2,1)S(1)} collective-permute-done((bf16[128,512]{1,0:T(8,128)(2,1)S(1)}, bf16[128,512]{1,0:T(8,128)(2,1)S(1)}, u32[]{:S(2)}, u32[]{:S(2)}) %collective-permute-start.14) | collective-permute-done | bytes 131104 | tf_op jit(solution)/shard_map/ppermute | solution.py:10
  156.6 4.7 %collective-permute-start.15 = (bf16[3,128,512]{2,1,0:T(8,128)(2,1)S(1)}, bf16[3,128,512]{2,1,0:T(8,128)(2,1)S(1)}, u32[]{:S(2)}, u32[]{:S(2)}) collective-permute-start(bf16[3,128,512]{2,1,0:T(8,128)(2,1)S(1)} %pad_maximum_fusion.4), channel_id=1, source_target_pairs={{0,2},{1,3},{2,4},{3,5},{4,6},{5,7},{6,0},{7,1},{8,10},{9,11},{10,... | collective-permute-start | bytes 1179656 | tf_op jit(solution)/shard_map/ppermute | solution.py:58
  171.9 7.0 %collective-permute-done.17 = bf16[3,128,512]{2,1,0:T(8,128)(2,1)S(1)} collective-permute-done((bf16[3,128,512]{2,1,0:T(8,128)(2,1)S(1)}, bf16[3,128,512]{2,1,0:T(8,128)(2,1)S(1)}, u32[]{:S(2)}, u32[]{:S(2)}) %collective-permute-start.17) | collective-permute-done | bytes 393248 | tf_op jit(solution)/shard_map/ppermute | solution.py:58
  179.4 4.7 %collective-permute-start.18 = (f32[128,512]{1,0:T(8,128)S(1)}, f32[128,512]{1,0:T(8,128)S(1)}, u32[]{:S(2)}, u32[]{:S(2)}) collective-permute-start(f32[128,512]{1,0:T(8,128)S(1)} %fusion.21), channel_id=1, source_target_pairs={{0,1},{1,0},{2,3},{3,2},{4,5},{5,4},{6,7},{7,6},{8,9},{9,8},{10,11... | collective-permute-start | bytes 786440 | tf_op jit(solution)/shard_map/ppermute | solution.py:59
  191.1 3.8 %collective-permute-done.20 = bf16[128,512]{1,0:T(8,128)(2,1)S(1)} collective-permute-done((bf16[128,512]{1,0:T(8,128)(2,1)S(1)}, bf16[128,512]{1,0:T(8,128)(2,1)S(1)}, u32[]{:S(2)}, u32[]{:S(2)}) %collective-permute-start.20) | collective-permute-done | bytes 131104 | tf_op jit(solution)/shard_map/ppermute | solution.py:10
  195.0 4.7 %collective-permute-start.21 = (bf16[3,128,512]{2,1,0:T(8,128)(2,1)S(1)}, bf16[3,128,512]{2,1,0:T(8,128)(2,1)S(1)}, u32[]{:S(2)}, u32[]{:S(2)}) collective-permute-start(bf16[3,128,512]{2,1,0:T(8,128)(2,1)S(1)} %pad_maximum_fusion.5), channel_id=1, source_target_pairs={{0,2},{1,3},{2,4},{3,5},{4,6},{5,7},{6,0},{7,1},{8,10},{9,11},{10,... | collective-permute-start | bytes 1179656 | tf_op jit(solution)/shard_map/ppermute | solution.py:58
  210.6 7.3 %collective-permute-done.23 = bf16[3,128,512]{2,1,0:T(8,128)(2,1)S(1)} collective-permute-done((bf16[3,128,512]{2,1,0:T(8,128)(2,1)S(1)}, bf16[3,128,512]{2,1,0:T(8,128)(2,1)S(1)}, u32[]{:S(2)}, u32[]{:S(2)}) %collective-permute-start.23) | collective-permute-done | bytes 393248 | tf_op jit(solution)/shard_map/ppermute | solution.py:58
  218.4 4.4 %collective-permute-start.24 = (f32[128,512]{1,0:T(8,128)S(1)}, f32[128,512]{1,0:T(8,128)S(1)}, u32[]{:S(2)}, u32[]{:S(2)}) collective-permute-start(f32[128,512]{1,0:T(8,128)S(1)} %fusion.28), channel_id=1, source_target_pairs={{0,1},{1,0},{2,3},{3,2},{4,5},{5,4},{6,7},{7,6},{8,9},{9,8},{10,11... | collective-permute-start | bytes 786440 | tf_op jit(solution)/shard_map/ppermute | solution.py:59
  224.2 10.5 %collective-permute-start.25 = (bf16[128,512]{1,0:T(8,128)(2,1)S(1)}, bf16[128,512]{1,0:T(8,128)(2,1)S(1)}, u32[]{:S(2)}, u32[]{:S(2)}) collective-permute-start(bf16[128,512]{1,0:T(8,128)(2,1)S(1)} %fusion.45), channel_id=1, source_target_pairs={{0,128},{8,136},{16,144},{24,152},{32,160},{40,168},{48,176},{56,1... | collective-permute-start | bytes 393224 | tf_op jit(solution)/shard_map/ppermute | solution.py:10
  237.2 4.7 %collective-permute-done.26 = bf16[128,512]{1,0:T(8,128)(2,1)S(1)} collective-permute-done((bf16[128,512]{1,0:T(8,128)(2,1)S(1)}, bf16[128,512]{1,0:T(8,128)(2,1)S(1)}, u32[]{:S(2)}, u32[]{:S(2)}) %collective-permute-start.26) | collective-permute-done | bytes 131104 | tf_op jit(solution)/shard_map/ppermute | solution.py:10
  241.9 4.7 %collective-permute-start.27 = (bf16[3,128,512]{2,1,0:T(8,128)(2,1)S(1)}, bf16[3,128,512]{2,1,0:T(8,128)(2,1)S(1)}, u32[]{:S(2)}, u32[]{:S(2)}) collective-permute-start(bf16[3,128,512]{2,1,0:T(8,128)(2,1)S(1)} %pad_maximum_fusion.6), channel_id=1, source_target_pairs={{0,2},{1,3},{2,4},{3,5},{4,6},{5,7},{6,0},{7,1},{8,10},{9,11},{10,... | collective-permute-start | bytes 1179656 | tf_op jit(solution)/shard_map/ppermute | solution.py:58
  257.3 7.0 %collective-permute-done.29 = bf16[3,128,512]{2,1,0:T(8,128)(2,1)S(1)} collective-permute-done((bf16[3,128,512]{2,1,0:T(8,128)(2,1)S(1)}, bf16[3,128,512]{2,1,0:T(8,128)(2,1)S(1)}, u32[]{:S(2)}, u32[]{:S(2)}) %collective-permute-start.29) | collective-permute-done | bytes 393248 | tf_op jit(solution)/shard_map/ppermute | solution.py:58
  264.8 4.6 %collective-permute-start.30 = (f32[128,512]{1,0:T(8,128)S(1)}, f32[128,512]{1,0:T(8,128)S(1)}, u32[]{:S(2)}, u32[]{:S(2)}) collective-permute-start(f32[128,512]{1,0:T(8,128)S(1)} %fusion.35), channel_id=1, source_target_pairs={{0,1},{1,0},{2,3},{3,2},{4,5},{5,4},{6,7},{7,6},{8,9},{9,8},{10,11... | collective-permute-start | bytes 786440 | tf_op jit(solution)/shard_map/ppermute | solution.py:59
  270.8 5.7 %collective-permute-start.31 = (bf16[128,512]{1,0:T(8,128)(2,1)S(1)}, bf16[128,512]{1,0:T(8,128)(2,1)S(1)}, u32[]{:S(2)}, u32[]{:S(2)}) collective-permute-start(bf16[128,512]{1,0:T(8,128)(2,1)S(1)} %fusion.44), channel_id=1, source_target_pairs={{0,256},{8,264},{16,272},{24,280},{32,288},{40,296},{48,304},{56,3... | collective-permute-start | bytes 393224 | tf_op jit(solution)/shard_map/ppermute | solution.py:10
  279.0 7.7 %collective-permute-done.32 = bf16[128,512]{1,0:T(8,128)(2,1)S(1)} collective-permute-done((bf16[128,512]{1,0:T(8,128)(2,1)S(1)}, bf16[128,512]{1,0:T(8,128)(2,1)S(1)}, u32[]{:S(2)}, u32[]{:S(2)}) %collective-permute-start.32) | collective-permute-done | bytes 131104 | tf_op jit(solution)/shard_map/ppermute | solution.py:10
  286.7 4.7 %collective-permute-start.33 = (bf16[3,128,512]{2,1,0:T(8,128)(2,1)S(1)}, bf16[3,128,512]{2,1,0:T(8,128)(2,1)S(1)}, u32[]{:S(2)}, u32[]{:S(2)}) collective-permute-start(bf16[3,128,512]{2,1,0:T(8,128)(2,1)S(1)} %pad_maximum_fusion.7), channel_id=1, source_target_pairs={{0,2},{1,3},{2,4},{3,5},{4,6},{5,7},{6,0},{7,1},{8,10},{9,11},{10,... | collective-permute-start | bytes 1179656 | tf_op jit(solution)/shard_map/ppermute | solution.py:58
  302.4 7.4 %collective-permute-done.35 = bf16[3,128,512]{2,1,0:T(8,128)(2,1)S(1)} collective-permute-done((bf16[3,128,512]{2,1,0:T(8,128)(2,1)S(1)}, bf16[3,128,512]{2,1,0:T(8,128)(2,1)S(1)}, u32[]{:S(2)}, u32[]{:S(2)}) %collective-permute-start.35) | collective-permute-done | bytes 393248 | tf_op jit(solution)/shard_map/ppermute | solution.py:58
  310.2 4.4 %collective-permute-start.36 = (f32[128,512]{1,0:T(8,128)S(1)}, f32[128,512]{1,0:T(8,128)S(1)}, u32[]{:S(2)}, u32[]{:S(2)}) collective-permute-start(f32[128,512]{1,0:T(8,128)S(1)} %fusion.42), channel_id=1, source_target_pairs={{0,1},{1,0},{2,3},{3,2},{4,5},{5,4},{6,7},{7,6},{8,9},{9,8},{10,11... | collective-permute-start | bytes 786440 | tf_op jit(solution)/shard_map/ppermute | solution.py:59
  (153 shorter events, 130.4 us)
Async XLA Ops:
  29.8 46.4 %collective-permute-start.5 = (bf16[6,128,4,3,128]{4,1,3,2,0:T(8,128)(2,1)}, bf16[6,128,4,3,128]{4,1,3,2,0:T(8,128)(2,1)}, u32[]{:S(2)}, u32[]{:S(2)}) collective-permute-start(bf16[6,128,4,3,128]{4,1,3,2,0:T(8,128)(2,1)} %fusion), channel_id=1, source_target_pairs={{0,1},{1,0},{2,3},{3,2},{4,5},{5,4},{6,7},{7,6},{8,9},{9,8},{10,11... | collective-permute-start | bytes 7077896 | tf_op jit(solution)/shard_map/ppermute | solution.py:40
  39.9 7.0 %collective-permute-start.1 = (bf16[128,512]{1,0:T(8,128)(2,1)S(1)}, bf16[128,512]{1,0:T(8,128)(2,1)S(1)}, u32[]{:S(2)}, u32[]{:S(2)}) collective-permute-start(bf16[128,512]{1,0:T(8,128)(2,1)S(1)} %bitcast.486), channel_id=1, source_target_pairs={{8,0},{16,8},{24,16},{32,24},{40,32},{48,40},{56,48},{64,56},{72,6... | collective-permute-start | bytes 393224 | tf_op jit(solution)/shard_map/ppermute | solution.py:10
  48.3 27.5 %collective-permute-start.2 = (bf16[3,128,512]{2,1,0:T(8,128)(2,1)}, bf16[3,128,512]{2,1,0:T(8,128)(2,1)S(1)}, u32[]{:S(2)}, u32[]{:S(2)}) collective-permute-start(bf16[3,128,512]{2,1,0:T(8,128)(2,1)} %pad_maximum_fusion.2), channel_id=1, source_target_pairs={{0,2},{1,3},{2,4},{3,5},{4,6},{5,7},{6,0},{7,1},{8,10},{9,11},{10,... | collective-permute-start | bytes 1179656 | tf_op jit(solution)/shard_map/ppermute | solution.py:58
  69.4 12.9 %collective-permute-start.3 = (bf16[3,128,512]{2,1,0:T(8,128)(2,1)}, bf16[3,128,512]{2,1,0:T(8,128)(2,1)S(1)}, u32[]{:S(2)}, u32[]{:S(2)}) collective-permute-start(bf16[3,128,512]{2,1,0:T(8,128)(2,1)} %pad_maximum_fusion.2), channel_id=1, source_target_pairs={{0,6},{1,7},{2,0},{3,1},{4,2},{5,3},{6,4},{7,5},{8,14},{9,15},{10,... | collective-permute-start | bytes 1179656 | tf_op jit(solution)/shard_map/ppermute | solution.py:58
  74.0 12.9 %collective-permute-start.4 = (bf16[3,128,512]{2,1,0:T(8,128)(2,1)}, bf16[3,128,512]{2,1,0:T(8,128)(2,1)S(1)}, u32[]{:S(2)}, u32[]{:S(2)}) collective-permute-start(bf16[3,128,512]{2,1,0:T(8,128)(2,1)} %pad_maximum_fusion.2), channel_id=1, source_target_pairs={{0,4},{1,5},{2,6},{3,7},{4,0},{5,1},{6,2},{7,3},{8,12},{9,13},{10,... | collective-permute-start | bytes 1179656 | tf_op jit(solution)/shard_map/ppermute | solution.py:58
  87.3 8.5 %collective-permute-start.6 = (f32[128,512]{1,0:T(8,128)S(1)}, f32[128,512]{1,0:T(8,128)S(1)}, u32[]{:S(2)}, u32[]{:S(2)}) collective-permute-start(f32[128,512]{1,0:T(8,128)S(1)} %fusion.7), channel_id=1, source_target_pairs={{0,1},{1,0},{2,3},{3,2},{4,5},{5,4},{6,7},{7,6},{8,9},{9,8},{10,11... | collective-permute-start | bytes 786440 | tf_op jit(solution)/shard_map/ppermute | solution.py:59
  96.1 7.5 %collective-permute-start.7 = (bf16[128,512]{1,0:T(8,128)(2,1)S(1)}, bf16[128,512]{1,0:T(8,128)(2,1)S(1)}, u32[]{:S(2)}, u32[]{:S(2)}) collective-permute-start(bf16[128,512]{1,0:T(8,128)(2,1)S(1)} %fusion.48), channel_id=1, source_target_pairs={{0,16},{8,24},{16,32},{24,40},{32,48},{40,56},{48,64},{56,72},{64,... | collective-permute-start | bytes 393224 | tf_op jit(solution)/shard_map/ppermute | solution.py:10
  101.1 7.2 %collective-permute-start.8 = (bf16[128,512]{1,0:T(8,128)(2,1)S(1)}, bf16[128,512]{1,0:T(8,128)(2,1)S(1)}, u32[]{:S(2)}, u32[]{:S(2)}) collective-permute-start(bf16[128,512]{1,0:T(8,128)(2,1)S(1)} %fusion.48), channel_id=1, source_target_pairs={{16,0},{24,8},{32,16},{40,24},{48,32},{56,40},{64,48},{72,56},{80,... | collective-permute-start | bytes 393224 | tf_op jit(solution)/shard_map/ppermute | solution.py:10
  108.3 11.4 %collective-permute-start.9 = (bf16[3,128,512]{2,1,0:T(8,128)(2,1)S(1)}, bf16[3,128,512]{2,1,0:T(8,128)(2,1)S(1)}, u32[]{:S(2)}, u32[]{:S(2)}) collective-permute-start(bf16[3,128,512]{2,1,0:T(8,128)(2,1)S(1)} %pad_maximum_fusion.3), channel_id=1, source_target_pairs={{0,2},{1,3},{2,4},{3,5},{4,6},{5,7},{6,0},{7,1},{8,10},{9,11},{10,... | collective-permute-start | bytes 1179656 | tf_op jit(solution)/shard_map/ppermute | solution.py:58
  112.5 9.0 %collective-permute-start.10 = (bf16[3,128,512]{2,1,0:T(8,128)(2,1)S(1)}, bf16[3,128,512]{2,1,0:T(8,128)(2,1)S(1)}, u32[]{:S(2)}, u32[]{:S(2)}) collective-permute-start(bf16[3,128,512]{2,1,0:T(8,128)(2,1)S(1)} %pad_maximum_fusion.3), channel_id=1, source_target_pairs={{0,6},{1,7},{2,0},{3,1},{4,2},{5,3},{6,4},{7,5},{8,14},{9,15},{10,... | collective-permute-start | bytes 1179656 | tf_op jit(solution)/shard_map/ppermute | solution.py:58
  115.5 14.6 %collective-permute-start.11 = (bf16[3,128,512]{2,1,0:T(8,128)(2,1)S(1)}, bf16[3,128,512]{2,1,0:T(8,128)(2,1)S(1)}, u32[]{:S(2)}, u32[]{:S(2)}) collective-permute-start(bf16[3,128,512]{2,1,0:T(8,128)(2,1)S(1)} %pad_maximum_fusion.3), channel_id=1, source_target_pairs={{0,4},{1,5},{2,6},{3,7},{4,0},{5,1},{6,2},{7,3},{8,12},{9,13},{10,... | collective-permute-start | bytes 1179656 | tf_op jit(solution)/shard_map/ppermute | solution.py:58
  130.5 6.2 %collective-permute-start.12 = (f32[128,512]{1,0:T(8,128)S(1)}, f32[128,512]{1,0:T(8,128)S(1)}, u32[]{:S(2)}, u32[]{:S(2)}) collective-permute-start(f32[128,512]{1,0:T(8,128)S(1)} %fusion.14), channel_id=1, source_target_pairs={{0,1},{1,0},{2,3},{3,2},{4,5},{5,4},{6,7},{7,6},{8,9},{9,8},{10,11... | collective-permute-start | bytes 786440 | tf_op jit(solution)/shard_map/ppermute | solution.py:59
  137.0 8.3 %collective-permute-start.13 = (bf16[128,512]{1,0:T(8,128)(2,1)S(1)}, bf16[128,512]{1,0:T(8,128)(2,1)S(1)}, u32[]{:S(2)}, u32[]{:S(2)}) collective-permute-start(bf16[128,512]{1,0:T(8,128)(2,1)S(1)} %fusion.47), channel_id=1, source_target_pairs={{0,32},{8,40},{16,48},{24,56},{32,64},{40,72},{48,80},{56,88},{64,... | collective-permute-start | bytes 393224 | tf_op jit(solution)/shard_map/ppermute | solution.py:10
  142.8 13.8 %collective-permute-start.14 = (bf16[128,512]{1,0:T(8,128)(2,1)S(1)}, bf16[128,512]{1,0:T(8,128)(2,1)S(1)}, u32[]{:S(2)}, u32[]{:S(2)}) collective-permute-start(bf16[128,512]{1,0:T(8,128)(2,1)S(1)} %fusion.47), channel_id=1, source_target_pairs={{32,0},{40,8},{48,16},{56,24},{64,32},{72,40},{80,48},{88,56},{96,... | collective-permute-start | bytes 393224 | tf_op jit(solution)/shard_map/ppermute | solution.py:10
  156.6 13.0 %collective-permute-start.15 = (bf16[3,128,512]{2,1,0:T(8,128)(2,1)S(1)}, bf16[3,128,512]{2,1,0:T(8,128)(2,1)S(1)}, u32[]{:S(2)}, u32[]{:S(2)}) collective-permute-start(bf16[3,128,512]{2,1,0:T(8,128)(2,1)S(1)} %pad_maximum_fusion.4), channel_id=1, source_target_pairs={{0,2},{1,3},{2,4},{3,5},{4,6},{5,7},{6,0},{7,1},{8,10},{9,11},{10,... | collective-permute-start | bytes 1179656 | tf_op jit(solution)/shard_map/ppermute | solution.py:58
  161.3 10.4 %collective-permute-start.16 = (bf16[3,128,512]{2,1,0:T(8,128)(2,1)S(1)}, bf16[3,128,512]{2,1,0:T(8,128)(2,1)S(1)}, u32[]{:S(2)}, u32[]{:S(2)}) collective-permute-start(bf16[3,128,512]{2,1,0:T(8,128)(2,1)S(1)} %pad_maximum_fusion.4), channel_id=1, source_target_pairs={{0,6},{1,7},{2,0},{3,1},{4,2},{5,3},{6,4},{7,5},{8,14},{9,15},{10,... | collective-permute-start | bytes 1179656 | tf_op jit(solution)/shard_map/ppermute | solution.py:58
  164.0 15.0 %collective-permute-start.17 = (bf16[3,128,512]{2,1,0:T(8,128)(2,1)S(1)}, bf16[3,128,512]{2,1,0:T(8,128)(2,1)S(1)}, u32[]{:S(2)}, u32[]{:S(2)}) collective-permute-start(bf16[3,128,512]{2,1,0:T(8,128)(2,1)S(1)} %pad_maximum_fusion.4), channel_id=1, source_target_pairs={{0,4},{1,5},{2,6},{3,7},{4,0},{5,1},{6,2},{7,3},{8,12},{9,13},{10,... | collective-permute-start | bytes 1179656 | tf_op jit(solution)/shard_map/ppermute | solution.py:58
  179.4 5.8 %collective-permute-start.18 = (f32[128,512]{1,0:T(8,128)S(1)}, f32[128,512]{1,0:T(8,128)S(1)}, u32[]{:S(2)}, u32[]{:S(2)}) collective-permute-start(f32[128,512]{1,0:T(8,128)S(1)} %fusion.21), channel_id=1, source_target_pairs={{0,1},{1,0},{2,3},{3,2},{4,5},{5,4},{6,7},{7,6},{8,9},{9,8},{10,11... | collective-permute-start | bytes 786440 | tf_op jit(solution)/shard_map/ppermute | solution.py:59
  188.7 6.3 %collective-permute-start.20 = (bf16[128,512]{1,0:T(8,128)(2,1)S(1)}, bf16[128,512]{1,0:T(8,128)(2,1)S(1)}, u32[]{:S(2)}, u32[]{:S(2)}) collective-permute-start(bf16[128,512]{1,0:T(8,128)(2,1)S(1)} %fusion.46), channel_id=1, source_target_pairs={{64,0},{72,8},{80,16},{88,24},{96,32},{104,40},{112,48},{120,56},{... | collective-permute-start | bytes 393224 | tf_op jit(solution)/shard_map/ppermute | solution.py:10
  195.0 13.6 %collective-permute-start.21 = (bf16[3,128,512]{2,1,0:T(8,128)(2,1)S(1)}, bf16[3,128,512]{2,1,0:T(8,128)(2,1)S(1)}, u32[]{:S(2)}, u32[]{:S(2)}) collective-permute-start(bf16[3,128,512]{2,1,0:T(8,128)(2,1)S(1)} %pad_maximum_fusion.5), channel_id=1, source_target_pairs={{0,2},{1,3},{2,4},{3,5},{4,6},{5,7},{6,0},{7,1},{8,10},{9,11},{10,... | collective-permute-start | bytes 1179656 | tf_op jit(solution)/shard_map/ppermute | solution.py:58
  199.7 10.7 %collective-permute-start.22 = (bf16[3,128,512]{2,1,0:T(8,128)(2,1)S(1)}, bf16[3,128,512]{2,1,0:T(8,128)(2,1)S(1)}, u32[]{:S(2)}, u32[]{:S(2)}) collective-permute-start(bf16[3,128,512]{2,1,0:T(8,128)(2,1)S(1)} %pad_maximum_fusion.5), channel_id=1, source_target_pairs={{0,6},{1,7},{2,0},{3,1},{4,2},{5,3},{6,4},{7,5},{8,14},{9,15},{10,... | collective-permute-start | bytes 1179656 | tf_op jit(solution)/shard_map/ppermute | solution.py:58
  202.9 15.1 %collective-permute-start.23 = (bf16[3,128,512]{2,1,0:T(8,128)(2,1)S(1)}, bf16[3,128,512]{2,1,0:T(8,128)(2,1)S(1)}, u32[]{:S(2)}, u32[]{:S(2)}) collective-permute-start(bf16[3,128,512]{2,1,0:T(8,128)(2,1)S(1)} %pad_maximum_fusion.5), channel_id=1, source_target_pairs={{0,4},{1,5},{2,6},{3,7},{4,0},{5,1},{6,2},{7,3},{8,12},{9,13},{10,... | collective-permute-start | bytes 1179656 | tf_op jit(solution)/shard_map/ppermute | solution.py:58
  224.2 13.0 %collective-permute-start.25 = (bf16[128,512]{1,0:T(8,128)(2,1)S(1)}, bf16[128,512]{1,0:T(8,128)(2,1)S(1)}, u32[]{:S(2)}, u32[]{:S(2)}) collective-permute-start(bf16[128,512]{1,0:T(8,128)(2,1)S(1)} %fusion.45), channel_id=1, source_target_pairs={{0,128},{8,136},{16,144},{24,152},{32,160},{40,168},{48,176},{56,1... | collective-permute-start | bytes 393224 | tf_op jit(solution)/shard_map/ppermute | solution.py:10
  234.7 7.2 %collective-permute-start.26 = (bf16[128,512]{1,0:T(8,128)(2,1)S(1)}, bf16[128,512]{1,0:T(8,128)(2,1)S(1)}, u32[]{:S(2)}, u32[]{:S(2)}) collective-permute-start(bf16[128,512]{1,0:T(8,128)(2,1)S(1)} %fusion.45), channel_id=1, source_target_pairs={{128,0},{136,8},{144,16},{152,24},{160,32},{168,40},{176,48},{184,... | collective-permute-start | bytes 393224 | tf_op jit(solution)/shard_map/ppermute | solution.py:10
  241.9 13.0 %collective-permute-start.27 = (bf16[3,128,512]{2,1,0:T(8,128)(2,1)S(1)}, bf16[3,128,512]{2,1,0:T(8,128)(2,1)S(1)}, u32[]{:S(2)}, u32[]{:S(2)}) collective-permute-start(bf16[3,128,512]{2,1,0:T(8,128)(2,1)S(1)} %pad_maximum_fusion.6), channel_id=1, source_target_pairs={{0,2},{1,3},{2,4},{3,5},{4,6},{5,7},{6,0},{7,1},{8,10},{9,11},{10,... | collective-permute-start | bytes 1179656 | tf_op jit(solution)/shard_map/ppermute | solution.py:58
  246.6 10.4 %collective-permute-start.28 = (bf16[3,128,512]{2,1,0:T(8,128)(2,1)S(1)}, bf16[3,128,512]{2,1,0:T(8,128)(2,1)S(1)}, u32[]{:S(2)}, u32[]{:S(2)}) collective-permute-start(bf16[3,128,512]{2,1,0:T(8,128)(2,1)S(1)} %pad_maximum_fusion.6), channel_id=1, source_target_pairs={{0,6},{1,7},{2,0},{3,1},{4,2},{5,3},{6,4},{7,5},{8,14},{9,15},{10,... | collective-permute-start | bytes 1179656 | tf_op jit(solution)/shard_map/ppermute | solution.py:58
  249.3 15.0 %collective-permute-start.29 = (bf16[3,128,512]{2,1,0:T(8,128)(2,1)S(1)}, bf16[3,128,512]{2,1,0:T(8,128)(2,1)S(1)}, u32[]{:S(2)}, u32[]{:S(2)}) collective-permute-start(bf16[3,128,512]{2,1,0:T(8,128)(2,1)S(1)} %pad_maximum_fusion.6), channel_id=1, source_target_pairs={{0,4},{1,5},{2,6},{3,7},{4,0},{5,1},{6,2},{7,3},{8,12},{9,13},{10,... | collective-permute-start | bytes 1179656 | tf_op jit(solution)/shard_map/ppermute | solution.py:58
  270.8 8.2 %collective-permute-start.31 = (bf16[128,512]{1,0:T(8,128)(2,1)S(1)}, bf16[128,512]{1,0:T(8,128)(2,1)S(1)}, u32[]{:S(2)}, u32[]{:S(2)}) collective-permute-start(bf16[128,512]{1,0:T(8,128)(2,1)S(1)} %fusion.44), channel_id=1, source_target_pairs={{0,256},{8,264},{16,272},{24,280},{32,288},{40,296},{48,304},{56,3... | collective-permute-start | bytes 393224 | tf_op jit(solution)/shard_map/ppermute | solution.py:10
  276.5 10.2 %collective-permute-start.32 = (bf16[128,512]{1,0:T(8,128)(2,1)S(1)}, bf16[128,512]{1,0:T(8,128)(2,1)S(1)}, u32[]{:S(2)}, u32[]{:S(2)}) collective-permute-start(bf16[128,512]{1,0:T(8,128)(2,1)S(1)} %fusion.44), channel_id=1, source_target_pairs={{256,0},{264,8},{272,16},{280,24},{288,32},{296,40},{304,48},{312,... | collective-permute-start | bytes 393224 | tf_op jit(solution)/shard_map/ppermute | solution.py:10
  286.7 13.7 %collective-permute-start.33 = (bf16[3,128,512]{2,1,0:T(8,128)(2,1)S(1)}, bf16[3,128,512]{2,1,0:T(8,128)(2,1)S(1)}, u32[]{:S(2)}, u32[]{:S(2)}) collective-permute-start(bf16[3,128,512]{2,1,0:T(8,128)(2,1)S(1)} %pad_maximum_fusion.7), channel_id=1, source_target_pairs={{0,2},{1,3},{2,4},{3,5},{4,6},{5,7},{6,0},{7,1},{8,10},{9,11},{10,... | collective-permute-start | bytes 1179656 | tf_op jit(solution)/shard_map/ppermute | solution.py:58
  291.4 10.7 %collective-permute-start.34 = (bf16[3,128,512]{2,1,0:T(8,128)(2,1)S(1)}, bf16[3,128,512]{2,1,0:T(8,128)(2,1)S(1)}, u32[]{:S(2)}, u32[]{:S(2)}) collective-permute-start(bf16[3,128,512]{2,1,0:T(8,128)(2,1)S(1)} %pad_maximum_fusion.7), channel_id=1, source_target_pairs={{0,6},{1,7},{2,0},{3,1},{4,2},{5,3},{6,4},{7,5},{8,14},{9,15},{10,... | collective-permute-start | bytes 1179656 | tf_op jit(solution)/shard_map/ppermute | solution.py:58
  294.5 15.3 %collective-permute-start.35 = (bf16[3,128,512]{2,1,0:T(8,128)(2,1)S(1)}, bf16[3,128,512]{2,1,0:T(8,128)(2,1)S(1)}, u32[]{:S(2)}, u32[]{:S(2)}) collective-permute-start(bf16[3,128,512]{2,1,0:T(8,128)(2,1)S(1)} %pad_maximum_fusion.7), channel_id=1, source_target_pairs={{0,4},{1,5},{2,6},{3,7},{4,0},{5,1},{6,2},{7,3},{8,12},{9,13},{10,... | collective-permute-start | bytes 1179656 | tf_op jit(solution)/shard_map/ppermute | solution.py:58
  (18 other events, 106.1 us)

commit v8 on v5

--- a/solution.py
+++ b/solution.py
@@ -22,19 +22,16 @@
     chip = cross // 2
     core = cross % 2
 
-    def columns_for(which_core):
-        return jnp.stack([2 * ((chip + off) % chips) + which_core for off in OFFSETS])
+    signed = jnp.stack([self_factor[:, 0], -lower_factor[:, 0], -upper_factor[:, 0]], axis=2)
+    signed = signed.reshape(levels, rows, 3, chips, 2, rows)
 
-    blocks = [f[:, 0].reshape(levels, rows, ncross, rows) for f in (self_factor, lower_factor, upper_factor)]
+    def core_columns(which_core):
+        return lax.dynamic_index_in_dim(signed, which_core, axis=4, keepdims=False)
 
-    def pick(which_core):
-        idx = columns_for(which_core)
-        parts = [jnp.take(blocks[0], idx, axis=2)] + [-jnp.take(f, idx, axis=2) for f in blocks[1:]]
-        return jnp.stack(parts, axis=3)
-
-    mine = pick(core)
     swap = [(2 * c + b, 2 * c + 1 - b) for c in range(chips) for b in range(2)]
-    theirs = lax.ppermute(pick(1 - core), "cross", swap)
+    mine = core_columns(core)
+    theirs = lax.ppermute(core_columns(1 - core), "cross", swap)
+    slot_chips = [(chip + off) % chips for off in OFFSETS]
 
     def same_core(offset):
         return [(2 * c + b, 2 * ((c + offset) % chips) + b) for c in range(chips) for b in range(2)]
@@ -42,7 +39,8 @@
     def partial(mat, pieces):
         total = None
         for j, piece in enumerate(pieces):
-            term = jnp.einsum("ibk,bkr->ir", mat[:, j], piece, preferred_element_type=jnp.float32)
+            block = lax.dynamic_index_in_dim(mat, slot_chips[j], axis=2, keepdims=False)
+            term = jnp.einsum("ibk,bkr->ir", block, piece, preferred_element_type=jnp.float32)
             total = term if total is None else total + term
         return total
 

time: 293 us -> 314 us (1.072); the launches traced: 292 us -> 309 us
  matrix products: 11.7 us -> 34.2 us
  local copies, waits for them, and re-layouts: 25 us -> 16.7 us
  starting transfers between devices: 138 us -> 133 us
  waiting for transfers between devices: 111 us -> 116 us
    ppermute x12, waiting for transfers between devices: 22.7 us -> 45.7 us  [shifted(): lax.ppermute(value, axis, [(source, source + steps) for source in range(i...]
    dot_general x48, matrix products: 11.7 us -> 34.2 us  [partial(): jnp.einsum('ibk,bkr->ir', block, piece, preferred_element_type=jnp.float32)]
    ppermute x12, starting transfers between devices: 58.8 us -> 39.1 us  [shifted(): lax.ppermute(value, axis, [(source, source + steps) for source in range(i...]
    ppermute x18, waiting for transfers between devices: 85.5 us -> 70.1 us  [body(): lax.ppermute(own, 'cross', same_core(-off))]
    ppermute x18, starting transfers between devices: 47.7 us -> 61.7 us  [body(): lax.ppermute(own, 'cross', same_core(-off))]
    gather x6 -> x0, local copies, waits for them, and re-layouts: 10.4 us -> none  [the longest x4 7.36 us: pick(): jnp.take(f, idx, axis=2)]
    another operation x6 -> x0, other arithmetic: 5.39 us -> none  [pick(): return jnp.stack(parts, axis=3)]
    neg x0 -> x2, other arithmetic: none -> 4.8 us  [the longest x1 2.99 us: body(): -upper_factor[:, 0]]
  transfers between devices with their start and end apart: 37 -> 37, of which waited for: 30 -> 29; matrix products, arithmetic and copies ran while one was open for 5% -> 8% of each run, Pallas kernels for 0% -> 0%
where the time goes in v8:
time: 314 us; the launch traced here: 309 us
  starting transfers between devices  133 us (42%)
  waiting for transfers between devices  116 us (37%)
  matrix products  34.2 us (11%)
  local copies, waits for them, and re-layouts  16.7 us (5%)
  other arithmetic  8.11 us (3%)
    ppermute x18, waiting for transfers between devices, body(): lax.ppermute(own, 'cross', same_core(-off))  70.1 us
    ppermute x18, starting transfers between devices, body(): lax.ppermute(own, 'cross', same_core(-off))  61.7 us
    ppermute x12, waiting for transfers between devices, shifted(): lax.ppermute(value, axis, [(source, source + steps) for source in range(i...  45.7 us
    ppermute x12, starting transfers between devices, shifted(): lax.ppermute(value, axis, [(source, source + steps) for source in range(i...  39.1 us
    dot_general x48, matrix products, partial(): jnp.einsum('ibk,bkr->ir', block, piece, preferred_element_type=jnp.float32)  34.2 us
    ppermute x6, starting transfers between devices, body(): given = lax.ppermute(partial(theirs[level], pieces), 'cross', swap)  23.7 us
    ppermute x1, starting transfers between devices, body(): theirs = lax.ppermute(core_columns(1 - core), 'cross', swap)  8.77 us
  transfers between devices with their start and end apart: 37, of which 29 were waited for; matrix products, arithmetic and copies ran while one was open for 8% of the time, Pallas kernels for 0%

profile of v8, /device:TPU:1, one launch (start us, length us, event | category | flops | bytes accessed | tf_op | source)
XLA Modules:
  0.0 308.9 jit_solution(12826367507874798876)
XLA Ops:
  16.3 3.4 %dynamic-slice_bitcast_fusion = bf16[6,128,3,4,128]{4,1,2,3,0:T(8,128)(2,1)} fusion(bf16[6,128,3,4,2,128]{5,1,2,4,3,0:T(8,128)(2,1)} %copy_dynamic-update-slice_fusion, s32[]{:T(128)S(6)} %select_n.102), kind=kLoop, calls=%fused_computation | loop fusion | bytes 4718596 | tf_op jit(solution)/shard_map/jit(dynamic_index_in_dim)/squeeze | solution.py:29
  19.7 8.8 %collective-permute-start.5 = (bf16[6,128,3,4,128]{4,1,2,3,0:T(8,128)(2,1)}, bf16[6,128,3,4,128]{4,1,2,3,0:T(8,128)(2,1)S(1)}, u32[]{:S(2)}, u32[]{:S(2)}) collective-permute-start(bf16[6,128,3,4,128]{4,1,2,3,0:T(8,128)(2,1)} %dynamic-slice_bitcast_fusion), channel_id=1, source_target_pairs={{0,1},{1,0},{2,3},{3,2},{4,5},{5,4},{6,7},{7,6},{8,9},{9,8},{10,11... | collective-permute-start | bytes 7077896 | tf_op jit(solution)/shard_map/ppermute | solution.py:33
  32.9 3.9 %collective-permute-done.1 = bf16[128,512]{1,0:T(8,128)(2,1)S(1)} collective-permute-done((bf16[128,512]{1,0:T(8,128)(2,1)S(1)}, bf16[128,512]{1,0:T(8,128)(2,1)S(1)}, u32[]{:S(2)}, u32[]{:S(2)}) %collective-permute-start.1) | collective-permute-done | bytes 131104 | tf_op jit(solution)/shard_map/ppermute | solution.py:10
  43.3 4.3 %collective-permute-start.3 = (bf16[3,128,512]{2,1,0:T(8,128)(2,1)}, bf16[3,128,512]{2,1,0:T(8,128)(2,1)S(1)}, u32[]{:S(2)}, u32[]{:S(2)}) collective-permute-start(bf16[3,128,512]{2,1,0:T(8,128)(2,1)} %pad_maximum_fusion), channel_id=1, source_target_pairs={{0,6},{1,7},{2,0},{3,1},{4,2},{5,3},{6,4},{7,5},{8,14},{9,15},{10,... | collective-permute-start | bytes 1179656 | tf_op jit(solution)/shard_map/ppermute | solution.py:53
  47.6 4.1 %collective-permute-done.4 = bf16[3,128,512]{2,1,0:T(8,128)(2,1)S(1)} collective-permute-done((bf16[3,128,512]{2,1,0:T(8,128)(2,1)}, bf16[3,128,512]{2,1,0:T(8,128)(2,1)S(1)}, u32[]{:S(2)}, u32[]{:S(2)}) %collective-permute-start.4) | collective-permute-done | bytes 393248 | tf_op jit(solution)/shard_map/ppermute | solution.py:53
  54.3 7.0 %collective-permute-done.2 = bf16[3,128,512]{2,1,0:T(8,128)(2,1)S(1)} collective-permute-done((bf16[3,128,512]{2,1,0:T(8,128)(2,1)}, bf16[3,128,512]{2,1,0:T(8,128)(2,1)S(1)}, u32[]{:S(2)}, u32[]{:S(2)}) %collective-permute-start.2) | collective-permute-done | bytes 393248 | tf_op jit(solution)/shard_map/ppermute | solution.py:53
  68.8 5.1 %collective-permute-start.7 = (bf16[128,512]{1,0:T(8,128)(2,1)S(1)}, bf16[128,512]{1,0:T(8,128)(2,1)S(1)}, u32[]{:S(2)}, u32[]{:S(2)}) collective-permute-start(bf16[128,512]{1,0:T(8,128)(2,1)S(1)} %fusion.47), channel_id=1, source_target_pairs={{0,16},{8,24},{16,32},{24,40},{32,48},{40,56},{48,64},{56,72},{64,... | collective-permute-start | bytes 393224 | tf_op jit(solution)/shard_map/ppermute | solution.py:10
  76.8 4.7 %collective-permute-done.8 = bf16[128,512]{1,0:T(8,128)(2,1)S(1)} collective-permute-done((bf16[128,512]{1,0:T(8,128)(2,1)S(1)}, bf16[128,512]{1,0:T(8,128)(2,1)S(1)}, u32[]{:S(2)}, u32[]{:S(2)}) %collective-permute-start.8) | collective-permute-done | bytes 131104 | tf_op jit(solution)/shard_map/ppermute | solution.py:10
  88.9 3.5 %collective-permute-start.11 = (bf16[3,128,512]{2,1,0:T(8,128)(2,1)}, bf16[3,128,512]{2,1,0:T(8,128)(2,1)S(1)}, u32[]{:S(2)}, u32[]{:S(2)}) collective-permute-start(bf16[3,128,512]{2,1,0:T(8,128)(2,1)} %pad_maximum_fusion.1), channel_id=1, source_target_pairs={{0,4},{1,5},{2,6},{3,7},{4,0},{5,1},{6,2},{7,3},{8,12},{9,13},{10,... | collective-permute-start | bytes 1179656 | tf_op jit(solution)/shard_map/ppermute | solution.py:53
  95.5 8.2 %collective-permute-done.11 = bf16[3,128,512]{2,1,0:T(8,128)(2,1)S(1)} collective-permute-done((bf16[3,128,512]{2,1,0:T(8,128)(2,1)}, bf16[3,128,512]{2,1,0:T(8,128)(2,1)S(1)}, u32[]{:S(2)}, u32[]{:S(2)}) %collective-permute-start.11) | collective-permute-done | bytes 393248 | tf_op jit(solution)/shard_map/ppermute | solution.py:53
  104.1 4.6 %collective-permute-start.12 = (f32[128,512]{1,0:T(8,128)S(1)}, f32[128,512]{1,0:T(8,128)S(1)}, u32[]{:S(2)}, u32[]{:S(2)}) collective-permute-start(f32[128,512]{1,0:T(8,128)S(1)} %fusion.13), channel_id=1, source_target_pairs={{0,1},{1,0},{2,3},{3,2},{4,5},{5,4},{6,7},{7,6},{8,9},{9,8},{10,11... | collective-permute-start | bytes 786440 | tf_op jit(solution)/shard_map/ppermute | solution.py:54
  113.3 5.8 %collective-permute-start.13 = (bf16[128,512]{1,0:T(8,128)(2,1)S(1)}, bf16[128,512]{1,0:T(8,128)(2,1)S(1)}, u32[]{:S(2)}, u32[]{:S(2)}) collective-permute-start(bf16[128,512]{1,0:T(8,128)(2,1)S(1)} %fusion.46), channel_id=1, source_target_pairs={{0,32},{8,40},{16,48},{24,56},{32,64},{40,72},{48,80},{56,88},{64,... | collective-permute-start | bytes 393224 | tf_op jit(solution)/shard_map/ppermute | solution.py:10
  122.0 11.1 %collective-permute-done.14 = bf16[128,512]{1,0:T(8,128)(2,1)S(1)} collective-permute-done((bf16[128,512]{1,0:T(8,128)(2,1)S(1)}, bf16[128,512]{1,0:T(8,128)(2,1)S(1)}, u32[]{:S(2)}, u32[]{:S(2)}) %collective-permute-start.14) | collective-permute-done | bytes 131104 | tf_op jit(solution)/shard_map/ppermute | solution.py:10
  134.0 4.7 %collective-permute-start.15 = (bf16[3,128,512]{2,1,0:T(8,128)(2,1)}, bf16[3,128,512]{2,1,0:T(8,128)(2,1)S(1)}, u32[]{:S(2)}, u32[]{:S(2)}) collective-permute-start(bf16[3,128,512]{2,1,0:T(8,128)(2,1)} %pad_maximum_fusion.2), channel_id=1, source_target_pairs={{0,2},{1,3},{2,4},{3,5},{4,6},{5,7},{6,0},{7,1},{8,10},{9,11},{10,... | collective-permute-start | bytes 1179656 | tf_op jit(solution)/shard_map/ppermute | solution.py:53
  149.6 7.6 %collective-permute-done.17 = bf16[3,128,512]{2,1,0:T(8,128)(2,1)S(1)} collective-permute-done((bf16[3,128,512]{2,1,0:T(8,128)(2,1)}, bf16[3,128,512]{2,1,0:T(8,128)(2,1)S(1)}, u32[]{:S(2)}, u32[]{:S(2)}) %collective-permute-start.17) | collective-permute-done | bytes 393248 | tf_op jit(solution)/shard_map/ppermute | solution.py:53
  157.7 4.5 %collective-permute-start.18 = (f32[128,512]{1,0:T(8,128)S(1)}, f32[128,512]{1,0:T(8,128)S(1)}, u32[]{:S(2)}, u32[]{:S(2)}) collective-permute-start(f32[128,512]{1,0:T(8,128)S(1)} %fusion.20), channel_id=1, source_target_pairs={{0,1},{1,0},{2,3},{3,2},{4,5},{5,4},{6,7},{7,6},{8,9},{9,8},{10,11... | collective-permute-start | bytes 786440 | tf_op jit(solution)/shard_map/ppermute | solution.py:54
  166.8 3.6 %collective-permute-start.19 = (bf16[128,512]{1,0:T(8,128)(2,1)S(1)}, bf16[128,512]{1,0:T(8,128)(2,1)S(1)}, u32[]{:S(2)}, u32[]{:S(2)}) collective-permute-start(bf16[128,512]{1,0:T(8,128)(2,1)S(1)} %fusion.45), channel_id=1, source_target_pairs={{0,64},{8,72},{16,80},{24,88},{32,96},{40,104},{48,112},{56,120},{... | collective-permute-start | bytes 393224 | tf_op jit(solution)/shard_map/ppermute | solution.py:10
  173.2 3.8 %collective-permute-done.20 = bf16[128,512]{1,0:T(8,128)(2,1)S(1)} collective-permute-done((bf16[128,512]{1,0:T(8,128)(2,1)S(1)}, bf16[128,512]{1,0:T(8,128)(2,1)S(1)}, u32[]{:S(2)}, u32[]{:S(2)}) %collective-permute-start.20) | collective-permute-done | bytes 131104 | tf_op jit(solution)/shard_map/ppermute | solution.py:10
  177.9 4.7 %collective-permute-start.21 = (bf16[3,128,512]{2,1,0:T(8,128)(2,1)}, bf16[3,128,512]{2,1,0:T(8,128)(2,1)S(1)}, u32[]{:S(2)}, u32[]{:S(2)}) collective-permute-start(bf16[3,128,512]{2,1,0:T(8,128)(2,1)} %pad_maximum_fusion.3), channel_id=1, source_target_pairs={{0,2},{1,3},{2,4},{3,5},{4,6},{5,7},{6,0},{7,1},{8,10},{9,11},{10,... | collective-permute-start | bytes 1179656 | tf_op jit(solution)/shard_map/ppermute | solution.py:53
  188.2 3.5 %collective-permute-done.21 = bf16[3,128,512]{2,1,0:T(8,128)(2,1)S(1)} collective-permute-done((bf16[3,128,512]{2,1,0:T(8,128)(2,1)}, bf16[3,128,512]{2,1,0:T(8,128)(2,1)S(1)}, u32[]{:S(2)}, u32[]{:S(2)}) %collective-permute-start.21) | collective-permute-done | bytes 393248 | tf_op jit(solution)/shard_map/ppermute | solution.py:53
  194.1 6.9 %collective-permute-done.23 = bf16[3,128,512]{2,1,0:T(8,128)(2,1)S(1)} collective-permute-done((bf16[3,128,512]{2,1,0:T(8,128)(2,1)}, bf16[3,128,512]{2,1,0:T(8,128)(2,1)S(1)}, u32[]{:S(2)}, u32[]{:S(2)}) %collective-permute-start.23) | collective-permute-done | bytes 393248 | tf_op jit(solution)/shard_map/ppermute | solution.py:53
  201.5 3.9 %collective-permute-start.24 = (f32[128,512]{1,0:T(8,128)S(1)}, f32[128,512]{1,0:T(8,128)S(1)}, u32[]{:S(2)}, u32[]{:S(2)}) collective-permute-start(f32[128,512]{1,0:T(8,128)S(1)} %fusion.27), channel_id=1, source_target_pairs={{0,1},{1,0},{2,3},{3,2},{4,5},{5,4},{6,7},{7,6},{8,9},{9,8},{10,11... | collective-permute-start | bytes 786440 | tf_op jit(solution)/shard_map/ppermute | solution.py:54
  210.0 10.2 %collective-permute-start.25 = (bf16[128,512]{1,0:T(8,128)(2,1)S(1)}, bf16[128,512]{1,0:T(8,128)(2,1)S(1)}, u32[]{:S(2)}, u32[]{:S(2)}) collective-permute-start(bf16[128,512]{1,0:T(8,128)(2,1)S(1)} %fusion.44), channel_id=1, source_target_pairs={{0,128},{8,136},{16,144},{24,152},{32,160},{40,168},{48,176},{56,1... | collective-permute-start | bytes 393224 | tf_op jit(solution)/shard_map/ppermute | solution.py:10
  223.2 4.7 %collective-permute-done.26 = bf16[128,512]{1,0:T(8,128)(2,1)S(1)} collective-permute-done((bf16[128,512]{1,0:T(8,128)(2,1)S(1)}, bf16[128,512]{1,0:T(8,128)(2,1)S(1)}, u32[]{:S(2)}, u32[]{:S(2)}) %collective-permute-start.26) | collective-permute-done | bytes 131104 | tf_op jit(solution)/shard_map/ppermute | solution.py:10
  227.9 4.7 %collective-permute-start.27 = (bf16[3,128,512]{2,1,0:T(8,128)(2,1)S(1)}, bf16[3,128,512]{2,1,0:T(8,128)(2,1)S(1)}, u32[]{:S(2)}, u32[]{:S(2)}) collective-permute-start(bf16[3,128,512]{2,1,0:T(8,128)(2,1)S(1)} %pad_maximum_fusion.4), channel_id=1, source_target_pairs={{0,2},{1,3},{2,4},{3,5},{4,6},{5,7},{6,0},{7,1},{8,10},{9,11},{10,... | collective-permute-start | bytes 1179656 | tf_op jit(solution)/shard_map/ppermute | solution.py:53
  243.7 7.2 %collective-permute-done.29 = bf16[3,128,512]{2,1,0:T(8,128)(2,1)S(1)} collective-permute-done((bf16[3,128,512]{2,1,0:T(8,128)(2,1)S(1)}, bf16[3,128,512]{2,1,0:T(8,128)(2,1)S(1)}, u32[]{:S(2)}, u32[]{:S(2)}) %collective-permute-start.29) | collective-permute-done | bytes 393248 | tf_op jit(solution)/shard_map/ppermute | solution.py:53
  251.3 4.2 %collective-permute-start.30 = (f32[128,512]{1,0:T(8,128)S(1)}, f32[128,512]{1,0:T(8,128)S(1)}, u32[]{:S(2)}, u32[]{:S(2)}) collective-permute-start(f32[128,512]{1,0:T(8,128)S(1)} %fusion.34), channel_id=1, source_target_pairs={{0,1},{1,0},{2,3},{3,2},{4,5},{5,4},{6,7},{7,6},{8,9},{9,8},{10,11... | collective-permute-start | bytes 786440 | tf_op jit(solution)/shard_map/ppermute | solution.py:54
  260.1 5.3 %collective-permute-start.31 = (bf16[128,512]{1,0:T(8,128)(2,1)S(1)}, bf16[128,512]{1,0:T(8,128)(2,1)S(1)}, u32[]{:S(2)}, u32[]{:S(2)}) collective-permute-start(bf16[128,512]{1,0:T(8,128)(2,1)S(1)} %fusion.43), channel_id=1, source_target_pairs={{0,256},{8,264},{16,272},{24,280},{32,288},{40,296},{48,304},{56,3... | collective-permute-start | bytes 393224 | tf_op jit(solution)/shard_map/ppermute | solution.py:10
  268.4 7.7 %collective-permute-done.32 = bf16[128,512]{1,0:T(8,128)(2,1)S(1)} collective-permute-done((bf16[128,512]{1,0:T(8,128)(2,1)S(1)}, bf16[128,512]{1,0:T(8,128)(2,1)S(1)}, u32[]{:S(2)}, u32[]{:S(2)}) %collective-permute-start.32) | collective-permute-done | bytes 131104 | tf_op jit(solution)/shard_map/ppermute | solution.py:10
  276.1 4.7 %collective-permute-start.33 = (bf16[3,128,512]{2,1,0:T(8,128)(2,1)S(1)}, bf16[3,128,512]{2,1,0:T(8,128)(2,1)S(1)}, u32[]{:S(2)}, u32[]{:S(2)}) collective-permute-start(bf16[3,128,512]{2,1,0:T(8,128)(2,1)S(1)} %pad_maximum_fusion.5), channel_id=1, source_target_pairs={{0,2},{1,3},{2,4},{3,5},{4,6},{5,7},{6,0},{7,1},{8,10},{9,11},{10,... | collective-permute-start | bytes 1179656 | tf_op jit(solution)/shard_map/ppermute | solution.py:53
  292.1 7.2 %collective-permute-done.35 = bf16[3,128,512]{2,1,0:T(8,128)(2,1)S(1)} collective-permute-done((bf16[3,128,512]{2,1,0:T(8,128)(2,1)S(1)}, bf16[3,128,512]{2,1,0:T(8,128)(2,1)S(1)}, u32[]{:S(2)}, u32[]{:S(2)}) %collective-permute-start.35) | collective-permute-done | bytes 393248 | tf_op jit(solution)/shard_map/ppermute | solution.py:53
  299.8 3.9 %collective-permute-start.36 = (f32[128,512]{1,0:T(8,128)S(1)}, f32[128,512]{1,0:T(8,128)S(1)}, u32[]{:S(2)}, u32[]{:S(2)}) collective-permute-start(f32[128,512]{1,0:T(8,128)S(1)} %fusion.41), channel_id=1, source_target_pairs={{0,1},{1,0},{2,3},{3,2},{4,5},{5,4},{6,7},{7,6},{8,9},{9,8},{10,11... | collective-permute-start | bytes 786440 | tf_op jit(solution)/shard_map/ppermute | solution.py:54
  (126 shorter events, 130.5 us)
Async XLA Ops:
  19.7 33.3 %collective-permute-start.5 = (bf16[6,128,3,4,128]{4,1,2,3,0:T(8,128)(2,1)}, bf16[6,128,3,4,128]{4,1,2,3,0:T(8,128)(2,1)S(1)}, u32[]{:S(2)}, u32[]{:S(2)}) collective-permute-start(bf16[6,128,3,4,128]{4,1,2,3,0:T(8,128)(2,1)} %dynamic-slice_bitcast_fusion), channel_id=1, source_target_pairs={{0,1},{1,0},{2,3},{3,2},{4,5},{5,4},{6,7},{7,6},{8,9},{9,8},{10,11... | collective-permute-start | bytes 7077896 | tf_op jit(solution)/shard_map/ppermute | solution.py:33
  38.2 13.5 %collective-permute-start.4 = (bf16[3,128,512]{2,1,0:T(8,128)(2,1)}, bf16[3,128,512]{2,1,0:T(8,128)(2,1)S(1)}, u32[]{:S(2)}, u32[]{:S(2)}) collective-permute-start(bf16[3,128,512]{2,1,0:T(8,128)(2,1)} %pad_maximum_fusion), channel_id=1, source_target_pairs={{0,4},{1,5},{2,6},{3,7},{4,0},{5,1},{6,2},{7,3},{8,12},{9,13},{10,... | collective-permute-start | bytes 1179656 | tf_op jit(solution)/shard_map/ppermute | solution.py:53
  41.0 20.3 %collective-permute-start.2 = (bf16[3,128,512]{2,1,0:T(8,128)(2,1)}, bf16[3,128,512]{2,1,0:T(8,128)(2,1)S(1)}, u32[]{:S(2)}, u32[]{:S(2)}) collective-permute-start(bf16[3,128,512]{2,1,0:T(8,128)(2,1)} %pad_maximum_fusion), channel_id=1, source_target_pairs={{0,2},{1,3},{2,4},{3,5},{4,6},{5,7},{6,0},{7,1},{8,10},{9,11},{10,... | collective-permute-start | bytes 1179656 | tf_op jit(solution)/shard_map/ppermute | solution.py:53
  43.3 18.2 %collective-permute-start.3 = (bf16[3,128,512]{2,1,0:T(8,128)(2,1)}, bf16[3,128,512]{2,1,0:T(8,128)(2,1)S(1)}, u32[]{:S(2)}, u32[]{:S(2)}) collective-permute-start(bf16[3,128,512]{2,1,0:T(8,128)(2,1)} %pad_maximum_fusion), channel_id=1, source_target_pairs={{0,6},{1,7},{2,0},{3,1},{4,2},{5,3},{6,4},{7,5},{8,14},{9,15},{10,... | collective-permute-start | bytes 1179656 | tf_op jit(solution)/shard_map/ppermute | solution.py:53
  68.8 8.0 %collective-permute-start.7 = (bf16[128,512]{1,0:T(8,128)(2,1)S(1)}, bf16[128,512]{1,0:T(8,128)(2,1)S(1)}, u32[]{:S(2)}, u32[]{:S(2)}) collective-permute-start(bf16[128,512]{1,0:T(8,128)(2,1)S(1)} %fusion.47), channel_id=1, source_target_pairs={{0,16},{8,24},{16,32},{24,40},{32,48},{40,56},{48,64},{56,72},{64,... | collective-permute-start | bytes 393224 | tf_op jit(solution)/shard_map/ppermute | solution.py:10
  74.0 7.6 %collective-permute-start.8 = (bf16[128,512]{1,0:T(8,128)(2,1)S(1)}, bf16[128,512]{1,0:T(8,128)(2,1)S(1)}, u32[]{:S(2)}, u32[]{:S(2)}) collective-permute-start(bf16[128,512]{1,0:T(8,128)(2,1)S(1)} %fusion.47), channel_id=1, source_target_pairs={{16,0},{24,8},{32,16},{40,24},{48,32},{56,40},{64,48},{72,56},{80,... | collective-permute-start | bytes 393224 | tf_op jit(solution)/shard_map/ppermute | solution.py:10
  82.4 11.1 %collective-permute-start.9 = (bf16[3,128,512]{2,1,0:T(8,128)(2,1)}, bf16[3,128,512]{2,1,0:T(8,128)(2,1)S(1)}, u32[]{:S(2)}, u32[]{:S(2)}) collective-permute-start(bf16[3,128,512]{2,1,0:T(8,128)(2,1)} %pad_maximum_fusion.1), channel_id=1, source_target_pairs={{0,2},{1,3},{2,4},{3,5},{4,6},{5,7},{6,0},{7,1},{8,10},{9,11},{10,... | collective-permute-start | bytes 1179656 | tf_op jit(solution)/shard_map/ppermute | solution.py:53
  85.6 9.7 %collective-permute-start.10 = (bf16[3,128,512]{2,1,0:T(8,128)(2,1)}, bf16[3,128,512]{2,1,0:T(8,128)(2,1)S(1)}, u32[]{:S(2)}, u32[]{:S(2)}) collective-permute-start(bf16[3,128,512]{2,1,0:T(8,128)(2,1)} %pad_maximum_fusion.1), channel_id=1, source_target_pairs={{0,6},{1,7},{2,0},{3,1},{4,2},{5,3},{6,4},{7,5},{8,14},{9,15},{10,... | collective-permute-start | bytes 1179656 | tf_op jit(solution)/shard_map/ppermute | solution.py:53
  88.9 14.8 %collective-permute-start.11 = (bf16[3,128,512]{2,1,0:T(8,128)(2,1)}, bf16[3,128,512]{2,1,0:T(8,128)(2,1)S(1)}, u32[]{:S(2)}, u32[]{:S(2)}) collective-permute-start(bf16[3,128,512]{2,1,0:T(8,128)(2,1)} %pad_maximum_fusion.1), channel_id=1, source_target_pairs={{0,4},{1,5},{2,6},{3,7},{4,0},{5,1},{6,2},{7,3},{8,12},{9,13},{10,... | collective-permute-start | bytes 1179656 | tf_op jit(solution)/shard_map/ppermute | solution.py:53
  104.1 8.0 %collective-permute-start.12 = (f32[128,512]{1,0:T(8,128)S(1)}, f32[128,512]{1,0:T(8,128)S(1)}, u32[]{:S(2)}, u32[]{:S(2)}) collective-permute-start(f32[128,512]{1,0:T(8,128)S(1)} %fusion.13), channel_id=1, source_target_pairs={{0,1},{1,0},{2,3},{3,2},{4,5},{5,4},{6,7},{7,6},{8,9},{9,8},{10,11... | collective-permute-start | bytes 786440 | tf_op jit(solution)/shard_map/ppermute | solution.py:54
  113.3 8.7 %collective-permute-start.13 = (bf16[128,512]{1,0:T(8,128)(2,1)S(1)}, bf16[128,512]{1,0:T(8,128)(2,1)S(1)}, u32[]{:S(2)}, u32[]{:S(2)}) collective-permute-start(bf16[128,512]{1,0:T(8,128)(2,1)S(1)} %fusion.46), channel_id=1, source_target_pairs={{0,32},{8,40},{16,48},{24,56},{32,64},{40,72},{48,80},{56,88},{64,... | collective-permute-start | bytes 393224 | tf_op jit(solution)/shard_map/ppermute | solution.py:10
  119.1 14.0 %collective-permute-start.14 = (bf16[128,512]{1,0:T(8,128)(2,1)S(1)}, bf16[128,512]{1,0:T(8,128)(2,1)S(1)}, u32[]{:S(2)}, u32[]{:S(2)}) collective-permute-start(bf16[128,512]{1,0:T(8,128)(2,1)S(1)} %fusion.46), channel_id=1, source_target_pairs={{32,0},{40,8},{48,16},{56,24},{64,32},{72,40},{80,48},{88,56},{96,... | collective-permute-start | bytes 393224 | tf_op jit(solution)/shard_map/ppermute | solution.py:10
  134.0 13.9 %collective-permute-start.15 = (bf16[3,128,512]{2,1,0:T(8,128)(2,1)}, bf16[3,128,512]{2,1,0:T(8,128)(2,1)S(1)}, u32[]{:S(2)}, u32[]{:S(2)}) collective-permute-start(bf16[3,128,512]{2,1,0:T(8,128)(2,1)} %pad_maximum_fusion.2), channel_id=1, source_target_pairs={{0,2},{1,3},{2,4},{3,5},{4,6},{5,7},{6,0},{7,1},{8,10},{9,11},{10,... | collective-permute-start | bytes 1179656 | tf_op jit(solution)/shard_map/ppermute | solution.py:53
  138.6 10.8 %collective-permute-start.16 = (bf16[3,128,512]{2,1,0:T(8,128)(2,1)}, bf16[3,128,512]{2,1,0:T(8,128)(2,1)S(1)}, u32[]{:S(2)}, u32[]{:S(2)}) collective-permute-start(bf16[3,128,512]{2,1,0:T(8,128)(2,1)} %pad_maximum_fusion.2), channel_id=1, source_target_pairs={{0,6},{1,7},{2,0},{3,1},{4,2},{5,3},{6,4},{7,5},{8,14},{9,15},{10,... | collective-permute-start | bytes 1179656 | tf_op jit(solution)/shard_map/ppermute | solution.py:53
  141.9 15.3 %collective-permute-start.17 = (bf16[3,128,512]{2,1,0:T(8,128)(2,1)}, bf16[3,128,512]{2,1,0:T(8,128)(2,1)S(1)}, u32[]{:S(2)}, u32[]{:S(2)}) collective-permute-start(bf16[3,128,512]{2,1,0:T(8,128)(2,1)} %pad_maximum_fusion.2), channel_id=1, source_target_pairs={{0,4},{1,5},{2,6},{3,7},{4,0},{5,1},{6,2},{7,3},{8,12},{9,13},{10,... | collective-permute-start | bytes 1179656 | tf_op jit(solution)/shard_map/ppermute | solution.py:53
  157.7 7.9 %collective-permute-start.18 = (f32[128,512]{1,0:T(8,128)S(1)}, f32[128,512]{1,0:T(8,128)S(1)}, u32[]{:S(2)}, u32[]{:S(2)}) collective-permute-start(f32[128,512]{1,0:T(8,128)S(1)} %fusion.20), channel_id=1, source_target_pairs={{0,1},{1,0},{2,3},{3,2},{4,5},{5,4},{6,7},{7,6},{8,9},{9,8},{10,11... | collective-permute-start | bytes 786440 | tf_op jit(solution)/shard_map/ppermute | solution.py:54
  177.9 13.9 %collective-permute-start.21 = (bf16[3,128,512]{2,1,0:T(8,128)(2,1)}, bf16[3,128,512]{2,1,0:T(8,128)(2,1)S(1)}, u32[]{:S(2)}, u32[]{:S(2)}) collective-permute-start(bf16[3,128,512]{2,1,0:T(8,128)(2,1)} %pad_maximum_fusion.3), channel_id=1, source_target_pairs={{0,2},{1,3},{2,4},{3,5},{4,6},{5,7},{6,0},{7,1},{8,10},{9,11},{10,... | collective-permute-start | bytes 1179656 | tf_op jit(solution)/shard_map/ppermute | solution.py:53
  182.5 11.3 %collective-permute-start.22 = (bf16[3,128,512]{2,1,0:T(8,128)(2,1)}, bf16[3,128,512]{2,1,0:T(8,128)(2,1)S(1)}, u32[]{:S(2)}, u32[]{:S(2)}) collective-permute-start(bf16[3,128,512]{2,1,0:T(8,128)(2,1)} %pad_maximum_fusion.3), channel_id=1, source_target_pairs={{0,6},{1,7},{2,0},{3,1},{4,2},{5,3},{6,4},{7,5},{8,14},{9,15},{10,... | collective-permute-start | bytes 1179656 | tf_op jit(solution)/shard_map/ppermute | solution.py:53
  185.1 15.9 %collective-permute-start.23 = (bf16[3,128,512]{2,1,0:T(8,128)(2,1)}, bf16[3,128,512]{2,1,0:T(8,128)(2,1)S(1)}, u32[]{:S(2)}, u32[]{:S(2)}) collective-permute-start(bf16[3,128,512]{2,1,0:T(8,128)(2,1)} %pad_maximum_fusion.3), channel_id=1, source_target_pairs={{0,4},{1,5},{2,6},{3,7},{4,0},{5,1},{6,2},{7,3},{8,12},{9,13},{10,... | collective-permute-start | bytes 1179656 | tf_op jit(solution)/shard_map/ppermute | solution.py:53
  201.5 7.3 %collective-permute-start.24 = (f32[128,512]{1,0:T(8,128)S(1)}, f32[128,512]{1,0:T(8,128)S(1)}, u32[]{:S(2)}, u32[]{:S(2)}) collective-permute-start(f32[128,512]{1,0:T(8,128)S(1)} %fusion.27), channel_id=1, source_target_pairs={{0,1},{1,0},{2,3},{3,2},{4,5},{5,4},{6,7},{7,6},{8,9},{9,8},{10,11... | collective-permute-start | bytes 786440 | tf_op jit(solution)/shard_map/ppermute | solution.py:54
  210.0 13.1 %collective-permute-start.25 = (bf16[128,512]{1,0:T(8,128)(2,1)S(1)}, bf16[128,512]{1,0:T(8,128)(2,1)S(1)}, u32[]{:S(2)}, u32[]{:S(2)}) collective-permute-start(bf16[128,512]{1,0:T(8,128)(2,1)S(1)} %fusion.44), channel_id=1, source_target_pairs={{0,128},{8,136},{16,144},{24,152},{32,160},{40,168},{48,176},{56,1... | collective-permute-start | bytes 393224 | tf_op jit(solution)/shard_map/ppermute | solution.py:10
  220.3 7.6 %collective-permute-start.26 = (bf16[128,512]{1,0:T(8,128)(2,1)S(1)}, bf16[128,512]{1,0:T(8,128)(2,1)S(1)}, u32[]{:S(2)}, u32[]{:S(2)}) collective-permute-start(bf16[128,512]{1,0:T(8,128)(2,1)S(1)} %fusion.44), channel_id=1, source_target_pairs={{128,0},{136,8},{144,16},{152,24},{160,32},{168,40},{176,48},{184,... | collective-permute-start | bytes 393224 | tf_op jit(solution)/shard_map/ppermute | solution.py:10
  227.9 13.6 %collective-permute-start.27 = (bf16[3,128,512]{2,1,0:T(8,128)(2,1)S(1)}, bf16[3,128,512]{2,1,0:T(8,128)(2,1)S(1)}, u32[]{:S(2)}, u32[]{:S(2)}) collective-permute-start(bf16[3,128,512]{2,1,0:T(8,128)(2,1)S(1)} %pad_maximum_fusion.4), channel_id=1, source_target_pairs={{0,2},{1,3},{2,4},{3,5},{4,6},{5,7},{6,0},{7,1},{8,10},{9,11},{10,... | collective-permute-start | bytes 1179656 | tf_op jit(solution)/shard_map/ppermute | solution.py:53
  232.6 10.8 %collective-permute-start.28 = (bf16[3,128,512]{2,1,0:T(8,128)(2,1)S(1)}, bf16[3,128,512]{2,1,0:T(8,128)(2,1)S(1)}, u32[]{:S(2)}, u32[]{:S(2)}) collective-permute-start(bf16[3,128,512]{2,1,0:T(8,128)(2,1)S(1)} %pad_maximum_fusion.4), channel_id=1, source_target_pairs={{0,6},{1,7},{2,0},{3,1},{4,2},{5,3},{6,4},{7,5},{8,14},{9,15},{10,... | collective-permute-start | bytes 1179656 | tf_op jit(solution)/shard_map/ppermute | solution.py:53
  235.5 15.4 %collective-permute-start.29 = (bf16[3,128,512]{2,1,0:T(8,128)(2,1)S(1)}, bf16[3,128,512]{2,1,0:T(8,128)(2,1)S(1)}, u32[]{:S(2)}, u32[]{:S(2)}) collective-permute-start(bf16[3,128,512]{2,1,0:T(8,128)(2,1)S(1)} %pad_maximum_fusion.4), channel_id=1, source_target_pairs={{0,4},{1,5},{2,6},{3,7},{4,0},{5,1},{6,2},{7,3},{8,12},{9,13},{10,... | collective-permute-start | bytes 1179656 | tf_op jit(solution)/shard_map/ppermute | solution.py:53
  251.3 7.6 %collective-permute-start.30 = (f32[128,512]{1,0:T(8,128)S(1)}, f32[128,512]{1,0:T(8,128)S(1)}, u32[]{:S(2)}, u32[]{:S(2)}) collective-permute-start(f32[128,512]{1,0:T(8,128)S(1)} %fusion.34), channel_id=1, source_target_pairs={{0,1},{1,0},{2,3},{3,2},{4,5},{5,4},{6,7},{7,6},{8,9},{9,8},{10,11... | collective-permute-start | bytes 786440 | tf_op jit(solution)/shard_map/ppermute | solution.py:54
  260.1 8.2 %collective-permute-start.31 = (bf16[128,512]{1,0:T(8,128)(2,1)S(1)}, bf16[128,512]{1,0:T(8,128)(2,1)S(1)}, u32[]{:S(2)}, u32[]{:S(2)}) collective-permute-start(bf16[128,512]{1,0:T(8,128)(2,1)S(1)} %fusion.43), channel_id=1, source_target_pairs={{0,256},{8,264},{16,272},{24,280},{32,288},{40,296},{48,304},{56,3... | collective-permute-start | bytes 393224 | tf_op jit(solution)/shard_map/ppermute | solution.py:10
  265.5 10.6 %collective-permute-start.32 = (bf16[128,512]{1,0:T(8,128)(2,1)S(1)}, bf16[128,512]{1,0:T(8,128)(2,1)S(1)}, u32[]{:S(2)}, u32[]{:S(2)}) collective-permute-start(bf16[128,512]{1,0:T(8,128)(2,1)S(1)} %fusion.43), channel_id=1, source_target_pairs={{256,0},{264,8},{272,16},{280,24},{288,32},{296,40},{304,48},{312,... | collective-permute-start | bytes 393224 | tf_op jit(solution)/shard_map/ppermute | solution.py:10
  276.1 13.9 %collective-permute-start.33 = (bf16[3,128,512]{2,1,0:T(8,128)(2,1)S(1)}, bf16[3,128,512]{2,1,0:T(8,128)(2,1)S(1)}, u32[]{:S(2)}, u32[]{:S(2)}) collective-permute-start(bf16[3,128,512]{2,1,0:T(8,128)(2,1)S(1)} %pad_maximum_fusion.5), channel_id=1, source_target_pairs={{0,2},{1,3},{2,4},{3,5},{4,6},{5,7},{6,0},{7,1},{8,10},{9,11},{10,... | collective-permute-start | bytes 1179656 | tf_op jit(solution)/shard_map/ppermute | solution.py:53
  280.8 11.1 %collective-permute-start.34 = (bf16[3,128,512]{2,1,0:T(8,128)(2,1)S(1)}, bf16[3,128,512]{2,1,0:T(8,128)(2,1)S(1)}, u32[]{:S(2)}, u32[]{:S(2)}) collective-permute-start(bf16[3,128,512]{2,1,0:T(8,128)(2,1)S(1)} %pad_maximum_fusion.5), channel_id=1, source_target_pairs={{0,6},{1,7},{2,0},{3,1},{4,2},{5,3},{6,4},{7,5},{8,14},{9,15},{10,... | collective-permute-start | bytes 1179656 | tf_op jit(solution)/shard_map/ppermute | solution.py:53
  283.6 15.7 %collective-permute-start.35 = (bf16[3,128,512]{2,1,0:T(8,128)(2,1)S(1)}, bf16[3,128,512]{2,1,0:T(8,128)(2,1)S(1)}, u32[]{:S(2)}, u32[]{:S(2)}) collective-permute-start(bf16[3,128,512]{2,1,0:T(8,128)(2,1)S(1)} %pad_maximum_fusion.5), channel_id=1, source_target_pairs={{0,4},{1,5},{2,6},{3,7},{4,0},{5,1},{6,2},{7,3},{8,12},{9,13},{10,... | collective-permute-start | bytes 1179656 | tf_op jit(solution)/shard_map/ppermute | solution.py:53
  299.8 7.3 %collective-permute-start.36 = (f32[128,512]{1,0:T(8,128)S(1)}, f32[128,512]{1,0:T(8,128)S(1)}, u32[]{:S(2)}, u32[]{:S(2)}) collective-permute-start(f32[128,512]{1,0:T(8,128)S(1)} %fusion.41), channel_id=1, source_target_pairs={{0,1},{1,0},{2,3},{3,2},{4,5},{5,4},{6,7},{7,6},{8,9},{9,8},{10,11... | collective-permute-start | bytes 786440 | tf_op jit(solution)/shard_map/ppermute | solution.py:54
  (15 other events, 224.6 us)

commit v9 on v6

--- a/solution.py
+++ b/solution.py
@@ -55,11 +55,11 @@
         dist = 2**level
         lower = shifted(current, "chain", dist)
         upper = shifted(current, "chain", -dist)
+        if level == 0 and levels > 1:
+            lower, upper, rest = lax.optimization_barrier((lower, upper, tuple(f[1:] for f in factors)))
+            later_mine, later_theirs = prepare(rest)
         own = jnp.stack([current, lower, upper])
         pieces = [own] + [lax.ppermute(own, "cross", same_core(-off)) for off in OFFSETS[1:]]
-        if level == 0 and levels > 1:
-            pieces, rest = lax.optimization_barrier((pieces, tuple(f[1:] for f in factors)))
-            later_mine, later_theirs = prepare(rest)
         at = 0 if level == 0 else level - 1
         use_mine, use_theirs = (mine, theirs) if level == 0 else (later_mine, later_theirs)
         given = lax.ppermute(partial(use_theirs[at], pieces), "cross", swap)

time: 288 us -> 286 us (level)
  waiting for transfers between devices: 82.7 us -> 86.8 us
  starting transfers between devices: 142 us -> 139 us
    ppermute x12, starting transfers between devices: 56.7 us -> 62.3 us  [shifted(): lax.ppermute(value, axis, [(source, source + steps) for source in range(i...]
    ppermute x18, starting transfers between devices: 55.1 us -> 50.8 us  [body(): lax.ppermute(own, 'cross', same_core(-off))]
    ppermute x2, starting transfers between devices: 11.2 us -> 7.99 us  [prepare(): lax.ppermute(arranged(factors, 1 - core), 'cross', swap)]
  transfers between devices with their start and end apart: 38 -> 38, of which waited for: 30 -> 26; matrix products, arithmetic and copies ran while one was open for 11% -> 18% of each run, Pallas kernels for 0% -> 0%
where the time goes in v9:
time: 286 us; the launch traced here: 284 us
  starting transfers between devices  139 us (49%)
  waiting for transfers between devices  86.8 us (30%)
  local copies, waits for them, and re-layouts  27.1 us (9%)
  matrix products  17.5 us (6%)
  other arithmetic  13 us (5%)
    ppermute x18, waiting for transfers between devices, body(): lax.ppermute(own, 'cross', same_core(-off))  63.4 us
    ppermute x12, starting transfers between devices, shifted(): lax.ppermute(value, axis, [(source, source + steps) for source in range(i...  62.3 us
    ppermute x18, starting transfers between devices, body(): lax.ppermute(own, 'cross', same_core(-off))  50.8 us
    ppermute x12, waiting for transfers between devices, shifted(): lax.ppermute(value, axis, [(source, source + steps) for source in range(i...  19.9 us
    ppermute x6, starting transfers between devices, body(): given = lax.ppermute(partial(use_theirs[at], pieces), 'cross', swap)  17.7 us
    dot_general x48, matrix products, partial(): jnp.einsum('ibk,bkr->ir', mat[:, j], piece, preferred_element_type=jnp.fl...  17.5 us
    gather x4, local copies, waits for them, and re-layouts, arranged(): part = jnp.take(signed, columns_for(which_core), axis=3)  8.06 us
    ppermute x2, starting transfers between devices, prepare(): lax.ppermute(arranged(factors, 1 - core), 'cross', swap)  7.99 us
  transfers between devices with their start and end apart: 38, of which 26 were waited for; matrix products, arithmetic and copies ran while one was open for 18% of the time, Pallas kernels for 0%

profile of v9, /device:TPU:1, one launch (start us, length us, event | category | flops | bytes accessed | tf_op | source)
XLA Modules:
  0.0 284.3 jit_solution(7905650814083927583)
XLA Ops:
  0.0 5.6 %collective-permute-start = (bf16[128,512]{1,0:T(8,128)(2,1)}, bf16[128,512]{1,0:T(8,128)(2,1)}, u32[]{:S(2)}, u32[]{:S(2)}) collective-permute-start(bf16[128,512]{1,0:T(8,128)(2,1)} %bitcast.509), channel_id=1, source_target_pairs={{0,8},{8,16},{16,24},{24,32},{32,40},{40,48},{48,56},{56,64},{64,7... | collective-permute-start | bytes 393224 | tf_op jit(solution)/shard_map/ppermute | solution.py:10
  11.2 5.2 %collective-permute-start.5 = (bf16[1,128,4,3,128]{4,1,3,2,0:T(8,128)(2,1)}, bf16[1,128,4,3,128]{4,1,3,2,0:T(8,128)(2,1)}, u32[]{:S(2)}, u32[]{:S(2)}) collective-permute-start(bf16[1,128,4,3,128]{4,1,3,2,0:T(8,128)(2,1)} %fusion.51), channel_id=1, source_target_pairs={{0,1},{1,0},{2,3},{3,2},{4,5},{5,4},{6,7},{7,6},{8,9},{9,8},{10,11... | collective-permute-start | bytes 1179656 | tf_op jit(solution)/shard_map/ppermute | solution.py:38
  46.8 3.4 %pad_maximum_fusion = bf16[5,128,3,8,128]{4,1,3,2,0:T(8,128)(2,1)} fusion(bf16[5,128,1,8,128]{4,1,3,2,0:T(8,128)(2,1)S(1)} %copy-done.1, bf16[5,128,1,8,128]{4,1,3,2,0:T(8,128)(2,1)} %copy.11, bf16[5,128,1,8,128]{4,1,3,2,0:T(8,128)(2,1)} %copy.10), kind=kLoop, calls=%fused_computation.4 | loop fusion | flops 3932160 | bytes 7864320 | tf_op jit(solution)/shard_map/stack | solution.py:32
  69.6 6.4 %collective-permute-start.7 = (bf16[128,512]{1,0:T(8,128)(2,1)S(1)}, bf16[128,512]{1,0:T(8,128)(2,1)S(1)}, u32[]{:S(2)}, u32[]{:S(2)}) collective-permute-start(bf16[128,512]{1,0:T(8,128)(2,1)S(1)} %fusion.49), channel_id=1, source_target_pairs={{0,16},{8,24},{16,32},{24,40},{32,48},{40,56},{48,64},{56,72},{64,... | collective-permute-start | bytes 393224 | tf_op jit(solution)/shard_map/ppermute | solution.py:10
  82.7 3.5 %collective-permute-start.10 = (bf16[3,128,512]{2,1,0:T(8,128)(2,1)S(1)}, bf16[3,128,512]{2,1,0:T(8,128)(2,1)S(1)}, u32[]{:S(2)}, u32[]{:S(2)}) collective-permute-start(bf16[3,128,512]{2,1,0:T(8,128)(2,1)S(1)} %pad_maximum_fusion.2), channel_id=1, source_target_pairs={{0,6},{1,7},{2,0},{3,1},{4,2},{5,3},{6,4},{7,5},{8,14},{9,15},{10,... | collective-permute-start | bytes 1179656 | tf_op jit(solution)/shard_map/ppermute | solution.py:62
  88.2 4.5 %collective-permute-done.11 = bf16[3,128,512]{2,1,0:T(8,128)(2,1)S(1)} collective-permute-done((bf16[3,128,512]{2,1,0:T(8,128)(2,1)S(1)}, bf16[3,128,512]{2,1,0:T(8,128)(2,1)S(1)}, u32[]{:S(2)}, u32[]{:S(2)}) %collective-permute-start.11) | collective-permute-done | bytes 393248 | tf_op jit(solution)/shard_map/ppermute | solution.py:62
  94.7 6.1 %collective-permute-done.10 = bf16[3,128,512]{2,1,0:T(8,128)(2,1)S(1)} collective-permute-done((bf16[3,128,512]{2,1,0:T(8,128)(2,1)S(1)}, bf16[3,128,512]{2,1,0:T(8,128)(2,1)S(1)}, u32[]{:S(2)}, u32[]{:S(2)}) %collective-permute-start.10) | collective-permute-done | bytes 393248 | tf_op jit(solution)/shard_map/ppermute | solution.py:62
  107.7 14.5 %collective-permute-start.14 = (bf16[128,512]{1,0:T(8,128)(2,1)S(1)}, bf16[128,512]{1,0:T(8,128)(2,1)S(1)}, u32[]{:S(2)}, u32[]{:S(2)}) collective-permute-start(bf16[128,512]{1,0:T(8,128)(2,1)S(1)} %fusion.48), channel_id=1, source_target_pairs={{0,32},{8,40},{16,48},{24,56},{32,64},{40,72},{48,80},{56,88},{64,... | collective-permute-start | bytes 393224 | tf_op jit(solution)/shard_map/ppermute | solution.py:10
  123.8 6.3 %collective-permute-done.14 = bf16[128,512]{1,0:T(8,128)(2,1)S(1)} collective-permute-done((bf16[128,512]{1,0:T(8,128)(2,1)S(1)}, bf16[128,512]{1,0:T(8,128)(2,1)S(1)}, u32[]{:S(2)}, u32[]{:S(2)}) %collective-permute-start.14) | collective-permute-done | bytes 131104 | tf_op jit(solution)/shard_map/ppermute | solution.py:10
  133.2 3.6 %collective-permute-start.17 = (bf16[3,128,512]{2,1,0:T(8,128)(2,1)S(1)}, bf16[3,128,512]{2,1,0:T(8,128)(2,1)S(1)}, u32[]{:S(2)}, u32[]{:S(2)}) collective-permute-start(bf16[3,128,512]{2,1,0:T(8,128)(2,1)S(1)} %pad_maximum_fusion.3), channel_id=1, source_target_pairs={{0,6},{1,7},{2,0},{3,1},{4,2},{5,3},{6,4},{7,5},{8,14},{9,15},{10,... | collective-permute-start | bytes 1179656 | tf_op jit(solution)/shard_map/ppermute | solution.py:62
  138.7 4.9 %collective-permute-done.18 = bf16[3,128,512]{2,1,0:T(8,128)(2,1)S(1)} collective-permute-done((bf16[3,128,512]{2,1,0:T(8,128)(2,1)S(1)}, bf16[3,128,512]{2,1,0:T(8,128)(2,1)S(1)}, u32[]{:S(2)}, u32[]{:S(2)}) %collective-permute-start.18) | collective-permute-done | bytes 393248 | tf_op jit(solution)/shard_map/ppermute | solution.py:62
  143.9 8.1 %collective-permute-done.17 = bf16[3,128,512]{2,1,0:T(8,128)(2,1)S(1)} collective-permute-done((bf16[3,128,512]{2,1,0:T(8,128)(2,1)S(1)}, bf16[3,128,512]{2,1,0:T(8,128)(2,1)S(1)}, u32[]{:S(2)}, u32[]{:S(2)}) %collective-permute-start.17) | collective-permute-done | bytes 393248 | tf_op jit(solution)/shard_map/ppermute | solution.py:62
  158.7 10.4 %collective-permute-start.20 = (bf16[128,512]{1,0:T(8,128)(2,1)S(1)}, bf16[128,512]{1,0:T(8,128)(2,1)S(1)}, u32[]{:S(2)}, u32[]{:S(2)}) collective-permute-start(bf16[128,512]{1,0:T(8,128)(2,1)S(1)} %fusion.47), channel_id=1, source_target_pairs={{0,64},{8,72},{16,80},{24,88},{32,96},{40,104},{48,112},{56,120},{... | collective-permute-start | bytes 393224 | tf_op jit(solution)/shard_map/ppermute | solution.py:10
  171.7 3.1 %collective-permute-start.24 = (bf16[3,128,512]{2,1,0:T(8,128)(2,1)S(1)}, bf16[3,128,512]{2,1,0:T(8,128)(2,1)S(1)}, u32[]{:S(2)}, u32[]{:S(2)}) collective-permute-start(bf16[3,128,512]{2,1,0:T(8,128)(2,1)S(1)} %pad_maximum_fusion.4), channel_id=1, source_target_pairs={{0,4},{1,5},{2,6},{3,7},{4,0},{5,1},{6,2},{7,3},{8,12},{9,13},{10,... | collective-permute-start | bytes 1179656 | tf_op jit(solution)/shard_map/ppermute | solution.py:62
  174.8 3.6 %collective-permute-start.23 = (bf16[3,128,512]{2,1,0:T(8,128)(2,1)S(1)}, bf16[3,128,512]{2,1,0:T(8,128)(2,1)S(1)}, u32[]{:S(2)}, u32[]{:S(2)}) collective-permute-start(bf16[3,128,512]{2,1,0:T(8,128)(2,1)S(1)} %pad_maximum_fusion.4), channel_id=1, source_target_pairs={{0,6},{1,7},{2,0},{3,1},{4,2},{5,3},{6,4},{7,5},{8,14},{9,15},{10,... | collective-permute-start | bytes 1179656 | tf_op jit(solution)/shard_map/ppermute | solution.py:62
  180.4 4.1 %collective-permute-done.24 = bf16[3,128,512]{2,1,0:T(8,128)(2,1)S(1)} collective-permute-done((bf16[3,128,512]{2,1,0:T(8,128)(2,1)S(1)}, bf16[3,128,512]{2,1,0:T(8,128)(2,1)S(1)}, u32[]{:S(2)}, u32[]{:S(2)}) %collective-permute-start.24) | collective-permute-done | bytes 393248 | tf_op jit(solution)/shard_map/ppermute | solution.py:62
  184.7 8.8 %collective-permute-done.23 = bf16[3,128,512]{2,1,0:T(8,128)(2,1)S(1)} collective-permute-done((bf16[3,128,512]{2,1,0:T(8,128)(2,1)S(1)}, bf16[3,128,512]{2,1,0:T(8,128)(2,1)S(1)}, u32[]{:S(2)}, u32[]{:S(2)}) %collective-permute-start.23) | collective-permute-done | bytes 393248 | tf_op jit(solution)/shard_map/ppermute | solution.py:62
  194.2 3.5 %collective-permute-start.25 = (f32[128,512]{1,0:T(8,128)S(1)}, f32[128,512]{1,0:T(8,128)S(1)}, u32[]{:S(2)}, u32[]{:S(2)}) collective-permute-start(f32[128,512]{1,0:T(8,128)S(1)} %fusion.29), channel_id=1, source_target_pairs={{0,1},{1,0},{2,3},{3,2},{4,5},{5,4},{6,7},{7,6},{8,9},{9,8},{10,11... | collective-permute-start | bytes 786440 | tf_op jit(solution)/shard_map/ppermute | solution.py:65
  200.3 5.6 %collective-permute-start.26 = (bf16[128,512]{1,0:T(8,128)(2,1)S(1)}, bf16[128,512]{1,0:T(8,128)(2,1)S(1)}, u32[]{:S(2)}, u32[]{:S(2)}) collective-permute-start(bf16[128,512]{1,0:T(8,128)(2,1)S(1)} %fusion.46), channel_id=1, source_target_pairs={{0,128},{8,136},{16,144},{24,152},{32,160},{40,168},{48,176},{56,1... | collective-permute-start | bytes 393224 | tf_op jit(solution)/shard_map/ppermute | solution.py:10
  205.9 4.4 %collective-permute-done.27 = bf16[128,512]{1,0:T(8,128)(2,1)S(1)} collective-permute-done((bf16[128,512]{1,0:T(8,128)(2,1)S(1)}, bf16[128,512]{1,0:T(8,128)(2,1)S(1)}, u32[]{:S(2)}, u32[]{:S(2)}) %collective-permute-start.27) | collective-permute-done | bytes 131104 | tf_op jit(solution)/shard_map/ppermute | solution.py:10
  210.4 3.1 %collective-permute-start.30 = (bf16[3,128,512]{2,1,0:T(8,128)(2,1)S(1)}, bf16[3,128,512]{2,1,0:T(8,128)(2,1)S(1)}, u32[]{:S(2)}, u32[]{:S(2)}) collective-permute-start(bf16[3,128,512]{2,1,0:T(8,128)(2,1)S(1)} %pad_maximum_fusion.5), channel_id=1, source_target_pairs={{0,4},{1,5},{2,6},{3,7},{4,0},{5,1},{6,2},{7,3},{8,12},{9,13},{10,... | collective-permute-start | bytes 1179656 | tf_op jit(solution)/shard_map/ppermute | solution.py:62
  213.6 3.7 %collective-permute-start.29 = (bf16[3,128,512]{2,1,0:T(8,128)(2,1)S(1)}, bf16[3,128,512]{2,1,0:T(8,128)(2,1)S(1)}, u32[]{:S(2)}, u32[]{:S(2)}) collective-permute-start(bf16[3,128,512]{2,1,0:T(8,128)(2,1)S(1)} %pad_maximum_fusion.5), channel_id=1, source_target_pairs={{0,6},{1,7},{2,0},{3,1},{4,2},{5,3},{6,4},{7,5},{8,14},{9,15},{10,... | collective-permute-start | bytes 1179656 | tf_op jit(solution)/shard_map/ppermute | solution.py:62
  219.2 4.4 %collective-permute-done.30 = bf16[3,128,512]{2,1,0:T(8,128)(2,1)S(1)} collective-permute-done((bf16[3,128,512]{2,1,0:T(8,128)(2,1)S(1)}, bf16[3,128,512]{2,1,0:T(8,128)(2,1)S(1)}, u32[]{:S(2)}, u32[]{:S(2)}) %collective-permute-start.30) | collective-permute-done | bytes 393248 | tf_op jit(solution)/shard_map/ppermute | solution.py:62
  223.8 8.4 %collective-permute-done.29 = bf16[3,128,512]{2,1,0:T(8,128)(2,1)S(1)} collective-permute-done((bf16[3,128,512]{2,1,0:T(8,128)(2,1)S(1)}, bf16[3,128,512]{2,1,0:T(8,128)(2,1)S(1)}, u32[]{:S(2)}, u32[]{:S(2)}) %collective-permute-start.29) | collective-permute-done | bytes 393248 | tf_op jit(solution)/shard_map/ppermute | solution.py:62
  233.1 3.3 %collective-permute-start.31 = (f32[128,512]{1,0:T(8,128)S(1)}, f32[128,512]{1,0:T(8,128)S(1)}, u32[]{:S(2)}, u32[]{:S(2)}) collective-permute-start(f32[128,512]{1,0:T(8,128)S(1)} %fusion.36), channel_id=1, source_target_pairs={{0,1},{1,0},{2,3},{3,2},{4,5},{5,4},{6,7},{7,6},{8,9},{9,8},{10,11... | collective-permute-start | bytes 786440 | tf_op jit(solution)/shard_map/ppermute | solution.py:65
  239.1 12.0 %collective-permute-start.32 = (bf16[128,512]{1,0:T(8,128)(2,1)S(1)}, bf16[128,512]{1,0:T(8,128)(2,1)S(1)}, u32[]{:S(2)}, u32[]{:S(2)}) collective-permute-start(bf16[128,512]{1,0:T(8,128)(2,1)S(1)} %fusion.45), channel_id=1, source_target_pairs={{0,256},{8,264},{16,272},{24,280},{32,288},{40,296},{48,304},{56,3... | collective-permute-start | bytes 393224 | tf_op jit(solution)/shard_map/ppermute | solution.py:10
  252.7 3.5 %collective-permute-done.32 = bf16[128,512]{1,0:T(8,128)(2,1)S(1)} collective-permute-done((bf16[128,512]{1,0:T(8,128)(2,1)S(1)}, bf16[128,512]{1,0:T(8,128)(2,1)S(1)}, u32[]{:S(2)}, u32[]{:S(2)}) %collective-permute-start.32) | collective-permute-done | bytes 131104 | tf_op jit(solution)/shard_map/ppermute | solution.py:10
  256.2 3.1 %collective-permute-start.36 = (bf16[3,128,512]{2,1,0:T(8,128)(2,1)S(1)}, bf16[3,128,512]{2,1,0:T(8,128)(2,1)S(1)}, u32[]{:S(2)}, u32[]{:S(2)}) collective-permute-start(bf16[3,128,512]{2,1,0:T(8,128)(2,1)S(1)} %pad_maximum_fusion.6), channel_id=1, source_target_pairs={{0,4},{1,5},{2,6},{3,7},{4,0},{5,1},{6,2},{7,3},{8,12},{9,13},{10,... | collective-permute-start | bytes 1179656 | tf_op jit(solution)/shard_map/ppermute | solution.py:62
  259.4 3.6 %collective-permute-start.35 = (bf16[3,128,512]{2,1,0:T(8,128)(2,1)S(1)}, bf16[3,128,512]{2,1,0:T(8,128)(2,1)S(1)}, u32[]{:S(2)}, u32[]{:S(2)}) collective-permute-start(bf16[3,128,512]{2,1,0:T(8,128)(2,1)S(1)} %pad_maximum_fusion.6), channel_id=1, source_target_pairs={{0,6},{1,7},{2,0},{3,1},{4,2},{5,3},{6,4},{7,5},{8,14},{9,15},{10,... | collective-permute-start | bytes 1179656 | tf_op jit(solution)/shard_map/ppermute | solution.py:62
  265.0 4.1 %collective-permute-done.36 = bf16[3,128,512]{2,1,0:T(8,128)(2,1)S(1)} collective-permute-done((bf16[3,128,512]{2,1,0:T(8,128)(2,1)S(1)}, bf16[3,128,512]{2,1,0:T(8,128)(2,1)S(1)}, u32[]{:S(2)}, u32[]{:S(2)}) %collective-permute-start.36) | collective-permute-done | bytes 393248 | tf_op jit(solution)/shard_map/ppermute | solution.py:62
  269.3 8.7 %collective-permute-done.35 = bf16[3,128,512]{2,1,0:T(8,128)(2,1)S(1)} collective-permute-done((bf16[3,128,512]{2,1,0:T(8,128)(2,1)S(1)}, bf16[3,128,512]{2,1,0:T(8,128)(2,1)S(1)}, u32[]{:S(2)}, u32[]{:S(2)}) %collective-permute-start.35) | collective-permute-done | bytes 393248 | tf_op jit(solution)/shard_map/ppermute | solution.py:62
  278.8 3.5 %collective-permute-start.37 = (f32[128,512]{1,0:T(8,128)S(1)}, f32[128,512]{1,0:T(8,128)S(1)}, u32[]{:S(2)}, u32[]{:S(2)}) collective-permute-start(f32[128,512]{1,0:T(8,128)S(1)} %fusion.43), channel_id=1, source_target_pairs={{0,1},{1,0},{2,3},{3,2},{4,5},{5,4},{6,7},{7,6},{8,9},{9,8},{10,11... | collective-permute-start | bytes 786440 | tf_op jit(solution)/shard_map/ppermute | solution.py:65
  (151 shorter events, 106.0 us)
Async XLA Ops:
  0.0 28.6 %collective-permute-start = (bf16[128,512]{1,0:T(8,128)(2,1)}, bf16[128,512]{1,0:T(8,128)(2,1)}, u32[]{:S(2)}, u32[]{:S(2)}) collective-permute-start(bf16[128,512]{1,0:T(8,128)(2,1)} %bitcast.509), channel_id=1, source_target_pairs={{0,8},{8,16},{16,24},{24,32},{32,40},{40,48},{48,56},{56,64},{64,7... | collective-permute-start | bytes 393224 | tf_op jit(solution)/shard_map/ppermute | solution.py:10
  5.6 23.0 %collective-permute-start.1 = (bf16[128,512]{1,0:T(8,128)(2,1)}, bf16[128,512]{1,0:T(8,128)(2,1)}, u32[]{:S(2)}, u32[]{:S(2)}) collective-permute-start(bf16[128,512]{1,0:T(8,128)(2,1)} %bitcast.510), channel_id=1, source_target_pairs={{8,0},{16,8},{24,16},{32,24},{40,32},{48,40},{56,48},{64,56},{72,6... | collective-permute-start | bytes 393224 | tf_op jit(solution)/shard_map/ppermute | solution.py:10
  11.2 47.6 %collective-permute-start.5 = (bf16[1,128,4,3,128]{4,1,3,2,0:T(8,128)(2,1)}, bf16[1,128,4,3,128]{4,1,3,2,0:T(8,128)(2,1)}, u32[]{:S(2)}, u32[]{:S(2)}) collective-permute-start(bf16[1,128,4,3,128]{4,1,3,2,0:T(8,128)(2,1)} %fusion.51), channel_id=1, source_target_pairs={{0,1},{1,0},{2,3},{3,2},{4,5},{5,4},{6,7},{7,6},{8,9},{9,8},{10,11... | collective-permute-start | bytes 1179656 | tf_op jit(solution)/shard_map/ppermute | solution.py:38
  30.3 28.5 %collective-permute-start.4 = (bf16[3,128,512]{2,1,0:T(8,128)(2,1)}, bf16[3,128,512]{2,1,0:T(8,128)(2,1)S(1)}, u32[]{:S(2)}, u32[]{:S(2)}) collective-permute-start(bf16[3,128,512]{2,1,0:T(8,128)(2,1)} %pad_maximum_fusion.1), channel_id=1, source_target_pairs={{0,4},{1,5},{2,6},{3,7},{4,0},{5,1},{6,2},{7,3},{8,12},{9,13},{10,... | collective-permute-start | bytes 1179656 | tf_op jit(solution)/shard_map/ppermute | solution.py:62
  32.6 27.4 %collective-permute-start.3 = (bf16[3,128,512]{2,1,0:T(8,128)(2,1)}, bf16[3,128,512]{2,1,0:T(8,128)(2,1)S(1)}, u32[]{:S(2)}, u32[]{:S(2)}) collective-permute-start(bf16[3,128,512]{2,1,0:T(8,128)(2,1)} %pad_maximum_fusion.1), channel_id=1, source_target_pairs={{0,6},{1,7},{2,0},{3,1},{4,2},{5,3},{6,4},{7,5},{8,14},{9,15},{10,... | collective-permute-start | bytes 1179656 | tf_op jit(solution)/shard_map/ppermute | solution.py:62
  35.4 25.7 %collective-permute-start.2 = (bf16[3,128,512]{2,1,0:T(8,128)(2,1)}, bf16[3,128,512]{2,1,0:T(8,128)(2,1)}, u32[]{:S(2)}, u32[]{:S(2)}) collective-permute-start(bf16[3,128,512]{2,1,0:T(8,128)(2,1)} %pad_maximum_fusion.1), channel_id=1, source_target_pairs={{0,2},{1,3},{2,4},{3,5},{4,6},{5,7},{6,0},{7,1},{8,10},{9,11},{10,... | collective-permute-start | bytes 1179656 | tf_op jit(solution)/shard_map/ppermute | solution.py:62
  54.9 38.0 %collective-permute-start.12 = (bf16[5,128,4,3,128]{4,1,3,2,0:T(8,128)(2,1)}, bf16[5,128,4,3,128]{4,1,3,2,0:T(8,128)(2,1)}, u32[]{:S(2)}, u32[]{:S(2)}) collective-permute-start(bf16[5,128,4,3,128]{4,1,3,2,0:T(8,128)(2,1)} %fusion), channel_id=1, source_target_pairs={{0,1},{1,0},{2,3},{3,2},{4,5},{5,4},{6,7},{7,6},{8,9},{9,8},{10,11... | collective-permute-start | bytes 5898248 | tf_op jit(solution)/shard_map/ppermute | solution.py:38
  68.3 10.8 %collective-permute-start.8 = (bf16[128,512]{1,0:T(8,128)(2,1)S(1)}, bf16[128,512]{1,0:T(8,128)(2,1)S(1)}, u32[]{:S(2)}, u32[]{:S(2)}) collective-permute-start(bf16[128,512]{1,0:T(8,128)(2,1)S(1)} %fusion.49), channel_id=1, source_target_pairs={{16,0},{24,8},{32,16},{40,24},{48,32},{56,40},{64,48},{72,56},{80,... | collective-permute-start | bytes 393224 | tf_op jit(solution)/shard_map/ppermute | solution.py:10
  69.6 9.5 %collective-permute-start.7 = (bf16[128,512]{1,0:T(8,128)(2,1)S(1)}, bf16[128,512]{1,0:T(8,128)(2,1)S(1)}, u32[]{:S(2)}, u32[]{:S(2)}) collective-permute-start(bf16[128,512]{1,0:T(8,128)(2,1)S(1)} %fusion.49), channel_id=1, source_target_pairs={{0,16},{8,24},{16,32},{24,40},{32,48},{40,56},{48,64},{56,72},{64,... | collective-permute-start | bytes 393224 | tf_op jit(solution)/shard_map/ppermute | solution.py:10
  79.2 13.5 %collective-permute-start.11 = (bf16[3,128,512]{2,1,0:T(8,128)(2,1)S(1)}, bf16[3,128,512]{2,1,0:T(8,128)(2,1)S(1)}, u32[]{:S(2)}, u32[]{:S(2)}) collective-permute-start(bf16[3,128,512]{2,1,0:T(8,128)(2,1)S(1)} %pad_maximum_fusion.2), channel_id=1, source_target_pairs={{0,4},{1,5},{2,6},{3,7},{4,0},{5,1},{6,2},{7,3},{8,12},{9,13},{10,... | collective-permute-start | bytes 1179656 | tf_op jit(solution)/shard_map/ppermute | solution.py:62
  82.7 18.1 %collective-permute-start.10 = (bf16[3,128,512]{2,1,0:T(8,128)(2,1)S(1)}, bf16[3,128,512]{2,1,0:T(8,128)(2,1)S(1)}, u32[]{:S(2)}, u32[]{:S(2)}) collective-permute-start(bf16[3,128,512]{2,1,0:T(8,128)(2,1)S(1)} %pad_maximum_fusion.2), channel_id=1, source_target_pairs={{0,6},{1,7},{2,0},{3,1},{4,2},{5,3},{6,4},{7,5},{8,14},{9,15},{10,... | collective-permute-start | bytes 1179656 | tf_op jit(solution)/shard_map/ppermute | solution.py:62
  86.2 15.4 %collective-permute-start.9 = (bf16[3,128,512]{2,1,0:T(8,128)(2,1)S(1)}, bf16[3,128,512]{2,1,0:T(8,128)(2,1)S(1)}, u32[]{:S(2)}, u32[]{:S(2)}) collective-permute-start(bf16[3,128,512]{2,1,0:T(8,128)(2,1)S(1)} %pad_maximum_fusion.2), channel_id=1, source_target_pairs={{0,2},{1,3},{2,4},{3,5},{4,6},{5,7},{6,0},{7,1},{8,10},{9,11},{10,... | collective-permute-start | bytes 1179656 | tf_op jit(solution)/shard_map/ppermute | solution.py:62
  106.4 17.4 %collective-permute-start.15 = (bf16[128,512]{1,0:T(8,128)(2,1)S(1)}, bf16[128,512]{1,0:T(8,128)(2,1)S(1)}, u32[]{:S(2)}, u32[]{:S(2)}) collective-permute-start(bf16[128,512]{1,0:T(8,128)(2,1)S(1)} %fusion.48), channel_id=1, source_target_pairs={{32,0},{40,8},{48,16},{56,24},{64,32},{72,40},{80,48},{88,56},{96,... | collective-permute-start | bytes 393224 | tf_op jit(solution)/shard_map/ppermute | solution.py:10
  107.7 22.4 %collective-permute-start.14 = (bf16[128,512]{1,0:T(8,128)(2,1)S(1)}, bf16[128,512]{1,0:T(8,128)(2,1)S(1)}, u32[]{:S(2)}, u32[]{:S(2)}) collective-permute-start(bf16[128,512]{1,0:T(8,128)(2,1)S(1)} %fusion.48), channel_id=1, source_target_pairs={{0,32},{8,40},{16,48},{24,56},{32,64},{40,72},{48,80},{56,88},{64,... | collective-permute-start | bytes 393224 | tf_op jit(solution)/shard_map/ppermute | solution.py:10
  130.1 13.6 %collective-permute-start.18 = (bf16[3,128,512]{2,1,0:T(8,128)(2,1)S(1)}, bf16[3,128,512]{2,1,0:T(8,128)(2,1)S(1)}, u32[]{:S(2)}, u32[]{:S(2)}) collective-permute-start(bf16[3,128,512]{2,1,0:T(8,128)(2,1)S(1)} %pad_maximum_fusion.3), channel_id=1, source_target_pairs={{0,4},{1,5},{2,6},{3,7},{4,0},{5,1},{6,2},{7,3},{8,12},{9,13},{10,... | collective-permute-start | bytes 1179656 | tf_op jit(solution)/shard_map/ppermute | solution.py:62
  133.2 18.9 %collective-permute-start.17 = (bf16[3,128,512]{2,1,0:T(8,128)(2,1)S(1)}, bf16[3,128,512]{2,1,0:T(8,128)(2,1)S(1)}, u32[]{:S(2)}, u32[]{:S(2)}) collective-permute-start(bf16[3,128,512]{2,1,0:T(8,128)(2,1)S(1)} %pad_maximum_fusion.3), channel_id=1, source_target_pairs={{0,6},{1,7},{2,0},{3,1},{4,2},{5,3},{6,4},{7,5},{8,14},{9,15},{10,... | collective-permute-start | bytes 1179656 | tf_op jit(solution)/shard_map/ppermute | solution.py:62
  136.8 16.0 %collective-permute-start.16 = (bf16[3,128,512]{2,1,0:T(8,128)(2,1)S(1)}, bf16[3,128,512]{2,1,0:T(8,128)(2,1)S(1)}, u32[]{:S(2)}, u32[]{:S(2)}) collective-permute-start(bf16[3,128,512]{2,1,0:T(8,128)(2,1)S(1)} %pad_maximum_fusion.3), channel_id=1, source_target_pairs={{0,2},{1,3},{2,4},{3,5},{4,6},{5,7},{6,0},{7,1},{8,10},{9,11},{10,... | collective-permute-start | bytes 1179656 | tf_op jit(solution)/shard_map/ppermute | solution.py:62
  157.4 13.4 %collective-permute-start.21 = (bf16[128,512]{1,0:T(8,128)(2,1)S(1)}, bf16[128,512]{1,0:T(8,128)(2,1)S(1)}, u32[]{:S(2)}, u32[]{:S(2)}) collective-permute-start(bf16[128,512]{1,0:T(8,128)(2,1)S(1)} %fusion.47), channel_id=1, source_target_pairs={{64,0},{72,8},{80,16},{88,24},{96,32},{104,40},{112,48},{120,56},{... | collective-permute-start | bytes 393224 | tf_op jit(solution)/shard_map/ppermute | solution.py:10
  158.7 12.9 %collective-permute-start.20 = (bf16[128,512]{1,0:T(8,128)(2,1)S(1)}, bf16[128,512]{1,0:T(8,128)(2,1)S(1)}, u32[]{:S(2)}, u32[]{:S(2)}) collective-permute-start(bf16[128,512]{1,0:T(8,128)(2,1)S(1)} %fusion.47), channel_id=1, source_target_pairs={{0,64},{8,72},{16,80},{24,88},{32,96},{40,104},{48,112},{56,120},{... | collective-permute-start | bytes 393224 | tf_op jit(solution)/shard_map/ppermute | solution.py:10
  171.7 12.8 %collective-permute-start.24 = (bf16[3,128,512]{2,1,0:T(8,128)(2,1)S(1)}, bf16[3,128,512]{2,1,0:T(8,128)(2,1)S(1)}, u32[]{:S(2)}, u32[]{:S(2)}) collective-permute-start(bf16[3,128,512]{2,1,0:T(8,128)(2,1)S(1)} %pad_maximum_fusion.4), channel_id=1, source_target_pairs={{0,4},{1,5},{2,6},{3,7},{4,0},{5,1},{6,2},{7,3},{8,12},{9,13},{10,... | collective-permute-start | bytes 1179656 | tf_op jit(solution)/shard_map/ppermute | solution.py:62
  174.8 18.6 %collective-permute-start.23 = (bf16[3,128,512]{2,1,0:T(8,128)(2,1)S(1)}, bf16[3,128,512]{2,1,0:T(8,128)(2,1)S(1)}, u32[]{:S(2)}, u32[]{:S(2)}) collective-permute-start(bf16[3,128,512]{2,1,0:T(8,128)(2,1)S(1)} %pad_maximum_fusion.4), channel_id=1, source_target_pairs={{0,6},{1,7},{2,0},{3,1},{4,2},{5,3},{6,4},{7,5},{8,14},{9,15},{10,... | collective-permute-start | bytes 1179656 | tf_op jit(solution)/shard_map/ppermute | solution.py:62
  178.5 15.2 %collective-permute-start.22 = (bf16[3,128,512]{2,1,0:T(8,128)(2,1)S(1)}, bf16[3,128,512]{2,1,0:T(8,128)(2,1)S(1)}, u32[]{:S(2)}, u32[]{:S(2)}) collective-permute-start(bf16[3,128,512]{2,1,0:T(8,128)(2,1)S(1)} %pad_maximum_fusion.4), channel_id=1, source_target_pairs={{0,2},{1,3},{2,4},{3,5},{4,6},{5,7},{6,0},{7,1},{8,10},{9,11},{10,... | collective-permute-start | bytes 1179656 | tf_op jit(solution)/shard_map/ppermute | solution.py:62
  199.0 11.3 %collective-permute-start.27 = (bf16[128,512]{1,0:T(8,128)(2,1)S(1)}, bf16[128,512]{1,0:T(8,128)(2,1)S(1)}, u32[]{:S(2)}, u32[]{:S(2)}) collective-permute-start(bf16[128,512]{1,0:T(8,128)(2,1)S(1)} %fusion.46), channel_id=1, source_target_pairs={{128,0},{136,8},{144,16},{152,24},{160,32},{168,40},{176,48},{184,... | collective-permute-start | bytes 393224 | tf_op jit(solution)/shard_map/ppermute | solution.py:10
  200.3 10.0 %collective-permute-start.26 = (bf16[128,512]{1,0:T(8,128)(2,1)S(1)}, bf16[128,512]{1,0:T(8,128)(2,1)S(1)}, u32[]{:S(2)}, u32[]{:S(2)}) collective-permute-start(bf16[128,512]{1,0:T(8,128)(2,1)S(1)} %fusion.46), channel_id=1, source_target_pairs={{0,128},{8,136},{16,144},{24,152},{32,160},{40,168},{48,176},{56,1... | collective-permute-start | bytes 393224 | tf_op jit(solution)/shard_map/ppermute | solution.py:10
  210.4 13.1 %collective-permute-start.30 = (bf16[3,128,512]{2,1,0:T(8,128)(2,1)S(1)}, bf16[3,128,512]{2,1,0:T(8,128)(2,1)S(1)}, u32[]{:S(2)}, u32[]{:S(2)}) collective-permute-start(bf16[3,128,512]{2,1,0:T(8,128)(2,1)S(1)} %pad_maximum_fusion.5), channel_id=1, source_target_pairs={{0,4},{1,5},{2,6},{3,7},{4,0},{5,1},{6,2},{7,3},{8,12},{9,13},{10,... | collective-permute-start | bytes 1179656 | tf_op jit(solution)/shard_map/ppermute | solution.py:62
  213.6 18.6 %collective-permute-start.29 = (bf16[3,128,512]{2,1,0:T(8,128)(2,1)S(1)}, bf16[3,128,512]{2,1,0:T(8,128)(2,1)S(1)}, u32[]{:S(2)}, u32[]{:S(2)}) collective-permute-start(bf16[3,128,512]{2,1,0:T(8,128)(2,1)S(1)} %pad_maximum_fusion.5), channel_id=1, source_target_pairs={{0,6},{1,7},{2,0},{3,1},{4,2},{5,3},{6,4},{7,5},{8,14},{9,15},{10,... | collective-permute-start | bytes 1179656 | tf_op jit(solution)/shard_map/ppermute | solution.py:62
  217.2 15.4 %collective-permute-start.28 = (bf16[3,128,512]{2,1,0:T(8,128)(2,1)S(1)}, bf16[3,128,512]{2,1,0:T(8,128)(2,1)S(1)}, u32[]{:S(2)}, u32[]{:S(2)}) collective-permute-start(bf16[3,128,512]{2,1,0:T(8,128)(2,1)S(1)} %pad_maximum_fusion.5), channel_id=1, source_target_pairs={{0,2},{1,3},{2,4},{3,5},{4,6},{5,7},{6,0},{7,1},{8,10},{9,11},{10,... | collective-permute-start | bytes 1179656 | tf_op jit(solution)/shard_map/ppermute | solution.py:62
  237.8 14.9 %collective-permute-start.33 = (bf16[128,512]{1,0:T(8,128)(2,1)S(1)}, bf16[128,512]{1,0:T(8,128)(2,1)S(1)}, u32[]{:S(2)}, u32[]{:S(2)}) collective-permute-start(bf16[128,512]{1,0:T(8,128)(2,1)S(1)} %fusion.45), channel_id=1, source_target_pairs={{256,0},{264,8},{272,16},{280,24},{288,32},{296,40},{304,48},{312,... | collective-permute-start | bytes 393224 | tf_op jit(solution)/shard_map/ppermute | solution.py:10
  239.1 17.1 %collective-permute-start.32 = (bf16[128,512]{1,0:T(8,128)(2,1)S(1)}, bf16[128,512]{1,0:T(8,128)(2,1)S(1)}, u32[]{:S(2)}, u32[]{:S(2)}) collective-permute-start(bf16[128,512]{1,0:T(8,128)(2,1)S(1)} %fusion.45), channel_id=1, source_target_pairs={{0,256},{8,264},{16,272},{24,280},{32,288},{40,296},{48,304},{56,3... | collective-permute-start | bytes 393224 | tf_op jit(solution)/shard_map/ppermute | solution.py:10
  256.2 12.8 %collective-permute-start.36 = (bf16[3,128,512]{2,1,0:T(8,128)(2,1)S(1)}, bf16[3,128,512]{2,1,0:T(8,128)(2,1)S(1)}, u32[]{:S(2)}, u32[]{:S(2)}) collective-permute-start(bf16[3,128,512]{2,1,0:T(8,128)(2,1)S(1)} %pad_maximum_fusion.6), channel_id=1, source_target_pairs={{0,4},{1,5},{2,6},{3,7},{4,0},{5,1},{6,2},{7,3},{8,12},{9,13},{10,... | collective-permute-start | bytes 1179656 | tf_op jit(solution)/shard_map/ppermute | solution.py:62
  259.4 18.7 %collective-permute-start.35 = (bf16[3,128,512]{2,1,0:T(8,128)(2,1)S(1)}, bf16[3,128,512]{2,1,0:T(8,128)(2,1)S(1)}, u32[]{:S(2)}, u32[]{:S(2)}) collective-permute-start(bf16[3,128,512]{2,1,0:T(8,128)(2,1)S(1)} %pad_maximum_fusion.6), channel_id=1, source_target_pairs={{0,6},{1,7},{2,0},{3,1},{4,2},{5,3},{6,4},{7,5},{8,14},{9,15},{10,... | collective-permute-start | bytes 1179656 | tf_op jit(solution)/shard_map/ppermute | solution.py:62
  263.0 15.2 %collective-permute-start.34 = (bf16[3,128,512]{2,1,0:T(8,128)(2,1)S(1)}, bf16[3,128,512]{2,1,0:T(8,128)(2,1)S(1)}, u32[]{:S(2)}, u32[]{:S(2)}) collective-permute-start(bf16[3,128,512]{2,1,0:T(8,128)(2,1)S(1)} %pad_maximum_fusion.6), channel_id=1, source_target_pairs={{0,2},{1,3},{2,4},{3,5},{4,6},{5,7},{6,0},{7,1},{8,10},{9,11},{10,... | collective-permute-start | bytes 1179656 | tf_op jit(solution)/shard_map/ppermute | solution.py:62
  (15 other events, 67.7 us)

commit v10 on v5

--- a/solution.py
+++ b/solution.py
@@ -25,12 +25,14 @@
     def columns_for(which_core):
         return jnp.stack([2 * ((chip + off) % chips) + which_core for off in OFFSETS])
 
-    blocks = [f[:, 0].reshape(levels, rows, ncross, rows) for f in (self_factor, lower_factor, upper_factor)]
+    factors = [f[:, 0] for f in (self_factor, lower_factor, upper_factor)]
 
     def pick(which_core):
-        idx = columns_for(which_core)
-        parts = [jnp.take(blocks[0], idx, axis=2)] + [-jnp.take(f, idx, axis=2) for f in blocks[1:]]
-        return jnp.stack(parts, axis=3)
+        slots = []
+        for c in columns_for(which_core):
+            blocks = [lax.dynamic_slice_in_dim(f, c * rows, rows, axis=2) for f in factors]
+            slots.append(jnp.stack([blocks[0], -blocks[1], -blocks[2]], axis=2))
+        return jnp.stack(slots, axis=2)
 
     mine = pick(core)
     swap = [(2 * c + b, 2 * c + 1 - b) for c in range(chips) for b in range(2)]

time: 293 us -> 261 us (0.89)
  local copies, waits for them, and re-layouts: 25 us -> 3.07 us
  waiting for transfers between devices: 111 us -> 106 us
  other arithmetic: 5.84 us -> 2.29 us
    gather x6 -> x0, local copies, waits for them, and re-layouts: 10.4 us -> none  [the longest x4 7.36 us: pick(): jnp.take(f, idx, axis=2)]
    ppermute x18, waiting for transfers between devices: 85.5 us -> 78.3 us  [body(): lax.ppermute(own, 'cross', same_core(-off))]
    unnamed x7 -> x6, local copies, waits for them, and re-layouts: 7.09 us -> 0.77 us
    another operation x6 -> x10, other arithmetic: 5.39 us -> 1.1 us  [pick(): return jnp.stack(slots, axis=2)]
    another operation x3 -> x1, local copies, waits for them, and re-layouts: 5.43 us -> 1.74 us  [pick(): slots.append(jnp.stack([blocks[0], -blocks[1], -blocks[2]], axis=2))]
    ppermute x6, starting transfers between devices: 22.3 us -> 19.2 us  [body(): given = lax.ppermute(partial(theirs[level], pieces), 'cross', swap)]
  transfers between devices with their start and end apart: 37 -> 37, of which waited for: 30 -> 34; matrix products, arithmetic and copies ran while one was open for 5% -> 3% of each run, Pallas kernels for 0% -> 0%
where the time goes in v10:
time: 261 us; the launch traced here: 260 us
  starting transfers between devices  137 us (52%)
  waiting for transfers between devices  106 us (41%)
  matrix products  11.6 us (4%)
  local copies, waits for them, and re-layouts  3.07 us (1%)
    ppermute x18, waiting for transfers between devices, body(): lax.ppermute(own, 'cross', same_core(-off))  78.3 us
    ppermute x12, starting transfers between devices, shifted(): lax.ppermute(value, axis, [(source, source + steps) for source in range(i...  58.6 us
    ppermute x18, starting transfers between devices, body(): lax.ppermute(own, 'cross', same_core(-off))  50.3 us
    ppermute x12, waiting for transfers between devices, shifted(): lax.ppermute(value, axis, [(source, source + steps) for source in range(i...  24.3 us
    ppermute x6, starting transfers between devices, body(): given = lax.ppermute(partial(theirs[level], pieces), 'cross', swap)  19.2 us
    dot_general x48, matrix products, partial(): jnp.einsum('ibk,bkr->ir', mat[:, j], piece, preferred_element_type=jnp.fl...  11.6 us
    ppermute x1, starting transfers between devices, body(): theirs = lax.ppermute(pick(1 - core), 'cross', swap)  8.79 us
  transfers between devices with their start and end apart: 37, of which 34 were waited for; matrix products, arithmetic and copies ran while one was open for 3% of the time, Pallas kernels for 0%

profile of v10, /device:TPU:1, one launch (start us, length us, event | category | flops | bytes accessed | tf_op | source)
XLA Modules:
  0.0 260.2 jit_solution(10023736920664127671)
XLA Ops:
  4.0 8.8 %collective-permute-start.5 = (bf16[6,128,4,3,128]{4,1,3,2,0:T(8,128)(2,1)S(1)}, bf16[6,128,4,3,128]{4,1,3,2,0:T(8,128)(2,1)S(1)}, u32[]{:S(2)}, u32[]{:S(2)}) collective-permute-start(bf16[6,128,4,3,128]{4,1,3,2,0:T(8,128)(2,1)S(1)} %pad_maximum_fusion.1), channel_id=1, source_target_pairs={{0,1},{1,0},{2,3},{3,2},{4,5},{5,4},{6,7},{7,6},{8,9},{9,8},{10,11... | collective-permute-start | bytes 7077896 | tf_op jit(solution)/shard_map/ppermute | solution.py:39
  14.1 4.0 %collective-permute-start = (bf16[128,512]{1,0:T(8,128)(2,1)S(1)}, bf16[128,512]{1,0:T(8,128)(2,1)S(1)}, u32[]{:S(2)}, u32[]{:S(2)}) collective-permute-start(bf16[128,512]{1,0:T(8,128)(2,1)S(1)} %bitcast.516), channel_id=1, source_target_pairs={{0,8},{8,16},{16,24},{24,32},{32,40},{40,48},{48,56},{56,64},{64,7... | collective-permute-start | bytes 393224 | tf_op jit(solution)/shard_map/ppermute | solution.py:10
  25.2 3.4 %collective-permute-start.2 = (bf16[3,128,512]{2,1,0:T(8,128)(2,1)S(1)}, bf16[3,128,512]{2,1,0:T(8,128)(2,1)S(1)}, u32[]{:S(2)}, u32[]{:S(2)}) collective-permute-start(bf16[3,128,512]{2,1,0:T(8,128)(2,1)S(1)} %pad_maximum_fusion.2), channel_id=1, source_target_pairs={{0,2},{1,3},{2,4},{3,5},{4,6},{5,7},{6,0},{7,1},{8,10},{9,11},{10,... | collective-permute-start | bytes 1179656 | tf_op jit(solution)/shard_map/ppermute | solution.py:57
  28.6 5.1 %collective-permute-done.4 = bf16[3,128,512]{2,1,0:T(8,128)(2,1)S(1)} collective-permute-done((bf16[3,128,512]{2,1,0:T(8,128)(2,1)S(1)}, bf16[3,128,512]{2,1,0:T(8,128)(2,1)S(1)}, u32[]{:S(2)}, u32[]{:S(2)}) %collective-permute-start.4) | collective-permute-done | bytes 393248 | tf_op jit(solution)/shard_map/ppermute | solution.py:57
  34.5 3.8 %collective-permute-done.3 = bf16[3,128,512]{2,1,0:T(8,128)(2,1)S(1)} collective-permute-done((bf16[3,128,512]{2,1,0:T(8,128)(2,1)S(1)}, bf16[3,128,512]{2,1,0:T(8,128)(2,1)S(1)}, u32[]{:S(2)}, u32[]{:S(2)}) %collective-permute-start.3) | collective-permute-done | bytes 393248 | tf_op jit(solution)/shard_map/ppermute | solution.py:57
  38.5 5.1 %collective-permute-done.2 = bf16[3,128,512]{2,1,0:T(8,128)(2,1)S(1)} collective-permute-done((bf16[3,128,512]{2,1,0:T(8,128)(2,1)S(1)}, bf16[3,128,512]{2,1,0:T(8,128)(2,1)S(1)}, u32[]{:S(2)}, u32[]{:S(2)}) %collective-permute-start.2) | collective-permute-done | bytes 393248 | tf_op jit(solution)/shard_map/ppermute | solution.py:57
  49.2 4.9 %collective-permute-start.7 = (bf16[128,512]{1,0:T(8,128)(2,1)S(1)}, bf16[128,512]{1,0:T(8,128)(2,1)S(1)}, u32[]{:S(2)}, u32[]{:S(2)}) collective-permute-start(bf16[128,512]{1,0:T(8,128)(2,1)S(1)} %fusion.47), channel_id=1, source_target_pairs={{0,16},{8,24},{16,32},{24,40},{32,48},{40,56},{48,64},{56,72},{64,... | collective-permute-start | bytes 393224 | tf_op jit(solution)/shard_map/ppermute | solution.py:10
  63.6 3.6 %collective-permute-done.11 = bf16[3,128,512]{2,1,0:T(8,128)(2,1)S(1)} collective-permute-done((bf16[3,128,512]{2,1,0:T(8,128)(2,1)S(1)}, bf16[3,128,512]{2,1,0:T(8,128)(2,1)S(1)}, u32[]{:S(2)}, u32[]{:S(2)}) %collective-permute-start.11) | collective-permute-done | bytes 393248 | tf_op jit(solution)/shard_map/ppermute | solution.py:57
  67.4 8.5 %collective-permute-done.10 = bf16[3,128,512]{2,1,0:T(8,128)(2,1)S(1)} collective-permute-done((bf16[3,128,512]{2,1,0:T(8,128)(2,1)S(1)}, bf16[3,128,512]{2,1,0:T(8,128)(2,1)S(1)}, u32[]{:S(2)}, u32[]{:S(2)}) %collective-permute-start.10) | collective-permute-done | bytes 393248 | tf_op jit(solution)/shard_map/ppermute | solution.py:57
  78.4 3.7 %collective-permute-start.12 = (f32[128,512]{1,0:T(8,128)S(1)}, f32[128,512]{1,0:T(8,128)S(1)}, u32[]{:S(2)}, u32[]{:S(2)}) collective-permute-start(f32[128,512]{1,0:T(8,128)S(1)} %fusion.13), channel_id=1, source_target_pairs={{0,1},{1,0},{2,3},{3,2},{4,5},{5,4},{6,7},{7,6},{8,9},{9,8},{10,11... | collective-permute-start | bytes 786440 | tf_op jit(solution)/shard_map/ppermute | solution.py:58
  84.8 13.6 %collective-permute-start.13 = (bf16[128,512]{1,0:T(8,128)(2,1)S(1)}, bf16[128,512]{1,0:T(8,128)(2,1)S(1)}, u32[]{:S(2)}, u32[]{:S(2)}) collective-permute-start(bf16[128,512]{1,0:T(8,128)(2,1)S(1)} %fusion.46), channel_id=1, source_target_pairs={{0,32},{8,40},{16,48},{24,56},{32,64},{40,72},{48,80},{56,88},{64,... | collective-permute-start | bytes 393224 | tf_op jit(solution)/shard_map/ppermute | solution.py:10
  100.0 6.6 %collective-permute-done.13 = bf16[128,512]{1,0:T(8,128)(2,1)S(1)} collective-permute-done((bf16[128,512]{1,0:T(8,128)(2,1)S(1)}, bf16[128,512]{1,0:T(8,128)(2,1)S(1)}, u32[]{:S(2)}, u32[]{:S(2)}) %collective-permute-start.13) | collective-permute-done | bytes 131104 | tf_op jit(solution)/shard_map/ppermute | solution.py:10
  106.7 4.1 %collective-permute-start.17 = (bf16[3,128,512]{2,1,0:T(8,128)(2,1)S(1)}, bf16[3,128,512]{2,1,0:T(8,128)(2,1)S(1)}, u32[]{:S(2)}, u32[]{:S(2)}) collective-permute-start(bf16[3,128,512]{2,1,0:T(8,128)(2,1)S(1)} %pad_maximum_fusion.4), channel_id=1, source_target_pairs={{0,4},{1,5},{2,6},{3,7},{4,0},{5,1},{6,2},{7,3},{8,12},{9,13},{10,... | collective-permute-start | bytes 1179656 | tf_op jit(solution)/shard_map/ppermute | solution.py:57
  116.1 4.2 %collective-permute-done.17 = bf16[3,128,512]{2,1,0:T(8,128)(2,1)S(1)} collective-permute-done((bf16[3,128,512]{2,1,0:T(8,128)(2,1)S(1)}, bf16[3,128,512]{2,1,0:T(8,128)(2,1)S(1)}, u32[]{:S(2)}, u32[]{:S(2)}) %collective-permute-start.17) | collective-permute-done | bytes 393248 | tf_op jit(solution)/shard_map/ppermute | solution.py:57
  120.5 8.1 %collective-permute-done.16 = bf16[3,128,512]{2,1,0:T(8,128)(2,1)S(1)} collective-permute-done((bf16[3,128,512]{2,1,0:T(8,128)(2,1)S(1)}, bf16[3,128,512]{2,1,0:T(8,128)(2,1)S(1)}, u32[]{:S(2)}, u32[]{:S(2)}) %collective-permute-start.16) | collective-permute-done | bytes 393248 | tf_op jit(solution)/shard_map/ppermute | solution.py:57
  135.3 12.4 %collective-permute-start.19 = (bf16[128,512]{1,0:T(8,128)(2,1)S(1)}, bf16[128,512]{1,0:T(8,128)(2,1)S(1)}, u32[]{:S(2)}, u32[]{:S(2)}) collective-permute-start(bf16[128,512]{1,0:T(8,128)(2,1)S(1)} %fusion.45), channel_id=1, source_target_pairs={{0,64},{8,72},{16,80},{24,88},{32,96},{40,104},{48,112},{56,120},{... | collective-permute-start | bytes 393224 | tf_op jit(solution)/shard_map/ppermute | solution.py:10
  150.3 3.5 %collective-permute-start.23 = (bf16[3,128,512]{2,1,0:T(8,128)(2,1)S(1)}, bf16[3,128,512]{2,1,0:T(8,128)(2,1)S(1)}, u32[]{:S(2)}, u32[]{:S(2)}) collective-permute-start(bf16[3,128,512]{2,1,0:T(8,128)(2,1)S(1)} %pad_maximum_fusion.5), channel_id=1, source_target_pairs={{0,4},{1,5},{2,6},{3,7},{4,0},{5,1},{6,2},{7,3},{8,12},{9,13},{10,... | collective-permute-start | bytes 1179656 | tf_op jit(solution)/shard_map/ppermute | solution.py:57
  153.8 3.5 %collective-permute-start.22 = (bf16[3,128,512]{2,1,0:T(8,128)(2,1)S(1)}, bf16[3,128,512]{2,1,0:T(8,128)(2,1)S(1)}, u32[]{:S(2)}, u32[]{:S(2)}) collective-permute-start(bf16[3,128,512]{2,1,0:T(8,128)(2,1)S(1)} %pad_maximum_fusion.5), channel_id=1, source_target_pairs={{0,6},{1,7},{2,0},{3,1},{4,2},{5,3},{6,4},{7,5},{8,14},{9,15},{10,... | collective-permute-start | bytes 1179656 | tf_op jit(solution)/shard_map/ppermute | solution.py:57
  159.3 3.8 %collective-permute-done.23 = bf16[3,128,512]{2,1,0:T(8,128)(2,1)S(1)} collective-permute-done((bf16[3,128,512]{2,1,0:T(8,128)(2,1)S(1)}, bf16[3,128,512]{2,1,0:T(8,128)(2,1)S(1)}, u32[]{:S(2)}, u32[]{:S(2)}) %collective-permute-start.23) | collective-permute-done | bytes 393248 | tf_op jit(solution)/shard_map/ppermute | solution.py:57
  163.3 8.5 %collective-permute-done.22 = bf16[3,128,512]{2,1,0:T(8,128)(2,1)S(1)} collective-permute-done((bf16[3,128,512]{2,1,0:T(8,128)(2,1)S(1)}, bf16[3,128,512]{2,1,0:T(8,128)(2,1)S(1)}, u32[]{:S(2)}, u32[]{:S(2)}) %collective-permute-start.22) | collective-permute-done | bytes 393248 | tf_op jit(solution)/shard_map/ppermute | solution.py:57
  172.6 3.5 %collective-permute-start.24 = (f32[128,512]{1,0:T(8,128)S(1)}, f32[128,512]{1,0:T(8,128)S(1)}, u32[]{:S(2)}, u32[]{:S(2)}) collective-permute-start(f32[128,512]{1,0:T(8,128)S(1)} %fusion.27), channel_id=1, source_target_pairs={{0,1},{1,0},{2,3},{3,2},{4,5},{5,4},{6,7},{7,6},{8,9},{9,8},{10,11... | collective-permute-start | bytes 786440 | tf_op jit(solution)/shard_map/ppermute | solution.py:58
  178.8 5.8 %collective-permute-start.25 = (bf16[128,512]{1,0:T(8,128)(2,1)S(1)}, bf16[128,512]{1,0:T(8,128)(2,1)S(1)}, u32[]{:S(2)}, u32[]{:S(2)}) collective-permute-start(bf16[128,512]{1,0:T(8,128)(2,1)S(1)} %fusion.44), channel_id=1, source_target_pairs={{0,128},{8,136},{16,144},{24,152},{32,160},{40,168},{48,176},{56,1... | collective-permute-start | bytes 393224 | tf_op jit(solution)/shard_map/ppermute | solution.py:10
  184.5 4.4 %collective-permute-done.26 = bf16[128,512]{1,0:T(8,128)(2,1)S(1)} collective-permute-done((bf16[128,512]{1,0:T(8,128)(2,1)S(1)}, bf16[128,512]{1,0:T(8,128)(2,1)S(1)}, u32[]{:S(2)}, u32[]{:S(2)}) %collective-permute-start.26) | collective-permute-done | bytes 131104 | tf_op jit(solution)/shard_map/ppermute | solution.py:10
  189.0 3.4 %collective-permute-start.29 = (bf16[3,128,512]{2,1,0:T(8,128)(2,1)S(1)}, bf16[3,128,512]{2,1,0:T(8,128)(2,1)S(1)}, u32[]{:S(2)}, u32[]{:S(2)}) collective-permute-start(bf16[3,128,512]{2,1,0:T(8,128)(2,1)S(1)} %pad_maximum_fusion.6), channel_id=1, source_target_pairs={{0,4},{1,5},{2,6},{3,7},{4,0},{5,1},{6,2},{7,3},{8,12},{9,13},{10,... | collective-permute-start | bytes 1179656 | tf_op jit(solution)/shard_map/ppermute | solution.py:57
  192.4 3.7 %collective-permute-start.28 = (bf16[3,128,512]{2,1,0:T(8,128)(2,1)S(1)}, bf16[3,128,512]{2,1,0:T(8,128)(2,1)S(1)}, u32[]{:S(2)}, u32[]{:S(2)}) collective-permute-start(bf16[3,128,512]{2,1,0:T(8,128)(2,1)S(1)} %pad_maximum_fusion.6), channel_id=1, source_target_pairs={{0,6},{1,7},{2,0},{3,1},{4,2},{5,3},{6,4},{7,5},{8,14},{9,15},{10,... | collective-permute-start | bytes 1179656 | tf_op jit(solution)/shard_map/ppermute | solution.py:57
  198.0 4.1 %collective-permute-done.29 = bf16[3,128,512]{2,1,0:T(8,128)(2,1)S(1)} collective-permute-done((bf16[3,128,512]{2,1,0:T(8,128)(2,1)S(1)}, bf16[3,128,512]{2,1,0:T(8,128)(2,1)S(1)}, u32[]{:S(2)}, u32[]{:S(2)}) %collective-permute-start.29) | collective-permute-done | bytes 393248 | tf_op jit(solution)/shard_map/ppermute | solution.py:57
  202.4 8.2 %collective-permute-done.28 = bf16[3,128,512]{2,1,0:T(8,128)(2,1)S(1)} collective-permute-done((bf16[3,128,512]{2,1,0:T(8,128)(2,1)S(1)}, bf16[3,128,512]{2,1,0:T(8,128)(2,1)S(1)}, u32[]{:S(2)}, u32[]{:S(2)}) %collective-permute-start.28) | collective-permute-done | bytes 393248 | tf_op jit(solution)/shard_map/ppermute | solution.py:57
  217.5 10.2 %collective-permute-start.31 = (bf16[128,512]{1,0:T(8,128)(2,1)S(1)}, bf16[128,512]{1,0:T(8,128)(2,1)S(1)}, u32[]{:S(2)}, u32[]{:S(2)}) collective-permute-start(bf16[128,512]{1,0:T(8,128)(2,1)S(1)} %fusion.43), channel_id=1, source_target_pairs={{0,256},{8,264},{16,272},{24,280},{32,288},{40,296},{48,304},{56,3... | collective-permute-start | bytes 393224 | tf_op jit(solution)/shard_map/ppermute | solution.py:10
  235.5 3.7 %collective-permute-start.34 = (bf16[3,128,512]{2,1,0:T(8,128)(2,1)S(1)}, bf16[3,128,512]{2,1,0:T(8,128)(2,1)S(1)}, u32[]{:S(2)}, u32[]{:S(2)}) collective-permute-start(bf16[3,128,512]{2,1,0:T(8,128)(2,1)S(1)} %pad_maximum_fusion.7), channel_id=1, source_target_pairs={{0,6},{1,7},{2,0},{3,1},{4,2},{5,3},{6,4},{7,5},{8,14},{9,15},{10,... | collective-permute-start | bytes 1179656 | tf_op jit(solution)/shard_map/ppermute | solution.py:57
  241.1 4.2 %collective-permute-done.35 = bf16[3,128,512]{2,1,0:T(8,128)(2,1)S(1)} collective-permute-done((bf16[3,128,512]{2,1,0:T(8,128)(2,1)S(1)}, bf16[3,128,512]{2,1,0:T(8,128)(2,1)S(1)}, u32[]{:S(2)}, u32[]{:S(2)}) %collective-permute-start.35) | collective-permute-done | bytes 393248 | tf_op jit(solution)/shard_map/ppermute | solution.py:57
  245.5 8.2 %collective-permute-done.34 = bf16[3,128,512]{2,1,0:T(8,128)(2,1)S(1)} collective-permute-done((bf16[3,128,512]{2,1,0:T(8,128)(2,1)S(1)}, bf16[3,128,512]{2,1,0:T(8,128)(2,1)S(1)}, u32[]{:S(2)}, u32[]{:S(2)}) %collective-permute-start.34) | collective-permute-done | bytes 393248 | tf_op jit(solution)/shard_map/ppermute | solution.py:57
  254.8 3.3 %collective-permute-start.36 = (f32[128,512]{1,0:T(8,128)S(1)}, f32[128,512]{1,0:T(8,128)S(1)}, u32[]{:S(2)}, u32[]{:S(2)}) collective-permute-start(f32[128,512]{1,0:T(8,128)S(1)} %fusion.41), channel_id=1, source_target_pairs={{0,1},{1,0},{2,3},{3,2},{4,5},{5,4},{6,7},{7,6},{8,9},{9,8},{10,11... | collective-permute-start | bytes 786440 | tf_op jit(solution)/shard_map/ppermute | solution.py:58
  (116 shorter events, 77.4 us)
Async XLA Ops:
  4.0 29.9 %collective-permute-start.5 = (bf16[6,128,4,3,128]{4,1,3,2,0:T(8,128)(2,1)S(1)}, bf16[6,128,4,3,128]{4,1,3,2,0:T(8,128)(2,1)S(1)}, u32[]{:S(2)}, u32[]{:S(2)}) collective-permute-start(bf16[6,128,4,3,128]{4,1,3,2,0:T(8,128)(2,1)S(1)} %pad_maximum_fusion.1), channel_id=1, source_target_pairs={{0,1},{1,0},{2,3},{3,2},{4,5},{5,4},{6,7},{7,6},{8,9},{9,8},{10,11... | collective-permute-start | bytes 7077896 | tf_op jit(solution)/shard_map/ppermute | solution.py:39
  12.8 7.0 %collective-permute-start.1 = (bf16[128,512]{1,0:T(8,128)(2,1)S(1)}, bf16[128,512]{1,0:T(8,128)(2,1)S(1)}, u32[]{:S(2)}, u32[]{:S(2)}) collective-permute-start(bf16[128,512]{1,0:T(8,128)(2,1)S(1)} %bitcast.515), channel_id=1, source_target_pairs={{8,0},{16,8},{24,16},{32,24},{40,32},{48,40},{56,48},{64,56},{72,6... | collective-permute-start | bytes 393224 | tf_op jit(solution)/shard_map/ppermute | solution.py:10
  14.1 6.6 %collective-permute-start = (bf16[128,512]{1,0:T(8,128)(2,1)S(1)}, bf16[128,512]{1,0:T(8,128)(2,1)S(1)}, u32[]{:S(2)}, u32[]{:S(2)}) collective-permute-start(bf16[128,512]{1,0:T(8,128)(2,1)S(1)} %bitcast.516), channel_id=1, source_target_pairs={{0,8},{8,16},{16,24},{24,32},{32,40},{40,48},{48,56},{56,64},{64,7... | collective-permute-start | bytes 393224 | tf_op jit(solution)/shard_map/ppermute | solution.py:10
  20.8 12.9 %collective-permute-start.4 = (bf16[3,128,512]{2,1,0:T(8,128)(2,1)S(1)}, bf16[3,128,512]{2,1,0:T(8,128)(2,1)S(1)}, u32[]{:S(2)}, u32[]{:S(2)}) collective-permute-start(bf16[3,128,512]{2,1,0:T(8,128)(2,1)S(1)} %pad_maximum_fusion.2), channel_id=1, source_target_pairs={{0,4},{1,5},{2,6},{3,7},{4,0},{5,1},{6,2},{7,3},{8,12},{9,13},{10,... | collective-permute-start | bytes 1179656 | tf_op jit(solution)/shard_map/ppermute | solution.py:57
  23.3 15.0 %collective-permute-start.3 = (bf16[3,128,512]{2,1,0:T(8,128)(2,1)S(1)}, bf16[3,128,512]{2,1,0:T(8,128)(2,1)S(1)}, u32[]{:S(2)}, u32[]{:S(2)}) collective-permute-start(bf16[3,128,512]{2,1,0:T(8,128)(2,1)S(1)} %pad_maximum_fusion.2), channel_id=1, source_target_pairs={{0,6},{1,7},{2,0},{3,1},{4,2},{5,3},{6,4},{7,5},{8,14},{9,15},{10,... | collective-permute-start | bytes 1179656 | tf_op jit(solution)/shard_map/ppermute | solution.py:57
  25.2 18.4 %collective-permute-start.2 = (bf16[3,128,512]{2,1,0:T(8,128)(2,1)S(1)}, bf16[3,128,512]{2,1,0:T(8,128)(2,1)S(1)}, u32[]{:S(2)}, u32[]{:S(2)}) collective-permute-start(bf16[3,128,512]{2,1,0:T(8,128)(2,1)S(1)} %pad_maximum_fusion.2), channel_id=1, source_target_pairs={{0,2},{1,3},{2,4},{3,5},{4,6},{5,7},{6,0},{7,1},{8,10},{9,11},{10,... | collective-permute-start | bytes 1179656 | tf_op jit(solution)/shard_map/ppermute | solution.py:57
  47.9 7.5 %collective-permute-start.8 = (bf16[128,512]{1,0:T(8,128)(2,1)S(1)}, bf16[128,512]{1,0:T(8,128)(2,1)S(1)}, u32[]{:S(2)}, u32[]{:S(2)}) collective-permute-start(bf16[128,512]{1,0:T(8,128)(2,1)S(1)} %fusion.47), channel_id=1, source_target_pairs={{16,0},{24,8},{32,16},{40,24},{48,32},{56,40},{64,48},{72,56},{80,... | collective-permute-start | bytes 393224 | tf_op jit(solution)/shard_map/ppermute | solution.py:10
  49.2 7.1 %collective-permute-start.7 = (bf16[128,512]{1,0:T(8,128)(2,1)S(1)}, bf16[128,512]{1,0:T(8,128)(2,1)S(1)}, u32[]{:S(2)}, u32[]{:S(2)}) collective-permute-start(bf16[128,512]{1,0:T(8,128)(2,1)S(1)} %fusion.47), channel_id=1, source_target_pairs={{0,16},{8,24},{16,32},{24,40},{32,48},{40,56},{48,64},{56,72},{64,... | collective-permute-start | bytes 393224 | tf_op jit(solution)/shard_map/ppermute | solution.py:10
  56.3 10.9 %collective-permute-start.11 = (bf16[3,128,512]{2,1,0:T(8,128)(2,1)S(1)}, bf16[3,128,512]{2,1,0:T(8,128)(2,1)S(1)}, u32[]{:S(2)}, u32[]{:S(2)}) collective-permute-start(bf16[3,128,512]{2,1,0:T(8,128)(2,1)S(1)} %pad_maximum_fusion.3), channel_id=1, source_target_pairs={{0,4},{1,5},{2,6},{3,7},{4,0},{5,1},{6,2},{7,3},{8,12},{9,13},{10,... | collective-permute-start | bytes 1179656 | tf_op jit(solution)/shard_map/ppermute | solution.py:57
  58.3 17.7 %collective-permute-start.10 = (bf16[3,128,512]{2,1,0:T(8,128)(2,1)S(1)}, bf16[3,128,512]{2,1,0:T(8,128)(2,1)S(1)}, u32[]{:S(2)}, u32[]{:S(2)}) collective-permute-start(bf16[3,128,512]{2,1,0:T(8,128)(2,1)S(1)} %pad_maximum_fusion.3), channel_id=1, source_target_pairs={{0,6},{1,7},{2,0},{3,1},{4,2},{5,3},{6,4},{7,5},{8,14},{9,15},{10,... | collective-permute-start | bytes 1179656 | tf_op jit(solution)/shard_map/ppermute | solution.py:57
  61.5 16.4 %collective-permute-start.9 = (bf16[3,128,512]{2,1,0:T(8,128)(2,1)S(1)}, bf16[3,128,512]{2,1,0:T(8,128)(2,1)S(1)}, u32[]{:S(2)}, u32[]{:S(2)}) collective-permute-start(bf16[3,128,512]{2,1,0:T(8,128)(2,1)S(1)} %pad_maximum_fusion.3), channel_id=1, source_target_pairs={{0,2},{1,3},{2,4},{3,5},{4,6},{5,7},{6,0},{7,1},{8,10},{9,11},{10,... | collective-permute-start | bytes 1179656 | tf_op jit(solution)/shard_map/ppermute | solution.py:57
  78.4 4.8 %collective-permute-start.12 = (f32[128,512]{1,0:T(8,128)S(1)}, f32[128,512]{1,0:T(8,128)S(1)}, u32[]{:S(2)}, u32[]{:S(2)}) collective-permute-start(f32[128,512]{1,0:T(8,128)S(1)} %fusion.13), channel_id=1, source_target_pairs={{0,1},{1,0},{2,3},{3,2},{4,5},{5,4},{6,7},{7,6},{8,9},{9,8},{10,11... | collective-permute-start | bytes 786440 | tf_op jit(solution)/shard_map/ppermute | solution.py:58
  83.5 16.5 %collective-permute-start.14 = (bf16[128,512]{1,0:T(8,128)(2,1)S(1)}, bf16[128,512]{1,0:T(8,128)(2,1)S(1)}, u32[]{:S(2)}, u32[]{:S(2)}) collective-permute-start(bf16[128,512]{1,0:T(8,128)(2,1)S(1)} %fusion.46), channel_id=1, source_target_pairs={{32,0},{40,8},{48,16},{56,24},{64,32},{72,40},{80,48},{88,56},{96,... | collective-permute-start | bytes 393224 | tf_op jit(solution)/shard_map/ppermute | solution.py:10
  84.8 21.8 %collective-permute-start.13 = (bf16[128,512]{1,0:T(8,128)(2,1)S(1)}, bf16[128,512]{1,0:T(8,128)(2,1)S(1)}, u32[]{:S(2)}, u32[]{:S(2)}) collective-permute-start(bf16[128,512]{1,0:T(8,128)(2,1)S(1)} %fusion.46), channel_id=1, source_target_pairs={{0,32},{8,40},{16,48},{24,56},{32,64},{40,72},{48,80},{56,88},{64,... | collective-permute-start | bytes 393224 | tf_op jit(solution)/shard_map/ppermute | solution.py:10
  106.7 13.6 %collective-permute-start.17 = (bf16[3,128,512]{2,1,0:T(8,128)(2,1)S(1)}, bf16[3,128,512]{2,1,0:T(8,128)(2,1)S(1)}, u32[]{:S(2)}, u32[]{:S(2)}) collective-permute-start(bf16[3,128,512]{2,1,0:T(8,128)(2,1)S(1)} %pad_maximum_fusion.4), channel_id=1, source_target_pairs={{0,4},{1,5},{2,6},{3,7},{4,0},{5,1},{6,2},{7,3},{8,12},{9,13},{10,... | collective-permute-start | bytes 1179656 | tf_op jit(solution)/shard_map/ppermute | solution.py:57
  110.8 17.9 %collective-permute-start.16 = (bf16[3,128,512]{2,1,0:T(8,128)(2,1)S(1)}, bf16[3,128,512]{2,1,0:T(8,128)(2,1)S(1)}, u32[]{:S(2)}, u32[]{:S(2)}) collective-permute-start(bf16[3,128,512]{2,1,0:T(8,128)(2,1)S(1)} %pad_maximum_fusion.4), channel_id=1, source_target_pairs={{0,6},{1,7},{2,0},{3,1},{4,2},{5,3},{6,4},{7,5},{8,14},{9,15},{10,... | collective-permute-start | bytes 1179656 | tf_op jit(solution)/shard_map/ppermute | solution.py:57
  114.0 15.1 %collective-permute-start.15 = (bf16[3,128,512]{2,1,0:T(8,128)(2,1)S(1)}, bf16[3,128,512]{2,1,0:T(8,128)(2,1)S(1)}, u32[]{:S(2)}, u32[]{:S(2)}) collective-permute-start(bf16[3,128,512]{2,1,0:T(8,128)(2,1)S(1)} %pad_maximum_fusion.4), channel_id=1, source_target_pairs={{0,2},{1,3},{2,4},{3,5},{4,6},{5,7},{6,0},{7,1},{8,10},{9,11},{10,... | collective-permute-start | bytes 1179656 | tf_op jit(solution)/shard_map/ppermute | solution.py:57
  134.0 15.4 %collective-permute-start.20 = (bf16[128,512]{1,0:T(8,128)(2,1)S(1)}, bf16[128,512]{1,0:T(8,128)(2,1)S(1)}, u32[]{:S(2)}, u32[]{:S(2)}) collective-permute-start(bf16[128,512]{1,0:T(8,128)(2,1)S(1)} %fusion.45), channel_id=1, source_target_pairs={{64,0},{72,8},{80,16},{88,24},{96,32},{104,40},{112,48},{120,56},{... | collective-permute-start | bytes 393224 | tf_op jit(solution)/shard_map/ppermute | solution.py:10
  135.3 14.9 %collective-permute-start.19 = (bf16[128,512]{1,0:T(8,128)(2,1)S(1)}, bf16[128,512]{1,0:T(8,128)(2,1)S(1)}, u32[]{:S(2)}, u32[]{:S(2)}) collective-permute-start(bf16[128,512]{1,0:T(8,128)(2,1)S(1)} %fusion.45), channel_id=1, source_target_pairs={{0,64},{8,72},{16,80},{24,88},{32,96},{40,104},{48,112},{56,120},{... | collective-permute-start | bytes 393224 | tf_op jit(solution)/shard_map/ppermute | solution.py:10
  150.3 12.8 %collective-permute-start.23 = (bf16[3,128,512]{2,1,0:T(8,128)(2,1)S(1)}, bf16[3,128,512]{2,1,0:T(8,128)(2,1)S(1)}, u32[]{:S(2)}, u32[]{:S(2)}) collective-permute-start(bf16[3,128,512]{2,1,0:T(8,128)(2,1)S(1)} %pad_maximum_fusion.5), channel_id=1, source_target_pairs={{0,4},{1,5},{2,6},{3,7},{4,0},{5,1},{6,2},{7,3},{8,12},{9,13},{10,... | collective-permute-start | bytes 1179656 | tf_op jit(solution)/shard_map/ppermute | solution.py:57
  153.8 18.0 %collective-permute-start.22 = (bf16[3,128,512]{2,1,0:T(8,128)(2,1)S(1)}, bf16[3,128,512]{2,1,0:T(8,128)(2,1)S(1)}, u32[]{:S(2)}, u32[]{:S(2)}) collective-permute-start(bf16[3,128,512]{2,1,0:T(8,128)(2,1)S(1)} %pad_maximum_fusion.5), channel_id=1, source_target_pairs={{0,6},{1,7},{2,0},{3,1},{4,2},{5,3},{6,4},{7,5},{8,14},{9,15},{10,... | collective-permute-start | bytes 1179656 | tf_op jit(solution)/shard_map/ppermute | solution.py:57
  157.3 14.8 %collective-permute-start.21 = (bf16[3,128,512]{2,1,0:T(8,128)(2,1)S(1)}, bf16[3,128,512]{2,1,0:T(8,128)(2,1)S(1)}, u32[]{:S(2)}, u32[]{:S(2)}) collective-permute-start(bf16[3,128,512]{2,1,0:T(8,128)(2,1)S(1)} %pad_maximum_fusion.5), channel_id=1, source_target_pairs={{0,2},{1,3},{2,4},{3,5},{4,6},{5,7},{6,0},{7,1},{8,10},{9,11},{10,... | collective-permute-start | bytes 1179656 | tf_op jit(solution)/shard_map/ppermute | solution.py:57
  177.5 11.5 %collective-permute-start.26 = (bf16[128,512]{1,0:T(8,128)(2,1)S(1)}, bf16[128,512]{1,0:T(8,128)(2,1)S(1)}, u32[]{:S(2)}, u32[]{:S(2)}) collective-permute-start(bf16[128,512]{1,0:T(8,128)(2,1)S(1)} %fusion.44), channel_id=1, source_target_pairs={{128,0},{136,8},{144,16},{152,24},{160,32},{168,40},{176,48},{184,... | collective-permute-start | bytes 393224 | tf_op jit(solution)/shard_map/ppermute | solution.py:10
  178.8 10.2 %collective-permute-start.25 = (bf16[128,512]{1,0:T(8,128)(2,1)S(1)}, bf16[128,512]{1,0:T(8,128)(2,1)S(1)}, u32[]{:S(2)}, u32[]{:S(2)}) collective-permute-start(bf16[128,512]{1,0:T(8,128)(2,1)S(1)} %fusion.44), channel_id=1, source_target_pairs={{0,128},{8,136},{16,144},{24,152},{32,160},{40,168},{48,176},{56,1... | collective-permute-start | bytes 393224 | tf_op jit(solution)/shard_map/ppermute | solution.py:10
  189.0 13.1 %collective-permute-start.29 = (bf16[3,128,512]{2,1,0:T(8,128)(2,1)S(1)}, bf16[3,128,512]{2,1,0:T(8,128)(2,1)S(1)}, u32[]{:S(2)}, u32[]{:S(2)}) collective-permute-start(bf16[3,128,512]{2,1,0:T(8,128)(2,1)S(1)} %pad_maximum_fusion.6), channel_id=1, source_target_pairs={{0,4},{1,5},{2,6},{3,7},{4,0},{5,1},{6,2},{7,3},{8,12},{9,13},{10,... | collective-permute-start | bytes 1179656 | tf_op jit(solution)/shard_map/ppermute | solution.py:57
  192.4 18.2 %collective-permute-start.28 = (bf16[3,128,512]{2,1,0:T(8,128)(2,1)S(1)}, bf16[3,128,512]{2,1,0:T(8,128)(2,1)S(1)}, u32[]{:S(2)}, u32[]{:S(2)}) collective-permute-start(bf16[3,128,512]{2,1,0:T(8,128)(2,1)S(1)} %pad_maximum_fusion.6), channel_id=1, source_target_pairs={{0,6},{1,7},{2,0},{3,1},{4,2},{5,3},{6,4},{7,5},{8,14},{9,15},{10,... | collective-permute-start | bytes 1179656 | tf_op jit(solution)/shard_map/ppermute | solution.py:57
  196.1 15.0 %collective-permute-start.27 = (bf16[3,128,512]{2,1,0:T(8,128)(2,1)S(1)}, bf16[3,128,512]{2,1,0:T(8,128)(2,1)S(1)}, u32[]{:S(2)}, u32[]{:S(2)}) collective-permute-start(bf16[3,128,512]{2,1,0:T(8,128)(2,1)S(1)} %pad_maximum_fusion.6), channel_id=1, source_target_pairs={{0,2},{1,3},{2,4},{3,5},{4,6},{5,7},{6,0},{7,1},{8,10},{9,11},{10,... | collective-permute-start | bytes 1179656 | tf_op jit(solution)/shard_map/ppermute | solution.py:57
  216.2 13.1 %collective-permute-start.32 = (bf16[128,512]{1,0:T(8,128)(2,1)S(1)}, bf16[128,512]{1,0:T(8,128)(2,1)S(1)}, u32[]{:S(2)}, u32[]{:S(2)}) collective-permute-start(bf16[128,512]{1,0:T(8,128)(2,1)S(1)} %fusion.43), channel_id=1, source_target_pairs={{256,0},{264,8},{272,16},{280,24},{288,32},{296,40},{304,48},{312,... | collective-permute-start | bytes 393224 | tf_op jit(solution)/shard_map/ppermute | solution.py:10
  217.5 14.9 %collective-permute-start.31 = (bf16[128,512]{1,0:T(8,128)(2,1)S(1)}, bf16[128,512]{1,0:T(8,128)(2,1)S(1)}, u32[]{:S(2)}, u32[]{:S(2)}) collective-permute-start(bf16[128,512]{1,0:T(8,128)(2,1)S(1)} %fusion.43), channel_id=1, source_target_pairs={{0,256},{8,264},{16,272},{24,280},{32,288},{40,296},{48,304},{56,3... | collective-permute-start | bytes 393224 | tf_op jit(solution)/shard_map/ppermute | solution.py:10
  232.4 12.8 %collective-permute-start.35 = (bf16[3,128,512]{2,1,0:T(8,128)(2,1)S(1)}, bf16[3,128,512]{2,1,0:T(8,128)(2,1)S(1)}, u32[]{:S(2)}, u32[]{:S(2)}) collective-permute-start(bf16[3,128,512]{2,1,0:T(8,128)(2,1)S(1)} %pad_maximum_fusion.7), channel_id=1, source_target_pairs={{0,4},{1,5},{2,6},{3,7},{4,0},{5,1},{6,2},{7,3},{8,12},{9,13},{10,... | collective-permute-start | bytes 1179656 | tf_op jit(solution)/shard_map/ppermute | solution.py:57
  235.5 18.2 %collective-permute-start.34 = (bf16[3,128,512]{2,1,0:T(8,128)(2,1)S(1)}, bf16[3,128,512]{2,1,0:T(8,128)(2,1)S(1)}, u32[]{:S(2)}, u32[]{:S(2)}) collective-permute-start(bf16[3,128,512]{2,1,0:T(8,128)(2,1)S(1)} %pad_maximum_fusion.7), channel_id=1, source_target_pairs={{0,6},{1,7},{2,0},{3,1},{4,2},{5,3},{6,4},{7,5},{8,14},{9,15},{10,... | collective-permute-start | bytes 1179656 | tf_op jit(solution)/shard_map/ppermute | solution.py:57
  239.1 15.2 %collective-permute-start.33 = (bf16[3,128,512]{2,1,0:T(8,128)(2,1)S(1)}, bf16[3,128,512]{2,1,0:T(8,128)(2,1)S(1)}, u32[]{:S(2)}, u32[]{:S(2)}) collective-permute-start(bf16[3,128,512]{2,1,0:T(8,128)(2,1)S(1)} %pad_maximum_fusion.7), channel_id=1, source_target_pairs={{0,2},{1,3},{2,4},{3,5},{4,6},{5,7},{6,0},{7,1},{8,10},{9,11},{10,... | collective-permute-start | bytes 1179656 | tf_op jit(solution)/shard_map/ppermute | solution.py:57
  (8 other events, 34.9 us)

commit v11 on v10

--- a/solution.py
+++ b/solution.py
@@ -36,7 +36,10 @@
 
     mine = pick(core)
     swap = [(2 * c + b, 2 * c + 1 - b) for c in range(chips) for b in range(2)]
-    theirs = lax.ppermute(pick(1 - core), "cross", swap)
+    current = right_side[0]
+    first = (shifted(current, "chain", 1), shifted(current, "chain", -1))
+    first, given_factors = lax.optimization_barrier((first, pick(1 - core)))
+    theirs = lax.ppermute(given_factors, "cross", swap)
 
     def same_core(offset):
         return [(2 * c + b, 2 * ((c + offset) % chips) + b) for c in range(chips) for b in range(2)]
@@ -48,11 +51,13 @@
             total = term if total is None else total + term
         return total
 
-    current = right_side[0]
     for level in range(levels):
         dist = 2**level
-        lower = shifted(current, "chain", dist)
-        upper = shifted(current, "chain", -dist)
+        if level == 0:
+            lower, upper = first
+        else:
+            lower = shifted(current, "chain", dist)
+            upper = shifted(current, "chain", -dist)
         own = jnp.stack([current, lower, upper])
         pieces = [own] + [lax.ppermute(own, "cross", same_core(-off)) for off in OFFSETS[1:]]
         given = lax.ppermute(partial(theirs[level], pieces), "cross", swap)

time: 261 us -> 259 us (level)
  waiting for transfers between devices: 106 us -> 101 us
    ppermute x18, starting transfers between devices: 50.3 us -> 54.6 us  [body(): lax.ppermute(own, 'cross', same_core(-off))]
    ppermute x18, waiting for transfers between devices: 78.3 us -> 75.2 us  [body(): lax.ppermute(own, 'cross', same_core(-off))]
    ppermute x1, starting transfers between devices: 8.79 us -> 5.75 us  [body(): theirs = lax.ppermute(given_factors, 'cross', swap)]
  transfers between devices with their start and end apart: 37 -> 37, of which waited for: 34 -> 32; matrix products, arithmetic and copies ran while one was open for 3% -> 4% of each run, Pallas kernels for 0% -> 0%
where the time goes in v11:
time: 259 us; the launch traced here: 258 us
  starting transfers between devices  139 us (54%)
  waiting for transfers between devices  101 us (39%)
  matrix products  11.6 us (4%)
  local copies, waits for them, and re-layouts  2.8 us (1%)
    ppermute x18, waiting for transfers between devices, body(): lax.ppermute(own, 'cross', same_core(-off))  75.2 us
    ppermute x12, starting transfers between devices, shifted(): lax.ppermute(value, axis, [(source, source + steps) for source in range(i...  60 us
    ppermute x18, starting transfers between devices, body(): lax.ppermute(own, 'cross', same_core(-off))  54.6 us
    ppermute x12, waiting for transfers between devices, shifted(): lax.ppermute(value, axis, [(source, source + steps) for source in range(i...  22.8 us
    ppermute x6, starting transfers between devices, body(): given = lax.ppermute(partial(theirs[level], pieces), 'cross', swap)  18.9 us
    dot_general x48, matrix products, partial(): jnp.einsum('ibk,bkr->ir', mat[:, j], piece, preferred_element_type=jnp.fl...  11.6 us
    ppermute x1, starting transfers between devices, body(): theirs = lax.ppermute(given_factors, 'cross', swap)  5.75 us
  transfers between devices with their start and end apart: 37, of which 32 were waited for; matrix products, arithmetic and copies ran while one was open for 4% of the time, Pallas kernels for 0%

profile of v11, /device:TPU:1, one launch (start us, length us, event | category | flops | bytes accessed | tf_op | source)
XLA Modules:
  0.0 257.7 jit_solution(16277110889122728829)
XLA Ops:
  0.0 5.1 %collective-permute-start = (bf16[128,512]{1,0:T(8,128)(2,1)}, bf16[128,512]{1,0:T(8,128)(2,1)S(1)}, u32[]{:S(2)}, u32[]{:S(2)}) collective-permute-start(bf16[128,512]{1,0:T(8,128)(2,1)} %bitcast.545), channel_id=1, source_target_pairs={{0,8},{8,16},{16,24},{24,32},{32,40},{40,48},{48,56},{56,64},{64,7... | collective-permute-start | bytes 393224 | tf_op jit(solution)/shard_map/ppermute | solution.py:10
  11.7 5.8 %collective-permute-start.5 = (bf16[6,128,4,3,128]{4,1,3,2,0:T(8,128)(2,1)S(1)}, bf16[6,128,4,3,128]{4,1,3,2,0:T(8,128)(2,1)S(1)}, u32[]{:S(2)}, u32[]{:S(2)}) collective-permute-start(bf16[6,128,4,3,128]{4,1,3,2,0:T(8,128)(2,1)S(1)} %pad_maximum_fusion.1), channel_id=1, source_target_pairs={{0,1},{1,0},{2,3},{3,2},{4,5},{5,4},{6,7},{7,6},{8,9},{9,8},{10,11... | collective-permute-start | bytes 7077896 | tf_op jit(solution)/shard_map/ppermute | solution.py:42
  27.7 5.4 %collective-permute-done.4 = bf16[3,128,512]{2,1,0:T(8,128)(2,1)S(1)} collective-permute-done((bf16[3,128,512]{2,1,0:T(8,128)(2,1)S(1)}, bf16[3,128,512]{2,1,0:T(8,128)(2,1)S(1)}, u32[]{:S(2)}, u32[]{:S(2)}) %collective-permute-start.4) | collective-permute-done | bytes 393248 | tf_op jit(solution)/shard_map/ppermute | solution.py:62
  33.4 6.5 %collective-permute-done.3 = bf16[3,128,512]{2,1,0:T(8,128)(2,1)S(1)} collective-permute-done((bf16[3,128,512]{2,1,0:T(8,128)(2,1)S(1)}, bf16[3,128,512]{2,1,0:T(8,128)(2,1)S(1)}, u32[]{:S(2)}, u32[]{:S(2)}) %collective-permute-start.3) | collective-permute-done | bytes 393248 | tf_op jit(solution)/shard_map/ppermute | solution.py:62
  47.4 6.3 %collective-permute-start.7 = (bf16[128,512]{1,0:T(8,128)(2,1)S(1)}, bf16[128,512]{1,0:T(8,128)(2,1)S(1)}, u32[]{:S(2)}, u32[]{:S(2)}) collective-permute-start(bf16[128,512]{1,0:T(8,128)(2,1)S(1)} %fusion.47), channel_id=1, source_target_pairs={{0,16},{8,24},{16,32},{24,40},{32,48},{40,56},{48,64},{56,72},{64,... | collective-permute-start | bytes 393224 | tf_op jit(solution)/shard_map/ppermute | solution.py:10
  56.2 4.3 %collective-permute-start.11 = (bf16[3,128,512]{2,1,0:T(8,128)(2,1)S(1)}, bf16[3,128,512]{2,1,0:T(8,128)(2,1)S(1)}, u32[]{:S(2)}, u32[]{:S(2)}) collective-permute-start(bf16[3,128,512]{2,1,0:T(8,128)(2,1)S(1)} %pad_maximum_fusion.3), channel_id=1, source_target_pairs={{0,4},{1,5},{2,6},{3,7},{4,0},{5,1},{6,2},{7,3},{8,12},{9,13},{10,... | collective-permute-start | bytes 1179656 | tf_op jit(solution)/shard_map/ppermute | solution.py:62
  69.2 8.8 %collective-permute-done.10 = bf16[3,128,512]{2,1,0:T(8,128)(2,1)S(1)} collective-permute-done((bf16[3,128,512]{2,1,0:T(8,128)(2,1)S(1)}, bf16[3,128,512]{2,1,0:T(8,128)(2,1)S(1)}, u32[]{:S(2)}, u32[]{:S(2)}) %collective-permute-start.10) | collective-permute-done | bytes 393248 | tf_op jit(solution)/shard_map/ppermute | solution.py:62
  78.7 3.5 %collective-permute-start.12 = (f32[128,512]{1,0:T(8,128)S(1)}, f32[128,512]{1,0:T(8,128)S(1)}, u32[]{:S(2)}, u32[]{:S(2)}) collective-permute-start(f32[128,512]{1,0:T(8,128)S(1)} %fusion.13), channel_id=1, source_target_pairs={{0,1},{1,0},{2,3},{3,2},{4,5},{5,4},{6,7},{7,6},{8,9},{9,8},{10,11... | collective-permute-start | bytes 786440 | tf_op jit(solution)/shard_map/ppermute | solution.py:63
  84.9 12.8 %collective-permute-start.13 = (bf16[128,512]{1,0:T(8,128)(2,1)S(1)}, bf16[128,512]{1,0:T(8,128)(2,1)S(1)}, u32[]{:S(2)}, u32[]{:S(2)}) collective-permute-start(bf16[128,512]{1,0:T(8,128)(2,1)S(1)} %fusion.46), channel_id=1, source_target_pairs={{0,32},{8,40},{16,48},{24,56},{32,64},{40,72},{48,80},{56,88},{64,... | collective-permute-start | bytes 393224 | tf_op jit(solution)/shard_map/ppermute | solution.py:10
  99.3 4.7 %collective-permute-done.13 = bf16[128,512]{1,0:T(8,128)(2,1)S(1)} collective-permute-done((bf16[128,512]{1,0:T(8,128)(2,1)S(1)}, bf16[128,512]{1,0:T(8,128)(2,1)S(1)}, u32[]{:S(2)}, u32[]{:S(2)}) %collective-permute-start.13) | collective-permute-done | bytes 131104 | tf_op jit(solution)/shard_map/ppermute | solution.py:10
  104.1 4.5 %collective-permute-start.17 = (bf16[3,128,512]{2,1,0:T(8,128)(2,1)S(1)}, bf16[3,128,512]{2,1,0:T(8,128)(2,1)S(1)}, u32[]{:S(2)}, u32[]{:S(2)}) collective-permute-start(bf16[3,128,512]{2,1,0:T(8,128)(2,1)S(1)} %pad_maximum_fusion.4), channel_id=1, source_target_pairs={{0,4},{1,5},{2,6},{3,7},{4,0},{5,1},{6,2},{7,3},{8,12},{9,13},{10,... | collective-permute-start | bytes 1179656 | tf_op jit(solution)/shard_map/ppermute | solution.py:62
  113.8 3.8 %collective-permute-done.17 = bf16[3,128,512]{2,1,0:T(8,128)(2,1)S(1)} collective-permute-done((bf16[3,128,512]{2,1,0:T(8,128)(2,1)S(1)}, bf16[3,128,512]{2,1,0:T(8,128)(2,1)S(1)}, u32[]{:S(2)}, u32[]{:S(2)}) %collective-permute-start.17) | collective-permute-done | bytes 393248 | tf_op jit(solution)/shard_map/ppermute | solution.py:62
  117.9 7.2 %collective-permute-done.16 = bf16[3,128,512]{2,1,0:T(8,128)(2,1)S(1)} collective-permute-done((bf16[3,128,512]{2,1,0:T(8,128)(2,1)S(1)}, bf16[3,128,512]{2,1,0:T(8,128)(2,1)S(1)}, u32[]{:S(2)}, u32[]{:S(2)}) %collective-permute-start.16) | collective-permute-done | bytes 393248 | tf_op jit(solution)/shard_map/ppermute | solution.py:62
  132.5 10.9 %collective-permute-start.19 = (bf16[128,512]{1,0:T(8,128)(2,1)S(1)}, bf16[128,512]{1,0:T(8,128)(2,1)S(1)}, u32[]{:S(2)}, u32[]{:S(2)}) collective-permute-start(bf16[128,512]{1,0:T(8,128)(2,1)S(1)} %fusion.45), channel_id=1, source_target_pairs={{0,64},{8,72},{16,80},{24,88},{32,96},{40,104},{48,112},{56,120},{... | collective-permute-start | bytes 393224 | tf_op jit(solution)/shard_map/ppermute | solution.py:10
  146.0 3.5 %collective-permute-start.23 = (bf16[3,128,512]{2,1,0:T(8,128)(2,1)S(1)}, bf16[3,128,512]{2,1,0:T(8,128)(2,1)S(1)}, u32[]{:S(2)}, u32[]{:S(2)}) collective-permute-start(bf16[3,128,512]{2,1,0:T(8,128)(2,1)S(1)} %pad_maximum_fusion.5), channel_id=1, source_target_pairs={{0,4},{1,5},{2,6},{3,7},{4,0},{5,1},{6,2},{7,3},{8,12},{9,13},{10,... | collective-permute-start | bytes 1179656 | tf_op jit(solution)/shard_map/ppermute | solution.py:62
  149.5 3.5 %collective-permute-start.22 = (bf16[3,128,512]{2,1,0:T(8,128)(2,1)S(1)}, bf16[3,128,512]{2,1,0:T(8,128)(2,1)S(1)}, u32[]{:S(2)}, u32[]{:S(2)}) collective-permute-start(bf16[3,128,512]{2,1,0:T(8,128)(2,1)S(1)} %pad_maximum_fusion.5), channel_id=1, source_target_pairs={{0,6},{1,7},{2,0},{3,1},{4,2},{5,3},{6,4},{7,5},{8,14},{9,15},{10,... | collective-permute-start | bytes 1179656 | tf_op jit(solution)/shard_map/ppermute | solution.py:62
  154.9 3.9 %collective-permute-done.23 = bf16[3,128,512]{2,1,0:T(8,128)(2,1)S(1)} collective-permute-done((bf16[3,128,512]{2,1,0:T(8,128)(2,1)S(1)}, bf16[3,128,512]{2,1,0:T(8,128)(2,1)S(1)}, u32[]{:S(2)}, u32[]{:S(2)}) %collective-permute-start.23) | collective-permute-done | bytes 393248 | tf_op jit(solution)/shard_map/ppermute | solution.py:62
  159.0 8.4 %collective-permute-done.22 = bf16[3,128,512]{2,1,0:T(8,128)(2,1)S(1)} collective-permute-done((bf16[3,128,512]{2,1,0:T(8,128)(2,1)S(1)}, bf16[3,128,512]{2,1,0:T(8,128)(2,1)S(1)}, u32[]{:S(2)}, u32[]{:S(2)}) %collective-permute-start.22) | collective-permute-done | bytes 393248 | tf_op jit(solution)/shard_map/ppermute | solution.py:62
  168.3 3.5 %collective-permute-start.24 = (f32[128,512]{1,0:T(8,128)S(1)}, f32[128,512]{1,0:T(8,128)S(1)}, u32[]{:S(2)}, u32[]{:S(2)}) collective-permute-start(f32[128,512]{1,0:T(8,128)S(1)} %fusion.27), channel_id=1, source_target_pairs={{0,1},{1,0},{2,3},{3,2},{4,5},{5,4},{6,7},{7,6},{8,9},{9,8},{10,11... | collective-permute-start | bytes 786440 | tf_op jit(solution)/shard_map/ppermute | solution.py:63
  174.4 5.8 %collective-permute-start.25 = (bf16[128,512]{1,0:T(8,128)(2,1)S(1)}, bf16[128,512]{1,0:T(8,128)(2,1)S(1)}, u32[]{:S(2)}, u32[]{:S(2)}) collective-permute-start(bf16[128,512]{1,0:T(8,128)(2,1)S(1)} %fusion.44), channel_id=1, source_target_pairs={{0,128},{8,136},{16,144},{24,152},{32,160},{40,168},{48,176},{56,1... | collective-permute-start | bytes 393224 | tf_op jit(solution)/shard_map/ppermute | solution.py:10
  180.2 4.4 %collective-permute-done.26 = bf16[128,512]{1,0:T(8,128)(2,1)S(1)} collective-permute-done((bf16[128,512]{1,0:T(8,128)(2,1)S(1)}, bf16[128,512]{1,0:T(8,128)(2,1)S(1)}, u32[]{:S(2)}, u32[]{:S(2)}) %collective-permute-start.26) | collective-permute-done | bytes 131104 | tf_op jit(solution)/shard_map/ppermute | solution.py:10
  184.7 3.4 %collective-permute-start.29 = (bf16[3,128,512]{2,1,0:T(8,128)(2,1)S(1)}, bf16[3,128,512]{2,1,0:T(8,128)(2,1)S(1)}, u32[]{:S(2)}, u32[]{:S(2)}) collective-permute-start(bf16[3,128,512]{2,1,0:T(8,128)(2,1)S(1)} %pad_maximum_fusion.6), channel_id=1, source_target_pairs={{0,4},{1,5},{2,6},{3,7},{4,0},{5,1},{6,2},{7,3},{8,12},{9,13},{10,... | collective-permute-start | bytes 1179656 | tf_op jit(solution)/shard_map/ppermute | solution.py:62
  188.1 3.6 %collective-permute-start.28 = (bf16[3,128,512]{2,1,0:T(8,128)(2,1)S(1)}, bf16[3,128,512]{2,1,0:T(8,128)(2,1)S(1)}, u32[]{:S(2)}, u32[]{:S(2)}) collective-permute-start(bf16[3,128,512]{2,1,0:T(8,128)(2,1)S(1)} %pad_maximum_fusion.6), channel_id=1, source_target_pairs={{0,6},{1,7},{2,0},{3,1},{4,2},{5,3},{6,4},{7,5},{8,14},{9,15},{10,... | collective-permute-start | bytes 1179656 | tf_op jit(solution)/shard_map/ppermute | solution.py:62
  193.7 4.2 %collective-permute-done.29 = bf16[3,128,512]{2,1,0:T(8,128)(2,1)S(1)} collective-permute-done((bf16[3,128,512]{2,1,0:T(8,128)(2,1)S(1)}, bf16[3,128,512]{2,1,0:T(8,128)(2,1)S(1)}, u32[]{:S(2)}, u32[]{:S(2)}) %collective-permute-start.29) | collective-permute-done | bytes 393248 | tf_op jit(solution)/shard_map/ppermute | solution.py:62
  198.1 8.2 %collective-permute-done.28 = bf16[3,128,512]{2,1,0:T(8,128)(2,1)S(1)} collective-permute-done((bf16[3,128,512]{2,1,0:T(8,128)(2,1)S(1)}, bf16[3,128,512]{2,1,0:T(8,128)(2,1)S(1)}, u32[]{:S(2)}, u32[]{:S(2)}) %collective-permute-start.28) | collective-permute-done | bytes 393248 | tf_op jit(solution)/shard_map/ppermute | solution.py:62
  213.1 11.4 %collective-permute-start.31 = (bf16[128,512]{1,0:T(8,128)(2,1)S(1)}, bf16[128,512]{1,0:T(8,128)(2,1)S(1)}, u32[]{:S(2)}, u32[]{:S(2)}) collective-permute-start(bf16[128,512]{1,0:T(8,128)(2,1)S(1)} %fusion.43), channel_id=1, source_target_pairs={{0,256},{8,264},{16,272},{24,280},{32,288},{40,296},{48,304},{56,3... | collective-permute-start | bytes 393224 | tf_op jit(solution)/shard_map/ppermute | solution.py:10
  226.1 3.5 %collective-permute-done.31 = bf16[128,512]{1,0:T(8,128)(2,1)S(1)} collective-permute-done((bf16[128,512]{1,0:T(8,128)(2,1)S(1)}, bf16[128,512]{1,0:T(8,128)(2,1)S(1)}, u32[]{:S(2)}, u32[]{:S(2)}) %collective-permute-start.31) | collective-permute-done | bytes 131104 | tf_op jit(solution)/shard_map/ppermute | solution.py:10
  229.7 3.7 %collective-permute-start.35 = (bf16[3,128,512]{2,1,0:T(8,128)(2,1)S(1)}, bf16[3,128,512]{2,1,0:T(8,128)(2,1)S(1)}, u32[]{:S(2)}, u32[]{:S(2)}) collective-permute-start(bf16[3,128,512]{2,1,0:T(8,128)(2,1)S(1)} %pad_maximum_fusion.7), channel_id=1, source_target_pairs={{0,4},{1,5},{2,6},{3,7},{4,0},{5,1},{6,2},{7,3},{8,12},{9,13},{10,... | collective-permute-start | bytes 1179656 | tf_op jit(solution)/shard_map/ppermute | solution.py:62
  233.3 3.7 %collective-permute-start.34 = (bf16[3,128,512]{2,1,0:T(8,128)(2,1)S(1)}, bf16[3,128,512]{2,1,0:T(8,128)(2,1)S(1)}, u32[]{:S(2)}, u32[]{:S(2)}) collective-permute-start(bf16[3,128,512]{2,1,0:T(8,128)(2,1)S(1)} %pad_maximum_fusion.7), channel_id=1, source_target_pairs={{0,6},{1,7},{2,0},{3,1},{4,2},{5,3},{6,4},{7,5},{8,14},{9,15},{10,... | collective-permute-start | bytes 1179656 | tf_op jit(solution)/shard_map/ppermute | solution.py:62
  238.9 3.6 %collective-permute-done.35 = bf16[3,128,512]{2,1,0:T(8,128)(2,1)S(1)} collective-permute-done((bf16[3,128,512]{2,1,0:T(8,128)(2,1)S(1)}, bf16[3,128,512]{2,1,0:T(8,128)(2,1)S(1)}, u32[]{:S(2)}, u32[]{:S(2)}) %collective-permute-start.35) | collective-permute-done | bytes 393248 | tf_op jit(solution)/shard_map/ppermute | solution.py:62
  242.7 8.7 %collective-permute-done.34 = bf16[3,128,512]{2,1,0:T(8,128)(2,1)S(1)} collective-permute-done((bf16[3,128,512]{2,1,0:T(8,128)(2,1)S(1)}, bf16[3,128,512]{2,1,0:T(8,128)(2,1)S(1)}, u32[]{:S(2)}, u32[]{:S(2)}) %collective-permute-start.34) | collective-permute-done | bytes 393248 | tf_op jit(solution)/shard_map/ppermute | solution.py:62
  252.2 3.5 %collective-permute-start.36 = (f32[128,512]{1,0:T(8,128)S(1)}, f32[128,512]{1,0:T(8,128)S(1)}, u32[]{:S(2)}, u32[]{:S(2)}) collective-permute-start(f32[128,512]{1,0:T(8,128)S(1)} %fusion.41), channel_id=1, source_target_pairs={{0,1},{1,0},{2,3},{3,2},{4,5},{5,4},{6,7},{7,6},{8,9},{9,8},{10,11... | collective-permute-start | bytes 786440 | tf_op jit(solution)/shard_map/ppermute | solution.py:63
  (116 shorter events, 76.9 us)
Async XLA Ops:
  0.0 9.7 %collective-permute-start = (bf16[128,512]{1,0:T(8,128)(2,1)}, bf16[128,512]{1,0:T(8,128)(2,1)S(1)}, u32[]{:S(2)}, u32[]{:S(2)}) collective-permute-start(bf16[128,512]{1,0:T(8,128)(2,1)} %bitcast.545), channel_id=1, source_target_pairs={{0,8},{8,16},{16,24},{24,32},{32,40},{40,48},{48,56},{56,64},{64,7... | collective-permute-start | bytes 393224 | tf_op jit(solution)/shard_map/ppermute | solution.py:10
  5.1 6.6 %collective-permute-start.1 = (bf16[128,512]{1,0:T(8,128)(2,1)}, bf16[128,512]{1,0:T(8,128)(2,1)S(1)}, u32[]{:S(2)}, u32[]{:S(2)}) collective-permute-start(bf16[128,512]{1,0:T(8,128)(2,1)} %bitcast.546), channel_id=1, source_target_pairs={{8,0},{16,8},{24,16},{32,24},{40,32},{48,40},{56,48},{64,56},{72,6... | collective-permute-start | bytes 393224 | tf_op jit(solution)/shard_map/ppermute | solution.py:10
  11.7 15.8 %collective-permute-start.5 = (bf16[6,128,4,3,128]{4,1,3,2,0:T(8,128)(2,1)S(1)}, bf16[6,128,4,3,128]{4,1,3,2,0:T(8,128)(2,1)S(1)}, u32[]{:S(2)}, u32[]{:S(2)}) collective-permute-start(bf16[6,128,4,3,128]{4,1,3,2,0:T(8,128)(2,1)S(1)} %pad_maximum_fusion.1), channel_id=1, source_target_pairs={{0,1},{1,0},{2,3},{3,2},{4,5},{5,4},{6,7},{7,6},{8,9},{9,8},{10,11... | collective-permute-start | bytes 7077896 | tf_op jit(solution)/shard_map/ppermute | solution.py:42
  19.0 14.2 %collective-permute-start.4 = (bf16[3,128,512]{2,1,0:T(8,128)(2,1)S(1)}, bf16[3,128,512]{2,1,0:T(8,128)(2,1)S(1)}, u32[]{:S(2)}, u32[]{:S(2)}) collective-permute-start(bf16[3,128,512]{2,1,0:T(8,128)(2,1)S(1)} %pad_maximum_fusion.2), channel_id=1, source_target_pairs={{0,4},{1,5},{2,6},{3,7},{4,0},{5,1},{6,2},{7,3},{8,12},{9,13},{10,... | collective-permute-start | bytes 1179656 | tf_op jit(solution)/shard_map/ppermute | solution.py:62
  21.9 18.0 %collective-permute-start.3 = (bf16[3,128,512]{2,1,0:T(8,128)(2,1)S(1)}, bf16[3,128,512]{2,1,0:T(8,128)(2,1)S(1)}, u32[]{:S(2)}, u32[]{:S(2)}) collective-permute-start(bf16[3,128,512]{2,1,0:T(8,128)(2,1)S(1)} %pad_maximum_fusion.2), channel_id=1, source_target_pairs={{0,6},{1,7},{2,0},{3,1},{4,2},{5,3},{6,4},{7,5},{8,14},{9,15},{10,... | collective-permute-start | bytes 1179656 | tf_op jit(solution)/shard_map/ppermute | solution.py:62
  24.6 17.2 %collective-permute-start.2 = (bf16[3,128,512]{2,1,0:T(8,128)(2,1)S(1)}, bf16[3,128,512]{2,1,0:T(8,128)(2,1)S(1)}, u32[]{:S(2)}, u32[]{:S(2)}) collective-permute-start(bf16[3,128,512]{2,1,0:T(8,128)(2,1)S(1)} %pad_maximum_fusion.2), channel_id=1, source_target_pairs={{0,2},{1,3},{2,4},{3,5},{4,6},{5,7},{6,0},{7,1},{8,10},{9,11},{10,... | collective-permute-start | bytes 1179656 | tf_op jit(solution)/shard_map/ppermute | solution.py:62
  46.1 9.2 %collective-permute-start.8 = (bf16[128,512]{1,0:T(8,128)(2,1)S(1)}, bf16[128,512]{1,0:T(8,128)(2,1)S(1)}, u32[]{:S(2)}, u32[]{:S(2)}) collective-permute-start(bf16[128,512]{1,0:T(8,128)(2,1)S(1)} %fusion.47), channel_id=1, source_target_pairs={{16,0},{24,8},{32,16},{40,24},{48,32},{56,40},{64,48},{72,56},{80,... | collective-permute-start | bytes 393224 | tf_op jit(solution)/shard_map/ppermute | solution.py:10
  47.4 8.7 %collective-permute-start.7 = (bf16[128,512]{1,0:T(8,128)(2,1)S(1)}, bf16[128,512]{1,0:T(8,128)(2,1)S(1)}, u32[]{:S(2)}, u32[]{:S(2)}) collective-permute-start(bf16[128,512]{1,0:T(8,128)(2,1)S(1)} %fusion.47), channel_id=1, source_target_pairs={{0,16},{8,24},{16,32},{24,40},{32,48},{40,56},{48,64},{56,72},{64,... | collective-permute-start | bytes 393224 | tf_op jit(solution)/shard_map/ppermute | solution.py:10
  56.2 12.8 %collective-permute-start.11 = (bf16[3,128,512]{2,1,0:T(8,128)(2,1)S(1)}, bf16[3,128,512]{2,1,0:T(8,128)(2,1)S(1)}, u32[]{:S(2)}, u32[]{:S(2)}) collective-permute-start(bf16[3,128,512]{2,1,0:T(8,128)(2,1)S(1)} %pad_maximum_fusion.3), channel_id=1, source_target_pairs={{0,4},{1,5},{2,6},{3,7},{4,0},{5,1},{6,2},{7,3},{8,12},{9,13},{10,... | collective-permute-start | bytes 1179656 | tf_op jit(solution)/shard_map/ppermute | solution.py:62
  60.5 17.5 %collective-permute-start.10 = (bf16[3,128,512]{2,1,0:T(8,128)(2,1)S(1)}, bf16[3,128,512]{2,1,0:T(8,128)(2,1)S(1)}, u32[]{:S(2)}, u32[]{:S(2)}) collective-permute-start(bf16[3,128,512]{2,1,0:T(8,128)(2,1)S(1)} %pad_maximum_fusion.3), channel_id=1, source_target_pairs={{0,6},{1,7},{2,0},{3,1},{4,2},{5,3},{6,4},{7,5},{8,14},{9,15},{10,... | collective-permute-start | bytes 1179656 | tf_op jit(solution)/shard_map/ppermute | solution.py:62
  63.5 14.7 %collective-permute-start.9 = (bf16[3,128,512]{2,1,0:T(8,128)(2,1)S(1)}, bf16[3,128,512]{2,1,0:T(8,128)(2,1)S(1)}, u32[]{:S(2)}, u32[]{:S(2)}) collective-permute-start(bf16[3,128,512]{2,1,0:T(8,128)(2,1)S(1)} %pad_maximum_fusion.3), channel_id=1, source_target_pairs={{0,2},{1,3},{2,4},{3,5},{4,6},{5,7},{6,0},{7,1},{8,10},{9,11},{10,... | collective-permute-start | bytes 1179656 | tf_op jit(solution)/shard_map/ppermute | solution.py:62
  83.6 15.7 %collective-permute-start.14 = (bf16[128,512]{1,0:T(8,128)(2,1)S(1)}, bf16[128,512]{1,0:T(8,128)(2,1)S(1)}, u32[]{:S(2)}, u32[]{:S(2)}) collective-permute-start(bf16[128,512]{1,0:T(8,128)(2,1)S(1)} %fusion.46), channel_id=1, source_target_pairs={{32,0},{40,8},{48,16},{56,24},{64,32},{72,40},{80,48},{88,56},{96,... | collective-permute-start | bytes 393224 | tf_op jit(solution)/shard_map/ppermute | solution.py:10
  84.9 19.1 %collective-permute-start.13 = (bf16[128,512]{1,0:T(8,128)(2,1)S(1)}, bf16[128,512]{1,0:T(8,128)(2,1)S(1)}, u32[]{:S(2)}, u32[]{:S(2)}) collective-permute-start(bf16[128,512]{1,0:T(8,128)(2,1)S(1)} %fusion.46), channel_id=1, source_target_pairs={{0,32},{8,40},{16,48},{24,56},{32,64},{40,72},{48,80},{56,88},{64,... | collective-permute-start | bytes 393224 | tf_op jit(solution)/shard_map/ppermute | solution.py:10
  104.1 13.6 %collective-permute-start.17 = (bf16[3,128,512]{2,1,0:T(8,128)(2,1)S(1)}, bf16[3,128,512]{2,1,0:T(8,128)(2,1)S(1)}, u32[]{:S(2)}, u32[]{:S(2)}) collective-permute-start(bf16[3,128,512]{2,1,0:T(8,128)(2,1)S(1)} %pad_maximum_fusion.4), channel_id=1, source_target_pairs={{0,4},{1,5},{2,6},{3,7},{4,0},{5,1},{6,2},{7,3},{8,12},{9,13},{10,... | collective-permute-start | bytes 1179656 | tf_op jit(solution)/shard_map/ppermute | solution.py:62
  108.5 16.6 %collective-permute-start.16 = (bf16[3,128,512]{2,1,0:T(8,128)(2,1)S(1)}, bf16[3,128,512]{2,1,0:T(8,128)(2,1)S(1)}, u32[]{:S(2)}, u32[]{:S(2)}) collective-permute-start(bf16[3,128,512]{2,1,0:T(8,128)(2,1)S(1)} %pad_maximum_fusion.4), channel_id=1, source_target_pairs={{0,6},{1,7},{2,0},{3,1},{4,2},{5,3},{6,4},{7,5},{8,14},{9,15},{10,... | collective-permute-start | bytes 1179656 | tf_op jit(solution)/shard_map/ppermute | solution.py:62
  111.4 15.1 %collective-permute-start.15 = (bf16[3,128,512]{2,1,0:T(8,128)(2,1)S(1)}, bf16[3,128,512]{2,1,0:T(8,128)(2,1)S(1)}, u32[]{:S(2)}, u32[]{:S(2)}) collective-permute-start(bf16[3,128,512]{2,1,0:T(8,128)(2,1)S(1)} %pad_maximum_fusion.4), channel_id=1, source_target_pairs={{0,2},{1,3},{2,4},{3,5},{4,6},{5,7},{6,0},{7,1},{8,10},{9,11},{10,... | collective-permute-start | bytes 1179656 | tf_op jit(solution)/shard_map/ppermute | solution.py:62
  131.2 13.9 %collective-permute-start.20 = (bf16[128,512]{1,0:T(8,128)(2,1)S(1)}, bf16[128,512]{1,0:T(8,128)(2,1)S(1)}, u32[]{:S(2)}, u32[]{:S(2)}) collective-permute-start(bf16[128,512]{1,0:T(8,128)(2,1)S(1)} %fusion.45), channel_id=1, source_target_pairs={{64,0},{72,8},{80,16},{88,24},{96,32},{104,40},{112,48},{120,56},{... | collective-permute-start | bytes 393224 | tf_op jit(solution)/shard_map/ppermute | solution.py:10
  132.5 13.4 %collective-permute-start.19 = (bf16[128,512]{1,0:T(8,128)(2,1)S(1)}, bf16[128,512]{1,0:T(8,128)(2,1)S(1)}, u32[]{:S(2)}, u32[]{:S(2)}) collective-permute-start(bf16[128,512]{1,0:T(8,128)(2,1)S(1)} %fusion.45), channel_id=1, source_target_pairs={{0,64},{8,72},{16,80},{24,88},{32,96},{40,104},{48,112},{56,120},{... | collective-permute-start | bytes 393224 | tf_op jit(solution)/shard_map/ppermute | solution.py:10
  146.0 12.8 %collective-permute-start.23 = (bf16[3,128,512]{2,1,0:T(8,128)(2,1)S(1)}, bf16[3,128,512]{2,1,0:T(8,128)(2,1)S(1)}, u32[]{:S(2)}, u32[]{:S(2)}) collective-permute-start(bf16[3,128,512]{2,1,0:T(8,128)(2,1)S(1)} %pad_maximum_fusion.5), channel_id=1, source_target_pairs={{0,4},{1,5},{2,6},{3,7},{4,0},{5,1},{6,2},{7,3},{8,12},{9,13},{10,... | collective-permute-start | bytes 1179656 | tf_op jit(solution)/shard_map/ppermute | solution.py:62
  149.5 18.0 %collective-permute-start.22 = (bf16[3,128,512]{2,1,0:T(8,128)(2,1)S(1)}, bf16[3,128,512]{2,1,0:T(8,128)(2,1)S(1)}, u32[]{:S(2)}, u32[]{:S(2)}) collective-permute-start(bf16[3,128,512]{2,1,0:T(8,128)(2,1)S(1)} %pad_maximum_fusion.5), channel_id=1, source_target_pairs={{0,6},{1,7},{2,0},{3,1},{4,2},{5,3},{6,4},{7,5},{8,14},{9,15},{10,... | collective-permute-start | bytes 1179656 | tf_op jit(solution)/shard_map/ppermute | solution.py:62
  153.0 14.8 %collective-permute-start.21 = (bf16[3,128,512]{2,1,0:T(8,128)(2,1)S(1)}, bf16[3,128,512]{2,1,0:T(8,128)(2,1)S(1)}, u32[]{:S(2)}, u32[]{:S(2)}) collective-permute-start(bf16[3,128,512]{2,1,0:T(8,128)(2,1)S(1)} %pad_maximum_fusion.5), channel_id=1, source_target_pairs={{0,2},{1,3},{2,4},{3,5},{4,6},{5,7},{6,0},{7,1},{8,10},{9,11},{10,... | collective-permute-start | bytes 1179656 | tf_op jit(solution)/shard_map/ppermute | solution.py:62
  168.3 4.6 %collective-permute-start.24 = (f32[128,512]{1,0:T(8,128)S(1)}, f32[128,512]{1,0:T(8,128)S(1)}, u32[]{:S(2)}, u32[]{:S(2)}) collective-permute-start(f32[128,512]{1,0:T(8,128)S(1)} %fusion.27), channel_id=1, source_target_pairs={{0,1},{1,0},{2,3},{3,2},{4,5},{5,4},{6,7},{7,6},{8,9},{9,8},{10,11... | collective-permute-start | bytes 786440 | tf_op jit(solution)/shard_map/ppermute | solution.py:63
  173.1 11.5 %collective-permute-start.26 = (bf16[128,512]{1,0:T(8,128)(2,1)S(1)}, bf16[128,512]{1,0:T(8,128)(2,1)S(1)}, u32[]{:S(2)}, u32[]{:S(2)}) collective-permute-start(bf16[128,512]{1,0:T(8,128)(2,1)S(1)} %fusion.44), channel_id=1, source_target_pairs={{128,0},{136,8},{144,16},{152,24},{160,32},{168,40},{176,48},{184,... | collective-permute-start | bytes 393224 | tf_op jit(solution)/shard_map/ppermute | solution.py:10
  174.4 10.2 %collective-permute-start.25 = (bf16[128,512]{1,0:T(8,128)(2,1)S(1)}, bf16[128,512]{1,0:T(8,128)(2,1)S(1)}, u32[]{:S(2)}, u32[]{:S(2)}) collective-permute-start(bf16[128,512]{1,0:T(8,128)(2,1)S(1)} %fusion.44), channel_id=1, source_target_pairs={{0,128},{8,136},{16,144},{24,152},{32,160},{40,168},{48,176},{56,1... | collective-permute-start | bytes 393224 | tf_op jit(solution)/shard_map/ppermute | solution.py:10
  184.7 13.1 %collective-permute-start.29 = (bf16[3,128,512]{2,1,0:T(8,128)(2,1)S(1)}, bf16[3,128,512]{2,1,0:T(8,128)(2,1)S(1)}, u32[]{:S(2)}, u32[]{:S(2)}) collective-permute-start(bf16[3,128,512]{2,1,0:T(8,128)(2,1)S(1)} %pad_maximum_fusion.6), channel_id=1, source_target_pairs={{0,4},{1,5},{2,6},{3,7},{4,0},{5,1},{6,2},{7,3},{8,12},{9,13},{10,... | collective-permute-start | bytes 1179656 | tf_op jit(solution)/shard_map/ppermute | solution.py:62
  188.1 18.1 %collective-permute-start.28 = (bf16[3,128,512]{2,1,0:T(8,128)(2,1)S(1)}, bf16[3,128,512]{2,1,0:T(8,128)(2,1)S(1)}, u32[]{:S(2)}, u32[]{:S(2)}) collective-permute-start(bf16[3,128,512]{2,1,0:T(8,128)(2,1)S(1)} %pad_maximum_fusion.6), channel_id=1, source_target_pairs={{0,6},{1,7},{2,0},{3,1},{4,2},{5,3},{6,4},{7,5},{8,14},{9,15},{10,... | collective-permute-start | bytes 1179656 | tf_op jit(solution)/shard_map/ppermute | solution.py:62
  191.8 15.0 %collective-permute-start.27 = (bf16[3,128,512]{2,1,0:T(8,128)(2,1)S(1)}, bf16[3,128,512]{2,1,0:T(8,128)(2,1)S(1)}, u32[]{:S(2)}, u32[]{:S(2)}) collective-permute-start(bf16[3,128,512]{2,1,0:T(8,128)(2,1)S(1)} %pad_maximum_fusion.6), channel_id=1, source_target_pairs={{0,2},{1,3},{2,4},{3,5},{4,6},{5,7},{6,0},{7,1},{8,10},{9,11},{10,... | collective-permute-start | bytes 1179656 | tf_op jit(solution)/shard_map/ppermute | solution.py:62
  211.8 14.3 %collective-permute-start.32 = (bf16[128,512]{1,0:T(8,128)(2,1)S(1)}, bf16[128,512]{1,0:T(8,128)(2,1)S(1)}, u32[]{:S(2)}, u32[]{:S(2)}) collective-permute-start(bf16[128,512]{1,0:T(8,128)(2,1)S(1)} %fusion.43), channel_id=1, source_target_pairs={{256,0},{264,8},{272,16},{280,24},{288,32},{296,40},{304,48},{312,... | collective-permute-start | bytes 393224 | tf_op jit(solution)/shard_map/ppermute | solution.py:10
  213.1 16.5 %collective-permute-start.31 = (bf16[128,512]{1,0:T(8,128)(2,1)S(1)}, bf16[128,512]{1,0:T(8,128)(2,1)S(1)}, u32[]{:S(2)}, u32[]{:S(2)}) collective-permute-start(bf16[128,512]{1,0:T(8,128)(2,1)S(1)} %fusion.43), channel_id=1, source_target_pairs={{0,256},{8,264},{16,272},{24,280},{32,288},{40,296},{48,304},{56,3... | collective-permute-start | bytes 393224 | tf_op jit(solution)/shard_map/ppermute | solution.py:10
  229.7 12.8 %collective-permute-start.35 = (bf16[3,128,512]{2,1,0:T(8,128)(2,1)S(1)}, bf16[3,128,512]{2,1,0:T(8,128)(2,1)S(1)}, u32[]{:S(2)}, u32[]{:S(2)}) collective-permute-start(bf16[3,128,512]{2,1,0:T(8,128)(2,1)S(1)} %pad_maximum_fusion.7), channel_id=1, source_target_pairs={{0,4},{1,5},{2,6},{3,7},{4,0},{5,1},{6,2},{7,3},{8,12},{9,13},{10,... | collective-permute-start | bytes 1179656 | tf_op jit(solution)/shard_map/ppermute | solution.py:62
  233.3 18.1 %collective-permute-start.34 = (bf16[3,128,512]{2,1,0:T(8,128)(2,1)S(1)}, bf16[3,128,512]{2,1,0:T(8,128)(2,1)S(1)}, u32[]{:S(2)}, u32[]{:S(2)}) collective-permute-start(bf16[3,128,512]{2,1,0:T(8,128)(2,1)S(1)} %pad_maximum_fusion.7), channel_id=1, source_target_pairs={{0,6},{1,7},{2,0},{3,1},{4,2},{5,3},{6,4},{7,5},{8,14},{9,15},{10,... | collective-permute-start | bytes 1179656 | tf_op jit(solution)/shard_map/ppermute | solution.py:62
  237.0 14.7 %collective-permute-start.33 = (bf16[3,128,512]{2,1,0:T(8,128)(2,1)S(1)}, bf16[3,128,512]{2,1,0:T(8,128)(2,1)S(1)}, u32[]{:S(2)}, u32[]{:S(2)}) collective-permute-start(bf16[3,128,512]{2,1,0:T(8,128)(2,1)S(1)} %pad_maximum_fusion.7), channel_id=1, source_target_pairs={{0,2},{1,3},{2,4},{3,5},{4,6},{5,7},{6,0},{7,1},{8,10},{9,11},{10,... | collective-permute-start | bytes 1179656 | tf_op jit(solution)/shard_map/ppermute | solution.py:62
  (8 other events, 38.3 us)

commit v12 on v11

--- a/solution.py
+++ b/solution.py
@@ -25,7 +25,11 @@
     def columns_for(which_core):
         return jnp.stack([2 * ((chip + off) % chips) + which_core for off in OFFSETS])
 
-    factors = [f[:, 0] for f in (self_factor, lower_factor, upper_factor)]
+    nchain = lax.axis_size("chain")
+    last = levels - 1
+    near_factor = jnp.where(lax.axis_index("chain") < nchain // 2, upper_factor[last, 0], lower_factor[last, 0])
+    lower_last = jnp.concatenate([lower_factor[:last, 0], near_factor[None]])
+    factors = [self_factor[:, 0], lower_last, upper_factor[:, 0]]
 
     def pick(which_core):
         slots = []
@@ -58,10 +62,14 @@
         else:
             lower = shifted(current, "chain", dist)
             upper = shifted(current, "chain", -dist)
-        own = jnp.stack([current, lower, upper])
+        if level == last and 2 * dist == nchain:
+            own = jnp.stack([current, lower + upper])
+        else:
+            own = jnp.stack([current, lower, upper])
+        used = own.shape[0]
         pieces = [own] + [lax.ppermute(own, "cross", same_core(-off)) for off in OFFSETS[1:]]
-        given = lax.ppermute(partial(theirs[level], pieces), "cross", swap)
-        total = partial(mine[level], pieces) + given
+        given = lax.ppermute(partial(theirs[level][:, :, :used], pieces), "cross", swap)
+        total = partial(mine[level][:, :, :used], pieces) + given
         current = total.astype(jnp.bfloat16)
     return current[None]
 

time: 259 us -> 261 us (level)
    ppermute x12, waiting for transfers between devices: 22.8 us -> 28.4 us  [shifted(): lax.ppermute(value, axis, [(source, source + steps) for source in range(i...]
    ppermute x18, waiting for transfers between devices: 75.2 us -> 69.7 us  [body(): lax.ppermute(own, 'cross', same_core(-off))]
  transfers between devices with their start and end apart: 37 -> 37, of which waited for: 32 -> 30; matrix products, arithmetic and copies ran while one was open for 4% -> 5% of each run, Pallas kernels for 0% -> 0%
where the time goes in v12:
time: 261 us; the launch traced here: 260 us
  starting transfers between devices  139 us (53%)
  waiting for transfers between devices  101 us (39%)
  matrix products  11.4 us (4%)
  local copies, waits for them, and re-layouts  3.96 us (2%)
  other arithmetic  3.12 us (1%)
    ppermute x18, waiting for transfers between devices, body(): lax.ppermute(own, 'cross', same_core(-off))  69.7 us
    ppermute x12, starting transfers between devices, shifted(): lax.ppermute(value, axis, [(source, source + steps) for source in range(i...  58.2 us
    ppermute x18, starting transfers between devices, body(): lax.ppermute(own, 'cross', same_core(-off))  54.5 us
    ppermute x12, waiting for transfers between devices, shifted(): lax.ppermute(value, axis, [(source, source + steps) for source in range(i...  28.4 us
    ppermute x6, starting transfers between devices, body(): lax.ppermute(partial(theirs[level][:, :, :used], pieces), 'cross', swap)  20.8 us
    dot_general x48, matrix products, partial(): jnp.einsum('ibk,bkr->ir', mat[:, j], piece, preferred_element_type=jnp.fl...  11.4 us
    ppermute x1, starting transfers between devices, body(): theirs = lax.ppermute(given_factors, 'cross', swap)  5.54 us
  transfers between devices with their start and end apart: 37, of which 30 were waited for; matrix products, arithmetic and copies ran while one was open for 5% of the time, Pallas kernels for 0%

profile of v12, /device:TPU:1, one launch (start us, length us, event | category | flops | bytes accessed | tf_op | source)
XLA Modules:
  0.0 259.7 jit_solution(11557858526934133104)
XLA Ops:
  0.0 5.0 %collective-permute-start = (bf16[128,512]{1,0:T(8,128)(2,1)}, bf16[128,512]{1,0:T(8,128)(2,1)S(1)}, u32[]{:S(2)}, u32[]{:S(2)}) collective-permute-start(bf16[128,512]{1,0:T(8,128)(2,1)} %bitcast.538), channel_id=1, source_target_pairs={{0,8},{8,16},{16,24},{24,32},{32,40},{40,48},{48,56},{56,64},{64,7... | collective-permute-start | bytes 393224 | tf_op jit(solution)/shard_map/ppermute | solution.py:10
  11.7 5.5 %collective-permute-start.5 = (bf16[6,128,4,3,128]{4,1,0,3,2:T(8,128)(2,1)S(1)}, bf16[6,128,4,3,128]{4,1,0,3,2:T(8,128)(2,1)S(1)}, u32[]{:S(2)}, u32[]{:S(2)}) collective-permute-start(bf16[6,128,4,3,128]{4,1,0,3,2:T(8,128)(2,1)S(1)} %pad_maximum_fusion.1), channel_id=1, source_target_pairs={{0,1},{1,0},{2,3},{3,2},{4,5},{5,4},{6,7},{7,6},{8,9},{9,8},{10,11... | collective-permute-start | bytes 7077896 | tf_op jit(solution)/shard_map/ppermute | solution.py:46
  27.4 5.4 %collective-permute-done.4 = bf16[3,128,512]{2,1,0:T(8,128)(2,1)S(1)} collective-permute-done((bf16[3,128,512]{2,1,0:T(8,128)(2,1)S(1)}, bf16[3,128,512]{2,1,0:T(8,128)(2,1)S(1)}, u32[]{:S(2)}, u32[]{:S(2)}) %collective-permute-start.4) | collective-permute-done | bytes 393248 | tf_op jit(solution)/shard_map/ppermute | solution.py:70
  33.1 6.5 %collective-permute-done.3 = bf16[3,128,512]{2,1,0:T(8,128)(2,1)S(1)} collective-permute-done((bf16[3,128,512]{2,1,0:T(8,128)(2,1)S(1)}, bf16[3,128,512]{2,1,0:T(8,128)(2,1)S(1)}, u32[]{:S(2)}, u32[]{:S(2)}) %collective-permute-start.3) | collective-permute-done | bytes 393248 | tf_op jit(solution)/shard_map/ppermute | solution.py:70
  47.1 6.3 %collective-permute-start.7 = (bf16[128,512]{1,0:T(8,128)(2,1)S(1)}, bf16[128,512]{1,0:T(8,128)(2,1)S(1)}, u32[]{:S(2)}, u32[]{:S(2)}) collective-permute-start(bf16[128,512]{1,0:T(8,128)(2,1)S(1)} %fusion.47), channel_id=1, source_target_pairs={{0,16},{8,24},{16,32},{24,40},{32,48},{40,56},{48,64},{56,72},{64,... | collective-permute-start | bytes 393224 | tf_op jit(solution)/shard_map/ppermute | solution.py:10
  55.9 4.3 %collective-permute-start.11 = (bf16[3,128,512]{2,1,0:T(8,128)(2,1)S(1)}, bf16[3,128,512]{2,1,0:T(8,128)(2,1)S(1)}, u32[]{:S(2)}, u32[]{:S(2)}) collective-permute-start(bf16[3,128,512]{2,1,0:T(8,128)(2,1)S(1)} %pad_maximum_fusion.3), channel_id=1, source_target_pairs={{0,4},{1,5},{2,6},{3,7},{4,0},{5,1},{6,2},{7,3},{8,12},{9,13},{10,... | collective-permute-start | bytes 1179656 | tf_op jit(solution)/shard_map/ppermute | solution.py:70
  68.3 9.4 %collective-permute-done.10 = bf16[3,128,512]{2,1,0:T(8,128)(2,1)S(1)} collective-permute-done((bf16[3,128,512]{2,1,0:T(8,128)(2,1)S(1)}, bf16[3,128,512]{2,1,0:T(8,128)(2,1)S(1)}, u32[]{:S(2)}, u32[]{:S(2)}) %collective-permute-start.10) | collective-permute-done | bytes 393248 | tf_op jit(solution)/shard_map/ppermute | solution.py:70
  78.5 3.7 %collective-permute-start.12 = (f32[128,512]{1,0:T(8,128)S(1)}, f32[128,512]{1,0:T(8,128)S(1)}, u32[]{:S(2)}, u32[]{:S(2)}) collective-permute-start(f32[128,512]{1,0:T(8,128)S(1)} %fusion.13), channel_id=1, source_target_pairs={{0,1},{1,0},{2,3},{3,2},{4,5},{5,4},{6,7},{7,6},{8,9},{9,8},{10,11... | collective-permute-start | bytes 786440 | tf_op jit(solution)/shard_map/ppermute | solution.py:71
  84.9 13.8 %collective-permute-start.13 = (bf16[128,512]{1,0:T(8,128)(2,1)S(1)}, bf16[128,512]{1,0:T(8,128)(2,1)S(1)}, u32[]{:S(2)}, u32[]{:S(2)}) collective-permute-start(bf16[128,512]{1,0:T(8,128)(2,1)S(1)} %fusion.46), channel_id=1, source_target_pairs={{0,32},{8,40},{16,48},{24,56},{32,64},{40,72},{48,80},{56,88},{64,... | collective-permute-start | bytes 393224 | tf_op jit(solution)/shard_map/ppermute | solution.py:10
  100.3 6.2 %collective-permute-done.13 = bf16[128,512]{1,0:T(8,128)(2,1)S(1)} collective-permute-done((bf16[128,512]{1,0:T(8,128)(2,1)S(1)}, bf16[128,512]{1,0:T(8,128)(2,1)S(1)}, u32[]{:S(2)}, u32[]{:S(2)}) %collective-permute-start.13) | collective-permute-done | bytes 131104 | tf_op jit(solution)/shard_map/ppermute | solution.py:10
  106.6 4.0 %collective-permute-start.17 = (bf16[3,128,512]{2,1,0:T(8,128)(2,1)S(1)}, bf16[3,128,512]{2,1,0:T(8,128)(2,1)S(1)}, u32[]{:S(2)}, u32[]{:S(2)}) collective-permute-start(bf16[3,128,512]{2,1,0:T(8,128)(2,1)S(1)} %pad_maximum_fusion.4), channel_id=1, source_target_pairs={{0,4},{1,5},{2,6},{3,7},{4,0},{5,1},{6,2},{7,3},{8,12},{9,13},{10,... | collective-permute-start | bytes 1179656 | tf_op jit(solution)/shard_map/ppermute | solution.py:70
  116.0 4.3 %collective-permute-done.17 = bf16[3,128,512]{2,1,0:T(8,128)(2,1)S(1)} collective-permute-done((bf16[3,128,512]{2,1,0:T(8,128)(2,1)S(1)}, bf16[3,128,512]{2,1,0:T(8,128)(2,1)S(1)}, u32[]{:S(2)}, u32[]{:S(2)}) %collective-permute-start.17) | collective-permute-done | bytes 393248 | tf_op jit(solution)/shard_map/ppermute | solution.py:70
  120.5 8.2 %collective-permute-done.16 = bf16[3,128,512]{2,1,0:T(8,128)(2,1)S(1)} collective-permute-done((bf16[3,128,512]{2,1,0:T(8,128)(2,1)S(1)}, bf16[3,128,512]{2,1,0:T(8,128)(2,1)S(1)}, u32[]{:S(2)}, u32[]{:S(2)}) %collective-permute-start.16) | collective-permute-done | bytes 393248 | tf_op jit(solution)/shard_map/ppermute | solution.py:70
  135.3 9.1 %collective-permute-start.19 = (bf16[128,512]{1,0:T(8,128)(2,1)S(1)}, bf16[128,512]{1,0:T(8,128)(2,1)S(1)}, u32[]{:S(2)}, u32[]{:S(2)}) collective-permute-start(bf16[128,512]{1,0:T(8,128)(2,1)S(1)} %fusion.45), channel_id=1, source_target_pairs={{0,64},{8,72},{16,80},{24,88},{32,96},{40,104},{48,112},{56,120},{... | collective-permute-start | bytes 393224 | tf_op jit(solution)/shard_map/ppermute | solution.py:10
  146.9 3.8 %collective-permute-start.23 = (bf16[3,128,512]{2,1,0:T(8,128)(2,1)S(1)}, bf16[3,128,512]{2,1,0:T(8,128)(2,1)S(1)}, u32[]{:S(2)}, u32[]{:S(2)}) collective-permute-start(bf16[3,128,512]{2,1,0:T(8,128)(2,1)S(1)} %pad_maximum_fusion.5), channel_id=1, source_target_pairs={{0,4},{1,5},{2,6},{3,7},{4,0},{5,1},{6,2},{7,3},{8,12},{9,13},{10,... | collective-permute-start | bytes 1179656 | tf_op jit(solution)/shard_map/ppermute | solution.py:70
  150.7 3.5 %collective-permute-start.22 = (bf16[3,128,512]{2,1,0:T(8,128)(2,1)S(1)}, bf16[3,128,512]{2,1,0:T(8,128)(2,1)S(1)}, u32[]{:S(2)}, u32[]{:S(2)}) collective-permute-start(bf16[3,128,512]{2,1,0:T(8,128)(2,1)S(1)} %pad_maximum_fusion.5), channel_id=1, source_target_pairs={{0,6},{1,7},{2,0},{3,1},{4,2},{5,3},{6,4},{7,5},{8,14},{9,15},{10,... | collective-permute-start | bytes 1179656 | tf_op jit(solution)/shard_map/ppermute | solution.py:70
  156.1 3.6 %collective-permute-done.23 = bf16[3,128,512]{2,1,0:T(8,128)(2,1)S(1)} collective-permute-done((bf16[3,128,512]{2,1,0:T(8,128)(2,1)S(1)}, bf16[3,128,512]{2,1,0:T(8,128)(2,1)S(1)}, u32[]{:S(2)}, u32[]{:S(2)}) %collective-permute-start.23) | collective-permute-done | bytes 393248 | tf_op jit(solution)/shard_map/ppermute | solution.py:70
  160.0 8.8 %collective-permute-done.22 = bf16[3,128,512]{2,1,0:T(8,128)(2,1)S(1)} collective-permute-done((bf16[3,128,512]{2,1,0:T(8,128)(2,1)S(1)}, bf16[3,128,512]{2,1,0:T(8,128)(2,1)S(1)}, u32[]{:S(2)}, u32[]{:S(2)}) %collective-permute-start.22) | collective-permute-done | bytes 393248 | tf_op jit(solution)/shard_map/ppermute | solution.py:70
  169.4 3.5 %collective-permute-start.24 = (f32[128,512]{1,0:T(8,128)S(1)}, f32[128,512]{1,0:T(8,128)S(1)}, u32[]{:S(2)}, u32[]{:S(2)}) collective-permute-start(f32[128,512]{1,0:T(8,128)S(1)} %fusion.27), channel_id=1, source_target_pairs={{0,1},{1,0},{2,3},{3,2},{4,5},{5,4},{6,7},{7,6},{8,9},{9,8},{10,11... | collective-permute-start | bytes 786440 | tf_op jit(solution)/shard_map/ppermute | solution.py:71
  175.6 5.7 %collective-permute-start.25 = (bf16[128,512]{1,0:T(8,128)(2,1)S(1)}, bf16[128,512]{1,0:T(8,128)(2,1)S(1)}, u32[]{:S(2)}, u32[]{:S(2)}) collective-permute-start(bf16[128,512]{1,0:T(8,128)(2,1)S(1)} %fusion.44), channel_id=1, source_target_pairs={{0,128},{8,136},{16,144},{24,152},{32,160},{40,168},{48,176},{56,1... | collective-permute-start | bytes 393224 | tf_op jit(solution)/shard_map/ppermute | solution.py:10
  181.4 4.4 %collective-permute-done.26 = bf16[128,512]{1,0:T(8,128)(2,1)S(1)} collective-permute-done((bf16[128,512]{1,0:T(8,128)(2,1)S(1)}, bf16[128,512]{1,0:T(8,128)(2,1)S(1)}, u32[]{:S(2)}, u32[]{:S(2)}) %collective-permute-start.26) | collective-permute-done | bytes 131104 | tf_op jit(solution)/shard_map/ppermute | solution.py:10
  185.8 3.6 %collective-permute-start.29 = (bf16[3,128,512]{2,1,0:T(8,128)(2,1)S(1)}, bf16[3,128,512]{2,1,0:T(8,128)(2,1)S(1)}, u32[]{:S(2)}, u32[]{:S(2)}) collective-permute-start(bf16[3,128,512]{2,1,0:T(8,128)(2,1)S(1)} %pad_maximum_fusion.6), channel_id=1, source_target_pairs={{0,4},{1,5},{2,6},{3,7},{4,0},{5,1},{6,2},{7,3},{8,12},{9,13},{10,... | collective-permute-start | bytes 1179656 | tf_op jit(solution)/shard_map/ppermute | solution.py:70
  189.4 3.7 %collective-permute-start.28 = (bf16[3,128,512]{2,1,0:T(8,128)(2,1)S(1)}, bf16[3,128,512]{2,1,0:T(8,128)(2,1)S(1)}, u32[]{:S(2)}, u32[]{:S(2)}) collective-permute-start(bf16[3,128,512]{2,1,0:T(8,128)(2,1)S(1)} %pad_maximum_fusion.6), channel_id=1, source_target_pairs={{0,6},{1,7},{2,0},{3,1},{4,2},{5,3},{6,4},{7,5},{8,14},{9,15},{10,... | collective-permute-start | bytes 1179656 | tf_op jit(solution)/shard_map/ppermute | solution.py:70
  195.0 4.0 %collective-permute-done.29 = bf16[3,128,512]{2,1,0:T(8,128)(2,1)S(1)} collective-permute-done((bf16[3,128,512]{2,1,0:T(8,128)(2,1)S(1)}, bf16[3,128,512]{2,1,0:T(8,128)(2,1)S(1)}, u32[]{:S(2)}, u32[]{:S(2)}) %collective-permute-start.29) | collective-permute-done | bytes 393248 | tf_op jit(solution)/shard_map/ppermute | solution.py:70
  199.2 8.4 %collective-permute-done.28 = bf16[3,128,512]{2,1,0:T(8,128)(2,1)S(1)} collective-permute-done((bf16[3,128,512]{2,1,0:T(8,128)(2,1)S(1)}, bf16[3,128,512]{2,1,0:T(8,128)(2,1)S(1)}, u32[]{:S(2)}, u32[]{:S(2)}) %collective-permute-start.28) | collective-permute-done | bytes 393248 | tf_op jit(solution)/shard_map/ppermute | solution.py:70
  208.3 3.5 %collective-permute-start.30 = (f32[128,512]{1,0:T(8,128)S(1)}, f32[128,512]{1,0:T(8,128)S(1)}, u32[]{:S(2)}, u32[]{:S(2)}) collective-permute-start(f32[128,512]{1,0:T(8,128)S(1)} %fusion.34), channel_id=1, source_target_pairs={{0,1},{1,0},{2,3},{3,2},{4,5},{5,4},{6,7},{7,6},{8,9},{9,8},{10,11... | collective-permute-start | bytes 786440 | tf_op jit(solution)/shard_map/ppermute | solution.py:71
  213.2 10.7 %collective-permute-start.31 = (bf16[128,512]{1,0:T(8,128)(2,1)S(1)}, bf16[128,512]{1,0:T(8,128)(2,1)S(1)}, u32[]{:S(2)}, u32[]{:S(2)}) collective-permute-start(bf16[128,512]{1,0:T(8,128)(2,1)S(1)} %fusion.43), channel_id=1, source_target_pairs={{0,256},{8,264},{16,272},{24,280},{32,288},{40,296},{48,304},{56,3... | collective-permute-start | bytes 393224 | tf_op jit(solution)/shard_map/ppermute | solution.py:10
  226.4 10.0 %collective-permute-done.32 = bf16[128,512]{1,0:T(8,128)(2,1)S(1)} collective-permute-done((bf16[128,512]{1,0:T(8,128)(2,1)S(1)}, bf16[128,512]{1,0:T(8,128)(2,1)S(1)}, u32[]{:S(2)}, u32[]{:S(2)}) %collective-permute-start.32) | collective-permute-done | bytes 131104 | tf_op jit(solution)/shard_map/ppermute | solution.py:10
  236.5 3.5 %collective-permute-start.35 = (bf16[2,128,512]{2,1,0:T(8,128)(2,1)S(1)}, bf16[2,128,512]{2,1,0:T(8,128)(2,1)S(1)}, u32[]{:S(2)}, u32[]{:S(2)}) collective-permute-start(bf16[2,128,512]{2,1,0:T(8,128)(2,1)S(1)} %pad_maximum_fusion.7), channel_id=1, source_target_pairs={{0,4},{1,5},{2,6},{3,7},{4,0},{5,1},{6,2},{7,3},{8,12},{9,13},{10,... | collective-permute-start | bytes 786440 | tf_op jit(solution)/shard_map/ppermute | solution.py:70
  239.9 3.7 %collective-permute-start.34 = (bf16[2,128,512]{2,1,0:T(8,128)(2,1)S(1)}, bf16[2,128,512]{2,1,0:T(8,128)(2,1)S(1)}, u32[]{:S(2)}, u32[]{:S(2)}) collective-permute-start(bf16[2,128,512]{2,1,0:T(8,128)(2,1)S(1)} %pad_maximum_fusion.7), channel_id=1, source_target_pairs={{0,6},{1,7},{2,0},{3,1},{4,2},{5,3},{6,4},{7,5},{8,14},{9,15},{10,... | collective-permute-start | bytes 786440 | tf_op jit(solution)/shard_map/ppermute | solution.py:70
  246.5 3.7 %collective-permute-done.34 = bf16[2,128,512]{2,1,0:T(8,128)(2,1)S(1)} collective-permute-done((bf16[2,128,512]{2,1,0:T(8,128)(2,1)S(1)}, bf16[2,128,512]{2,1,0:T(8,128)(2,1)S(1)}, u32[]{:S(2)}, u32[]{:S(2)}) %collective-permute-start.34) | collective-permute-done | bytes 262176 | tf_op jit(solution)/shard_map/ppermute | solution.py:70
  253.0 4.7 %collective-permute-start.36 = (f32[128,512]{1,0:T(8,128)S(1)}, f32[128,512]{1,0:T(8,128)S(1)}, u32[]{:S(2)}, u32[]{:S(2)}) collective-permute-start(f32[128,512]{1,0:T(8,128)S(1)} %fusion.41), channel_id=1, source_target_pairs={{0,1},{1,0},{2,3},{3,2},{4,5},{5,4},{6,7},{7,6},{8,9},{9,8},{10,11... | collective-permute-start | bytes 786440 | tf_op jit(solution)/shard_map/ppermute | solution.py:71
  (117 shorter events, 74.5 us)
Async XLA Ops:
  0.0 11.7 %collective-permute-start = (bf16[128,512]{1,0:T(8,128)(2,1)}, bf16[128,512]{1,0:T(8,128)(2,1)S(1)}, u32[]{:S(2)}, u32[]{:S(2)}) collective-permute-start(bf16[128,512]{1,0:T(8,128)(2,1)} %bitcast.538), channel_id=1, source_target_pairs={{0,8},{8,16},{16,24},{24,32},{32,40},{40,48},{48,56},{56,64},{64,7... | collective-permute-start | bytes 393224 | tf_op jit(solution)/shard_map/ppermute | solution.py:10
  5.0 6.8 %collective-permute-start.1 = (bf16[128,512]{1,0:T(8,128)(2,1)}, bf16[128,512]{1,0:T(8,128)(2,1)S(1)}, u32[]{:S(2)}, u32[]{:S(2)}) collective-permute-start(bf16[128,512]{1,0:T(8,128)(2,1)} %bitcast.539), channel_id=1, source_target_pairs={{8,0},{16,8},{24,16},{32,24},{40,32},{48,40},{56,48},{64,56},{72,6... | collective-permute-start | bytes 393224 | tf_op jit(solution)/shard_map/ppermute | solution.py:10
  11.7 15.4 %collective-permute-start.5 = (bf16[6,128,4,3,128]{4,1,0,3,2:T(8,128)(2,1)S(1)}, bf16[6,128,4,3,128]{4,1,0,3,2:T(8,128)(2,1)S(1)}, u32[]{:S(2)}, u32[]{:S(2)}) collective-permute-start(bf16[6,128,4,3,128]{4,1,0,3,2:T(8,128)(2,1)S(1)} %pad_maximum_fusion.1), channel_id=1, source_target_pairs={{0,1},{1,0},{2,3},{3,2},{4,5},{5,4},{6,7},{7,6},{8,9},{9,8},{10,11... | collective-permute-start | bytes 7077896 | tf_op jit(solution)/shard_map/ppermute | solution.py:46
  18.7 14.2 %collective-permute-start.4 = (bf16[3,128,512]{2,1,0:T(8,128)(2,1)S(1)}, bf16[3,128,512]{2,1,0:T(8,128)(2,1)S(1)}, u32[]{:S(2)}, u32[]{:S(2)}) collective-permute-start(bf16[3,128,512]{2,1,0:T(8,128)(2,1)S(1)} %pad_maximum_fusion.2), channel_id=1, source_target_pairs={{0,4},{1,5},{2,6},{3,7},{4,0},{5,1},{6,2},{7,3},{8,12},{9,13},{10,... | collective-permute-start | bytes 1179656 | tf_op jit(solution)/shard_map/ppermute | solution.py:70
  21.6 18.0 %collective-permute-start.3 = (bf16[3,128,512]{2,1,0:T(8,128)(2,1)S(1)}, bf16[3,128,512]{2,1,0:T(8,128)(2,1)S(1)}, u32[]{:S(2)}, u32[]{:S(2)}) collective-permute-start(bf16[3,128,512]{2,1,0:T(8,128)(2,1)S(1)} %pad_maximum_fusion.2), channel_id=1, source_target_pairs={{0,6},{1,7},{2,0},{3,1},{4,2},{5,3},{6,4},{7,5},{8,14},{9,15},{10,... | collective-permute-start | bytes 1179656 | tf_op jit(solution)/shard_map/ppermute | solution.py:70
  24.4 17.2 %collective-permute-start.2 = (bf16[3,128,512]{2,1,0:T(8,128)(2,1)S(1)}, bf16[3,128,512]{2,1,0:T(8,128)(2,1)S(1)}, u32[]{:S(2)}, u32[]{:S(2)}) collective-permute-start(bf16[3,128,512]{2,1,0:T(8,128)(2,1)S(1)} %pad_maximum_fusion.2), channel_id=1, source_target_pairs={{0,2},{1,3},{2,4},{3,5},{4,6},{5,7},{6,0},{7,1},{8,10},{9,11},{10,... | collective-permute-start | bytes 1179656 | tf_op jit(solution)/shard_map/ppermute | solution.py:70
  45.8 9.2 %collective-permute-start.8 = (bf16[128,512]{1,0:T(8,128)(2,1)S(1)}, bf16[128,512]{1,0:T(8,128)(2,1)S(1)}, u32[]{:S(2)}, u32[]{:S(2)}) collective-permute-start(bf16[128,512]{1,0:T(8,128)(2,1)S(1)} %fusion.47), channel_id=1, source_target_pairs={{16,0},{24,8},{32,16},{40,24},{48,32},{56,40},{64,48},{72,56},{80,... | collective-permute-start | bytes 393224 | tf_op jit(solution)/shard_map/ppermute | solution.py:10
  47.1 8.8 %collective-permute-start.7 = (bf16[128,512]{1,0:T(8,128)(2,1)S(1)}, bf16[128,512]{1,0:T(8,128)(2,1)S(1)}, u32[]{:S(2)}, u32[]{:S(2)}) collective-permute-start(bf16[128,512]{1,0:T(8,128)(2,1)S(1)} %fusion.47), channel_id=1, source_target_pairs={{0,16},{8,24},{16,32},{24,40},{32,48},{40,56},{48,64},{56,72},{64,... | collective-permute-start | bytes 393224 | tf_op jit(solution)/shard_map/ppermute | solution.py:10
  55.9 12.1 %collective-permute-start.11 = (bf16[3,128,512]{2,1,0:T(8,128)(2,1)S(1)}, bf16[3,128,512]{2,1,0:T(8,128)(2,1)S(1)}, u32[]{:S(2)}, u32[]{:S(2)}) collective-permute-start(bf16[3,128,512]{2,1,0:T(8,128)(2,1)S(1)} %pad_maximum_fusion.3), channel_id=1, source_target_pairs={{0,4},{1,5},{2,6},{3,7},{4,0},{5,1},{6,2},{7,3},{8,12},{9,13},{10,... | collective-permute-start | bytes 1179656 | tf_op jit(solution)/shard_map/ppermute | solution.py:70
  60.2 17.5 %collective-permute-start.10 = (bf16[3,128,512]{2,1,0:T(8,128)(2,1)S(1)}, bf16[3,128,512]{2,1,0:T(8,128)(2,1)S(1)}, u32[]{:S(2)}, u32[]{:S(2)}) collective-permute-start(bf16[3,128,512]{2,1,0:T(8,128)(2,1)S(1)} %pad_maximum_fusion.3), channel_id=1, source_target_pairs={{0,6},{1,7},{2,0},{3,1},{4,2},{5,3},{6,4},{7,5},{8,14},{9,15},{10,... | collective-permute-start | bytes 1179656 | tf_op jit(solution)/shard_map/ppermute | solution.py:70
  63.3 14.7 %collective-permute-start.9 = (bf16[3,128,512]{2,1,0:T(8,128)(2,1)S(1)}, bf16[3,128,512]{2,1,0:T(8,128)(2,1)S(1)}, u32[]{:S(2)}, u32[]{:S(2)}) collective-permute-start(bf16[3,128,512]{2,1,0:T(8,128)(2,1)S(1)} %pad_maximum_fusion.3), channel_id=1, source_target_pairs={{0,2},{1,3},{2,4},{3,5},{4,6},{5,7},{6,0},{7,1},{8,10},{9,11},{10,... | collective-permute-start | bytes 1179656 | tf_op jit(solution)/shard_map/ppermute | solution.py:70
  83.6 16.7 %collective-permute-start.14 = (bf16[128,512]{1,0:T(8,128)(2,1)S(1)}, bf16[128,512]{1,0:T(8,128)(2,1)S(1)}, u32[]{:S(2)}, u32[]{:S(2)}) collective-permute-start(bf16[128,512]{1,0:T(8,128)(2,1)S(1)} %fusion.46), channel_id=1, source_target_pairs={{32,0},{40,8},{48,16},{56,24},{64,32},{72,40},{80,48},{88,56},{96,... | collective-permute-start | bytes 393224 | tf_op jit(solution)/shard_map/ppermute | solution.py:10
  84.9 21.7 %collective-permute-start.13 = (bf16[128,512]{1,0:T(8,128)(2,1)S(1)}, bf16[128,512]{1,0:T(8,128)(2,1)S(1)}, u32[]{:S(2)}, u32[]{:S(2)}) collective-permute-start(bf16[128,512]{1,0:T(8,128)(2,1)S(1)} %fusion.46), channel_id=1, source_target_pairs={{0,32},{8,40},{16,48},{24,56},{32,64},{40,72},{48,80},{56,88},{64,... | collective-permute-start | bytes 393224 | tf_op jit(solution)/shard_map/ppermute | solution.py:10
  106.6 13.6 %collective-permute-start.17 = (bf16[3,128,512]{2,1,0:T(8,128)(2,1)S(1)}, bf16[3,128,512]{2,1,0:T(8,128)(2,1)S(1)}, u32[]{:S(2)}, u32[]{:S(2)}) collective-permute-start(bf16[3,128,512]{2,1,0:T(8,128)(2,1)S(1)} %pad_maximum_fusion.4), channel_id=1, source_target_pairs={{0,4},{1,5},{2,6},{3,7},{4,0},{5,1},{6,2},{7,3},{8,12},{9,13},{10,... | collective-permute-start | bytes 1179656 | tf_op jit(solution)/shard_map/ppermute | solution.py:70
  110.7 18.0 %collective-permute-start.16 = (bf16[3,128,512]{2,1,0:T(8,128)(2,1)S(1)}, bf16[3,128,512]{2,1,0:T(8,128)(2,1)S(1)}, u32[]{:S(2)}, u32[]{:S(2)}) collective-permute-start(bf16[3,128,512]{2,1,0:T(8,128)(2,1)S(1)} %pad_maximum_fusion.4), channel_id=1, source_target_pairs={{0,6},{1,7},{2,0},{3,1},{4,2},{5,3},{6,4},{7,5},{8,14},{9,15},{10,... | collective-permute-start | bytes 1179656 | tf_op jit(solution)/shard_map/ppermute | solution.py:70
  113.9 15.1 %collective-permute-start.15 = (bf16[3,128,512]{2,1,0:T(8,128)(2,1)S(1)}, bf16[3,128,512]{2,1,0:T(8,128)(2,1)S(1)}, u32[]{:S(2)}, u32[]{:S(2)}) collective-permute-start(bf16[3,128,512]{2,1,0:T(8,128)(2,1)S(1)} %pad_maximum_fusion.4), channel_id=1, source_target_pairs={{0,2},{1,3},{2,4},{3,5},{4,6},{5,7},{6,0},{7,1},{8,10},{9,11},{10,... | collective-permute-start | bytes 1179656 | tf_op jit(solution)/shard_map/ppermute | solution.py:70
  134.0 12.0 %collective-permute-start.20 = (bf16[128,512]{1,0:T(8,128)(2,1)S(1)}, bf16[128,512]{1,0:T(8,128)(2,1)S(1)}, u32[]{:S(2)}, u32[]{:S(2)}) collective-permute-start(bf16[128,512]{1,0:T(8,128)(2,1)S(1)} %fusion.45), channel_id=1, source_target_pairs={{64,0},{72,8},{80,16},{88,24},{96,32},{104,40},{112,48},{120,56},{... | collective-permute-start | bytes 393224 | tf_op jit(solution)/shard_map/ppermute | solution.py:10
  135.3 11.5 %collective-permute-start.19 = (bf16[128,512]{1,0:T(8,128)(2,1)S(1)}, bf16[128,512]{1,0:T(8,128)(2,1)S(1)}, u32[]{:S(2)}, u32[]{:S(2)}) collective-permute-start(bf16[128,512]{1,0:T(8,128)(2,1)S(1)} %fusion.45), channel_id=1, source_target_pairs={{0,64},{8,72},{16,80},{24,88},{32,96},{40,104},{48,112},{56,120},{... | collective-permute-start | bytes 393224 | tf_op jit(solution)/shard_map/ppermute | solution.py:10
  146.9 12.8 %collective-permute-start.23 = (bf16[3,128,512]{2,1,0:T(8,128)(2,1)S(1)}, bf16[3,128,512]{2,1,0:T(8,128)(2,1)S(1)}, u32[]{:S(2)}, u32[]{:S(2)}) collective-permute-start(bf16[3,128,512]{2,1,0:T(8,128)(2,1)S(1)} %pad_maximum_fusion.5), channel_id=1, source_target_pairs={{0,4},{1,5},{2,6},{3,7},{4,0},{5,1},{6,2},{7,3},{8,12},{9,13},{10,... | collective-permute-start | bytes 1179656 | tf_op jit(solution)/shard_map/ppermute | solution.py:70
  150.7 18.0 %collective-permute-start.22 = (bf16[3,128,512]{2,1,0:T(8,128)(2,1)S(1)}, bf16[3,128,512]{2,1,0:T(8,128)(2,1)S(1)}, u32[]{:S(2)}, u32[]{:S(2)}) collective-permute-start(bf16[3,128,512]{2,1,0:T(8,128)(2,1)S(1)} %pad_maximum_fusion.5), channel_id=1, source_target_pairs={{0,6},{1,7},{2,0},{3,1},{4,2},{5,3},{6,4},{7,5},{8,14},{9,15},{10,... | collective-permute-start | bytes 1179656 | tf_op jit(solution)/shard_map/ppermute | solution.py:70
  154.2 14.7 %collective-permute-start.21 = (bf16[3,128,512]{2,1,0:T(8,128)(2,1)S(1)}, bf16[3,128,512]{2,1,0:T(8,128)(2,1)S(1)}, u32[]{:S(2)}, u32[]{:S(2)}) collective-permute-start(bf16[3,128,512]{2,1,0:T(8,128)(2,1)S(1)} %pad_maximum_fusion.5), channel_id=1, source_target_pairs={{0,2},{1,3},{2,4},{3,5},{4,6},{5,7},{6,0},{7,1},{8,10},{9,11},{10,... | collective-permute-start | bytes 1179656 | tf_op jit(solution)/shard_map/ppermute | solution.py:70
  174.3 11.5 %collective-permute-start.26 = (bf16[128,512]{1,0:T(8,128)(2,1)S(1)}, bf16[128,512]{1,0:T(8,128)(2,1)S(1)}, u32[]{:S(2)}, u32[]{:S(2)}) collective-permute-start(bf16[128,512]{1,0:T(8,128)(2,1)S(1)} %fusion.44), channel_id=1, source_target_pairs={{128,0},{136,8},{144,16},{152,24},{160,32},{168,40},{176,48},{184,... | collective-permute-start | bytes 393224 | tf_op jit(solution)/shard_map/ppermute | solution.py:10
  175.6 10.2 %collective-permute-start.25 = (bf16[128,512]{1,0:T(8,128)(2,1)S(1)}, bf16[128,512]{1,0:T(8,128)(2,1)S(1)}, u32[]{:S(2)}, u32[]{:S(2)}) collective-permute-start(bf16[128,512]{1,0:T(8,128)(2,1)S(1)} %fusion.44), channel_id=1, source_target_pairs={{0,128},{8,136},{16,144},{24,152},{32,160},{40,168},{48,176},{56,1... | collective-permute-start | bytes 393224 | tf_op jit(solution)/shard_map/ppermute | solution.py:10
  185.8 13.1 %collective-permute-start.29 = (bf16[3,128,512]{2,1,0:T(8,128)(2,1)S(1)}, bf16[3,128,512]{2,1,0:T(8,128)(2,1)S(1)}, u32[]{:S(2)}, u32[]{:S(2)}) collective-permute-start(bf16[3,128,512]{2,1,0:T(8,128)(2,1)S(1)} %pad_maximum_fusion.6), channel_id=1, source_target_pairs={{0,4},{1,5},{2,6},{3,7},{4,0},{5,1},{6,2},{7,3},{8,12},{9,13},{10,... | collective-permute-start | bytes 1179656 | tf_op jit(solution)/shard_map/ppermute | solution.py:70
  189.4 18.2 %collective-permute-start.28 = (bf16[3,128,512]{2,1,0:T(8,128)(2,1)S(1)}, bf16[3,128,512]{2,1,0:T(8,128)(2,1)S(1)}, u32[]{:S(2)}, u32[]{:S(2)}) collective-permute-start(bf16[3,128,512]{2,1,0:T(8,128)(2,1)S(1)} %pad_maximum_fusion.6), channel_id=1, source_target_pairs={{0,6},{1,7},{2,0},{3,1},{4,2},{5,3},{6,4},{7,5},{8,14},{9,15},{10,... | collective-permute-start | bytes 1179656 | tf_op jit(solution)/shard_map/ppermute | solution.py:70
  193.1 14.8 %collective-permute-start.27 = (bf16[3,128,512]{2,1,0:T(8,128)(2,1)S(1)}, bf16[3,128,512]{2,1,0:T(8,128)(2,1)S(1)}, u32[]{:S(2)}, u32[]{:S(2)}) collective-permute-start(bf16[3,128,512]{2,1,0:T(8,128)(2,1)S(1)} %pad_maximum_fusion.6), channel_id=1, source_target_pairs={{0,2},{1,3},{2,4},{3,5},{4,6},{5,7},{6,0},{7,1},{8,10},{9,11},{10,... | collective-permute-start | bytes 1179656 | tf_op jit(solution)/shard_map/ppermute | solution.py:70
  213.2 13.2 %collective-permute-start.31 = (bf16[128,512]{1,0:T(8,128)(2,1)S(1)}, bf16[128,512]{1,0:T(8,128)(2,1)S(1)}, u32[]{:S(2)}, u32[]{:S(2)}) collective-permute-start(bf16[128,512]{1,0:T(8,128)(2,1)S(1)} %fusion.43), channel_id=1, source_target_pairs={{0,256},{8,264},{16,272},{24,280},{32,288},{40,296},{48,304},{56,3... | collective-permute-start | bytes 393224 | tf_op jit(solution)/shard_map/ppermute | solution.py:10
  223.9 12.4 %collective-permute-start.32 = (bf16[128,512]{1,0:T(8,128)(2,1)S(1)}, bf16[128,512]{1,0:T(8,128)(2,1)S(1)}, u32[]{:S(2)}, u32[]{:S(2)}) collective-permute-start(bf16[128,512]{1,0:T(8,128)(2,1)S(1)} %fusion.43), channel_id=1, source_target_pairs={{256,0},{264,8},{272,16},{280,24},{288,32},{296,40},{304,48},{312,... | collective-permute-start | bytes 393224 | tf_op jit(solution)/shard_map/ppermute | solution.py:10
  236.5 9.9 %collective-permute-start.35 = (bf16[2,128,512]{2,1,0:T(8,128)(2,1)S(1)}, bf16[2,128,512]{2,1,0:T(8,128)(2,1)S(1)}, u32[]{:S(2)}, u32[]{:S(2)}) collective-permute-start(bf16[2,128,512]{2,1,0:T(8,128)(2,1)S(1)} %pad_maximum_fusion.7), channel_id=1, source_target_pairs={{0,4},{1,5},{2,6},{3,7},{4,0},{5,1},{6,2},{7,3},{8,12},{9,13},{10,... | collective-permute-start | bytes 786440 | tf_op jit(solution)/shard_map/ppermute | solution.py:70
  239.9 10.3 %collective-permute-start.34 = (bf16[2,128,512]{2,1,0:T(8,128)(2,1)S(1)}, bf16[2,128,512]{2,1,0:T(8,128)(2,1)S(1)}, u32[]{:S(2)}, u32[]{:S(2)}) collective-permute-start(bf16[2,128,512]{2,1,0:T(8,128)(2,1)S(1)} %pad_maximum_fusion.7), channel_id=1, source_target_pairs={{0,6},{1,7},{2,0},{3,1},{4,2},{5,3},{6,4},{7,5},{8,14},{9,15},{10,... | collective-permute-start | bytes 786440 | tf_op jit(solution)/shard_map/ppermute | solution.py:70
  243.6 9.0 %collective-permute-start.33 = (bf16[2,128,512]{2,1,0:T(8,128)(2,1)S(1)}, bf16[2,128,512]{2,1,0:T(8,128)(2,1)S(1)}, u32[]{:S(2)}, u32[]{:S(2)}) collective-permute-start(bf16[2,128,512]{2,1,0:T(8,128)(2,1)S(1)} %pad_maximum_fusion.7), channel_id=1, source_target_pairs={{0,2},{1,3},{2,4},{3,5},{4,6},{5,7},{6,0},{7,1},{8,10},{9,11},{10,... | collective-permute-start | bytes 786440 | tf_op jit(solution)/shard_map/ppermute | solution.py:70
  253.0 5.9 %collective-permute-start.36 = (f32[128,512]{1,0:T(8,128)S(1)}, f32[128,512]{1,0:T(8,128)S(1)}, u32[]{:S(2)}, u32[]{:S(2)}) collective-permute-start(f32[128,512]{1,0:T(8,128)S(1)} %fusion.41), channel_id=1, source_target_pairs={{0,1},{1,0},{2,3},{3,2},{4,5},{5,4},{6,7},{7,6},{8,9},{9,8},{10,11... | collective-permute-start | bytes 786440 | tf_op jit(solution)/shard_map/ppermute | solution.py:71
  (8 other events, 32.0 us)
